TPU v7x, 32 devices: a whole 2x2x4 slice. The times are simulated.
32 devices in a mesh: groups: 2 (over y), tiles: 4 (over z), bins: 2 (over x), vert: 2 (over core).
Axes of the slice: x: 2, y: 2, z: 4, core: 2. Of those that a mesh axis runs over, the one named last changes fastest.
Arguments:
- bin_mass: float32 [264, 32, 16, 128], P('bins', ('groups', 'tiles'), 'vert'), parts along dimension 1, may hold values from 0.25 to 4
- wind_east: float32 [32, 16, 128], P(('groups', 'tiles'), 'vert'), parts along dimension 0, may hold values from -0.7 to 0.7
- wind_north: float32 [32, 16, 128], P(('groups', 'tiles'), 'vert'), parts along dimension 0, may hold values from -0.3 to 0.3
- supersaturation: float32 [32, 16, 128], P(('groups', 'tiles'), 'vert'), parts along dimension 0, may hold values from -4 to 4
- potential_temp: float32 [32, 16, 128], P(('groups', 'tiles'), 'vert'), parts along dimension 0, may hold values from -6 to 6
- terrain_height: int32 [32, 128], P(('groups', 'tiles')), parts along dimension 0, may hold values from 0 to 3
- fall_speed: float32 [264], P('bins'), may hold values from 0.05 to 0.9
- growth_rate: float32 [264], P('bins'), may hold values from 0.05 to 0.5
- latent_factor: float32 [264], P('bins'), may hold values from 0.3 to 3
- bin_order: int32 [264], replicated, may hold values from 0 to 263, each once
- kernel_index: int32 [8, 8], replicated, may hold values from 0 to 3
- collision_kernels: bfloat16 [4, 33, 33], replicated, may hold values from -0.375 to 0.375
Outputs:
- mass_next: float32 [264, 32, 16, 128], P('bins', ('groups', 'tiles'), 'vert'), parts along dimension 1
- temp_next: float32 [32, 16, 128], P(('groups', 'tiles'), 'vert'), parts along dimension 0
- vapor_next: float32 [32, 16, 128], P(('groups', 'tiles'), 'vert'), parts along dimension 0
There are 2 independent parts, one for each index of `groups`. A program takes and returns all parts, laid end to end along the dimension named above; an argument that names none is the same for every part. Nothing has to cross between parts.
Inputs may be any that keep to these rules, and one draw needn't show every extreme that they name: `bin_order`: each bin number appears once.
All inputs are finite; a program needn't handle non-finite values.
Results may differ from a plain program's by a relative error of at most 0.0021.
Values may be sent and summed in bfloat16 or wider, within the bound.
No kernel may reach another device: no remote copies, remote signals or barrier semaphores. Data moves between devices by JAX's collectives and lax.ppermute only.
A program may use at most 64 MiB of HBM per device.

v0:
```python
import jax
import jax.numpy as jnp
from jax import lax
from jax.sharding import PartitionSpec as P

SUB = 8


collision_rate = 0.001
condense_rate = 0.02
heating_gain = 0.03
growth_gain = 0.5
highest = lax.Precision.HIGHEST


def extended_2(array, sides, width):
    for axis, dim in sides:
        size, length = (lax.axis_size(axis), array.shape[dim])
        up = [(i, (i + 1) % size) for i in range(size - 1)]
        down = [(j, i) for i, j in up]
        last = lax.slice_in_dim(array, length - width, length, axis=dim)
        first = lax.slice_in_dim(array, 0, width, axis=dim)
        before = lax.ppermute(last, axis, up)
        after = lax.ppermute(first, axis, down)
        array = jnp.concatenate([before, array, after], axis=dim)
    return array


def shifted(block, axis, distance):
    devices = range(lax.axis_size(axis))
    route = [(i - distance, i) for i in devices if i - distance in devices]
    return lax.ppermute(block, axis, route)


def tendency(center_cells, left_cells, right_cells, wind_x, wind_y):
    south_cells = jnp.roll(center_cells, 1, axis=3)
    north_cells = jnp.roll(center_cells, -1, axis=3)
    along_x = jnp.maximum(wind_x, 0.0) * (center_cells - left_cells) + jnp.minimum(wind_x, 0.0) * (
        right_cells - center_cells
    )
    along_y = jnp.maximum(wind_y, 0.0) * (center_cells - south_cells) + jnp.minimum(wind_y, 0.0) * (
        north_cells - center_cells
    )
    return -along_x - along_y


def coupling_table(bin_order, kernel_index, collision_kernels):
    class_count = kernel_index.shape[0]
    table_count = collision_kernels.shape[0]
    class_bins = collision_kernels.shape[1]
    bin_class = bin_order // class_bins
    bin_within = bin_order % class_bins
    kernel_pick = (kernel_index[:, :, None] == lax.iota(jnp.int32, table_count)).astype(jnp.float32)
    block_table = jnp.einsum(
        "ack,kmn->acmn", kernel_pick, collision_kernels.astype(jnp.float32), precision=highest
    )
    class_hot = (bin_class[:, None] == lax.iota(jnp.int32, class_count)).astype(jnp.float32)
    within_hot = (bin_within[:, None] == lax.iota(jnp.int32, class_bins)).astype(jnp.float32)
    row_table = jnp.einsum("bm,acmn->bacn", within_hot, block_table, precision=highest)
    row_table = jnp.einsum("ba,bacn->bcn", class_hot, row_table, precision=highest)
    coupling = jnp.einsum("bcn,dc,dn->bd", row_table, class_hot, within_hot, precision=highest)
    same_class = jnp.dot(class_hot, class_hot.T, precision=highest)
    return jnp.concatenate([coupling, same_class], axis=0).astype(jnp.bfloat16)


def collide(table, first):
    all_bins = table.shape[1]
    iterate = first
    for substep in range(SUB):
        products = jnp.dot(table, iterate.astype(jnp.bfloat16), preferred_element_type=jnp.float32)
        iterate = iterate + collision_rate * products[all_bins:] * products[:all_bins]
    return (iterate - first).astype(jnp.bfloat16)


def spread_collision(grown, bin_order, kernel_index, collision_kernels):
    local_bins, width_x, width_z, width_y = grown.shape
    table = coupling_table(bin_order, kernel_index, collision_kernels)
    all_bins = table.shape[1]
    start = grown.astype(jnp.bfloat16).reshape(local_bins, width_x, width_z * width_y)
    cell_block = lax.all_to_all(start, "bins", split_axis=2, concat_axis=0, tiled=True)
    block_shape = cell_block.shape
    first = cell_block.reshape(all_bins, -1).astype(jnp.float32)
    change = collide(table, first).reshape(block_shape)
    change = lax.all_to_all(change, "bins", split_axis=0, concat_axis=2, tiled=True)
    return change.reshape(local_bins, width_x, width_z, width_y).astype(jnp.float32)


def paired_collision(grown, bin_order, kernel_index, collision_kernels):
    local_bins, width_x, width_z, width_y = grown.shape
    swap = [(0, 1), (1, 0)]
    me = lax.axis_index("bins")
    order = lax.dynamic_slice_in_dim(
        jnp.concatenate([bin_order, bin_order]), me * local_bins, 2 * local_bins
    )
    table = coupling_table(order, kernel_index, collision_kernels)
    halves = grown.astype(jnp.bfloat16).reshape(local_bins, 2, width_x // 2, width_z, width_y)
    own = lax.dynamic_index_in_dim(halves, me, axis=1, keepdims=False)
    away = lax.dynamic_index_in_dim(halves, 1 - me, axis=1, keepdims=False)
    arrived = lax.ppermute(away, "bins", swap)
    first = jnp.concatenate([own, arrived], axis=0).reshape(2 * local_bins, -1).astype(jnp.float32)
    change = collide(table, first).reshape(2 * local_bins, width_x // 2, width_z, width_y)
    back = lax.ppermute(change[local_bins:], "bins", swap)
    pair = jnp.stack([change[:local_bins], back], axis=1)
    pair = jnp.where(me == 0, pair, pair[:, ::-1])
    return pair.reshape(local_bins, width_x, width_z, width_y).astype(jnp.float32)


def body(
    bin_mass,
    wind_east,
    wind_north,
    supersaturation,
    potential_temp,
    terrain_height,
    fall_speed,
    growth_rate,
    latent_factor,
    bin_order,
    kernel_index,
    collision_kernels,
):
    local_bins, width_x, width_z, width_y = bin_mass.shape
    levels = lax.axis_index("vert") * width_z + lax.iota(jnp.int32, width_z)
    open_cells = (levels[None, :, None] >= terrain_height[:, None, :]).astype(jnp.float32)
    wind_x = wind_east * open_cells
    wind_y = wind_north * open_cells
    section_weights = (1.0 / 3.0, 0.5, 1.0)
    section_field = bin_mass
    for weight_now in section_weights:
        extended = extended_2(section_field, (("tiles", 1),), 1)
        section_field = bin_mass + weight_now * tendency(
            extended[:, 1:-1], extended[:, :-2], extended[:, 2:], wind_x, wind_y
        )
    rim_above = shifted(section_field[:, :, :1, :], "vert", -1)
    from_above = jnp.concatenate([section_field[:, :, 1:], rim_above], axis=2)
    speed = fall_speed[:, None, None, None]
    settled = (1.0 - speed) * section_field + speed * from_above
    growth = growth_rate[:, None, None, None]
    partial = (
        jnp.sum(growth * settled, axis=0),
        jnp.sum(latent_factor[:, None, None, None] * growth * settled, axis=0),
    )
    bin_devices = lax.axis_size("bins")
    if bin_devices == 2:
        swap = [(0, 1), (1, 0)]
        other = lax.ppermute(jnp.stack(partial), "bins", swap)
        uptake, heating = partial[0] + other[0], partial[1] + other[1]
    else:
        uptake, heating = lax.psum(partial, "bins")
    midway = supersaturation * jnp.exp(-0.5 * condense_rate * uptake)
    grown = settled * (1.0 + growth_gain * growth * midway)
    temp_next = potential_temp + heating_gain * midway * heating
    vapor_next = supersaturation * jnp.exp(-condense_rate * uptake)
    if bin_devices == 2 and width_x % 2 == 0:
        change = paired_collision(grown, bin_order, kernel_index, collision_kernels)
    else:
        change = spread_collision(grown, bin_order, kernel_index, collision_kernels)
    mass_next = (grown + change) * open_cells
    return (mass_next, temp_next, vapor_next)


def solution(mesh):
    return jax.shard_map(
        body,
        mesh=mesh,
        in_specs=(
            P("bins", ("groups", "tiles"), "vert", None),
            P(("groups", "tiles"), "vert", None),
            P(("groups", "tiles"), "vert", None),
            P(("groups", "tiles"), "vert", None),
            P(("groups", "tiles"), "vert", None),
            P(("groups", "tiles"), None),
            P("bins"),
            P("bins"),
            P("bins"),
            P(),
            P(),
            P(),
        ),
        out_specs=(
            P("bins", ("groups", "tiles"), "vert", None),
            P(("groups", "tiles"), "vert", None),
            P(("groups", "tiles"), "vert", None),
        ),
        check_vma=False,
    )
```

profile of v0, /device:TPU:0, one launch (start us, length us, event | category | flops | bytes accessed | tf_op | source)
XLA Modules:
  0.0 124.8 jit_solution(14686874392274673735)
XLA Ops:
  0.7 2.4 %fusion.99 = (f32[132,1,8,128]{3,2,1,0:T(8,128)}, f32[132,1,8,128]{3,2,1,0:T(8,128)}) fusion(f32[132,4,8,128]{3,2,1,0:T(8,128)} %param.12), kind=kLoop, calls=%fused_computation.158 | loop fusion | bytes 2162688 | tf_op jit(solution)/shard_map/slice | solution.py:21
  3.1 4.9 %collective-permute-start = (f32[132,1,8,128]{3,2,1,0:T(8,128)}, f32[132,1,8,128]{3,2,1,0:T(8,128)S(1)}, u32[]{:S(2)}, u32[]{:S(2)}) collective-permute-start(f32[132,1,8,128]{3,2,1,0:T(8,128)} %get-tuple-element.27), channel_id=1, source_target_pairs={{0,4},{4,8},{8,12},{1,5},{5,9},{9,13},{2,6},{6,10},{10,14},{3,7},{... | collective-permute-start | bytes 1622024 | tf_op jit(solution)/shard_map/ppermute | solution.py:23
  8.1 1.3 %collective-permute-start.1 = (f32[132,1,8,128]{3,2,1,0:T(8,128)}, f32[132,1,8,128]{3,2,1,0:T(8,128)S(1)}, u32[]{:S(2)}, u32[]{:S(2)}) collective-permute-start(f32[132,1,8,128]{3,2,1,0:T(8,128)} %get-tuple-element.28), channel_id=1, source_target_pairs={{4,0},{8,4},{12,8},{5,1},{9,5},{13,9},{6,2},{10,6},{14,10},{7,3},{... | collective-permute-start | bytes 1622024 | tf_op jit(solution)/shard_map/ppermute | solution.py:24
  9.4 2.8 %fusion.97 = (f32[132,4,8,127]{3,2,1,0:T(8,128)}, f32[132,4,8,127]{3,2,1,0:T(8,128)}) fusion(f32[132,4,8,128]{3,2,1,0:T(8,128)S(1)} %copy-done.2), kind=kLoop, calls=%fused_computation.156 | loop fusion | bytes 8583168 | tf_op jit(solution)/shard_map/jit(_roll_static)/slice | solution.py:37
  13.4 6.5 %collective-permute-done = f32[132,1,8,128]{3,2,1,0:T(8,128)S(1)} collective-permute-done((f32[132,1,8,128]{3,2,1,0:T(8,128)}, f32[132,1,8,128]{3,2,1,0:T(8,128)S(1)}, u32[]{:S(2)}, u32[]{:S(2)}) %collective-permute-start) | collective-permute-done | bytes 540704 | tf_op jit(solution)/shard_map/ppermute | solution.py:23
  19.9 4.0 %collective-permute-done.1 = f32[132,1,8,128]{3,2,1,0:T(8,128)S(1)} collective-permute-done((f32[132,1,8,128]{3,2,1,0:T(8,128)}, f32[132,1,8,128]{3,2,1,0:T(8,128)S(1)}, u32[]{:S(2)}, u32[]{:S(2)}) %collective-permute-start.1) | collective-permute-done | bytes 540704 | tf_op jit(solution)/shard_map/ppermute | solution.py:24
  23.9 2.1 %fusion.31 = f32[132,4,8,128]{3,2,1,0:T(8,128)S(1)} fusion(f32[132,4,8,128]{3,2,1,0:T(8,128)S(1)} %copy-done.2, f32[132,1,8,128]{3,2,1,0:T(8,128)S(1)} %collective-permute-done.1, f32[132,1,8,128]{3,2,1,0:T(8,128)S(1)} %collective-permute-done, f32[132,4,8,127]{3,2,1,0:T(8,128)S(1)} %copy-done.4, f32[132,4,8,1]{3,2,1,0:T(8,128)S(1)} %get-tuple-element.26, ...), kind=kLoop, calls=%fused_computation.55 | loop fusion | flops 9732096 | bytes 9797632 | tf_op jit(solution)/shard_map/add | solution.py:131
  26.1 3.5 %collective-permute-start.2 = (f32[132,1,8,128]{3,2,1,0:T(8,128)S(1)}, f32[132,1,8,128]{3,2,1,0:T(8,128)S(1)}, u32[]{:S(2)}, u32[]{:S(2)}) collective-permute-start(f32[132,1,8,128]{3,2,1,0:T(8,128)S(1)} %get-tuple-element.21), channel_id=1, source_target_pairs={{0,4},{4,8},{8,12},{1,5},{5,9},{9,13},{2,6},{6,10},{10,14},{3,7},{... | collective-permute-start | bytes 1622024 | tf_op jit(solution)/shard_map/ppermute | solution.py:23
  29.6 1.3 %collective-permute-start.3 = (f32[132,1,8,128]{3,2,1,0:T(8,128)S(1)}, f32[132,1,8,128]{3,2,1,0:T(8,128)S(1)}, u32[]{:S(2)}, u32[]{:S(2)}) collective-permute-start(f32[132,1,8,128]{3,2,1,0:T(8,128)S(1)} %get-tuple-element.22), channel_id=1, source_target_pairs={{4,0},{8,4},{12,8},{5,1},{9,5},{13,9},{6,2},{10,6},{14,10},{7,3},{... | collective-permute-start | bytes 1622024 | tf_op jit(solution)/shard_map/ppermute | solution.py:24
  31.6 0.8 fusion.95
  32.4 7.5 %collective-permute-done.2 = f32[132,1,8,128]{3,2,1,0:T(8,128)S(1)} collective-permute-done((f32[132,1,8,128]{3,2,1,0:T(8,128)S(1)}, f32[132,1,8,128]{3,2,1,0:T(8,128)S(1)}, u32[]{:S(2)}, u32[]{:S(2)}) %collective-permute-start.2) | collective-permute-done | bytes 540704 | tf_op jit(solution)/shard_map/ppermute | solution.py:23
  39.9 4.1 %collective-permute-done.3 = f32[132,1,8,128]{3,2,1,0:T(8,128)S(1)} collective-permute-done((f32[132,1,8,128]{3,2,1,0:T(8,128)S(1)}, f32[132,1,8,128]{3,2,1,0:T(8,128)S(1)}, u32[]{:S(2)}, u32[]{:S(2)}) %collective-permute-start.3) | collective-permute-done | bytes 540704 | tf_op jit(solution)/shard_map/ppermute | solution.py:24
  44.0 2.3 %fusion.22 = f32[132,4,8,128]{3,2,1,0:T(8,128)S(1)} fusion(f32[132,4,8,128]{3,2,1,0:T(8,128)S(1)} %copy-done.2, f32[132,4,8,128]{3,2,1,0:T(8,128)S(1)} %fusion.31, f32[132,1,8,128]{3,2,1,0:T(8,128)S(1)} %collective-permute-done.3, f32[132,1,8,128]{3,2,1,0:T(8,128)S(1)} %collective-permute-done.2, f32[132,4,8,127]{3,2,1,0:T(8,128)S(1)} %get-tuple-element.18, ...), kind=kLoop, calls=%fused_computation.44 | loop fusion | flops 9732096 | bytes 11960320 | tf_op jit(solution)/shard_map/add | solution.py:131
  46.4 3.5 %collective-permute-start.4 = (f32[132,1,8,128]{3,2,1,0:T(8,128)S(1)}, f32[132,1,8,128]{3,2,1,0:T(8,128)S(1)}, u32[]{:S(2)}, u32[]{:S(2)}) collective-permute-start(f32[132,1,8,128]{3,2,1,0:T(8,128)S(1)} %get-tuple-element.15), channel_id=1, source_target_pairs={{0,4},{4,8},{8,12},{1,5},{5,9},{9,13},{2,6},{6,10},{10,14},{3,7},{... | collective-permute-start | bytes 1622024 | tf_op jit(solution)/shard_map/ppermute | solution.py:23
  49.9 1.3 %collective-permute-start.5 = (f32[132,1,8,128]{3,2,1,0:T(8,128)S(1)}, f32[132,1,8,128]{3,2,1,0:T(8,128)S(1)}, u32[]{:S(2)}, u32[]{:S(2)}) collective-permute-start(f32[132,1,8,128]{3,2,1,0:T(8,128)S(1)} %get-tuple-element.16), channel_id=1, source_target_pairs={{4,0},{8,4},{12,8},{5,1},{9,5},{13,9},{6,2},{10,6},{14,10},{7,3},{... | collective-permute-start | bytes 1622024 | tf_op jit(solution)/shard_map/ppermute | solution.py:24
  51.2 0.8 fusion.91
  51.9 0.8 fusion.92
  52.7 6.3 %collective-permute-done.4 = f32[132,1,8,128]{3,2,1,0:T(8,128)S(1)} collective-permute-done((f32[132,1,8,128]{3,2,1,0:T(8,128)S(1)}, f32[132,1,8,128]{3,2,1,0:T(8,128)S(1)}, u32[]{:S(2)}, u32[]{:S(2)}) %collective-permute-start.4) | collective-permute-done | bytes 540704 | tf_op jit(solution)/shard_map/ppermute | solution.py:23
  58.9 4.1 %collective-permute-done.5 = f32[132,1,8,128]{3,2,1,0:T(8,128)S(1)} collective-permute-done((f32[132,1,8,128]{3,2,1,0:T(8,128)S(1)}, f32[132,1,8,128]{3,2,1,0:T(8,128)S(1)}, u32[]{:S(2)}, u32[]{:S(2)}) %collective-permute-start.5) | collective-permute-done | bytes 540704 | tf_op jit(solution)/shard_map/ppermute | solution.py:24
  63.1 2.3 %fusion.13 = f32[132,4,8,128]{3,2,1,0:T(8,128)S(1)} fusion(f32[132,4,8,128]{3,2,1,0:T(8,128)S(1)} %copy-done.2, f32[132,4,8,128]{3,2,1,0:T(8,128)S(1)} %fusion.22, f32[132,1,8,128]{3,2,1,0:T(8,128)S(1)} %collective-permute-done.5, f32[132,1,8,128]{3,2,1,0:T(8,128)S(1)} %collective-permute-done.4, f32[132,4,8,127]{3,2,1,0:T(8,128)S(1)} %get-tuple-element.12, ...), kind=kLoop, calls=%fused_computation.33 | loop fusion | flops 9191424 | bytes 11960320 | tf_op jit(solution)/shard_map/add | solution.py:131
  65.6 1.5 %collective-permute-start.6 = (f32[132,4,1,128]{3,0,2,1:T(8,128)S(1)}, f32[132,4,1,128]{3,0,2,1:T(8,128)S(1)}, u32[]{:S(2)}, u32[]{:S(2)}) collective-permute-start(f32[132,4,1,128]{3,0,2,1:T(8,128)S(1)} %copy.36), channel_id=1, source_target_pairs={{1,0},{3,2},{5,4},{7,6},{9,8},{11,10},{13,12},{15,14},{17,16},{19,... | collective-permute-start | bytes 811016 | tf_op jit(solution)/shard_map/ppermute | solution.py:32
  67.8 1.3 %collective-permute-done.6 = f32[132,4,1,128]{3,0,2,1:T(8,128)S(1)} collective-permute-done((f32[132,4,1,128]{3,0,2,1:T(8,128)S(1)}, f32[132,4,1,128]{3,0,2,1:T(8,128)S(1)}, u32[]{:S(2)}, u32[]{:S(2)}) %collective-permute-start.6) | collective-permute-done | bytes 270368 | tf_op jit(solution)/shard_map/ppermute | solution.py:32
  69.4 1.1 multiply_reduce_fusion.1
  70.4 1.6 %collective-permute-start.7 = (f32[2,4,8,128]{3,2,1,0:T(8,128)S(1)}, f32[2,4,8,128]{3,2,1,0:T(8,128)S(1)}, u32[]{:S(2)}, u32[]{:S(2)}) collective-permute-start(f32[2,4,8,128]{3,2,1,0:T(8,128)S(1)} %pad_maximum_fusion.10), channel_id=1, source_target_pairs={{0,2},{2,0},{1,3},{3,1},{4,6},{6,4},{5,7},{7,5},{8,10},{10,8},{9,1... | collective-permute-start | bytes 98312 | tf_op jit(solution)/shard_map/ppermute | solution.py:146
  72.0 2.4 %collective-permute-done.7 = f32[2,4,8,128]{3,2,1,0:T(8,128)S(1)} collective-permute-done((f32[2,4,8,128]{3,2,1,0:T(8,128)S(1)}, f32[2,4,8,128]{3,2,1,0:T(8,128)S(1)}, u32[]{:S(2)}, u32[]{:S(2)}) %collective-permute-start.7) | collective-permute-done | bytes 32800 | tf_op jit(solution)/shard_map/ppermute | solution.py:146
  75.4 1.2 dynamic-slice_bitcast_fusion.1
  76.6 1.5 %collective-permute-start.8 = (bf16[132,2,8,128]{3,2,1,0:T(8,128)(2,1)}, bf16[132,2,8,128]{3,2,1,0:T(8,128)(2,1)}, u32[]{:S(2)}, u32[]{:S(2)}) collective-permute-start(bf16[132,2,8,128]{3,2,1,0:T(8,128)(2,1)} %get-tuple-element.32), channel_id=1, source_target_pairs={{0,2},{2,0},{1,3},{3,1},{4,6},{6,4},{5,7},{7,5},{8,10},{10,8},{9,1... | collective-permute-start | bytes 1622024 | tf_op jit(solution)/shard_map/ppermute | solution.py:99
  78.1 2.0 %multiply_reduce_fusion = f32[264,8,33]{0,2,1:T(8,128)S(1)} fusion(f32[264,8]{0,1:T(8,128)S(1)} %fusion.82, f32[8,8,33,33]{3,1,2,0:T(8,128)S(1)} %fusion.69, s32[264]{0:T(512)S(1)} %get-tuple-element.38), kind=kOutput, calls=%fused_computation | convolution fusion | flops 221851072 | bytes 567072 | tf_op jit(solution)/shard_map/bm,acmn->bacn/dot_general | solution.py:59
  80.4 1.1 fusion.46
  81.5 1.6 %concatenate.72 = bf16[132,2048]{1,0:T(8,128)(2,1)S(1)} reshape(bf16[132,1,2,8,128]{4,3,2,0,1:T(8,128)(2,1)} %get-tuple-element.31) | data formatting | bytes 1081344 | tf_op jit(solution)/shard_map/concatenate | solution.py:100
  83.1 7.0 %collective-permute-done.8 = bf16[132,2,8,128]{3,2,1,0:T(8,128)(2,1)} collective-permute-done((bf16[132,2,8,128]{3,2,1,0:T(8,128)(2,1)}, bf16[132,2,8,128]{3,2,1,0:T(8,128)(2,1)}, u32[]{:S(2)}, u32[]{:S(2)}) %collective-permute-start.8) | collective-permute-done | bytes 540704 | tf_op jit(solution)/shard_map/ppermute | solution.py:99
  90.1 1.1 pad.48
  91.4 1.5 %fusion.63 = f32[528,2048]{1,0:T(8,128)S(1)} fusion(bf16[132,2048]{1,0:T(8,128)(2,1)S(1)} %bitcast.63, bf16[132,2048]{1,0:T(8,128)(2,1)S(1)} %concatenate.72, bf16[264,264]{0,1:T(8,128)(2,1)S(1)} %convolution_convert_fusion, bf16[264,264]{0,1:T(8,128)(2,1)S(1)} %fusion.46), kind=kOutput, calls=%fused_computation.109 | convolution fusion | flops 573669888 | bytes 5685504 | tf_op jit(solution)/shard_map/dot_general | solution.py:70
  92.9 1.6 %fusion.60 = f32[528,2048]{1,0:T(8,128)S(1)} fusion(f32[528,2048]{1,0:T(8,128)S(1)} %fusion.63, bf16[132,2048]{1,0:T(8,128)(2,1)S(1)} %bitcast.64, bf16[132,2048]{1,0:T(8,128)(2,1)S(1)} %concatenate.72, bf16[264,264]{0,1:T(8,128)(2,1)S(1)} %convolution_convert_fusion, bf16[264,264]{0,1:T(8,128)(2,1)S(1)} %fusion.46), kind=kOutput, calls=%fused_computation.101 | convolution fusion | flops 575832576 | bytes 10010880 | tf_op jit(solution)/shard_map/dot_general | solution.py:70
  94.5 1.1 fusion.7
  95.5 1.5 %fusion.58 = f32[528,2048]{1,0:T(8,128)S(1)} fusion(f32[264,2048]{1,0:T(8,128)S(1)} %fusion.7, bf16[264,264]{0,1:T(8,128)(2,1)S(1)} %convolution_convert_fusion, bf16[264,264]{0,1:T(8,128)(2,1)S(1)} %fusion.46), kind=kOutput, calls=%fused_computation.99 | convolution fusion | flops 572047872 | bytes 6766848 | tf_op jit(solution)/shard_map/dot_general | solution.py:70
  97.0 1.5 %fusion.56 = f32[528,2048]{1,0:T(8,128)S(1)} fusion(f32[264,2048]{1,0:T(8,128)S(1)} %fusion.7, f32[528,2048]{1,0:T(8,128)S(1)} %fusion.58, bf16[264,264]{0,1:T(8,128)(2,1)S(1)} %convolution_convert_fusion, bf16[264,264]{0,1:T(8,128)(2,1)S(1)} %fusion.46), kind=kOutput, calls=%fused_computation.97 | convolution fusion | flops 573669888 | bytes 11092224 | tf_op jit(solution)/shard_map/dot_general | solution.py:70
  98.5 1.2 fusion.5
  99.6 1.5 %fusion.54 = f32[528,2048]{1,0:T(8,128)S(1)} fusion(f32[264,2048]{1,0:T(8,128)S(1)} %fusion.5, bf16[264,264]{0,1:T(8,128)(2,1)S(1)} %convolution_convert_fusion, bf16[264,264]{0,1:T(8,128)(2,1)S(1)} %fusion.46), kind=kOutput, calls=%fused_computation.95 | convolution fusion | flops 572047872 | bytes 6766848 | tf_op jit(solution)/shard_map/dot_general | solution.py:70
  101.1 1.6 %fusion.52 = f32[528,2048]{1,0:T(8,128)S(1)} fusion(f32[264,2048]{1,0:T(8,128)S(1)} %fusion.5, f32[528,2048]{1,0:T(8,128)S(1)} %fusion.54, bf16[264,264]{0,1:T(8,128)(2,1)S(1)} %convolution_convert_fusion, bf16[264,264]{0,1:T(8,128)(2,1)S(1)} %fusion.46), kind=kOutput, calls=%fused_computation.93 | convolution fusion | flops 573669888 | bytes 11092224 | tf_op jit(solution)/shard_map/dot_general | solution.py:70
  102.7 1.2 fusion.3
  103.9 1.8 %fusion.50 = f32[528,2048]{1,0:T(8,128)S(1)} fusion(f32[264,2048]{1,0:T(8,128)S(1)} %fusion.3, bf16[264,264]{0,1:T(8,128)(2,1)S(1)} %convolution_convert_fusion, bf16[264,264]{0,1:T(8,128)(2,1)S(1)} %fusion.46), kind=kOutput, calls=%fused_computation.91 | convolution fusion | flops 572047872 | bytes 6766848 | tf_op jit(solution)/shard_map/dot_general | solution.py:70
  105.7 1.5 %fusion.48 = f32[528,2048]{1,0:T(8,128)S(1)} fusion(f32[264,2048]{1,0:T(8,128)S(1)} %fusion.3, f32[528,2048]{1,0:T(8,128)S(1)} %fusion.50, bf16[264,264]{0,1:T(8,128)(2,1)S(1)} %convolution_convert_fusion, bf16[264,264]{0,1:T(8,128)(2,1)S(1)} %fusion.46), kind=kOutput, calls=%fused_computation.89 | convolution fusion | flops 573669888 | bytes 11092224 | tf_op jit(solution)/shard_map/dot_general | solution.py:70
  107.2 1.3 %fusion = bf16[264,2048]{1,0:T(8,128)(2,1)S(1)} fusion(f32[528,2048]{1,0:T(8,128)S(1)} %fusion.48, bf16[132,2048]{1,0:T(8,128)(2,1)S(1)} %bitcast.66, bf16[132,2048]{1,0:T(8,128)(2,1)S(1)} %concatenate.72, f32[264,2048]{1,0:T(8,128)S(1)} %fusion.3, f32[528,2048]{1,0:T(8,128)S(1)} %fusion.50), kind=kLoop, calls=%fused_computation.3 | loop fusion | flops 6488064 | bytes 12976128 | tf_op jit(solution)/shard_map/convert_element_type | solution.py:72
  108.9 1.6 %collective-permute-start.9 = (bf16[132,2,8,128]{3,2,1,0:T(8,128)(2,1)S(1)}, bf16[132,2,8,128]{3,2,1,0:T(8,128)(2,1)}, u32[]{:S(2)}, u32[]{:S(2)}) collective-permute-start(bf16[132,2,8,128]{3,2,1,0:T(8,128)(2,1)S(1)} %slice_bitcast_fusion), channel_id=1, source_target_pairs={{0,2},{2,0},{1,3},{3,1},{4,6},{6,4},{5,7},{7,5},{8,10},{10,8},{9,1... | collective-permute-start | bytes 1622024 | tf_op jit(solution)/shard_map/ppermute | solution.py:102
  110.8 10.6 %collective-permute-done.9 = bf16[132,2,8,128]{3,2,1,0:T(8,128)(2,1)} collective-permute-done((bf16[132,2,8,128]{3,2,1,0:T(8,128)(2,1)S(1)}, bf16[132,2,8,128]{3,2,1,0:T(8,128)(2,1)}, u32[]{:S(2)}, u32[]{:S(2)}) %collective-permute-start.9) | collective-permute-done | bytes 540704 | tf_op jit(solution)/shard_map/ppermute | solution.py:102
  121.3 1.1 pad_maximum_fusion.7
  123.0 1.8 %add_multiply_fusion = f32[132,4,8,128]{3,2,1,0:T(8,128)} fusion(f32[132,4,8,128]{3,2,1,0:T(8,128)S(1)} %bitcast.67, f32[132,4,8,128]{3,2,1,0:T(8,128)S(1)} %get-tuple-element.10, f32[4,8,128]{2,1,0:T(8,128)S(1)} %compare_convert_fusion, f32[4,8,128]{2,1,0:T(8,128)S(1)} %get-tuple-element.9, f32[132]{0:T(256)S(1)} %get-tuple-element.42), kind=kLoop, calls=%fused_computation.76 | loop fusion | flops 2703360 | bytes 6521360 | tf_op jit(solution)/shard_map/mul | solution.py:158
  (60 shorter events, 5.6 us)
Async XLA Ops:
  0.6 66.5 %copy-start = (bf16[4,33,33]{2,0,1:T(4,128)(2,1)S(1)}, bf16[4,33,33]{2,0,1:T(4,128)(2,1)}, u32[]{:S(2)}) copy-start(bf16[4,33,33]{2,0,1:T(4,128)(2,1)} %param.23) | copy-start | bytes 26140
  0.6 8.7 %copy-start.2 = (f32[132,4,8,128]{3,2,1,0:T(8,128)S(1)}, f32[132,4,8,128]{3,2,1,0:T(8,128)}, u32[]{:S(2)}) copy-start(f32[132,4,8,128]{3,2,1,0:T(8,128)} %param.12) | copy-start | bytes 6488068
  3.1 16.8 %collective-permute-start = (f32[132,1,8,128]{3,2,1,0:T(8,128)}, f32[132,1,8,128]{3,2,1,0:T(8,128)S(1)}, u32[]{:S(2)}, u32[]{:S(2)}) collective-permute-start(f32[132,1,8,128]{3,2,1,0:T(8,128)} %get-tuple-element.27), channel_id=1, source_target_pairs={{0,4},{4,8},{8,12},{1,5},{5,9},{9,13},{2,6},{6,10},{10,14},{3,7},{... | collective-permute-start | bytes 1622024 | tf_op jit(solution)/shard_map/ppermute | solution.py:23
  8.1 15.8 %collective-permute-start.1 = (f32[132,1,8,128]{3,2,1,0:T(8,128)}, f32[132,1,8,128]{3,2,1,0:T(8,128)S(1)}, u32[]{:S(2)}, u32[]{:S(2)}) collective-permute-start(f32[132,1,8,128]{3,2,1,0:T(8,128)} %get-tuple-element.28), channel_id=1, source_target_pairs={{4,0},{8,4},{12,8},{5,1},{9,5},{13,9},{6,2},{10,6},{14,10},{7,3},{... | collective-permute-start | bytes 1622024 | tf_op jit(solution)/shard_map/ppermute | solution.py:24
  9.4 2.9 %copy-start.13 = (s32[264]{0:T(512)S(1)}, s32[264]{0:T(512)}, u32[]{:S(2)}) copy-start(s32[264]{0:T(512)} %param.21) | copy-start | bytes 3172
  9.4 3.1 %copy-start.5 = (f32[4,8,128]{2,1,0:T(8,128)S(1)}, f32[4,8,128]{2,1,0:T(8,128)}, u32[]{:S(2)}) copy-start(f32[4,8,128]{2,1,0:T(8,128)} %param.13) | copy-start | bytes 49156
  9.4 3.1 %copy-start.6 = (f32[4,8,128]{2,1,0:T(8,128)S(1)}, f32[4,8,128]{2,1,0:T(8,128)}, u32[]{:S(2)}) copy-start(f32[4,8,128]{2,1,0:T(8,128)} %param.14) | copy-start | bytes 49156
  9.4 3.1 %copy-start.9 = (s32[4,128]{1,0:T(4,128)S(1)}, s32[4,128]{1,0:T(4,128)}, u32[]{:S(2)}) copy-start(s32[4,128]{1,0:T(4,128)} %param.17) | copy-start | bytes 6148
  9.4 3.2 %copy-start.12 = (f32[132]{0:T(256)S(1)}, f32[132]{0:T(256)}, u32[]{:S(2)}) copy-start(f32[132]{0:T(256)} %param.19) | copy-start | bytes 1588
  9.4 3.1 %copy-start.14 = (f32[132]{0:T(256)S(1)}, f32[132]{0:T(256)}, u32[]{:S(2)}) copy-start(f32[132]{0:T(256)} %param.20) | copy-start | bytes 1588
  12.6 11.3 %copy-start.3 = (f32[132,4,8,127]{3,2,1,0:T(8,128)S(1)}, f32[132,4,8,127]{3,2,1,0:T(8,128)}, u32[]{:S(2)}) copy-start(f32[132,4,8,127]{3,2,1,0:T(8,128)} %get-tuple-element.23) | copy-start | bytes 6437380
  12.6 11.3 %copy-start.4 = (f32[132,4,8,127]{3,2,1,0:T(8,128)S(1)}, f32[132,4,8,127]{3,2,1,0:T(8,128)}, u32[]{:S(2)}) copy-start(f32[132,4,8,127]{3,2,1,0:T(8,128)} %get-tuple-element.24) | copy-start | bytes 6437380
  26.1 13.8 %collective-permute-start.2 = (f32[132,1,8,128]{3,2,1,0:T(8,128)S(1)}, f32[132,1,8,128]{3,2,1,0:T(8,128)S(1)}, u32[]{:S(2)}, u32[]{:S(2)}) collective-permute-start(f32[132,1,8,128]{3,2,1,0:T(8,128)S(1)} %get-tuple-element.21), channel_id=1, source_target_pairs={{0,4},{4,8},{8,12},{1,5},{5,9},{9,13},{2,6},{6,10},{10,14},{3,7},{... | collective-permute-start | bytes 1622024 | tf_op jit(solution)/shard_map/ppermute | solution.py:23
  29.6 14.4 %collective-permute-start.3 = (f32[132,1,8,128]{3,2,1,0:T(8,128)S(1)}, f32[132,1,8,128]{3,2,1,0:T(8,128)S(1)}, u32[]{:S(2)}, u32[]{:S(2)}) collective-permute-start(f32[132,1,8,128]{3,2,1,0:T(8,128)S(1)} %get-tuple-element.22), channel_id=1, source_target_pairs={{4,0},{8,4},{12,8},{5,1},{9,5},{13,9},{6,2},{10,6},{14,10},{7,3},{... | collective-permute-start | bytes 1622024 | tf_op jit(solution)/shard_map/ppermute | solution.py:24
  46.4 12.6 %collective-permute-start.4 = (f32[132,1,8,128]{3,2,1,0:T(8,128)S(1)}, f32[132,1,8,128]{3,2,1,0:T(8,128)S(1)}, u32[]{:S(2)}, u32[]{:S(2)}) collective-permute-start(f32[132,1,8,128]{3,2,1,0:T(8,128)S(1)} %get-tuple-element.15), channel_id=1, source_target_pairs={{0,4},{4,8},{8,12},{1,5},{5,9},{9,13},{2,6},{6,10},{10,14},{3,7},{... | collective-permute-start | bytes 1622024 | tf_op jit(solution)/shard_map/ppermute | solution.py:23
  49.9 13.2 %collective-permute-start.5 = (f32[132,1,8,128]{3,2,1,0:T(8,128)S(1)}, f32[132,1,8,128]{3,2,1,0:T(8,128)S(1)}, u32[]{:S(2)}, u32[]{:S(2)}) collective-permute-start(f32[132,1,8,128]{3,2,1,0:T(8,128)S(1)} %get-tuple-element.16), channel_id=1, source_target_pairs={{4,0},{8,4},{12,8},{5,1},{9,5},{13,9},{6,2},{10,6},{14,10},{7,3},{... | collective-permute-start | bytes 1622024 | tf_op jit(solution)/shard_map/ppermute | solution.py:24
  63.1 4.0 %copy-start.11 = (f32[132]{0:T(256)S(1)}, f32[132]{0:T(256)}, u32[]{:S(2)}) copy-start(f32[132]{0:T(256)} %param.18) | copy-start | bytes 1588
  63.1 4.0 %copy-start.10 = (s32[8,8]{1,0:T(8,128)S(1)}, s32[8,8]{1,0:T(8,128)}, u32[]{:S(2)}) copy-start(s32[8,8]{1,0:T(8,128)} %param.22) | copy-start | bytes 772
  65.6 3.5 %collective-permute-start.6 = (f32[132,4,1,128]{3,0,2,1:T(8,128)S(1)}, f32[132,4,1,128]{3,0,2,1:T(8,128)S(1)}, u32[]{:S(2)}, u32[]{:S(2)}) collective-permute-start(f32[132,4,1,128]{3,0,2,1:T(8,128)S(1)} %copy.36), channel_id=1, source_target_pairs={{1,0},{3,2},{5,4},{7,6},{9,8},{11,10},{13,12},{15,14},{17,16},{19,... | collective-permute-start | bytes 811016 | tf_op jit(solution)/shard_map/ppermute | solution.py:32
  69.3 5.1 %copy-start.7 = (f32[4,8,128]{2,1,0:T(8,128)S(1)}, f32[4,8,128]{2,1,0:T(8,128)}, u32[]{:S(2)}) copy-start(f32[4,8,128]{2,1,0:T(8,128)} %param.16) | copy-start | bytes 49156
  69.3 5.1 %copy-start.8 = (f32[4,8,128]{2,1,0:T(8,128)S(1)}, f32[4,8,128]{2,1,0:T(8,128)}, u32[]{:S(2)}) copy-start(f32[4,8,128]{2,1,0:T(8,128)} %param.15) | copy-start | bytes 49156
  70.4 4.0 %collective-permute-start.7 = (f32[2,4,8,128]{3,2,1,0:T(8,128)S(1)}, f32[2,4,8,128]{3,2,1,0:T(8,128)S(1)}, u32[]{:S(2)}, u32[]{:S(2)}) collective-permute-start(f32[2,4,8,128]{3,2,1,0:T(8,128)S(1)} %pad_maximum_fusion.10), channel_id=1, source_target_pairs={{0,2},{2,0},{1,3},{3,1},{4,6},{6,4},{5,7},{7,5},{8,10},{10,8},{9,1... | collective-permute-start | bytes 98312 | tf_op jit(solution)/shard_map/ppermute | solution.py:146
  76.6 13.5 %collective-permute-start.8 = (bf16[132,2,8,128]{3,2,1,0:T(8,128)(2,1)}, bf16[132,2,8,128]{3,2,1,0:T(8,128)(2,1)}, u32[]{:S(2)}, u32[]{:S(2)}) collective-permute-start(bf16[132,2,8,128]{3,2,1,0:T(8,128)(2,1)} %get-tuple-element.32), channel_id=1, source_target_pairs={{0,2},{2,0},{1,3},{3,1},{4,6},{6,4},{5,7},{7,5},{8,10},{10,8},{9,1... | collective-permute-start | bytes 1622024 | tf_op jit(solution)/shard_map/ppermute | solution.py:99
  108.9 12.4 %collective-permute-start.9 = (bf16[132,2,8,128]{3,2,1,0:T(8,128)(2,1)S(1)}, bf16[132,2,8,128]{3,2,1,0:T(8,128)(2,1)}, u32[]{:S(2)}, u32[]{:S(2)}) collective-permute-start(bf16[132,2,8,128]{3,2,1,0:T(8,128)(2,1)S(1)} %slice_bitcast_fusion), channel_id=1, source_target_pairs={{0,2},{2,0},{1,3},{3,1},{4,6},{6,4},{5,7},{7,5},{8,10},{10,8},{9,1... | collective-permute-start | bytes 1622024 | tf_op jit(solution)/shard_map/ppermute | solution.py:102
  123.0 1.8 %copy-start.1 = (bf16[4,33,33]{2,0,1:T(4,128)(2,1)S(1)}, bf16[4,33,33]{2,0,1:T(4,128)(2,1)}, u32[]{:S(2)}) copy-start(bf16[4,33,33]{2,0,1:T(4,128)(2,1)} %param.23) | copy-start | bytes 26140
where the time goes:
time: 125 us
  waiting for transfers between devices  53.8 us (43%)
  starting transfers between devices  21.9 us (18%)
  other arithmetic  16.9 us (14%)
  matrix products  16.1 us (13%)
  local copies, waits for them, and re-layouts  14.9 us (12%)
    ppermute x3, waiting for transfers between devices, extended_2(): before = lax.ppermute(last, axis, up)  20.2 us
    ppermute x3, waiting for transfers between devices, extended_2(): after = lax.ppermute(first, axis, down)  12.3 us
    dot_general x8, matrix products, collide(): jnp.dot(table, iterate.astype(jnp.bfloat16), preferred_element_type=jnp.f...  12.3 us
    ppermute x3, starting transfers between devices, extended_2(): before = lax.ppermute(last, axis, up)  11.9 us
    ppermute x1, waiting for transfers between devices, paired_collision(): back = lax.ppermute(change[local_bins:], 'bins', swap)  10.6 us
    ppermute x1, waiting for transfers between devices, paired_collision(): arrived = lax.ppermute(away, 'bins', swap)  7.01 us
    add x3, other arithmetic, body(): bin_mass + weight_now * tendency(extended[:, 1:-1], extended[:, :-2], ext...  6.63 us
    slice x6, local copies, waits for them, and re-layouts, tendency(): north_cells = jnp.roll(center_cells, -1, axis=3)  6.59 us
  transfers between devices with their start and end apart: 10, of which 10 were waited for; matrix products, arithmetic and copies ran while one was open for 10% of the time, Pallas kernels for 0%

commit v1 on v0

--- a/solution.py
+++ b/solution.py
@@ -13,15 +13,15 @@
 highest = lax.Precision.HIGHEST
 
 
-def extended_2(array, sides, width):
+def extended_2(array, sides, width, link=jnp.float32):
     for axis, dim in sides:
         size, length = (lax.axis_size(axis), array.shape[dim])
         up = [(i, (i + 1) % size) for i in range(size - 1)]
         down = [(j, i) for i, j in up]
         last = lax.slice_in_dim(array, length - width, length, axis=dim)
         first = lax.slice_in_dim(array, 0, width, axis=dim)
-        before = lax.ppermute(last, axis, up)
-        after = lax.ppermute(first, axis, down)
+        before = lax.ppermute(last.astype(link), axis, up).astype(array.dtype)
+        after = lax.ppermute(first.astype(link), axis, down).astype(array.dtype)
         array = jnp.concatenate([before, array, after], axis=dim)
     return array
 
@@ -127,7 +127,7 @@
     section_weights = (1.0 / 3.0, 0.5, 1.0)
     section_field = bin_mass
     for weight_now in section_weights:
-        extended = extended_2(section_field, (("tiles", 1),), 1)
+        extended = extended_2(section_field, (("tiles", 1),), 1, jnp.bfloat16)
         section_field = bin_mass + weight_now * tendency(
             extended[:, 1:-1], extended[:, :-2], extended[:, 2:], wind_x, wind_y
         )

time: 125 us -> 115 us (0.920)
  waiting for transfers between devices: 53.8 us -> 35.8 us
  local copies, waits for them, and re-layouts: 14.9 us -> 20.5 us
  other arithmetic: 16.9 us -> 19.2 us
    ppermute x6, waiting for transfers between devices: 32.6 us -> 14.8 us  [the longest x3 9.87 us: extended_2(): after = lax.ppermute(first.astype(link), axis, down).astype(array.dtype)]
    another operation x1 -> x3, other arithmetic: 0.01 us -> 7.58 us
    slice x0 -> x4, local copies, waits for them, and re-layouts: none -> 7.02 us  [tendency(): south_cells = jnp.roll(center_cells, 1, axis=3)]
    unnamed x35 -> x40, local copies, waits for them, and re-layouts: 2.78 us -> 8.49 us
    slice x6 -> x2, local copies, waits for them, and re-layouts: 6.59 us -> 1.43 us  [tendency(): north_cells = jnp.roll(center_cells, -1, axis=3)]
    add x3 -> x1, other arithmetic: 6.63 us -> 2.6 us  [body(): bin_mass + weight_now * tendency(extended[:, 1:-1], extended[:, :-2], ext...]
    slice x3, local copies, waits for them, and re-layouts: 2.59 us -> 0.13 us  [extended_2(): last = lax.slice_in_dim(array, length - width, length, axis=dim)]
  transfers between devices with their start and end apart: 10 -> 10, of which waited for: 10 -> 9; matrix products, arithmetic and copies ran while one was open for 10% -> 13% of each run, Pallas kernels for 0% -> 0%
where the time goes in v1:
time: 115 us
  waiting for transfers between devices  35.8 us (31%)
  starting transfers between devices  21.9 us (19%)
  local copies, waits for them, and re-layouts  20.5 us (18%)
  other arithmetic  19.2 us (17%)
  matrix products  16 us (14%)
  between operations  1.23 us (1%)
    dot_general x8, matrix products, collide(): jnp.dot(table, iterate.astype(jnp.bfloat16), preferred_element_type=jnp.f...  12.3 us
    ppermute x3, starting transfers between devices, extended_2(): before = lax.ppermute(last.astype(link), axis, up).astype(array.dtype)  11.9 us
    ppermute x1, waiting for transfers between devices, paired_collision(): back = lax.ppermute(change[local_bins:], 'bins', swap)  10.6 us
    ppermute x3, waiting for transfers between devices, extended_2(): after = lax.ppermute(first.astype(link), axis, down).astype(array.dtype)  9.87 us
    unnamed x40, local copies, waits for them, and re-layouts  8.49 us
    another operation x3, other arithmetic  7.58 us
    slice x4, local copies, waits for them, and re-layouts, tendency(): south_cells = jnp.roll(center_cells, 1, axis=3)  7.02 us
    ppermute x1, waiting for transfers between devices, paired_collision(): arrived = lax.ppermute(away, 'bins', swap)  6.35 us
  transfers between devices with their start and end apart: 10, of which 9 were waited for; matrix products, arithmetic and copies ran while one was open for 13% of the time, Pallas kernels for 0%

profile of v1, /device:TPU:0, one launch (start us, length us, event | category | flops | bytes accessed | tf_op | source)
XLA Modules:
  0.0 114.6 jit_solution(3600429403396005560)
XLA Ops:
  0.7 3.0 %copy.71 = bf16[132,4,8,128]{3,0,2,1:T(8,128)(2,1)S(1)} copy(f32[132,4,8,128]{3,2,1,0:T(8,128)} %param.12) | data formatting | bytes 3244032 | tf_op args[0]
  3.7 4.9 %collective-permute-start = (bf16[132,1,8,128]{3,0,2,1:T(8,128)(2,1)S(1)}, bf16[132,1,8,128]{3,0,2,1:T(8,128)(2,1)S(1)}, u32[]{:S(2)}, u32[]{:S(2)}) collective-permute-start(bf16[132,1,8,128]{3,0,2,1:T(8,128)(2,1)S(1)} %get-tuple-element.36), channel_id=1, source_target_pairs={{0,4},{4,8},{8,12},{1,5},{5,9},{9,13},{2,6},{6,10},{10,14},{3,7},{... | collective-permute-start | bytes 811016 | tf_op jit(solution)/shard_map/ppermute | solution.py:23
  8.7 1.3 %collective-permute-start.1 = (bf16[132,1,8,128]{3,0,2,1:T(8,128)(2,1)S(1)}, bf16[132,1,8,128]{3,0,2,1:T(8,128)(2,1)S(1)}, u32[]{:S(2)}, u32[]{:S(2)}) collective-permute-start(bf16[132,1,8,128]{3,0,2,1:T(8,128)(2,1)S(1)} %get-tuple-element.37), channel_id=1, source_target_pairs={{4,0},{8,4},{12,8},{5,1},{9,5},{13,9},{6,2},{10,6},{14,10},{7,3},{... | collective-permute-start | bytes 811016 | tf_op jit(solution)/shard_map/ppermute | solution.py:24
  10.0 1.3 %copy.48 = f32[132,4,8,128]{3,0,2,1:T(8,128)S(1)} copy(f32[132,4,8,128]{3,2,1,0:T(8,128)S(1)} %copy-done.2) | data formatting | bytes 4325376 | tf_op args[0]
  11.3 2.7 %fusion.100 = (f32[132,4,8,1]{3,0,2,1:T(8,128)}, f32[132,4,8,1]{3,0,2,1:T(8,128)}) fusion(f32[132,4,8,128]{3,0,2,1:T(8,128)S(1)} %copy.48), kind=kLoop, calls=%fused_computation.159 | loop fusion | bytes 67584 | tf_op jit(solution)/shard_map/jit(_roll_static)/slice | solution.py:36
  14.0 2.8 %fusion.101 = (f32[132,4,8,127]{3,0,2,1:T(8,128)}, f32[132,4,8,127]{3,0,2,1:T(8,128)}) fusion(f32[132,4,8,128]{3,0,2,1:T(8,128)S(1)} %copy.48), kind=kLoop, calls=%fused_computation.160 | loop fusion | bytes 8583168 | tf_op jit(solution)/shard_map/jit(_roll_static)/slice | solution.py:36
  17.3 1.4 %collective-permute-done.1 = bf16[132,1,8,128]{3,0,2,1:T(8,128)(2,1)S(1)} collective-permute-done((bf16[132,1,8,128]{3,0,2,1:T(8,128)(2,1)S(1)}, bf16[132,1,8,128]{3,0,2,1:T(8,128)(2,1)S(1)}, u32[]{:S(2)}, u32[]{:S(2)}) %collective-permute-start.1) | collective-permute-done | bytes 270368 | tf_op jit(solution)/shard_map/ppermute | solution.py:24
  18.7 4.8 %fusion.94 = (bf16[132,4,8,128]{3,0,2,1:T(8,128)(2,1)S(1)}, f32[132,4,8,128]{3,0,2,1:T(8,128)S(1)}) fusion(f32[132,4,8,128]{3,0,2,1:T(8,128)S(1)} %copy.48, f32[132,4,8,1]{3,0,2,1:T(8,128)} %get-tuple-element.27, f32[132,4,8,127]{3,0,2,1:T(8,128)} %get-tuple-element.29, f32[4,8,128]{2,1,0:T(8,128)S(1)} %get-tuple-element.47, ...), kind=kLoop, calls=%fused_computation.154 | loop fusion | flops 10272768 | bytes 10878976 | tf_op jit(solution)/shard_map/convert.8
  23.5 0.7 fusion.98
  24.3 3.5 %collective-permute-start.2 = (bf16[132,1,8,128]{3,0,2,1:T(8,128)(2,1)S(1)}, bf16[132,1,8,128]{3,0,2,1:T(8,128)(2,1)S(1)}, u32[]{:S(2)}, u32[]{:S(2)}) collective-permute-start(bf16[132,1,8,128]{3,0,2,1:T(8,128)(2,1)S(1)} %get-tuple-element.34), channel_id=1, source_target_pairs={{0,4},{4,8},{8,12},{1,5},{5,9},{9,13},{2,6},{6,10},{10,14},{3,7},{... | collective-permute-start | bytes 811016 | tf_op jit(solution)/shard_map/ppermute | solution.py:23
  27.8 1.3 %collective-permute-start.3 = (bf16[132,1,8,128]{3,0,2,1:T(8,128)(2,1)S(1)}, bf16[132,1,8,128]{3,0,2,1:T(8,128)(2,1)S(1)}, u32[]{:S(2)}, u32[]{:S(2)}) collective-permute-start(bf16[132,1,8,128]{3,0,2,1:T(8,128)(2,1)S(1)} %get-tuple-element.35), channel_id=1, source_target_pairs={{4,0},{8,4},{12,8},{5,1},{9,5},{13,9},{6,2},{10,6},{14,10},{7,3},{... | collective-permute-start | bytes 811016 | tf_op jit(solution)/shard_map/ppermute | solution.py:24
  29.8 3.0 %collective-permute-done.2 = bf16[132,1,8,128]{3,0,2,1:T(8,128)(2,1)S(1)} collective-permute-done((bf16[132,1,8,128]{3,0,2,1:T(8,128)(2,1)S(1)}, bf16[132,1,8,128]{3,0,2,1:T(8,128)(2,1)S(1)}, u32[]{:S(2)}, u32[]{:S(2)}) %collective-permute-start.2) | collective-permute-done | bytes 270368 | tf_op jit(solution)/shard_map/ppermute | solution.py:23
  32.9 4.1 %collective-permute-done.3 = bf16[132,1,8,128]{3,0,2,1:T(8,128)(2,1)S(1)} collective-permute-done((bf16[132,1,8,128]{3,0,2,1:T(8,128)(2,1)S(1)}, bf16[132,1,8,128]{3,0,2,1:T(8,128)(2,1)S(1)}, u32[]{:S(2)}, u32[]{:S(2)}) %collective-permute-start.3) | collective-permute-done | bytes 270368 | tf_op jit(solution)/shard_map/ppermute | solution.py:24
  37.0 2.8 %fusion.92 = (bf16[132,4,8,128]{3,0,2,1:T(8,128)(2,1)S(1)}, f32[132,4,8,128]{3,0,2,1:T(8,128)S(1)}) fusion(f32[132,4,8,128]{3,0,2,1:T(8,128)S(1)} %get-tuple-element.17, f32[132,4,8,1]{3,0,2,1:T(8,128)S(1)} %get-tuple-element.23, f32[132,4,8,127]{3,0,2,1:T(8,128)S(1)} %get-tuple-element.25, f32[4,8,128]{2,1,0:T(8,128)S(1)} %get-tuple-element.47, ...), kind=kLoop, calls=%fused_computation.153 | loop fusion | flops 10272768 | bytes 13041664 | tf_op jit(solution)/shard_map/convert.6
  40.6 3.5 %collective-permute-start.4 = (bf16[132,1,8,128]{3,0,2,1:T(8,128)(2,1)S(1)}, bf16[132,1,8,128]{3,0,2,1:T(8,128)(2,1)S(1)}, u32[]{:S(2)}, u32[]{:S(2)}) collective-permute-start(bf16[132,1,8,128]{3,0,2,1:T(8,128)(2,1)S(1)} %get-tuple-element.32), channel_id=1, source_target_pairs={{0,4},{4,8},{8,12},{1,5},{5,9},{9,13},{2,6},{6,10},{10,14},{3,7},{... | collective-permute-start | bytes 811016 | tf_op jit(solution)/shard_map/ppermute | solution.py:23
  44.0 1.3 %collective-permute-start.5 = (bf16[132,1,8,128]{3,0,2,1:T(8,128)(2,1)S(1)}, bf16[132,1,8,128]{3,0,2,1:T(8,128)(2,1)S(1)}, u32[]{:S(2)}, u32[]{:S(2)}) collective-permute-start(bf16[132,1,8,128]{3,0,2,1:T(8,128)(2,1)S(1)} %get-tuple-element.33), channel_id=1, source_target_pairs={{4,0},{8,4},{12,8},{5,1},{9,5},{13,9},{6,2},{10,6},{14,10},{7,3},{... | collective-permute-start | bytes 811016 | tf_op jit(solution)/shard_map/ppermute | solution.py:24
  46.1 2.0 %collective-permute-done.4 = bf16[132,1,8,128]{3,0,2,1:T(8,128)(2,1)S(1)} collective-permute-done((bf16[132,1,8,128]{3,0,2,1:T(8,128)(2,1)S(1)}, bf16[132,1,8,128]{3,0,2,1:T(8,128)(2,1)S(1)}, u32[]{:S(2)}, u32[]{:S(2)}) %collective-permute-start.4) | collective-permute-done | bytes 270368 | tf_op jit(solution)/shard_map/ppermute | solution.py:23
  48.1 4.4 %collective-permute-done.5 = bf16[132,1,8,128]{3,0,2,1:T(8,128)(2,1)S(1)} collective-permute-done((bf16[132,1,8,128]{3,0,2,1:T(8,128)(2,1)S(1)}, bf16[132,1,8,128]{3,0,2,1:T(8,128)(2,1)S(1)}, u32[]{:S(2)}, u32[]{:S(2)}) %collective-permute-start.5) | collective-permute-done | bytes 270368 | tf_op jit(solution)/shard_map/ppermute | solution.py:24
  52.5 2.6 %fusion.5 = f32[132,4,8,128]{3,0,2,1:T(8,128)S(1)} fusion(f32[132,4,8,128]{3,0,2,1:T(8,128)S(1)} %get-tuple-element.15, f32[132,1,8,128]{3,0,2,1:T(8,128)S(1)} %convert_element_type.78, f32[132,1,8,128]{3,0,2,1:T(8,128)S(1)} %convert_element_type.77, f32[132,4,8,127]{3,0,2,1:T(8,128)S(1)} %get-tuple-element.19, f32[132,4,8,1]{3,0,2,1:T(8,128)S(1)} %get-tuple-element.21, ...), kind=kLoop, calls=%fused_computation.9 | loop fusion | flops 9191424 | bytes 11960320 | tf_op jit(solution)/shard_map/add | solution.py:131
  55.2 1.5 %collective-permute-start.6 = (f32[132,4,1,128]{3,0,2,1:T(8,128)S(1)}, f32[132,4,1,128]{3,0,2,1:T(8,128)S(1)}, u32[]{:S(2)}, u32[]{:S(2)}) collective-permute-start(f32[132,4,1,128]{3,0,2,1:T(8,128)S(1)} %slice.224), channel_id=1, source_target_pairs={{1,0},{3,2},{5,4},{7,6},{9,8},{11,10},{13,12},{15,14},{17,16},{19,... | collective-permute-start | bytes 811016 | tf_op jit(solution)/shard_map/ppermute | solution.py:32
  57.2 1.6 %collective-permute-done.6 = f32[132,4,1,128]{3,0,2,1:T(8,128)S(1)} collective-permute-done((f32[132,4,1,128]{3,0,2,1:T(8,128)S(1)}, f32[132,4,1,128]{3,0,2,1:T(8,128)S(1)}, u32[]{:S(2)}, u32[]{:S(2)}) %collective-permute-start.6) | collective-permute-done | bytes 270368 | tf_op jit(solution)/shard_map/ppermute | solution.py:32
  58.8 0.8 multiply_reduce_fusion.1
  59.6 1.6 %collective-permute-start.7 = (f32[2,4,8,128]{3,2,1,0:T(8,128)S(1)}, f32[2,4,8,128]{3,2,1,0:T(8,128)S(1)}, u32[]{:S(2)}, u32[]{:S(2)}) collective-permute-start(f32[2,4,8,128]{3,2,1,0:T(8,128)S(1)} %pad_maximum_fusion.10), channel_id=1, source_target_pairs={{0,2},{2,0},{1,3},{3,1},{4,6},{6,4},{5,7},{7,5},{8,10},{10,8},{9,1... | collective-permute-start | bytes 98312 | tf_op jit(solution)/shard_map/ppermute | solution.py:146
  61.2 2.4 %collective-permute-done.7 = f32[2,4,8,128]{3,2,1,0:T(8,128)S(1)} collective-permute-done((f32[2,4,8,128]{3,2,1,0:T(8,128)S(1)}, f32[2,4,8,128]{3,2,1,0:T(8,128)S(1)}, u32[]{:S(2)}, u32[]{:S(2)}) %collective-permute-start.7) | collective-permute-done | bytes 32800 | tf_op jit(solution)/shard_map/ppermute | solution.py:146
  64.7 0.9 copy.73
  65.6 1.5 %collective-permute-start.8 = (bf16[132,2,8,128]{3,2,1,0:T(8,128)(2,1)}, bf16[132,2,8,128]{3,2,1,0:T(8,128)(2,1)}, u32[]{:S(2)}, u32[]{:S(2)}) collective-permute-start(bf16[132,2,8,128]{3,2,1,0:T(8,128)(2,1)} %bitcast.64), channel_id=1, source_target_pairs={{0,2},{2,0},{1,3},{3,1},{4,6},{6,4},{5,7},{7,5},{8,10},{10,8},{9,1... | collective-permute-start | bytes 1622024 | tf_op jit(solution)/shard_map/ppermute | solution.py:99
  67.1 2.0 %multiply_reduce_fusion = f32[264,8,33]{0,2,1:T(8,128)S(1)} fusion(f32[264,8]{0,1:T(8,128)S(1)} %fusion.83, f32[8,8,33,33]{3,1,2,0:T(8,128)S(1)} %fusion.70, s32[264]{0:T(512)S(1)} %get-tuple-element.45), kind=kOutput, calls=%fused_computation | convolution fusion | flops 221851072 | bytes 567072 | tf_op jit(solution)/shard_map/bm,acmn->bacn/dot_general | solution.py:59
  69.4 1.1 fusion.47
  70.5 0.9 copy.60
  71.4 1.3 %concatenate.72 = bf16[132,2048]{1,0:T(8,128)(2,1)S(1)} reshape(bf16[132,1,2,8,128]{4,3,2,0,1:T(8,128)(2,1)} %copy.60) | data formatting | bytes 1081344 | tf_op jit(solution)/shard_map/concatenate | solution.py:100
  72.7 6.4 %collective-permute-done.8 = bf16[132,2,8,128]{3,2,1,0:T(8,128)(2,1)} collective-permute-done((bf16[132,2,8,128]{3,2,1,0:T(8,128)(2,1)}, bf16[132,2,8,128]{3,2,1,0:T(8,128)(2,1)}, u32[]{:S(2)}, u32[]{:S(2)}) %collective-permute-start.8) | collective-permute-done | bytes 540704 | tf_op jit(solution)/shard_map/ppermute | solution.py:99
  79.1 1.1 pad.48
  80.4 1.5 %fusion.64 = f32[528,2048]{1,0:T(8,128)S(1)} fusion(bf16[132,2048]{1,0:T(8,128)(2,1)S(1)} %bitcast.65, bf16[132,2048]{1,0:T(8,128)(2,1)S(1)} %concatenate.72, bf16[264,264]{0,1:T(8,128)(2,1)S(1)} %convolution_convert_fusion, bf16[264,264]{0,1:T(8,128)(2,1)S(1)} %fusion.47), kind=kOutput, calls=%fused_computation.109 | convolution fusion | flops 573669888 | bytes 5685504 | tf_op jit(solution)/shard_map/dot_general | solution.py:70
  81.9 1.6 %fusion.61 = f32[528,2048]{1,0:T(8,128)S(1)} fusion(f32[528,2048]{1,0:T(8,128)S(1)} %fusion.64, bf16[132,2048]{1,0:T(8,128)(2,1)S(1)} %bitcast.66, bf16[132,2048]{1,0:T(8,128)(2,1)S(1)} %concatenate.72, bf16[264,264]{0,1:T(8,128)(2,1)S(1)} %convolution_convert_fusion, bf16[264,264]{0,1:T(8,128)(2,1)S(1)} %fusion.47), kind=kOutput, calls=%fused_computation.102 | convolution fusion | flops 575832576 | bytes 10010880 | tf_op jit(solution)/shard_map/dot_general | solution.py:70
  83.4 1.1 fusion.44
  84.5 1.5 %fusion.59 = f32[528,2048]{1,0:T(8,128)S(1)} fusion(f32[264,2048]{1,0:T(8,128)S(1)} %fusion.44, bf16[264,264]{0,1:T(8,128)(2,1)S(1)} %convolution_convert_fusion, bf16[264,264]{0,1:T(8,128)(2,1)S(1)} %fusion.47), kind=kOutput, calls=%fused_computation.100 | convolution fusion | flops 572047872 | bytes 6766848 | tf_op jit(solution)/shard_map/dot_general | solution.py:70
  86.0 1.5 %fusion.57 = f32[528,2048]{1,0:T(8,128)S(1)} fusion(f32[264,2048]{1,0:T(8,128)S(1)} %fusion.44, f32[528,2048]{1,0:T(8,128)S(1)} %fusion.59, bf16[264,264]{0,1:T(8,128)(2,1)S(1)} %convolution_convert_fusion, bf16[264,264]{0,1:T(8,128)(2,1)S(1)} %fusion.47), kind=kOutput, calls=%fused_computation.98 | convolution fusion | flops 573669888 | bytes 11092224 | tf_op jit(solution)/shard_map/dot_general | solution.py:70
  87.5 1.2 %fusion.42 = f32[264,2048]{1,0:T(8,128)S(1)} fusion(f32[528,2048]{1,0:T(8,128)S(1)} %fusion.57, f32[264,2048]{1,0:T(8,128)S(1)} %fusion.44, f32[528,2048]{1,0:T(8,128)S(1)} %fusion.59), kind=kLoop, calls=%fused_computation.71 | loop fusion | flops 3244032 | bytes 12976128 | tf_op jit(solution)/shard_map/add | solution.py:71
  88.6 1.5 %fusion.55 = f32[528,2048]{1,0:T(8,128)S(1)} fusion(f32[264,2048]{1,0:T(8,128)S(1)} %fusion.42, bf16[264,264]{0,1:T(8,128)(2,1)S(1)} %convolution_convert_fusion, bf16[264,264]{0,1:T(8,128)(2,1)S(1)} %fusion.47), kind=kOutput, calls=%fused_computation.96 | convolution fusion | flops 572047872 | bytes 6766848 | tf_op jit(solution)/shard_map/dot_general | solution.py:70
  90.1 1.6 %fusion.53 = f32[528,2048]{1,0:T(8,128)S(1)} fusion(f32[264,2048]{1,0:T(8,128)S(1)} %fusion.42, f32[528,2048]{1,0:T(8,128)S(1)} %fusion.55, bf16[264,264]{0,1:T(8,128)(2,1)S(1)} %convolution_convert_fusion, bf16[264,264]{0,1:T(8,128)(2,1)S(1)} %fusion.47), kind=kOutput, calls=%fused_computation.94 | convolution fusion | flops 573669888 | bytes 11092224 | tf_op jit(solution)/shard_map/dot_general | solution.py:70
  91.7 1.2 %fusion.40 = f32[264,2048]{1,0:T(8,128)S(1)} fusion(f32[528,2048]{1,0:T(8,128)S(1)} %fusion.53, f32[264,2048]{1,0:T(8,128)S(1)} %fusion.42, f32[528,2048]{1,0:T(8,128)S(1)} %fusion.55), kind=kLoop, calls=%fused_computation.65 | loop fusion | flops 3244032 | bytes 12976128 | tf_op jit(solution)/shard_map/add | solution.py:71
  92.9 1.7 %fusion.51 = f32[528,2048]{1,0:T(8,128)S(1)} fusion(f32[264,2048]{1,0:T(8,128)S(1)} %fusion.40, bf16[264,264]{0,1:T(8,128)(2,1)S(1)} %convolution_convert_fusion, bf16[264,264]{0,1:T(8,128)(2,1)S(1)} %fusion.47), kind=kOutput, calls=%fused_computation.92 | convolution fusion | flops 572047872 | bytes 6766848 | tf_op jit(solution)/shard_map/dot_general | solution.py:70
  94.6 1.5 %fusion.49 = f32[528,2048]{1,0:T(8,128)S(1)} fusion(f32[264,2048]{1,0:T(8,128)S(1)} %fusion.40, f32[528,2048]{1,0:T(8,128)S(1)} %fusion.51, bf16[264,264]{0,1:T(8,128)(2,1)S(1)} %convolution_convert_fusion, bf16[264,264]{0,1:T(8,128)(2,1)S(1)} %fusion.47), kind=kOutput, calls=%fused_computation.90 | convolution fusion | flops 573669888 | bytes 11092224 | tf_op jit(solution)/shard_map/dot_general | solution.py:70
  96.1 1.3 %fusion.37 = bf16[264,2048]{1,0:T(8,128)(2,1)S(1)} fusion(f32[528,2048]{1,0:T(8,128)S(1)} %fusion.49, bf16[132,2048]{1,0:T(8,128)(2,1)S(1)} %bitcast.68, bf16[132,2048]{1,0:T(8,128)(2,1)S(1)} %concatenate.72, f32[264,2048]{1,0:T(8,128)S(1)} %fusion.40, f32[528,2048]{1,0:T(8,128)S(1)} %fusion.51), kind=kLoop, calls=%fused_computation.57 | loop fusion | flops 6488064 | bytes 12976128 | tf_op jit(solution)/shard_map/convert_element_type | solution.py:72
  97.9 1.6 %collective-permute-start.9 = (bf16[132,2,8,128]{3,2,1,0:T(8,128)(2,1)S(1)}, bf16[132,2,8,128]{3,2,1,0:T(8,128)(2,1)}, u32[]{:S(2)}, u32[]{:S(2)}) collective-permute-start(bf16[132,2,8,128]{3,2,1,0:T(8,128)(2,1)S(1)} %slice_bitcast_fusion), channel_id=1, source_target_pairs={{0,2},{2,0},{1,3},{3,1},{4,6},{6,4},{5,7},{7,5},{8,10},{10,8},{9,1... | collective-permute-start | bytes 1622024 | tf_op jit(solution)/shard_map/ppermute | solution.py:102
  99.7 10.6 %collective-permute-done.9 = bf16[132,2,8,128]{3,2,1,0:T(8,128)(2,1)} collective-permute-done((bf16[132,2,8,128]{3,2,1,0:T(8,128)(2,1)S(1)}, bf16[132,2,8,128]{3,2,1,0:T(8,128)(2,1)}, u32[]{:S(2)}, u32[]{:S(2)}) %collective-permute-start.9) | collective-permute-done | bytes 540704 | tf_op jit(solution)/shard_map/ppermute | solution.py:102
  110.3 1.1 %pad_maximum_fusion.7 = bf16[132,2,2,8,128]{4,3,2,0,1:T(8,128)(2,1)S(1)} fusion(bf16[132,1,2,8,128]{4,3,2,0,1:T(8,128)(2,1)} %bitcast.11, bf16[132,1,2,8,128]{4,3,2,0,1:T(8,128)(2,1)S(1)} %slice_bitcast_fusion.1), kind=kLoop, calls=%fused_computation.89 | loop fusion | flops 540672 | bytes 2162688 | tf_op jit(solution)/shard_map/stack | solution.py:103
  112.9 1.7 %copy.53 = f32[132,4,8,128]{3,2,1,0:T(8,128)} copy(f32[132,4,8,128]{3,0,2,1:T(8,128)S(1)} %fusion.36) | data formatting | bytes 4325376
  (71 shorter events, 6.9 us)
Async XLA Ops:
  0.6 56.1 %copy-start = (bf16[4,33,33]{2,0,1:T(4,128)(2,1)S(1)}, bf16[4,33,33]{2,0,1:T(4,128)(2,1)}, u32[]{:S(2)}) copy-start(bf16[4,33,33]{2,0,1:T(4,128)(2,1)} %param.23) | copy-start | bytes 26140
  0.6 9.3 %copy-start.2 = (f32[132,4,8,128]{3,2,1,0:T(8,128)S(1)}, f32[132,4,8,128]{3,2,1,0:T(8,128)}, u32[]{:S(2)}) copy-start(f32[132,4,8,128]{3,2,1,0:T(8,128)} %param.12) | copy-start | bytes 6488068
  3.7 13.5 %collective-permute-start = (bf16[132,1,8,128]{3,0,2,1:T(8,128)(2,1)S(1)}, bf16[132,1,8,128]{3,0,2,1:T(8,128)(2,1)S(1)}, u32[]{:S(2)}, u32[]{:S(2)}) collective-permute-start(bf16[132,1,8,128]{3,0,2,1:T(8,128)(2,1)S(1)} %get-tuple-element.36), channel_id=1, source_target_pairs={{0,4},{4,8},{8,12},{1,5},{5,9},{9,13},{2,6},{6,10},{10,14},{3,7},{... | collective-permute-start | bytes 811016 | tf_op jit(solution)/shard_map/ppermute | solution.py:23
  8.7 10.0 %collective-permute-start.1 = (bf16[132,1,8,128]{3,0,2,1:T(8,128)(2,1)S(1)}, bf16[132,1,8,128]{3,0,2,1:T(8,128)(2,1)S(1)}, u32[]{:S(2)}, u32[]{:S(2)}) collective-permute-start(bf16[132,1,8,128]{3,0,2,1:T(8,128)(2,1)S(1)} %get-tuple-element.37), channel_id=1, source_target_pairs={{4,0},{8,4},{12,8},{5,1},{9,5},{13,9},{6,2},{10,6},{14,10},{7,3},{... | collective-permute-start | bytes 811016 | tf_op jit(solution)/shard_map/ppermute | solution.py:24
  14.0 2.9 %copy-start.14 = (s32[264]{0:T(512)S(1)}, s32[264]{0:T(512)}, u32[]{:S(2)}) copy-start(s32[264]{0:T(512)} %param.21) | copy-start | bytes 3172
  14.0 3.1 %copy-start.11 = (f32[132]{0:T(256)S(1)}, f32[132]{0:T(256)}, u32[]{:S(2)}) copy-start(f32[132]{0:T(256)} %param.19) | copy-start | bytes 1588
  14.0 3.1 %copy-start.15 = (f32[132]{0:T(256)S(1)}, f32[132]{0:T(256)}, u32[]{:S(2)}) copy-start(f32[132]{0:T(256)} %param.20) | copy-start | bytes 1588
  14.0 3.1 %copy-start.4 = (f32[4,8,128]{2,1,0:T(8,128)S(1)}, f32[4,8,128]{2,1,0:T(8,128)}, u32[]{:S(2)}) copy-start(f32[4,8,128]{2,1,0:T(8,128)} %param.13) | copy-start | bytes 49156
  14.0 3.1 %copy-start.5 = (f32[4,8,128]{2,1,0:T(8,128)S(1)}, f32[4,8,128]{2,1,0:T(8,128)}, u32[]{:S(2)}) copy-start(f32[4,8,128]{2,1,0:T(8,128)} %param.14) | copy-start | bytes 49156
  14.0 3.1 %copy-start.8 = (s32[4,128]{1,0:T(4,128)S(1)}, s32[4,128]{1,0:T(4,128)}, u32[]{:S(2)}) copy-start(s32[4,128]{1,0:T(4,128)} %param.17) | copy-start | bytes 6148
  17.1 6.4 %copy-start.12 = (s32[8]{0:T(128)}, s32[8]{0:T(128)S(1)}, u32[]{:S(2)}) copy-start(s32[8]{0:T(128)S(1)} %iota_add_fusion) | copy-start | bytes 100
  24.3 8.5 %collective-permute-start.2 = (bf16[132,1,8,128]{3,0,2,1:T(8,128)(2,1)S(1)}, bf16[132,1,8,128]{3,0,2,1:T(8,128)(2,1)S(1)}, u32[]{:S(2)}, u32[]{:S(2)}) collective-permute-start(bf16[132,1,8,128]{3,0,2,1:T(8,128)(2,1)S(1)} %get-tuple-element.34), channel_id=1, source_target_pairs={{0,4},{4,8},{8,12},{1,5},{5,9},{9,13},{2,6},{6,10},{10,14},{3,7},{... | collective-permute-start | bytes 811016 | tf_op jit(solution)/shard_map/ppermute | solution.py:23
  27.8 9.1 %collective-permute-start.3 = (bf16[132,1,8,128]{3,0,2,1:T(8,128)(2,1)S(1)}, bf16[132,1,8,128]{3,0,2,1:T(8,128)(2,1)S(1)}, u32[]{:S(2)}, u32[]{:S(2)}) collective-permute-start(bf16[132,1,8,128]{3,0,2,1:T(8,128)(2,1)S(1)} %get-tuple-element.35), channel_id=1, source_target_pairs={{4,0},{8,4},{12,8},{5,1},{9,5},{13,9},{6,2},{10,6},{14,10},{7,3},{... | collective-permute-start | bytes 811016 | tf_op jit(solution)/shard_map/ppermute | solution.py:24
  29.1 7.9 %copy-start.3 = (f32[132,4,8,128]{3,2,1,0:T(8,128)S(1)}, f32[132,4,8,128]{3,2,1,0:T(8,128)}, u32[]{:S(2)}) copy-start(f32[132,4,8,128]{3,2,1,0:T(8,128)} %param.12) | copy-start | bytes 6488068
  40.6 7.5 %collective-permute-start.4 = (bf16[132,1,8,128]{3,0,2,1:T(8,128)(2,1)S(1)}, bf16[132,1,8,128]{3,0,2,1:T(8,128)(2,1)S(1)}, u32[]{:S(2)}, u32[]{:S(2)}) collective-permute-start(bf16[132,1,8,128]{3,0,2,1:T(8,128)(2,1)S(1)} %get-tuple-element.32), channel_id=1, source_target_pairs={{0,4},{4,8},{8,12},{1,5},{5,9},{9,13},{2,6},{6,10},{10,14},{3,7},{... | collective-permute-start | bytes 811016 | tf_op jit(solution)/shard_map/ppermute | solution.py:23
  44.0 8.4 %collective-permute-start.5 = (bf16[132,1,8,128]{3,0,2,1:T(8,128)(2,1)S(1)}, bf16[132,1,8,128]{3,0,2,1:T(8,128)(2,1)S(1)}, u32[]{:S(2)}, u32[]{:S(2)}) collective-permute-start(bf16[132,1,8,128]{3,0,2,1:T(8,128)(2,1)S(1)} %get-tuple-element.33), channel_id=1, source_target_pairs={{4,0},{8,4},{12,8},{5,1},{9,5},{13,9},{6,2},{10,6},{14,10},{7,3},{... | collective-permute-start | bytes 811016 | tf_op jit(solution)/shard_map/ppermute | solution.py:24
  52.5 4.1 %copy-start.10 = (f32[132]{0:T(256)S(1)}, f32[132]{0:T(256)}, u32[]{:S(2)}) copy-start(f32[132]{0:T(256)} %param.18) | copy-start | bytes 1588
  52.5 4.2 %copy-start.9 = (s32[8,8]{1,0:T(8,128)S(1)}, s32[8,8]{1,0:T(8,128)}, u32[]{:S(2)}) copy-start(s32[8,8]{1,0:T(8,128)} %param.22) | copy-start | bytes 772
  55.2 3.6 %collective-permute-start.6 = (f32[132,4,1,128]{3,0,2,1:T(8,128)S(1)}, f32[132,4,1,128]{3,0,2,1:T(8,128)S(1)}, u32[]{:S(2)}, u32[]{:S(2)}) collective-permute-start(f32[132,4,1,128]{3,0,2,1:T(8,128)S(1)} %slice.224), channel_id=1, source_target_pairs={{1,0},{3,2},{5,4},{7,6},{9,8},{11,10},{13,12},{15,14},{17,16},{19,... | collective-permute-start | bytes 811016 | tf_op jit(solution)/shard_map/ppermute | solution.py:32
  58.8 4.8 %copy-start.6 = (f32[4,8,128]{2,1,0:T(8,128)S(1)}, f32[4,8,128]{2,1,0:T(8,128)}, u32[]{:S(2)}) copy-start(f32[4,8,128]{2,1,0:T(8,128)} %param.16) | copy-start | bytes 49156
  58.8 4.8 %copy-start.7 = (f32[4,8,128]{2,1,0:T(8,128)S(1)}, f32[4,8,128]{2,1,0:T(8,128)}, u32[]{:S(2)}) copy-start(f32[4,8,128]{2,1,0:T(8,128)} %param.15) | copy-start | bytes 49156
  59.6 4.0 %collective-permute-start.7 = (f32[2,4,8,128]{3,2,1,0:T(8,128)S(1)}, f32[2,4,8,128]{3,2,1,0:T(8,128)S(1)}, u32[]{:S(2)}, u32[]{:S(2)}) collective-permute-start(f32[2,4,8,128]{3,2,1,0:T(8,128)S(1)} %pad_maximum_fusion.10), channel_id=1, source_target_pairs={{0,2},{2,0},{1,3},{3,1},{4,6},{6,4},{5,7},{7,5},{8,10},{10,8},{9,1... | collective-permute-start | bytes 98312 | tf_op jit(solution)/shard_map/ppermute | solution.py:146
  65.6 13.5 %collective-permute-start.8 = (bf16[132,2,8,128]{3,2,1,0:T(8,128)(2,1)}, bf16[132,2,8,128]{3,2,1,0:T(8,128)(2,1)}, u32[]{:S(2)}, u32[]{:S(2)}) collective-permute-start(bf16[132,2,8,128]{3,2,1,0:T(8,128)(2,1)} %bitcast.64), channel_id=1, source_target_pairs={{0,2},{2,0},{1,3},{3,1},{4,6},{6,4},{5,7},{7,5},{8,10},{10,8},{9,1... | collective-permute-start | bytes 1622024 | tf_op jit(solution)/shard_map/ppermute | solution.py:99
  97.5 1.9 %copy-start.13 = (s32[8]{0:T(128)S(1)}, s32[8]{0:T(128)}, u32[]{:S(2)}) copy-start(s32[8]{0:T(128)} %copy-done.12) | copy-start | bytes 100
  97.9 12.4 %collective-permute-start.9 = (bf16[132,2,8,128]{3,2,1,0:T(8,128)(2,1)S(1)}, bf16[132,2,8,128]{3,2,1,0:T(8,128)(2,1)}, u32[]{:S(2)}, u32[]{:S(2)}) collective-permute-start(bf16[132,2,8,128]{3,2,1,0:T(8,128)(2,1)S(1)} %slice_bitcast_fusion), channel_id=1, source_target_pairs={{0,2},{2,0},{1,3},{3,1},{4,6},{6,4},{5,7},{7,5},{8,10},{10,8},{9,1... | collective-permute-start | bytes 1622024 | tf_op jit(solution)/shard_map/ppermute | solution.py:102
  112.3 2.3 %copy-start.1 = (bf16[4,33,33]{2,0,1:T(4,128)(2,1)S(1)}, bf16[4,33,33]{2,0,1:T(4,128)(2,1)}, u32[]{:S(2)}) copy-start(bf16[4,33,33]{2,0,1:T(4,128)(2,1)} %param.23) | copy-start | bytes 26140

commit v2 on v1

--- a/solution.py
+++ b/solution.py
@@ -1,6 +1,7 @@
 import jax
 import jax.numpy as jnp
 from jax import lax
+from jax.experimental import pallas as pl
 from jax.sharding import PartitionSpec as P
 
 SUB = 8
@@ -85,25 +86,76 @@
     return change.reshape(local_bins, width_x, width_z, width_y).astype(jnp.float32)
 
 
+def collision_kernel(table_ref, first_ref, change_ref):
+    rows = first_ref.shape[0]
+    first = first_ref[...].astype(jnp.float32)
+    table = table_ref[...]
+    iterate = first
+    for substep in range(SUB):
+        products = jnp.dot(table, iterate.astype(jnp.bfloat16), preferred_element_type=jnp.float32)
+        iterate = iterate + collision_rate * products[rows:] * products[:rows]
+    change_ref[...] = (iterate - first).astype(change_ref.dtype)
+
+
+def collide_tiled(table, first, tile=512):
+    rows, cells = first.shape
+    tile = min(tile, cells)
+    return pl.pallas_call(
+        collision_kernel,
+        out_shape=jax.ShapeDtypeStruct((rows, cells), jnp.bfloat16),
+        grid=(cells // tile,),
+        in_specs=[
+            pl.BlockSpec((2 * rows, rows), lambda i: (0, 0)),
+            pl.BlockSpec((rows, tile), lambda i: (0, i)),
+        ],
+        out_specs=pl.BlockSpec((rows, tile), lambda i: (0, i)),
+        cost_estimate=pl.CostEstimate(
+            flops=SUB * 4 * rows * rows * cells,
+            bytes_accessed=4 * rows * cells + 4 * rows * rows,
+            transcendentals=0,
+        ),
+    )(table, first)
+
+
+def padded_bins(array, axis, part, pad):
+    pieces = []
+    for lo in (0, part):
+        pieces.append(lax.slice_in_dim(array, lo, lo + part, axis=axis))
+        shape = list(array.shape)
+        shape[axis] = pad
+        pieces.append(jnp.zeros(shape, array.dtype))
+    return jnp.concatenate(pieces, axis=axis)
+
+
 def paired_collision(grown, bin_order, kernel_index, collision_kernels):
     local_bins, width_x, width_z, width_y = grown.shape
+    pad = -local_bins % 8
+    part = local_bins + pad
     swap = [(0, 1), (1, 0)]
     me = lax.axis_index("bins")
     order = lax.dynamic_slice_in_dim(
         jnp.concatenate([bin_order, bin_order]), me * local_bins, 2 * local_bins
     )
     table = coupling_table(order, kernel_index, collision_kernels)
-    halves = grown.astype(jnp.bfloat16).reshape(local_bins, 2, width_x // 2, width_z, width_y)
+    all_bins = table.shape[1]
+    table = jnp.concatenate(
+        [
+            padded_bins(padded_bins(table[:all_bins], 0, local_bins, pad), 1, local_bins, pad),
+            padded_bins(padded_bins(table[all_bins:], 0, local_bins, pad), 1, local_bins, pad),
+        ],
+        axis=0,
+    )
+    halves = grown.astype(jnp.bfloat16).reshape(local_bins, 2, -1)
     own = lax.dynamic_index_in_dim(halves, me, axis=1, keepdims=False)
     away = lax.dynamic_index_in_dim(halves, 1 - me, axis=1, keepdims=False)
     arrived = lax.ppermute(away, "bins", swap)
-    first = jnp.concatenate([own, arrived], axis=0).reshape(2 * local_bins, -1).astype(jnp.float32)
-    change = collide(table, first).reshape(2 * local_bins, width_x // 2, width_z, width_y)
-    back = lax.ppermute(change[local_bins:], "bins", swap)
+    gap = jnp.zeros((pad, own.shape[1]), own.dtype)
+    first = jnp.concatenate([own, gap, arrived, gap], axis=0)
+    change = collide_tiled(table, first)
+    back = lax.ppermute(change[part : part + local_bins], "bins", swap)
     pair = jnp.stack([change[:local_bins], back], axis=1)
     pair = jnp.where(me == 0, pair, pair[:, ::-1])
     return pair.reshape(local_bins, width_x, width_z, width_y).astype(jnp.float32)
-
 
 def body(
     bin_mass,

time: 115 us -> 127 us (1.10)
  Pallas kernels: 0 us -> 15.6 us
  matrix products: 16 us -> 3.77 us
  local copies, waits for them, and re-layouts: 20.5 us -> 23.9 us
  waiting for transfers between devices: 35.8 us -> 38.2 us
  other arithmetic: 19.2 us -> 20.7 us
    pallas_call x0 -> x1, Pallas kernels: none -> 15.6 us  [collide_tiled(): pl.pallas_call(collision_kernel, out_shape=jax.ShapeDtypeStruct((rows, ce...]
    dot_general x8 -> x0, matrix products: 12.3 us -> none  [collide(): jnp.dot(table, iterate.astype(jnp.bfloat16), preferred_element_type=jnp.f...]
    unnamed x40 -> x36, local copies, waits for them, and re-layouts: 8.49 us -> 0.7 us
    convert_element_type x1 -> x2, local copies, waits for them, and re-layouts: 0.65 us -> 6.98 us  [paired_collision(): pair.reshape(local_bins, width_x, width_z, width_y).astype(jnp.float32)]
    ppermute x1, waiting for transfers between devices: 6.35 us -> 10.4 us  [paired_collision(): arrived = lax.ppermute(away, 'bins', swap)]
    add x3 -> x0, other arithmetic: 3.41 us -> none  [collide(): iterate + collision_rate * products[all_bins:] * products[:all_bins]]
    mul x1, other arithmetic: 0.59 us -> 3.4 us  [body(): mass_next = (grown + change) * open_cells]
    reshape x0 -> x1, local copies, waits for them, and re-layouts: none -> 2.5 us  [paired_collision(): halves = grown.astype(jnp.bfloat16).reshape(local_bins, 2, -1)]
  transfers between devices with their start and end apart: 10 -> 10, of which waited for: 9 -> 8; matrix products, arithmetic and copies ran while one was open for 13% -> 11% of each run, Pallas kernels for 0% -> 0%
where the time goes in v2:
time: 127 us; the launch traced here: 126 us
  waiting for transfers between devices  38.2 us (30%)
  local copies, waits for them, and re-layouts  23.9 us (19%)
  starting transfers between devices  23 us (18%)
  other arithmetic  20.7 us (16%)
  Pallas kernels  15.6 us (12%)
  matrix products  3.77 us (3%)
    pallas_call x1, Pallas kernels, collide_tiled(): pl.pallas_call(collision_kernel, out_shape=jax.ShapeDtypeStruct((rows, ce...  15.6 us
    ppermute x3, starting transfers between devices, extended_2(): before = lax.ppermute(last.astype(link), axis, up).astype(array.dtype)  13 us
    ppermute x1, waiting for transfers between devices, paired_collision(): back = lax.ppermute(change[part:part + local_bins], 'bins', swap)  11.2 us
    ppermute x1, waiting for transfers between devices, paired_collision(): arrived = lax.ppermute(away, 'bins', swap)  10.4 us
    ppermute x3, waiting for transfers between devices, extended_2(): after = lax.ppermute(first.astype(link), axis, down).astype(array.dtype)  8.46 us
    another operation x4, other arithmetic  7.78 us
    slice x4, local copies, waits for them, and re-layouts, tendency(): south_cells = jnp.roll(center_cells, 1, axis=3)  7.18 us
    convert_element_type x2, local copies, waits for them, and re-layouts, paired_collision(): pair.reshape(local_bins, width_x, width_z, width_y).astype(jnp.float32)  6.98 us
  transfers between devices with their start and end apart: 10, of which 8 were waited for; matrix products, arithmetic and copies ran while one was open for 11% of the time, Pallas kernels for 0%

profile of v2, /device:TPU:0, one launch (start us, length us, event | category | flops | bytes accessed | tf_op | source)
XLA Modules:
  0.0 126.3 jit_solution(12898009981773005258)
XLA Ops:
  0.7 2.0 %convert.25 = bf16[132,4,8,128]{3,2,1,0:T(8,128)(2,1)S(1)} convert(f32[132,4,8,128]{3,2,1,0:T(8,128)} %param.12) | non-fusion elementwise | flops 540672 | bytes 3244032 | tf_op jit(solution)/shard_map/convert.10
  2.7 4.9 %collective-permute-start = (bf16[132,1,8,128]{3,2,1,0:T(8,128)(2,1)S(1)}, bf16[132,1,8,128]{3,2,1,0:T(8,128)(2,1)S(1)}, u32[]{:S(2)}, u32[]{:S(2)}) collective-permute-start(bf16[132,1,8,128]{3,2,1,0:T(8,128)(2,1)S(1)} %get-tuple-element.32), channel_id=1, source_target_pairs={{0,4},{4,8},{8,12},{1,5},{5,9},{9,13},{2,6},{6,10},{10,14},{3,7},{... | collective-permute-start | bytes 811016 | tf_op jit(solution)/shard_map/ppermute | solution.py:24
  7.7 1.3 %collective-permute-start.1 = (bf16[132,1,8,128]{3,2,1,0:T(8,128)(2,1)S(1)}, bf16[132,1,8,128]{3,2,1,0:T(8,128)(2,1)S(1)}, u32[]{:S(2)}, u32[]{:S(2)}) collective-permute-start(bf16[132,1,8,128]{3,2,1,0:T(8,128)(2,1)S(1)} %get-tuple-element.33), channel_id=1, source_target_pairs={{4,0},{8,4},{12,8},{5,1},{9,5},{13,9},{6,2},{10,6},{14,10},{7,3},{... | collective-permute-start | bytes 811016 | tf_op jit(solution)/shard_map/ppermute | solution.py:25
  9.0 2.9 %fusion.74 = (f32[132,4,8,1]{3,2,1,0:T(8,128)}, f32[132,4,8,1]{3,2,1,0:T(8,128)}) fusion(f32[132,4,8,128]{3,2,1,0:T(8,128)S(1)} %copy-done.2), kind=kLoop, calls=%fused_computation.121 | loop fusion | bytes 67584 | tf_op jit(solution)/shard_map/jit(_roll_static)/slice | solution.py:37
  11.9 2.8 %fusion.75 = (f32[132,4,8,127]{3,2,1,0:T(8,128)}, f32[132,4,8,127]{3,2,1,0:T(8,128)}) fusion(f32[132,4,8,128]{3,2,1,0:T(8,128)S(1)} %copy-done.2), kind=kLoop, calls=%fused_computation.122 | loop fusion | bytes 8583168 | tf_op jit(solution)/shard_map/jit(_roll_static)/slice | solution.py:37
  14.9 0.4 fusion.48
  15.4 2.0 %multiply_reduce_fusion = f32[264,8,33]{0,2,1:T(8,128)S(1)} fusion(f32[264,8]{0,1:T(8,128)S(1)} %fusion.61, f32[8,8,33,33]{3,1,2,0:T(8,128)S(1)} %fusion.48, s32[264]{0:T(512)S(1)} %get-tuple-element.47), kind=kOutput, calls=%fused_computation | convolution fusion | flops 221851072 | bytes 567072 | tf_op jit(solution)/shard_map/bm,acmn->bacn/dot_general | solution.py:60
  17.4 1.1 fusion.38
  18.7 3.5 %fusion.68 = (bf16[132,4,8,128]{3,2,1,0:T(8,128)(2,1)S(1)}, f32[132,4,8,128]{3,2,1,0:T(8,128)S(1)}) fusion(f32[132,4,8,128]{3,2,1,0:T(8,128)S(1)} %copy-done.2, f32[132,4,8,1]{3,2,1,0:T(8,128)S(1)} %copy-done.4, f32[132,4,8,127]{3,2,1,0:T(8,128)} %get-tuple-element.23, f32[4,8,128]{2,1,0:T(8,128)S(1)} %get-tuple-element.51, ...), kind=kLoop, calls=%fused_computation.116 | loop fusion | flops 10272768 | bytes 10878976 | tf_op jit(solution)/shard_map/convert.8
  22.2 0.8 fusion.72
  23.0 4.6 %collective-permute-start.2 = (bf16[132,1,8,128]{3,2,1,0:T(8,128)(2,1)S(1)}, bf16[132,1,8,128]{3,2,1,0:T(8,128)(2,1)S(1)}, u32[]{:S(2)}, u32[]{:S(2)}) collective-permute-start(bf16[132,1,8,128]{3,2,1,0:T(8,128)(2,1)S(1)} %get-tuple-element.30), channel_id=1, source_target_pairs={{0,4},{4,8},{8,12},{1,5},{5,9},{9,13},{2,6},{6,10},{10,14},{3,7},{... | collective-permute-start | bytes 811016 | tf_op jit(solution)/shard_map/ppermute | solution.py:24
  27.6 1.3 %collective-permute-start.3 = (bf16[132,1,8,128]{3,2,1,0:T(8,128)(2,1)S(1)}, bf16[132,1,8,128]{3,2,1,0:T(8,128)(2,1)S(1)}, u32[]{:S(2)}, u32[]{:S(2)}) collective-permute-start(bf16[132,1,8,128]{3,2,1,0:T(8,128)(2,1)S(1)} %get-tuple-element.31), channel_id=1, source_target_pairs={{4,0},{8,4},{12,8},{5,1},{9,5},{13,9},{6,2},{10,6},{14,10},{7,3},{... | collective-permute-start | bytes 811016 | tf_op jit(solution)/shard_map/ppermute | solution.py:25
  28.9 0.8 fusion.73
  29.6 3.1 %collective-permute-done.2 = bf16[132,1,8,128]{3,2,1,0:T(8,128)(2,1)S(1)} collective-permute-done((bf16[132,1,8,128]{3,2,1,0:T(8,128)(2,1)S(1)}, bf16[132,1,8,128]{3,2,1,0:T(8,128)(2,1)S(1)}, u32[]{:S(2)}, u32[]{:S(2)}) %collective-permute-start.2) | collective-permute-done | bytes 270368 | tf_op jit(solution)/shard_map/ppermute | solution.py:24
  32.7 4.1 %collective-permute-done.3 = bf16[132,1,8,128]{3,2,1,0:T(8,128)(2,1)S(1)} collective-permute-done((bf16[132,1,8,128]{3,2,1,0:T(8,128)(2,1)S(1)}, bf16[132,1,8,128]{3,2,1,0:T(8,128)(2,1)S(1)}, u32[]{:S(2)}, u32[]{:S(2)}) %collective-permute-start.3) | collective-permute-done | bytes 270368 | tf_op jit(solution)/shard_map/ppermute | solution.py:25
  36.9 2.3 %fusion.66 = (bf16[132,4,8,128]{3,2,1,0:T(8,128)(2,1)S(1)}, f32[132,4,8,128]{3,2,1,0:T(8,128)S(1)}) fusion(f32[132,4,8,128]{3,2,1,0:T(8,128)S(1)} %copy-done.2, f32[132,4,8,128]{3,2,1,0:T(8,128)S(1)} %get-tuple-element.11, f32[132,4,8,1]{3,2,1,0:T(8,128)S(1)} %get-tuple-element.17, f32[132,4,8,127]{3,2,1,0:T(8,128)S(1)} %get-tuple-element.19, ...), kind=kLoop, calls=%fused_computation.115 | loop fusion | flops 10272768 | bytes 13041664 | tf_op jit(solution)/shard_map/convert.6
  39.2 0.8 fusion.70
  40.0 3.5 %collective-permute-start.4 = (bf16[132,1,8,128]{3,2,1,0:T(8,128)(2,1)S(1)}, bf16[132,1,8,128]{3,2,1,0:T(8,128)(2,1)S(1)}, u32[]{:S(2)}, u32[]{:S(2)}) collective-permute-start(bf16[132,1,8,128]{3,2,1,0:T(8,128)(2,1)S(1)} %get-tuple-element.28), channel_id=1, source_target_pairs={{0,4},{4,8},{8,12},{1,5},{5,9},{9,13},{2,6},{6,10},{10,14},{3,7},{... | collective-permute-start | bytes 811016 | tf_op jit(solution)/shard_map/ppermute | solution.py:24
  43.5 1.3 %collective-permute-start.5 = (bf16[132,1,8,128]{3,2,1,0:T(8,128)(2,1)S(1)}, bf16[132,1,8,128]{3,2,1,0:T(8,128)(2,1)S(1)}, u32[]{:S(2)}, u32[]{:S(2)}) collective-permute-start(bf16[132,1,8,128]{3,2,1,0:T(8,128)(2,1)S(1)} %get-tuple-element.29), channel_id=1, source_target_pairs={{4,0},{8,4},{12,8},{5,1},{9,5},{13,9},{6,2},{10,6},{14,10},{7,3},{... | collective-permute-start | bytes 811016 | tf_op jit(solution)/shard_map/ppermute | solution.py:25
  44.8 0.8 fusion.71
  45.5 1.9 %collective-permute-done.4 = bf16[132,1,8,128]{3,2,1,0:T(8,128)(2,1)S(1)} collective-permute-done((bf16[132,1,8,128]{3,2,1,0:T(8,128)(2,1)S(1)}, bf16[132,1,8,128]{3,2,1,0:T(8,128)(2,1)S(1)}, u32[]{:S(2)}, u32[]{:S(2)}) %collective-permute-start.4) | collective-permute-done | bytes 270368 | tf_op jit(solution)/shard_map/ppermute | solution.py:24
  47.4 4.4 %collective-permute-done.5 = bf16[132,1,8,128]{3,2,1,0:T(8,128)(2,1)S(1)} collective-permute-done((bf16[132,1,8,128]{3,2,1,0:T(8,128)(2,1)S(1)}, bf16[132,1,8,128]{3,2,1,0:T(8,128)(2,1)S(1)}, u32[]{:S(2)}, u32[]{:S(2)}) %collective-permute-start.5) | collective-permute-done | bytes 270368 | tf_op jit(solution)/shard_map/ppermute | solution.py:25
  51.9 2.3 %fusion.5 = f32[132,4,8,128]{3,2,1,0:T(8,128)S(1)} fusion(f32[132,4,8,128]{3,2,1,0:T(8,128)S(1)} %copy-done.2, f32[132,4,8,128]{3,2,1,0:T(8,128)S(1)} %get-tuple-element.9, f32[132,1,8,128]{3,2,1,0:T(8,128)S(1)} %convert_element_type.50, f32[132,1,8,128]{3,2,1,0:T(8,128)S(1)} %convert_element_type.49, f32[132,4,8,127]{3,2,1,0:T(8,128)S(1)} %get-tuple-element.13, ...), kind=kLoop, calls=%fused_computation.7 | loop fusion | flops 9191424 | bytes 11960320 | tf_op jit(solution)/shard_map/add | solution.py:183
  54.4 1.5 %collective-permute-start.6 = (f32[132,4,1,128]{3,2,1,0:T(1,128)S(1)}, f32[132,4,1,128]{3,2,1,0:T(1,128)S(1)}, u32[]{:S(2)}, u32[]{:S(2)}) collective-permute-start(f32[132,4,1,128]{3,2,1,0:T(1,128)S(1)} %slice.193), channel_id=1, source_target_pairs={{1,0},{3,2},{5,4},{7,6},{9,8},{11,10},{13,12},{15,14},{17,16},{19,... | collective-permute-start | bytes 811016 | tf_op jit(solution)/shard_map/ppermute | solution.py:33
  55.9 0.7 fusion.81
  56.8 1.0 collective-permute-done.6
  57.8 1.0 multiply_reduce_fusion.1
  58.9 1.6 %collective-permute-start.7 = (f32[2,4,8,128]{3,2,1,0:T(8,128)S(1)}, f32[2,4,8,128]{3,2,1,0:T(8,128)S(1)}, u32[]{:S(2)}, u32[]{:S(2)}) collective-permute-start(f32[2,4,8,128]{3,2,1,0:T(8,128)S(1)} %pad_maximum_fusion.12), channel_id=1, source_target_pairs={{0,2},{2,0},{1,3},{3,1},{4,6},{6,4},{5,7},{7,5},{8,10},{10,8},{9,1... | collective-permute-start | bytes 98312 | tf_op jit(solution)/shard_map/ppermute | solution.py:198
  60.4 0.3 convolution_convert_fusion
  60.7 2.1 %collective-permute-done.7 = f32[2,4,8,128]{3,2,1,0:T(8,128)S(1)} collective-permute-done((f32[2,4,8,128]{3,2,1,0:T(8,128)S(1)}, f32[2,4,8,128]{3,2,1,0:T(8,128)S(1)}, u32[]{:S(2)}, u32[]{:S(2)}) %collective-permute-start.7) | collective-permute-done | bytes 32800 | tf_op jit(solution)/shard_map/ppermute | solution.py:198
  62.9 0.6 fusion.53
  63.5 1.4 %fusion.36 = bf16[132,4,8,128]{3,2,1,0:T(8,128)(2,1)} fusion(f32[132,4,8,128]{3,2,1,0:T(8,128)S(1)} %get-tuple-element.7, f32[4,8,128]{2,1,0:T(8,128)S(1)} %get-tuple-element.6, f32[132]{0:T(256)S(1)} %get-tuple-element.53), kind=kLoop, calls=%fused_computation.54 | loop fusion | flops 2162688 | bytes 3260944 | tf_op jit(solution)/shard_map/convert_element_type | solution.py:148
  64.9 2.5 %reshape.35 = bf16[132,2,2048]{2,1,0:T(2,128)(2,1)S(1)} reshape(bf16[132,4,8,128]{3,2,1,0:T(8,128)(2,1)} %fusion.36) | data formatting | bytes 2162688 | tf_op jit(solution)/shard_map/reshape | solution.py:148
  67.4 2.2 %constant_dynamic-slice_fusion.1 = (bf16[132,1,2048]{2,1,0:T(2,128)(2,1)S(1)}, bf16[132,1,2048]{2,1,0:T(2,128)(2,1)S(1)}) fusion(bf16[132,2,2048]{2,1,0:T(2,128)(2,1)S(1)} %reshape.35, s32[]{:T(128)S(6)} %select_n.34, s32[]{:T(128)S(6)} %select_n.35), kind=kLoop, calls=%fused_computation.111 | loop fusion | bytes 2162696 | tf_op jit(solution)/shard_map/jit(dynamic_index_in_dim)/dynamic_slice | solution.py:149
  69.6 0.3 copy.37
  69.9 1.6 %collective-permute-start.8 = (bf16[132,2048]{1,0:T(8,128)(2,1)S(1)}, bf16[132,2048]{1,0:T(8,128)(2,1)S(1)}, u32[]{:S(2)}, u32[]{:S(2)}) collective-permute-start(bf16[132,2048]{1,0:T(8,128)(2,1)S(1)} %bitcast.49), channel_id=1, source_target_pairs={{0,2},{2,0},{1,3},{3,1},{4,6},{6,4},{5,7},{7,5},{8,10},{10,8},{9,1... | collective-permute-start | bytes 1622024 | tf_op jit(solution)/shard_map/ppermute | solution.py:151
  71.8 1.1 maximum_maximum_fusion.table_ref
  72.9 0.3 copy.38
  73.2 10.4 %collective-permute-done.8 = bf16[132,2048]{1,0:T(8,128)(2,1)S(1)} collective-permute-done((bf16[132,2048]{1,0:T(8,128)(2,1)S(1)}, bf16[132,2048]{1,0:T(8,128)(2,1)S(1)}, u32[]{:S(2)}, u32[]{:S(2)}) %collective-permute-start.8) | collective-permute-done | bytes 540704 | tf_op jit(solution)/shard_map/ppermute | solution.py:151
  83.6 1.1 pad_maximum_fusion.6.first_ref
  84.7 15.6 %shard_map.139 = bf16[272,2048]{1,0:T(8,128)(2,1)} custom-call(bf16[544,272]{1,0:T(8,128)(2,1)} %maximum_maximum_fusion.table_ref, bf16[272,2048]{1,0:T(8,128)(2,1)} %pad_maximum_fusion.6.first_ref), custom_call_target="tpu_custom_call" | custom-call | flops 4848615424 | bytes 2524160 | tf_op jit(solution)/shard_map/pallas_call | solution.py:103
  100.3 1.3 %slice_bitcast_fusion = (bf16[132,1,2048]{2,0,1:T(8,128)(2,1)S(1)}, bf16[132,2048]{1,0:T(8,128)(2,1)S(1)}) fusion(bf16[272,2048]{1,0:T(8,128)(2,1)} %shard_map.139), kind=kLoop, calls=%fused_computation.63 | loop fusion | bytes 2162688 | tf_op jit(solution)/shard_map/stack | solution.py:156
  101.6 1.6 %collective-permute-start.9 = (bf16[132,2048]{1,0:T(8,128)(2,1)S(1)}, bf16[132,2048]{1,0:T(8,128)(2,1)}, u32[]{:S(2)}, u32[]{:S(2)}) collective-permute-start(bf16[132,2048]{1,0:T(8,128)(2,1)S(1)} %get-tuple-element.25), channel_id=1, source_target_pairs={{0,2},{2,0},{1,3},{3,1},{4,6},{6,4},{5,7},{7,5},{8,10},{10,8},{9,1... | collective-permute-start | bytes 1622024 | tf_op jit(solution)/shard_map/ppermute | solution.py:155
  103.2 11.2 %collective-permute-done.9 = bf16[132,2048]{1,0:T(8,128)(2,1)} collective-permute-done((bf16[132,2048]{1,0:T(8,128)(2,1)S(1)}, bf16[132,2048]{1,0:T(8,128)(2,1)}, u32[]{:S(2)}, u32[]{:S(2)}) %collective-permute-start.9) | collective-permute-done | bytes 540704 | tf_op jit(solution)/shard_map/ppermute | solution.py:155
  114.5 1.2 pad_maximum_fusion.7
  115.9 3.0 %copy.23 = f32[132,2,2048]{2,1,0:T(2,128)} copy(f32[132,2,2048]{2,0,1:T(8,128)S(1)} %fusion.39) | data formatting | bytes 4325376 | tf_op jit(solution)/shard_map/convert_element_type | solution.py:158
  118.9 4.0 %reshape.36 = f32[132,4,8,128]{3,2,1,0:T(8,128)} reshape(f32[132,2,2048]{2,1,0:T(2,128)} %copy.23) | data formatting | bytes 4325376 | tf_op jit(solution)/shard_map/convert_element_type | solution.py:158
  122.9 3.4 %add_multiply_fusion = f32[132,4,8,128]{3,2,1,0:T(8,128)} fusion(f32[132,4,8,128]{3,2,1,0:T(8,128)} %reshape.36, f32[132,4,8,128]{3,2,1,0:T(8,128)S(1)} %get-tuple-element.7, f32[4,8,128]{2,1,0:T(8,128)S(1)} %compare_convert_fusion, f32[4,8,128]{2,1,0:T(8,128)S(1)} %get-tuple-element.6, f32[132]{0:T(256)S(1)} %get-tuple-element.53), kind=kLoop, calls=%fused_computation.50 | loop fusion | flops 2703360 | bytes 6521360 | tf_op jit(solution)/shard_map/mul | solution.py:210
  (64 shorter events, 1.7 us)
Async XLA Ops:
  0.6 14.3 %copy-start = (bf16[4,33,33]{2,0,1:T(4,128)(2,1)S(1)}, bf16[4,33,33]{2,0,1:T(4,128)(2,1)}, u32[]{:S(2)}) copy-start(bf16[4,33,33]{2,0,1:T(4,128)(2,1)} %param.23) | copy-start | bytes 26140
  0.6 8.3 %copy-start.2 = (f32[132,4,8,128]{3,2,1,0:T(8,128)S(1)}, f32[132,4,8,128]{3,2,1,0:T(8,128)}, u32[]{:S(2)}) copy-start(f32[132,4,8,128]{3,2,1,0:T(8,128)} %param.12) | copy-start | bytes 6488068
  2.7 15.9 %collective-permute-start = (bf16[132,1,8,128]{3,2,1,0:T(8,128)(2,1)S(1)}, bf16[132,1,8,128]{3,2,1,0:T(8,128)(2,1)S(1)}, u32[]{:S(2)}, u32[]{:S(2)}) collective-permute-start(bf16[132,1,8,128]{3,2,1,0:T(8,128)(2,1)S(1)} %get-tuple-element.32), channel_id=1, source_target_pairs={{0,4},{4,8},{8,12},{1,5},{5,9},{9,13},{2,6},{6,10},{10,14},{3,7},{... | collective-permute-start | bytes 811016 | tf_op jit(solution)/shard_map/ppermute | solution.py:24
  7.7 11.0 %collective-permute-start.1 = (bf16[132,1,8,128]{3,2,1,0:T(8,128)(2,1)S(1)}, bf16[132,1,8,128]{3,2,1,0:T(8,128)(2,1)S(1)}, u32[]{:S(2)}, u32[]{:S(2)}) collective-permute-start(bf16[132,1,8,128]{3,2,1,0:T(8,128)(2,1)S(1)} %get-tuple-element.33), channel_id=1, source_target_pairs={{4,0},{8,4},{12,8},{5,1},{9,5},{13,9},{6,2},{10,6},{14,10},{7,3},{... | collective-permute-start | bytes 811016 | tf_op jit(solution)/shard_map/ppermute | solution.py:25
  11.8 2.9 %copy-start.15 = (s32[264]{0:T(512)S(1)}, s32[264]{0:T(512)}, u32[]{:S(2)}) copy-start(s32[264]{0:T(512)} %param.21) | copy-start | bytes 3172
  11.8 3.1 %copy-start.14 = (f32[132]{0:T(256)S(1)}, f32[132]{0:T(256)}, u32[]{:S(2)}) copy-start(f32[132]{0:T(256)} %param.19) | copy-start | bytes 1588
  11.8 3.1 %copy-start.16 = (f32[132]{0:T(256)S(1)}, f32[132]{0:T(256)}, u32[]{:S(2)}) copy-start(f32[132]{0:T(256)} %param.20) | copy-start | bytes 1588
  11.8 3.1 %copy-start.12 = (s32[8,8]{1,0:T(8,128)S(1)}, s32[8,8]{1,0:T(8,128)}, u32[]{:S(2)}) copy-start(s32[8,8]{1,0:T(8,128)} %param.22) | copy-start | bytes 772
  11.8 3.5 %copy-start.7 = (f32[4,8,128]{2,1,0:T(8,128)S(1)}, f32[4,8,128]{2,1,0:T(8,128)}, u32[]{:S(2)}) copy-start(f32[4,8,128]{2,1,0:T(8,128)} %param.13) | copy-start | bytes 49156
  11.8 3.5 %copy-start.8 = (f32[4,8,128]{2,1,0:T(8,128)S(1)}, f32[4,8,128]{2,1,0:T(8,128)}, u32[]{:S(2)}) copy-start(f32[4,8,128]{2,1,0:T(8,128)} %param.14) | copy-start | bytes 49156
  11.9 3.5 %copy-start.11 = (s32[4,128]{1,0:T(4,128)S(1)}, s32[4,128]{1,0:T(4,128)}, u32[]{:S(2)}) copy-start(s32[4,128]{1,0:T(4,128)} %param.17) | copy-start | bytes 6148
  15.4 3.3 %copy-start.3 = (f32[132,4,8,1]{3,2,1,0:T(8,128)S(1)}, f32[132,4,8,1]{3,2,1,0:T(8,128)}, u32[]{:S(2)}) copy-start(f32[132,4,8,1]{3,2,1,0:T(8,128)} %get-tuple-element.20) | copy-start | bytes 50692
  15.4 3.3 %copy-start.4 = (f32[132,4,8,1]{3,2,1,0:T(8,128)S(1)}, f32[132,4,8,1]{3,2,1,0:T(8,128)}, u32[]{:S(2)}) copy-start(f32[132,4,8,1]{3,2,1,0:T(8,128)} %get-tuple-element.21) | copy-start | bytes 50692
  23.0 9.7 %collective-permute-start.2 = (bf16[132,1,8,128]{3,2,1,0:T(8,128)(2,1)S(1)}, bf16[132,1,8,128]{3,2,1,0:T(8,128)(2,1)S(1)}, u32[]{:S(2)}, u32[]{:S(2)}) collective-permute-start(bf16[132,1,8,128]{3,2,1,0:T(8,128)(2,1)S(1)} %get-tuple-element.30), channel_id=1, source_target_pairs={{0,4},{4,8},{8,12},{1,5},{5,9},{9,13},{2,6},{6,10},{10,14},{3,7},{... | collective-permute-start | bytes 811016 | tf_op jit(solution)/shard_map/ppermute | solution.py:24
  27.6 9.3 %collective-permute-start.3 = (bf16[132,1,8,128]{3,2,1,0:T(8,128)(2,1)S(1)}, bf16[132,1,8,128]{3,2,1,0:T(8,128)(2,1)S(1)}, u32[]{:S(2)}, u32[]{:S(2)}) collective-permute-start(bf16[132,1,8,128]{3,2,1,0:T(8,128)(2,1)S(1)} %get-tuple-element.31), channel_id=1, source_target_pairs={{4,0},{8,4},{12,8},{5,1},{9,5},{13,9},{6,2},{10,6},{14,10},{7,3},{... | collective-permute-start | bytes 811016 | tf_op jit(solution)/shard_map/ppermute | solution.py:25
  40.0 7.4 %collective-permute-start.4 = (bf16[132,1,8,128]{3,2,1,0:T(8,128)(2,1)S(1)}, bf16[132,1,8,128]{3,2,1,0:T(8,128)(2,1)S(1)}, u32[]{:S(2)}, u32[]{:S(2)}) collective-permute-start(bf16[132,1,8,128]{3,2,1,0:T(8,128)(2,1)S(1)} %get-tuple-element.28), channel_id=1, source_target_pairs={{0,4},{4,8},{8,12},{1,5},{5,9},{9,13},{2,6},{6,10},{10,14},{3,7},{... | collective-permute-start | bytes 811016 | tf_op jit(solution)/shard_map/ppermute | solution.py:24
  43.5 8.4 %collective-permute-start.5 = (bf16[132,1,8,128]{3,2,1,0:T(8,128)(2,1)S(1)}, bf16[132,1,8,128]{3,2,1,0:T(8,128)(2,1)S(1)}, u32[]{:S(2)}, u32[]{:S(2)}) collective-permute-start(bf16[132,1,8,128]{3,2,1,0:T(8,128)(2,1)S(1)} %get-tuple-element.29), channel_id=1, source_target_pairs={{4,0},{8,4},{12,8},{5,1},{9,5},{13,9},{6,2},{10,6},{14,10},{7,3},{... | collective-permute-start | bytes 811016 | tf_op jit(solution)/shard_map/ppermute | solution.py:25
  51.9 4.0 %copy-start.13 = (f32[132]{0:T(256)S(1)}, f32[132]{0:T(256)}, u32[]{:S(2)}) copy-start(f32[132]{0:T(256)} %param.18) | copy-start | bytes 1588
  54.4 3.4 %collective-permute-start.6 = (f32[132,4,1,128]{3,2,1,0:T(1,128)S(1)}, f32[132,4,1,128]{3,2,1,0:T(1,128)S(1)}, u32[]{:S(2)}, u32[]{:S(2)}) collective-permute-start(f32[132,4,1,128]{3,2,1,0:T(1,128)S(1)} %slice.193), channel_id=1, source_target_pairs={{1,0},{3,2},{5,4},{7,6},{9,8},{11,10},{13,12},{15,14},{17,16},{19,... | collective-permute-start | bytes 811016 | tf_op jit(solution)/shard_map/ppermute | solution.py:33
  57.8 5.1 %copy-start.9 = (f32[4,8,128]{2,1,0:T(8,128)S(1)}, f32[4,8,128]{2,1,0:T(8,128)}, u32[]{:S(2)}) copy-start(f32[4,8,128]{2,1,0:T(8,128)} %param.16) | copy-start | bytes 49156
  57.8 5.1 %copy-start.10 = (f32[4,8,128]{2,1,0:T(8,128)S(1)}, f32[4,8,128]{2,1,0:T(8,128)}, u32[]{:S(2)}) copy-start(f32[4,8,128]{2,1,0:T(8,128)} %param.15) | copy-start | bytes 49156
  58.9 4.0 %collective-permute-start.7 = (f32[2,4,8,128]{3,2,1,0:T(8,128)S(1)}, f32[2,4,8,128]{3,2,1,0:T(8,128)S(1)}, u32[]{:S(2)}, u32[]{:S(2)}) collective-permute-start(f32[2,4,8,128]{3,2,1,0:T(8,128)S(1)} %pad_maximum_fusion.12), channel_id=1, source_target_pairs={{0,2},{2,0},{1,3},{3,1},{4,6},{6,4},{5,7},{7,5},{8,10},{10,8},{9,1... | collective-permute-start | bytes 98312 | tf_op jit(solution)/shard_map/ppermute | solution.py:198
  67.4 4.2 %copy-start.5 = (bf16[132,264]{1,0:T(8,128)(2,1)S(1)}, bf16[132,264]{1,0:T(8,128)(2,1)}, u32[]{:S(2)}) copy-start(bf16[132,264]{1,0:T(8,128)(2,1)} %get-tuple-element.38) | copy-start | bytes 209092
  67.4 4.2 %copy-start.6 = (bf16[132,264]{1,0:T(8,128)(2,1)S(1)}, bf16[132,264]{1,0:T(8,128)(2,1)}, u32[]{:S(2)}) copy-start(bf16[132,264]{1,0:T(8,128)(2,1)} %get-tuple-element.39) | copy-start | bytes 209092
  69.9 13.7 %collective-permute-start.8 = (bf16[132,2048]{1,0:T(8,128)(2,1)S(1)}, bf16[132,2048]{1,0:T(8,128)(2,1)S(1)}, u32[]{:S(2)}, u32[]{:S(2)}) collective-permute-start(bf16[132,2048]{1,0:T(8,128)(2,1)S(1)} %bitcast.49), channel_id=1, source_target_pairs={{0,2},{2,0},{1,3},{3,1},{4,6},{6,4},{5,7},{7,5},{8,10},{10,8},{9,1... | collective-permute-start | bytes 1622024 | tf_op jit(solution)/shard_map/ppermute | solution.py:151
  101.6 12.9 %collective-permute-start.9 = (bf16[132,2048]{1,0:T(8,128)(2,1)S(1)}, bf16[132,2048]{1,0:T(8,128)(2,1)}, u32[]{:S(2)}, u32[]{:S(2)}) collective-permute-start(bf16[132,2048]{1,0:T(8,128)(2,1)S(1)} %get-tuple-element.25), channel_id=1, source_target_pairs={{0,2},{2,0},{1,3},{3,1},{4,6},{6,4},{5,7},{7,5},{8,10},{10,8},{9,1... | collective-permute-start | bytes 1622024 | tf_op jit(solution)/shard_map/ppermute | solution.py:155
  118.9 7.4 %copy-start.1 = (bf16[4,33,33]{2,0,1:T(4,128)(2,1)S(1)}, bf16[4,33,33]{2,0,1:T(4,128)(2,1)}, u32[]{:S(2)}) copy-start(bf16[4,33,33]{2,0,1:T(4,128)(2,1)} %param.23) | copy-start | bytes 26140

commit v3 on v1

--- a/solution.py
+++ b/solution.py
@@ -96,14 +96,16 @@
     halves = grown.astype(jnp.bfloat16).reshape(local_bins, 2, width_x // 2, width_z, width_y)
     own = lax.dynamic_index_in_dim(halves, me, axis=1, keepdims=False)
     away = lax.dynamic_index_in_dim(halves, 1 - me, axis=1, keepdims=False)
-    arrived = lax.ppermute(away, "bins", swap)
-    first = jnp.concatenate([own, arrived], axis=0).reshape(2 * local_bins, -1).astype(jnp.float32)
-    change = collide(table, first).reshape(2 * local_bins, width_x // 2, width_z, width_y)
-    back = lax.ppermute(change[local_bins:], "bins", swap)
-    pair = jnp.stack([change[:local_bins], back], axis=1)
+    kept, returned = [], []
+    for chunk in range(width_x // 2):
+        arrived = lax.ppermute(away[:, chunk], "bins", swap)
+        first = jnp.concatenate([own[:, chunk], arrived], axis=0).reshape(2 * local_bins, -1).astype(jnp.float32)
+        change = collide(table, first).reshape(2 * local_bins, width_z, width_y)
+        returned.append(lax.ppermute(change[local_bins:], "bins", swap))
+        kept.append(change[:local_bins])
+    pair = jnp.stack([jnp.stack(kept, axis=1), jnp.stack(returned, axis=1)], axis=1)
     pair = jnp.where(me == 0, pair, pair[:, ::-1])
     return pair.reshape(local_bins, width_x, width_z, width_y).astype(jnp.float32)
-
 
 def body(
     bin_mass,

time: 115 us -> 115 us (level)
  waiting for transfers between devices: 35.8 us -> 32.5 us
  starting transfers between devices: 21.9 us -> 24.1 us
  other arithmetic: 19.2 us -> 20.6 us
  local copies, waits for them, and re-layouts: 20.5 us -> 19.1 us
    ppermute x1, waiting for transfers between devices: 1.61 us -> 0.01 us  [shifted(): return lax.ppermute(block, axis, route)]
    ppermute x3, waiting for transfers between devices: 9.87 us -> 8.38 us  [extended_2(): after = lax.ppermute(first.astype(link), axis, down).astype(array.dtype)]
    another operation x4 -> x6, other arithmetic: 8.73 us -> 7.29 us
    concatenate x1 -> x0, local copies, waits for them, and re-layouts: 1.33 us -> none  [paired_collision(): jnp.concatenate([own, arrived], axis=0).reshape(2 * local_bins, -1)]
    ppermute x2 -> x4, starting transfers between devices: 3.05 us -> 4.18 us  [the longest x2 2.16 us: paired_collision(): returned.append(lax.ppermute(change[local_bins:], 'bins', swap))]
    dot_general x8 -> x16, matrix products: 12.3 us -> 12.6 us  [collide(): jnp.dot(table, iterate.astype(jnp.bfloat16), preferred_element_type=jnp.f...]
    unnamed x40 -> x64, local copies, waits for them, and re-layouts: 8.49 us -> 8.78 us
    add x3 -> x6, other arithmetic: 3.41 us -> 3.63 us  [collide(): iterate + collision_rate * products[all_bins:] * products[:all_bins]]
  transfers between devices with their start and end apart: 10 -> 12, of which waited for: 9 -> 8; matrix products, arithmetic and copies ran while one was open for 13% -> 22% of each run, Pallas kernels for 0% -> 0%
where the time goes in v3:
time: 115 us; the launch traced here: 114 us
  waiting for transfers between devices  32.5 us (28%)
  starting transfers between devices  24.1 us (21%)
  other arithmetic  20.6 us (18%)
  local copies, waits for them, and re-layouts  19.1 us (17%)
  matrix products  16.4 us (14%)
  between operations  1.49 us (1%)
    ppermute x3, starting transfers between devices, extended_2(): before = lax.ppermute(last.astype(link), axis, up).astype(array.dtype)  13 us
    dot_general x16, matrix products, collide(): jnp.dot(table, iterate.astype(jnp.bfloat16), preferred_element_type=jnp.f...  12.6 us
    ppermute x2, waiting for transfers between devices, paired_collision(): returned.append(lax.ppermute(change[local_bins:], 'bins', swap))  10.4 us
    unnamed x64, local copies, waits for them, and re-layouts  8.78 us
    ppermute x3, waiting for transfers between devices, extended_2(): after = lax.ppermute(first.astype(link), axis, down).astype(array.dtype)  8.38 us
    another operation x3, other arithmetic  7.08 us
    slice x4, local copies, waits for them, and re-layouts, tendency(): south_cells = jnp.roll(center_cells, 1, axis=3)  6.97 us
    ppermute x2, waiting for transfers between devices, paired_collision(): arrived = lax.ppermute(away[:, chunk], 'bins', swap)  6.46 us
  transfers between devices with their start and end apart: 12, of which 8 were waited for; matrix products, arithmetic and copies ran while one was open for 22% of the time, Pallas kernels for 0%

profile of v3, /device:TPU:0, one launch (start us, length us, event | category | flops | bytes accessed | tf_op | source)
XLA Modules:
  0.0 114.3 jit_solution(6154877381695163407)
XLA Ops:
  0.7 3.0 %copy.77 = bf16[132,4,8,128]{3,0,2,1:T(8,128)(2,1)S(1)} copy(f32[132,4,8,128]{3,2,1,0:T(8,128)} %param.12) | data formatting | bytes 3244032 | tf_op args[0]
  3.7 5.6 %collective-permute-start = (bf16[132,1,8,128]{3,0,2,1:T(8,128)(2,1)S(1)}, bf16[132,1,8,128]{3,0,2,1:T(8,128)(2,1)}, u32[]{:S(2)}, u32[]{:S(2)}) collective-permute-start(bf16[132,1,8,128]{3,0,2,1:T(8,128)(2,1)S(1)} %get-tuple-element.36), channel_id=1, source_target_pairs={{0,4},{4,8},{8,12},{1,5},{5,9},{9,13},{2,6},{6,10},{10,14},{3,7},{... | collective-permute-start | bytes 811016 | tf_op jit(solution)/shard_map/ppermute | solution.py:23
  9.4 1.3 %collective-permute-start.1 = (bf16[132,1,8,128]{3,0,2,1:T(8,128)(2,1)S(1)}, bf16[132,1,8,128]{3,0,2,1:T(8,128)(2,1)S(1)}, u32[]{:S(2)}, u32[]{:S(2)}) collective-permute-start(bf16[132,1,8,128]{3,0,2,1:T(8,128)(2,1)S(1)} %get-tuple-element.37), channel_id=1, source_target_pairs={{4,0},{8,4},{12,8},{5,1},{9,5},{13,9},{6,2},{10,6},{14,10},{7,3},{... | collective-permute-start | bytes 811016 | tf_op jit(solution)/shard_map/ppermute | solution.py:24
  10.7 1.3 %copy.49 = f32[132,4,8,128]{3,0,2,1:T(8,128)S(1)} copy(f32[132,4,8,128]{3,2,1,0:T(8,128)S(1)} %copy-done.2) | data formatting | bytes 4325376 | tf_op args[0]
  11.9 2.8 %fusion.127 = (f32[132,4,8,1]{3,0,2,1:T(8,128)}, f32[132,4,8,1]{3,0,2,1:T(8,128)}) fusion(f32[132,4,8,128]{3,0,2,1:T(8,128)S(1)} %copy.49), kind=kLoop, calls=%fused_computation.209 | loop fusion | bytes 67584 | tf_op jit(solution)/shard_map/jit(_roll_static)/slice | solution.py:36
  14.8 2.8 %fusion.128 = (f32[132,4,8,127]{3,0,2,1:T(8,128)}, f32[132,4,8,127]{3,0,2,1:T(8,128)}) fusion(f32[132,4,8,128]{3,0,2,1:T(8,128)S(1)} %copy.49), kind=kLoop, calls=%fused_computation.210 | loop fusion | bytes 8583168 | tf_op jit(solution)/shard_map/jit(_roll_static)/slice | solution.py:36
  19.1 1.0 convert_element_type.101
  20.2 4.2 %fusion.121 = (bf16[132,4,8,128]{3,0,2,1:T(8,128)(2,1)S(1)}, f32[132,4,8,128]{3,0,2,1:T(8,128)S(1)}) fusion(f32[132,4,8,128]{3,0,2,1:T(8,128)S(1)} %copy.49, f32[132,4,8,1]{3,0,2,1:T(8,128)} %get-tuple-element.27, f32[132,4,8,127]{3,0,2,1:T(8,128)} %get-tuple-element.29, f32[4,8,128]{2,1,0:T(8,128)S(1)} %get-tuple-element.53, ...), kind=kLoop, calls=%fused_computation.204 | loop fusion | flops 10272768 | bytes 10878976 | tf_op jit(solution)/shard_map/convert.8
  25.1 4.6 %collective-permute-start.2 = (bf16[132,1,8,128]{3,0,2,1:T(8,128)(2,1)S(1)}, bf16[132,1,8,128]{3,0,2,1:T(8,128)(2,1)S(1)}, u32[]{:S(2)}, u32[]{:S(2)}) collective-permute-start(bf16[132,1,8,128]{3,0,2,1:T(8,128)(2,1)S(1)} %get-tuple-element.34), channel_id=1, source_target_pairs={{0,4},{4,8},{8,12},{1,5},{5,9},{9,13},{2,6},{6,10},{10,14},{3,7},{... | collective-permute-start | bytes 811016 | tf_op jit(solution)/shard_map/ppermute | solution.py:23
  29.7 1.3 %collective-permute-start.3 = (bf16[132,1,8,128]{3,0,2,1:T(8,128)(2,1)S(1)}, bf16[132,1,8,128]{3,0,2,1:T(8,128)(2,1)S(1)}, u32[]{:S(2)}, u32[]{:S(2)}) collective-permute-start(bf16[132,1,8,128]{3,0,2,1:T(8,128)(2,1)S(1)} %get-tuple-element.35), channel_id=1, source_target_pairs={{4,0},{8,4},{12,8},{5,1},{9,5},{13,9},{6,2},{10,6},{14,10},{7,3},{... | collective-permute-start | bytes 811016 | tf_op jit(solution)/shard_map/ppermute | solution.py:24
  31.7 3.3 %collective-permute-done.2 = bf16[132,1,8,128]{3,0,2,1:T(8,128)(2,1)S(1)} collective-permute-done((bf16[132,1,8,128]{3,0,2,1:T(8,128)(2,1)S(1)}, bf16[132,1,8,128]{3,0,2,1:T(8,128)(2,1)S(1)}, u32[]{:S(2)}, u32[]{:S(2)}) %collective-permute-start.2) | collective-permute-done | bytes 270368 | tf_op jit(solution)/shard_map/ppermute | solution.py:23
  35.1 4.1 %collective-permute-done.3 = bf16[132,1,8,128]{3,0,2,1:T(8,128)(2,1)S(1)} collective-permute-done((bf16[132,1,8,128]{3,0,2,1:T(8,128)(2,1)S(1)}, bf16[132,1,8,128]{3,0,2,1:T(8,128)(2,1)S(1)}, u32[]{:S(2)}, u32[]{:S(2)}) %collective-permute-start.3) | collective-permute-done | bytes 270368 | tf_op jit(solution)/shard_map/ppermute | solution.py:24
  39.2 2.9 %fusion.119 = (bf16[132,4,8,128]{3,0,2,1:T(8,128)(2,1)S(1)}, f32[132,4,8,128]{3,0,2,1:T(8,128)S(1)}) fusion(f32[132,4,8,128]{3,0,2,1:T(8,128)S(1)} %get-tuple-element.17, f32[132,4,8,1]{3,0,2,1:T(8,128)S(1)} %get-tuple-element.23, f32[132,4,8,127]{3,0,2,1:T(8,128)S(1)} %get-tuple-element.25, f32[4,8,128]{2,1,0:T(8,128)S(1)} %get-tuple-element.53, ...), kind=kLoop, calls=%fused_computation.203 | loop fusion | flops 10272768 | bytes 13041664 | tf_op jit(solution)/shard_map/convert.6
  42.9 2.8 %collective-permute-start.4 = (bf16[132,1,8,128]{3,0,2,1:T(8,128)(2,1)S(1)}, bf16[132,1,8,128]{3,0,2,1:T(8,128)(2,1)S(1)}, u32[]{:S(2)}, u32[]{:S(2)}) collective-permute-start(bf16[132,1,8,128]{3,0,2,1:T(8,128)(2,1)S(1)} %get-tuple-element.32), channel_id=1, source_target_pairs={{0,4},{4,8},{8,12},{1,5},{5,9},{9,13},{2,6},{6,10},{10,14},{3,7},{... | collective-permute-start | bytes 811016 | tf_op jit(solution)/shard_map/ppermute | solution.py:23
  45.7 1.3 %collective-permute-start.5 = (bf16[132,1,8,128]{3,0,2,1:T(8,128)(2,1)S(1)}, bf16[132,1,8,128]{3,0,2,1:T(8,128)(2,1)S(1)}, u32[]{:S(2)}, u32[]{:S(2)}) collective-permute-start(bf16[132,1,8,128]{3,0,2,1:T(8,128)(2,1)S(1)} %get-tuple-element.33), channel_id=1, source_target_pairs={{4,0},{8,4},{12,8},{5,1},{9,5},{13,9},{6,2},{10,6},{14,10},{7,3},{... | collective-permute-start | bytes 811016 | tf_op jit(solution)/shard_map/ppermute | solution.py:24
  47.7 2.1 %collective-permute-done.4 = bf16[132,1,8,128]{3,0,2,1:T(8,128)(2,1)S(1)} collective-permute-done((bf16[132,1,8,128]{3,0,2,1:T(8,128)(2,1)S(1)}, bf16[132,1,8,128]{3,0,2,1:T(8,128)(2,1)S(1)}, u32[]{:S(2)}, u32[]{:S(2)}) %collective-permute-start.4) | collective-permute-done | bytes 270368 | tf_op jit(solution)/shard_map/ppermute | solution.py:23
  49.8 4.3 %collective-permute-done.5 = bf16[132,1,8,128]{3,0,2,1:T(8,128)(2,1)S(1)} collective-permute-done((bf16[132,1,8,128]{3,0,2,1:T(8,128)(2,1)S(1)}, bf16[132,1,8,128]{3,0,2,1:T(8,128)(2,1)S(1)}, u32[]{:S(2)}, u32[]{:S(2)}) %collective-permute-start.5) | collective-permute-done | bytes 270368 | tf_op jit(solution)/shard_map/ppermute | solution.py:24
  54.2 2.8 %fusion.5 = f32[132,4,8,128]{3,0,2,1:T(8,128)S(1)} fusion(f32[132,4,8,128]{3,0,2,1:T(8,128)S(1)} %get-tuple-element.15, f32[132,1,8,128]{3,0,2,1:T(8,128)S(1)} %convert_element_type.106, f32[132,1,8,128]{3,0,2,1:T(8,128)S(1)} %convert_element_type.105, f32[132,4,8,127]{3,0,2,1:T(8,128)S(1)} %get-tuple-element.19, f32[132,4,8,1]{3,0,2,1:T(8,128)S(1)} %get-tuple-element.21, ...), kind=kLoop, calls=%fused_computation.7 | loop fusion | flops 9191424 | bytes 11960320 | tf_op jit(solution)/shard_map/add | solution.py:133
  57.0 1.5 %collective-permute-start.6 = (f32[132,4,1,128]{3,0,2,1:T(8,128)S(1)}, f32[132,4,1,128]{3,0,2,1:T(8,128)S(1)}, u32[]{:S(2)}, u32[]{:S(2)}) collective-permute-start(f32[132,4,1,128]{3,0,2,1:T(8,128)S(1)} %slice.317), channel_id=1, source_target_pairs={{1,0},{3,2},{5,4},{7,6},{9,8},{11,10},{13,12},{15,14},{17,16},{19,... | collective-permute-start | bytes 811016 | tf_op jit(solution)/shard_map/ppermute | solution.py:32
  58.4 2.0 %multiply_reduce_fusion = f32[264,8,33]{0,2,1:T(8,128)S(1)} fusion(f32[264,8]{0,1:T(8,128)S(1)} %fusion.106, f32[8,8,33,33]{3,1,2,0:T(8,128)S(1)} %fusion.93, s32[264]{0:T(512)S(1)} %get-tuple-element.51), kind=kOutput, calls=%fused_computation | convolution fusion | flops 221851072 | bytes 567072 | tf_op jit(solution)/shard_map/bm,acmn->bacn/dot_general | solution.py:59
  60.5 1.1 %fusion.39 = bf16[264,264]{0,1:T(8,128)(2,1)S(1)} fusion(f32[264,8,33]{0,2,1:T(8,128)S(1)} %multiply_reduce_fusion, f32[264,8]{0,1:T(8,128)S(1)} %fusion.106, f32[264,33]{0,1:T(8,128)S(1)} %fusion.90), kind=kOutput, calls=%fused_computation.64 | convolution fusion | flops 220936320 | bytes 461472 | tf_op jit(solution)/shard_map/bcn,dc,dn->bd/dot_general | solution.py:61
  61.8 0.8 multiply_reduce_fusion.1
  62.7 1.6 %collective-permute-start.7 = (f32[2,4,8,128]{3,2,1,0:T(8,128)S(1)}, f32[2,4,8,128]{3,2,1,0:T(8,128)S(1)}, u32[]{:S(2)}, u32[]{:S(2)}) collective-permute-start(f32[2,4,8,128]{3,2,1,0:T(8,128)S(1)} %pad_maximum_fusion.12), channel_id=1, source_target_pairs={{0,2},{2,0},{1,3},{3,1},{4,6},{6,4},{5,7},{7,5},{8,10},{10,8},{9,1... | collective-permute-start | bytes 98312 | tf_op jit(solution)/shard_map/ppermute | solution.py:148
  64.9 1.9 %collective-permute-done.7 = f32[2,4,8,128]{3,2,1,0:T(8,128)S(1)} collective-permute-done((f32[2,4,8,128]{3,2,1,0:T(8,128)S(1)}, f32[2,4,8,128]{3,2,1,0:T(8,128)S(1)}, u32[]{:S(2)}, u32[]{:S(2)}) %collective-permute-start.7) | collective-permute-done | bytes 32800 | tf_op jit(solution)/shard_map/ppermute | solution.py:148
  68.2 0.8 slice_bitcast_fusion.4
  69.0 1.5 %collective-permute-start.8 = (bf16[132,8,128]{2,1,0:T(8,128)(2,1)}, bf16[132,8,128]{2,1,0:T(8,128)(2,1)}, u32[]{:S(2)}, u32[]{:S(2)}) collective-permute-start(bf16[132,8,128]{2,1,0:T(8,128)(2,1)} %get-tuple-element.44), channel_id=1, source_target_pairs={{0,2},{2,0},{1,3},{3,1},{4,6},{6,4},{5,7},{7,5},{8,10},{10,8},{9,1... | collective-permute-start | bytes 811016 | tf_op jit(solution)/shard_map/ppermute | solution.py:101
  70.8 0.8 copy-done.5
  72.2 6.5 %collective-permute-done.8 = bf16[132,8,128]{2,1,0:T(8,128)(2,1)} collective-permute-done((bf16[132,8,128]{2,1,0:T(8,128)(2,1)}, bf16[132,8,128]{2,1,0:T(8,128)(2,1)}, u32[]{:S(2)}, u32[]{:S(2)}) %collective-permute-start.8) | collective-permute-done | bytes 270368 | tf_op jit(solution)/shard_map/ppermute | solution.py:101
  78.7 1.0 pad.55
  79.7 0.8 fusion.89
  80.5 0.8 fusion.83
  81.9 0.8 fusion.81
  82.6 0.8 fusion.79
  84.1 0.8 fusion.77
  84.9 0.8 fusion.75
  86.3 0.8 fusion.73
  87.1 0.8 fusion.71
  87.9 0.9 fusion.40
  89.1 0.8 fusion.88
  89.8 0.8 fusion.69
  92.0 0.8 fusion.65
  94.3 0.8 fusion.61
  95.7 0.8 fusion.59
  96.5 0.8 fusion.57
  98.2 1.6 %collective-permute-start.10 = (bf16[132,8,128]{2,1,0:T(8,128)(2,1)S(1)}, bf16[132,8,128]{2,1,0:T(8,128)(2,1)S(1)}, u32[]{:S(2)}, u32[]{:S(2)}) collective-permute-start(bf16[132,8,128]{2,1,0:T(8,128)(2,1)S(1)} %slice.362), channel_id=1, source_target_pairs={{0,2},{2,0},{1,3},{3,1},{4,6},{6,4},{5,7},{7,5},{8,10},{10,8},{9,1... | collective-permute-start | bytes 811016 | tf_op jit(solution)/shard_map/ppermute | solution.py:104
  100.5 7.2 %collective-permute-done.10 = bf16[132,8,128]{2,1,0:T(8,128)(2,1)S(1)} collective-permute-done((bf16[132,8,128]{2,1,0:T(8,128)(2,1)S(1)}, bf16[132,8,128]{2,1,0:T(8,128)(2,1)S(1)}, u32[]{:S(2)}, u32[]{:S(2)}) %collective-permute-start.10) | collective-permute-done | bytes 270368 | tf_op jit(solution)/shard_map/ppermute | solution.py:104
  107.7 3.2 %collective-permute-done.11 = bf16[132,8,128]{2,1,0:T(8,128)(2,1)S(1)} collective-permute-done((bf16[132,8,128]{2,1,0:T(8,128)(2,1)S(1)}, bf16[132,8,128]{2,1,0:T(8,128)(2,1)S(1)}, u32[]{:S(2)}, u32[]{:S(2)}) %collective-permute-start.11) | collective-permute-done | bytes 270368 | tf_op jit(solution)/shard_map/ppermute | solution.py:104
  112.5 1.7 %copy.54 = f32[132,4,8,128]{3,2,1,0:T(8,128)} copy(f32[132,4,8,128]{3,0,2,1:T(8,128)S(1)} %fusion.36) | data formatting | bytes 4325376
  (117 shorter events, 16.3 us)
Async XLA Ops:
  0.6 18.1 %copy-start = (bf16[4,33,33]{2,0,1:T(4,128)(2,1)S(1)}, bf16[4,33,33]{2,0,1:T(4,128)(2,1)}, u32[]{:S(2)}) copy-start(bf16[4,33,33]{2,0,1:T(4,128)(2,1)} %param.23) | copy-start | bytes 26140
  0.6 10.0 %copy-start.2 = (f32[132,4,8,128]{3,2,1,0:T(8,128)S(1)}, f32[132,4,8,128]{3,2,1,0:T(8,128)}, u32[]{:S(2)}) copy-start(f32[132,4,8,128]{3,2,1,0:T(8,128)} %param.12) | copy-start | bytes 6488068
  3.7 15.4 %collective-permute-start = (bf16[132,1,8,128]{3,0,2,1:T(8,128)(2,1)S(1)}, bf16[132,1,8,128]{3,0,2,1:T(8,128)(2,1)}, u32[]{:S(2)}, u32[]{:S(2)}) collective-permute-start(bf16[132,1,8,128]{3,0,2,1:T(8,128)(2,1)S(1)} %get-tuple-element.36), channel_id=1, source_target_pairs={{0,4},{4,8},{8,12},{1,5},{5,9},{9,13},{2,6},{6,10},{10,14},{3,7},{... | collective-permute-start | bytes 811016 | tf_op jit(solution)/shard_map/ppermute | solution.py:23
  9.4 10.8 %collective-permute-start.1 = (bf16[132,1,8,128]{3,0,2,1:T(8,128)(2,1)S(1)}, bf16[132,1,8,128]{3,0,2,1:T(8,128)(2,1)S(1)}, u32[]{:S(2)}, u32[]{:S(2)}) collective-permute-start(bf16[132,1,8,128]{3,0,2,1:T(8,128)(2,1)S(1)} %get-tuple-element.37), channel_id=1, source_target_pairs={{4,0},{8,4},{12,8},{5,1},{9,5},{13,9},{6,2},{10,6},{14,10},{7,3},{... | collective-permute-start | bytes 811016 | tf_op jit(solution)/shard_map/ppermute | solution.py:24
  14.7 2.8 %copy-start.22 = (s32[264]{0:T(512)S(1)}, s32[264]{0:T(512)}, u32[]{:S(2)}) copy-start(s32[264]{0:T(512)} %param.21) | copy-start | bytes 3172
  14.7 3.3 %copy-start.20 = (f32[132]{0:T(256)S(1)}, f32[132]{0:T(256)}, u32[]{:S(2)}) copy-start(f32[132]{0:T(256)} %param.19) | copy-start | bytes 1588
  14.7 3.3 %copy-start.23 = (f32[132]{0:T(256)S(1)}, f32[132]{0:T(256)}, u32[]{:S(2)}) copy-start(f32[132]{0:T(256)} %param.20) | copy-start | bytes 1588
  14.7 3.9 %copy-start.9 = (f32[4,8,128]{2,1,0:T(8,128)S(1)}, f32[4,8,128]{2,1,0:T(8,128)}, u32[]{:S(2)}) copy-start(f32[4,8,128]{2,1,0:T(8,128)} %param.13) | copy-start | bytes 49156
  14.7 3.9 %copy-start.10 = (f32[4,8,128]{2,1,0:T(8,128)S(1)}, f32[4,8,128]{2,1,0:T(8,128)}, u32[]{:S(2)}) copy-start(f32[4,8,128]{2,1,0:T(8,128)} %param.14) | copy-start | bytes 49156
  14.7 3.9 %copy-start.15 = (s32[4,128]{1,0:T(4,128)S(1)}, s32[4,128]{1,0:T(4,128)}, u32[]{:S(2)}) copy-start(s32[4,128]{1,0:T(4,128)} %param.17) | copy-start | bytes 6148
  14.7 4.0 %copy-start.18 = (f32[132]{0:T(256)S(1)}, f32[132]{0:T(256)}, u32[]{:S(2)}) copy-start(f32[132]{0:T(256)} %param.18) | copy-start | bytes 1588
  14.8 4.0 %copy-start.17 = (s32[8,8]{1,0:T(8,128)S(1)}, s32[8,8]{1,0:T(8,128)}, u32[]{:S(2)}) copy-start(s32[8,8]{1,0:T(8,128)} %param.22) | copy-start | bytes 772
  18.0 2.2 %copy-start.4 = (f32[132,4,8,1]{3,0,2,1:T(8,128)S(1)}, f32[132,4,8,1]{3,0,2,1:T(8,128)}, u32[]{:S(2)}) copy-start(f32[132,4,8,1]{3,0,2,1:T(8,128)} %get-tuple-element.26) | copy-start | bytes 50692
  25.1 9.9 %collective-permute-start.2 = (bf16[132,1,8,128]{3,0,2,1:T(8,128)(2,1)S(1)}, bf16[132,1,8,128]{3,0,2,1:T(8,128)(2,1)S(1)}, u32[]{:S(2)}, u32[]{:S(2)}) collective-permute-start(bf16[132,1,8,128]{3,0,2,1:T(8,128)(2,1)S(1)} %get-tuple-element.34), channel_id=1, source_target_pairs={{0,4},{4,8},{8,12},{1,5},{5,9},{9,13},{2,6},{6,10},{10,14},{3,7},{... | collective-permute-start | bytes 811016 | tf_op jit(solution)/shard_map/ppermute | solution.py:23
  29.7 9.5 %collective-permute-start.3 = (bf16[132,1,8,128]{3,0,2,1:T(8,128)(2,1)S(1)}, bf16[132,1,8,128]{3,0,2,1:T(8,128)(2,1)S(1)}, u32[]{:S(2)}, u32[]{:S(2)}) collective-permute-start(bf16[132,1,8,128]{3,0,2,1:T(8,128)(2,1)S(1)} %get-tuple-element.35), channel_id=1, source_target_pairs={{4,0},{8,4},{12,8},{5,1},{9,5},{13,9},{6,2},{10,6},{14,10},{7,3},{... | collective-permute-start | bytes 811016 | tf_op jit(solution)/shard_map/ppermute | solution.py:24
  31.0 8.2 %copy-start.3 = (f32[132,4,8,128]{3,2,1,0:T(8,128)S(1)}, f32[132,4,8,128]{3,2,1,0:T(8,128)}, u32[]{:S(2)}) copy-start(f32[132,4,8,128]{3,2,1,0:T(8,128)} %param.12) | copy-start | bytes 6488068
  42.9 6.9 %collective-permute-start.4 = (bf16[132,1,8,128]{3,0,2,1:T(8,128)(2,1)S(1)}, bf16[132,1,8,128]{3,0,2,1:T(8,128)(2,1)S(1)}, u32[]{:S(2)}, u32[]{:S(2)}) collective-permute-start(bf16[132,1,8,128]{3,0,2,1:T(8,128)(2,1)S(1)} %get-tuple-element.32), channel_id=1, source_target_pairs={{0,4},{4,8},{8,12},{1,5},{5,9},{9,13},{2,6},{6,10},{10,14},{3,7},{... | collective-permute-start | bytes 811016 | tf_op jit(solution)/shard_map/ppermute | solution.py:23
  45.7 8.4 %collective-permute-start.5 = (bf16[132,1,8,128]{3,0,2,1:T(8,128)(2,1)S(1)}, bf16[132,1,8,128]{3,0,2,1:T(8,128)(2,1)S(1)}, u32[]{:S(2)}, u32[]{:S(2)}) collective-permute-start(bf16[132,1,8,128]{3,0,2,1:T(8,128)(2,1)S(1)} %get-tuple-element.33), channel_id=1, source_target_pairs={{4,0},{8,4},{12,8},{5,1},{9,5},{13,9},{6,2},{10,6},{14,10},{7,3},{... | collective-permute-start | bytes 811016 | tf_op jit(solution)/shard_map/ppermute | solution.py:24
  57.0 4.8 %collective-permute-start.6 = (f32[132,4,1,128]{3,0,2,1:T(8,128)S(1)}, f32[132,4,1,128]{3,0,2,1:T(8,128)S(1)}, u32[]{:S(2)}, u32[]{:S(2)}) collective-permute-start(f32[132,4,1,128]{3,0,2,1:T(8,128)S(1)} %slice.317), channel_id=1, source_target_pairs={{1,0},{3,2},{5,4},{7,6},{9,8},{11,10},{13,12},{15,14},{17,16},{19,... | collective-permute-start | bytes 811016 | tf_op jit(solution)/shard_map/ppermute | solution.py:32
  60.4 1.3 %copy-start.19 = (f32[132]{0:T(256)S(1)}, f32[132]{0:T(256)}, u32[]{:S(2)}) copy-start(f32[132]{0:T(256)} %param.18) | copy-start | bytes 1588
  60.5 1.3 %copy-start.21 = (f32[132]{0:T(256)S(1)}, f32[132]{0:T(256)}, u32[]{:S(2)}) copy-start(f32[132]{0:T(256)} %param.19) | copy-start | bytes 1588
  61.8 2.5 %copy-start.16 = (s32[4,128]{1,0:T(4,128)S(1)}, s32[4,128]{1,0:T(4,128)}, u32[]{:S(2)}) copy-start(s32[4,128]{1,0:T(4,128)} %param.17) | copy-start | bytes 6148
  61.8 5.0 %copy-start.11 = (f32[4,8,128]{2,1,0:T(8,128)S(1)}, f32[4,8,128]{2,1,0:T(8,128)}, u32[]{:S(2)}) copy-start(f32[4,8,128]{2,1,0:T(8,128)} %param.16) | copy-start | bytes 49156
  61.8 5.0 %copy-start.12 = (f32[4,8,128]{2,1,0:T(8,128)S(1)}, f32[4,8,128]{2,1,0:T(8,128)}, u32[]{:S(2)}) copy-start(f32[4,8,128]{2,1,0:T(8,128)} %param.15) | copy-start | bytes 49156
  61.8 5.6 %copy-start.13 = (f32[132]{0:T(256)S(1)}, f32[132]{0:T(256)}, u32[]{:S(2)}) copy-start(f32[132]{0:T(256)} %get-tuple-element.55) | copy-start | bytes 1588
  62.7 4.2 %collective-permute-start.7 = (f32[2,4,8,128]{3,2,1,0:T(8,128)S(1)}, f32[2,4,8,128]{3,2,1,0:T(8,128)S(1)}, u32[]{:S(2)}, u32[]{:S(2)}) collective-permute-start(f32[2,4,8,128]{3,2,1,0:T(8,128)S(1)} %pad_maximum_fusion.12), channel_id=1, source_target_pairs={{0,2},{2,0},{1,3},{3,1},{4,6},{6,4},{5,7},{7,5},{8,10},{10,8},{9,1... | collective-permute-start | bytes 98312 | tf_op jit(solution)/shard_map/ppermute | solution.py:148
  67.5 0.6 copy-start.6
  69.0 9.6 %collective-permute-start.8 = (bf16[132,8,128]{2,1,0:T(8,128)(2,1)}, bf16[132,8,128]{2,1,0:T(8,128)(2,1)}, u32[]{:S(2)}, u32[]{:S(2)}) collective-permute-start(bf16[132,8,128]{2,1,0:T(8,128)(2,1)} %get-tuple-element.44), channel_id=1, source_target_pairs={{0,2},{2,0},{1,3},{3,1},{4,6},{6,4},{5,7},{7,5},{8,10},{10,8},{9,1... | collective-permute-start | bytes 811016 | tf_op jit(solution)/shard_map/ppermute | solution.py:101
  70.7 1.0 copy-start.5
  71.6 17.4 %collective-permute-start.9 = (bf16[132,8,128]{2,1,0:T(8,128)(2,1)S(1)}, bf16[132,8,128]{2,1,0:T(8,128)(2,1)S(1)}, u32[]{:S(2)}, u32[]{:S(2)}) collective-permute-start(bf16[132,8,128]{2,1,0:T(8,128)(2,1)S(1)} %copy-done.5), channel_id=1, source_target_pairs={{0,2},{2,0},{1,3},{3,1},{4,6},{6,4},{5,7},{7,5},{8,10},{10,8},{9,1... | collective-permute-start | bytes 811016 | tf_op jit(solution)/shard_map/ppermute | solution.py:101
  98.2 9.5 %collective-permute-start.10 = (bf16[132,8,128]{2,1,0:T(8,128)(2,1)S(1)}, bf16[132,8,128]{2,1,0:T(8,128)(2,1)S(1)}, u32[]{:S(2)}, u32[]{:S(2)}) collective-permute-start(bf16[132,8,128]{2,1,0:T(8,128)(2,1)S(1)} %slice.362), channel_id=1, source_target_pairs={{0,2},{2,0},{1,3},{3,1},{4,6},{6,4},{5,7},{7,5},{8,10},{10,8},{9,1... | collective-permute-start | bytes 811016 | tf_op jit(solution)/shard_map/ppermute | solution.py:104
  99.8 11.0 %collective-permute-start.11 = (bf16[132,8,128]{2,1,0:T(8,128)(2,1)S(1)}, bf16[132,8,128]{2,1,0:T(8,128)(2,1)S(1)}, u32[]{:S(2)}, u32[]{:S(2)}) collective-permute-start(bf16[132,8,128]{2,1,0:T(8,128)(2,1)S(1)} %slice.363), channel_id=1, source_target_pairs={{0,2},{2,0},{1,3},{3,1},{4,6},{6,4},{5,7},{7,5},{8,10},{10,8},{9,1... | collective-permute-start | bytes 811016 | tf_op jit(solution)/shard_map/ppermute | solution.py:104
  111.2 0.7 copy-start.7
  111.2 0.7 copy-start.8
  111.2 0.7 copy-start.14
  111.9 2.3 %copy-start.1 = (bf16[4,33,33]{2,0,1:T(4,128)(2,1)S(1)}, bf16[4,33,33]{2,0,1:T(4,128)(2,1)}, u32[]{:S(2)}) copy-start(bf16[4,33,33]{2,0,1:T(4,128)(2,1)} %param.23) | copy-start | bytes 26140

commit v4 on v3

--- a/solution.py
+++ b/solution.py
@@ -1,6 +1,10 @@
+import functools
+
 import jax
 import jax.numpy as jnp
 from jax import lax
+from jax.experimental import pallas as pl
+from jax.experimental.pallas import tpu as pltpu
 from jax.sharding import PartitionSpec as P
 
 SUB = 8
@@ -24,6 +28,65 @@
         after = lax.ppermute(first.astype(link), axis, down).astype(array.dtype)
         array = jnp.concatenate([before, array, after], axis=dim)
     return array
+
+
+def advect_kernel(weights, q_ref, left_ref, right_ref, wx_ref, wy_ref, out_ref):
+    depth = len(weights)
+    width = q_ref.shape[1]
+    field = jnp.concatenate([left_ref[...], q_ref[...], right_ref[...]], axis=1)
+    wx = wx_ref[...]
+    wy = wy_ref[...]
+    section = field
+    for stage, weight_now in enumerate(weights, start=1):
+        span = width + 2 * (depth - stage)
+        center = section[:, 1 : 1 + span]
+        west = section[:, 0:span]
+        east = section[:, 2 : 2 + span]
+        south = pltpu.roll(center, 1, 3)
+        north = pltpu.roll(center, center.shape[3] - 1, 3)
+        wind_a = wx[stage : stage + span]
+        wind_b = wy[stage : stage + span]
+        along_x = jnp.maximum(wind_a, 0.0) * (center - west) + jnp.minimum(wind_a, 0.0) * (east - center)
+        along_y = jnp.maximum(wind_b, 0.0) * (center - south) + jnp.minimum(wind_b, 0.0) * (north - center)
+        section = field[:, stage : stage + span] + weight_now * (-along_x - along_y)
+    out_ref[...] = section
+
+
+def advect_kernel_call(bin_mass, wind_x, wind_y, section_weights):
+    local_bins, width_x, width_z, width_y = bin_mass.shape
+    depth = len(section_weights)
+    tiles = lax.axis_size("tiles")
+    up = [(i, i + 1) for i in range(tiles - 1)]
+    down = [(j, i) for i, j in up]
+
+    def rim(lo, hi):
+        winds = jnp.stack([wind_x[lo:hi], wind_y[lo:hi]])
+        high = winds.astype(jnp.bfloat16)
+        low = (winds - high.astype(jnp.float32)).astype(jnp.bfloat16)
+        return jnp.concatenate([bin_mass[:, lo:hi].astype(jnp.bfloat16), high, low], axis=0)
+
+    def unpack(message):
+        message = message.astype(jnp.float32)
+        winds = message[local_bins : local_bins + 2] + message[local_bins + 2 :]
+        return message[:local_bins], winds[0], winds[1]
+
+    q_left, wx_left, wy_left = unpack(lax.ppermute(rim(width_x - depth, width_x), "tiles", up))
+    q_right, wx_right, wy_right = unpack(lax.ppermute(rim(0, depth), "tiles", down))
+    wx = jnp.concatenate([wx_left, wind_x, wx_right], axis=0)
+    wy = jnp.concatenate([wy_left, wind_y, wy_right], axis=0)
+    block = max(d for d in range(1, 34) if local_bins % d == 0)
+    rim_spec = pl.BlockSpec((block, depth, width_z, width_y), lambda i: (i, 0, 0, 0))
+    own_spec = pl.BlockSpec((block, width_x, width_z, width_y), lambda i: (i, 0, 0, 0))
+    wind_spec = pl.BlockSpec(wx.shape, lambda i: (0, 0, 0))
+    cells = local_bins * width_x * width_z * width_y
+    return pl.pallas_call(
+        functools.partial(advect_kernel, section_weights),
+        out_shape=jax.ShapeDtypeStruct(bin_mass.shape, bin_mass.dtype),
+        grid=(local_bins // block,),
+        in_specs=[own_spec, rim_spec, rim_spec, wind_spec, wind_spec],
+        out_specs=own_spec,
+        cost_estimate=pl.CostEstimate(flops=80 * cells, bytes_accessed=20 * cells, transcendentals=0),
+    )(bin_mass, q_left, q_right, wx, wy)
 
 
 def shifted(block, axis, distance):
@@ -127,12 +190,15 @@
     wind_x = wind_east * open_cells
     wind_y = wind_north * open_cells
     section_weights = (1.0 / 3.0, 0.5, 1.0)
-    section_field = bin_mass
-    for weight_now in section_weights:
-        extended = extended_2(section_field, (("tiles", 1),), 1, jnp.bfloat16)
-        section_field = bin_mass + weight_now * tendency(
-            extended[:, 1:-1], extended[:, :-2], extended[:, 2:], wind_x, wind_y
-        )
+    if width_x >= len(section_weights):
+        section_field = advect_kernel_call(bin_mass, wind_x, wind_y, section_weights)
+    else:
+        section_field = bin_mass
+        for weight_now in section_weights:
+            extended = extended_2(section_field, (("tiles", 1),), 1, jnp.bfloat16)
+            section_field = bin_mass + weight_now * tendency(
+                extended[:, 1:-1], extended[:, :-2], extended[:, 2:], wind_x, wind_y
+            )
     rim_above = shifted(section_field[:, :, :1, :], "vert", -1)
     from_above = jnp.concatenate([section_field[:, :, 1:], rim_above], axis=2)
     speed = fall_speed[:, None, None, None]

time: 115 us -> 104 us (0.904)
  starting transfers between devices: 24.1 us -> 13.6 us
  local copies, waits for them, and re-layouts: 19.1 us -> 8.9 us
  Pallas kernels: 0 us -> 8.14 us
  waiting for transfers between devices: 32.5 us -> 38 us
  other arithmetic: 20.6 us -> 17 us
    ppermute x6 -> x2, starting transfers between devices: 16.9 us -> 6.39 us  [the longest x1 5.11 us: advect_kernel_call(): lax.ppermute(rim(width_x - depth, width_x), 'tiles', up)]
    pallas_call x0 -> x1, Pallas kernels: none -> 8.14 us  [advect_kernel_call(): pl.pallas_call(functools.partial(advect_kernel, section_weights), out_sha...]
    unnamed x64 -> x49, local copies, waits for them, and re-layouts: 8.78 us -> 2.73 us
    slice x9 -> x3, local copies, waits for them, and re-layouts: 8.53 us -> 2.84 us  [the longest x2 2.56 us: unpack(): return (message[:local_bins], winds[0], winds[1])]
    another operation x3 -> x2, other arithmetic: 7.08 us -> 1.85 us
    ppermute x6 -> x2, waiting for transfers between devices: 13.8 us -> 18.7 us  [the longest x1 13.7 us: advect_kernel_call(): lax.ppermute(rim(width_x - depth, width_x), 'tiles', up)]
    add x1 -> x2, other arithmetic: 2.75 us -> 0.01 us  [unpack(): winds = message[local_bins:local_bins + 2] + message[local_bins + 2:]]
    concatenate x0 -> x3, other arithmetic: none -> 2.66 us  [the longest x2 2.02 us: rim(): jnp.concatenate([bin_mass[:, lo:hi].astype(jnp.bfloat16), high, low], axi...]
  transfers between devices with their start and end apart: 12 -> 8, of which waited for: 8 -> 6; matrix products, arithmetic and copies ran while one was open for 22% -> 16% of each run, Pallas kernels for 0% -> 0%
where the time goes in v4:
time: 104 us; the launch traced here: 103 us
  waiting for transfers between devices  38 us (37%)
  other arithmetic  17 us (16%)
  matrix products  16.4 us (16%)
  starting transfers between devices  13.6 us (13%)
  local copies, waits for them, and re-layouts  8.9 us (9%)
  Pallas kernels  8.14 us (8%)
  between operations  1.31 us (1%)
    ppermute x1, waiting for transfers between devices, advect_kernel_call(): lax.ppermute(rim(width_x - depth, width_x), 'tiles', up)  13.7 us
    dot_general x16, matrix products, collide(): jnp.dot(table, iterate.astype(jnp.bfloat16), preferred_element_type=jnp.f...  12.6 us
    ppermute x2, waiting for transfers between devices, paired_collision(): returned.append(lax.ppermute(change[local_bins:], 'bins', swap))  10.3 us
    pallas_call x1, Pallas kernels, advect_kernel_call(): pl.pallas_call(functools.partial(advect_kernel, section_weights), out_sha...  8.14 us
    ppermute x2, waiting for transfers between devices, paired_collision(): arrived = lax.ppermute(away[:, chunk], 'bins', swap)  6.46 us
    ppermute x1, starting transfers between devices, advect_kernel_call(): lax.ppermute(rim(width_x - depth, width_x), 'tiles', up)  5.11 us
    ppermute x1, waiting for transfers between devices, advect_kernel_call(): lax.ppermute(rim(0, depth), 'tiles', down)  4.95 us
    add x6, other arithmetic, collide(): iterate + collision_rate * products[all_bins:] * products[:all_bins]  3.85 us
  transfers between devices with their start and end apart: 8, of which 6 were waited for; matrix products, arithmetic and copies ran while one was open for 16% of the time, Pallas kernels for 0%

profile of v4, /device:TPU:0, one launch (start us, length us, event | category | flops | bytes accessed | tf_op | source)
XLA Modules:
  0.0 103.3 jit_solution(13129847086052424355)
XLA Ops:
  0.7 0.8 compare_select_fusion.1
  1.5 1.8 %convert.17 = bf16[132,4,8,128]{3,2,1,0:T(8,128)(2,1)S(1)} convert(f32[132,4,8,128]{3,2,1,0:T(8,128)} %q_ref.1) | non-fusion elementwise | flops 540672 | bytes 3244032 | tf_op jit(solution)/shard_map/convert.6
  3.7 1.0 pad_maximum_fusion.1
  4.7 5.1 %collective-permute-start = (bf16[136,3,8,128]{3,2,1,0:T(8,128)(2,1)}, bf16[136,3,8,128]{3,2,1,0:T(8,128)(2,1)S(1)}, u32[]{:S(2)}, u32[]{:S(2)}) collective-permute-start(bf16[136,3,8,128]{3,2,1,0:T(8,128)(2,1)} %pad_maximum_fusion.1), channel_id=1, source_target_pairs={{0,4},{4,8},{8,12},{1,5},{5,9},{9,13},{2,6},{6,10},{10,14},{3,7},{... | collective-permute-start | bytes 2506760 | tf_op jit(solution)/shard_map/ppermute | solution.py:73
  9.9 1.0 pad_maximum_fusion.2
  10.9 1.3 %collective-permute-start.1 = (bf16[136,3,8,128]{3,2,1,0:T(8,128)(2,1)}, bf16[136,3,8,128]{3,2,1,0:T(8,128)(2,1)S(1)}, u32[]{:S(2)}, u32[]{:S(2)}) collective-permute-start(bf16[136,3,8,128]{3,2,1,0:T(8,128)(2,1)} %pad_maximum_fusion.2), channel_id=1, source_target_pairs={{4,0},{8,4},{12,8},{5,1},{9,5},{13,9},{6,2},{10,6},{14,10},{7,3},{... | collective-permute-start | bytes 2506760 | tf_op jit(solution)/shard_map/ppermute | solution.py:74
  14.2 13.7 %collective-permute-done = bf16[136,3,8,128]{3,2,1,0:T(8,128)(2,1)S(1)} collective-permute-done((bf16[136,3,8,128]{3,2,1,0:T(8,128)(2,1)}, bf16[136,3,8,128]{3,2,1,0:T(8,128)(2,1)S(1)}, u32[]{:S(2)}, u32[]{:S(2)}) %collective-permute-start) | collective-permute-done | bytes 835616 | tf_op jit(solution)/shard_map/ppermute | solution.py:73
  28.1 5.0 %collective-permute-done.1 = bf16[136,3,8,128]{3,2,1,0:T(8,128)(2,1)S(1)} collective-permute-done((bf16[136,3,8,128]{3,2,1,0:T(8,128)(2,1)}, bf16[136,3,8,128]{3,2,1,0:T(8,128)(2,1)S(1)}, u32[]{:S(2)}, u32[]{:S(2)}) %collective-permute-start.1) | collective-permute-done | bytes 835616 | tf_op jit(solution)/shard_map/ppermute | solution.py:74
  33.2 0.6 pad_maximum_fusion.8
  33.8 1.3 %slice.255.left_ref = f32[132,3,8,128]{3,2,1,0:T(8,128)} slice(bf16[136,3,8,128]{3,2,1,0:T(8,128)(2,1)S(1)} %collective-permute-done), slice={[0:132], [0:3], [0:8], [0:128]} | slice | bytes 3244032 | tf_op jit(solution)/shard_map/slice | solution.py:71
  35.1 1.3 %slice.259.right_ref = f32[132,3,8,128]{3,2,1,0:T(8,128)} slice(bf16[136,3,8,128]{3,2,1,0:T(8,128)(2,1)S(1)} %collective-permute-done.1), slice={[0:132], [0:3], [0:8], [0:128]} | slice | bytes 3244032 | tf_op jit(solution)/shard_map/slice | solution.py:71
  36.4 8.1 %shard_map.139 = f32[132,4,8,128]{3,2,1,0:T(8,128)} custom-call(f32[132,4,8,128]{3,2,1,0:T(8,128)} %q_ref.1, f32[132,3,8,128]{3,2,1,0:T(8,128)} %slice.255.left_ref, f32[132,3,8,128]{3,2,1,0:T(8,128)} %slice.259.right_ref, f32[10,8,128]{2,1,0:T(8,128)} %get-tuple-element.35.wx_ref, f32[10,8,128]{2,1,0:T(8,128)} %get-tuple-element.36.wy_ref), custom_call_target="tpu_custom_call" | custom-call | flops 43253760 | bytes 10813440 | tf_op jit(solution)/shard_map/pallas_call | solution.py:82
  44.5 1.8 %slice.269 = f32[132,4,1,128]{3,2,1,0:T(1,128)S(1)} slice(f32[132,4,8,128]{3,2,1,0:T(8,128)} %shard_map.139), slice={[0:132], [0:4], [0:1], [0:128]} | slice | bytes 540672 | tf_op jit(solution)/shard_map/slice | solution.py:202
  46.3 1.4 %collective-permute-start.2 = (f32[132,4,1,128]{3,2,1,0:T(1,128)S(1)}, f32[132,4,1,128]{3,2,1,0:T(1,128)S(1)}, u32[]{:S(2)}, u32[]{:S(2)}) collective-permute-start(f32[132,4,1,128]{3,2,1,0:T(1,128)S(1)} %slice.269), channel_id=1, source_target_pairs={{1,0},{3,2},{5,4},{7,6},{9,8},{11,10},{13,12},{15,14},{17,16},{19,... | collective-permute-start | bytes 811016 | tf_op jit(solution)/shard_map/ppermute | solution.py:95
  47.7 2.0 %multiply_reduce_fusion = f32[264,8,33]{0,2,1:T(8,128)S(1)} fusion(f32[264,8]{0,1:T(8,128)S(1)} %fusion.68, f32[8,8,33,33]{3,1,2,0:T(8,128)S(1)} %fusion.57, s32[264]{0:T(512)S(1)} %get-tuple-element.29), kind=kOutput, calls=%fused_computation | convolution fusion | flops 221851072 | bytes 567072 | tf_op jit(solution)/shard_map/bm,acmn->bacn/dot_general | solution.py:122
  49.7 1.1 %fusion.4 = bf16[264,264]{0,1:T(8,128)(2,1)S(1)} fusion(f32[264,8,33]{0,2,1:T(8,128)S(1)} %multiply_reduce_fusion, f32[264,8]{0,1:T(8,128)S(1)} %fusion.68, f32[264,33]{0,1:T(8,128)S(1)} %fusion.54), kind=kOutput, calls=%fused_computation.17 | convolution fusion | flops 220936320 | bytes 461472 | tf_op jit(solution)/shard_map/bcn,dc,dn->bd/dot_general | solution.py:124
  51.6 1.3 %multiply_reduce_fusion.1 = (f32[4,8,128]{2,1,0:T(8,128)S(1)}, f32[4,8,128]{2,1,0:T(8,128)S(1)}, f32[132,4,8,128]{3,2,1,0:T(8,128)S(1)}) fusion(f32[132]{0:T(256)S(1)} %copy-done.13, f32[132]{0:T(256)S(1)} %copy-done.12, f32[132,4,1,128]{3,2,1,0:T(1,128)S(1)} %collective-permute-done.2, f32[132,4,7,128]{3,2,1,0:T(8,128)S(1)} %slice.268, f32[132]{0:T(256)S(1)} %copy-done.9, ...), kind=kLoop, calls=%fused_computation.6 | loop fusion | flops 4317184 | bytes 6522944 | tf_op jit(solution)/shard_map/reduce_sum | solution.py:209
  52.9 1.6 %collective-permute-start.3 = (f32[2,4,8,128]{3,2,1,0:T(8,128)S(1)}, f32[2,4,8,128]{3,2,1,0:T(8,128)S(1)}, u32[]{:S(2)}, u32[]{:S(2)}) collective-permute-start(f32[2,4,8,128]{3,2,1,0:T(8,128)S(1)} %pad_maximum_fusion.10), channel_id=1, source_target_pairs={{0,2},{2,0},{1,3},{3,1},{4,6},{6,4},{5,7},{7,5},{8,10},{10,8},{9,1... | collective-permute-start | bytes 98312 | tf_op jit(solution)/shard_map/ppermute | solution.py:214
  54.5 2.5 %collective-permute-done.3 = f32[2,4,8,128]{3,2,1,0:T(8,128)S(1)} collective-permute-done((f32[2,4,8,128]{3,2,1,0:T(8,128)S(1)}, f32[2,4,8,128]{3,2,1,0:T(8,128)S(1)}, u32[]{:S(2)}, u32[]{:S(2)}) %collective-permute-start.3) | collective-permute-done | bytes 32800 | tf_op jit(solution)/shard_map/ppermute | solution.py:214
  58.3 0.8 slice_bitcast_fusion.2
  59.1 1.5 %collective-permute-start.4 = (bf16[132,8,128]{2,1,0:T(8,128)(2,1)}, bf16[132,8,128]{2,1,0:T(8,128)(2,1)}, u32[]{:S(2)}, u32[]{:S(2)}) collective-permute-start(bf16[132,8,128]{2,1,0:T(8,128)(2,1)} %get-tuple-element.18), channel_id=1, source_target_pairs={{0,2},{2,0},{1,3},{3,1},{4,6},{6,4},{5,7},{7,5},{8,10},{10,8},{9,1... | collective-permute-start | bytes 811016 | tf_op jit(solution)/shard_map/ppermute | solution.py:164
  60.9 0.8 copy-done.3
  62.3 6.5 %collective-permute-done.4 = bf16[132,8,128]{2,1,0:T(8,128)(2,1)} collective-permute-done((bf16[132,8,128]{2,1,0:T(8,128)(2,1)}, bf16[132,8,128]{2,1,0:T(8,128)(2,1)}, u32[]{:S(2)}, u32[]{:S(2)}) %collective-permute-start.4) | collective-permute-done | bytes 270368 | tf_op jit(solution)/shard_map/ppermute | solution.py:164
  68.8 1.0 pad.35
  69.8 0.8 fusion.53
  70.6 0.8 fusion.47
  72.0 0.8 fusion.45
  72.7 0.8 fusion.43
  73.5 0.7 fusion.18
  74.2 0.8 fusion.41
  75.0 0.8 fusion.39
  76.4 0.8 fusion.37
  77.2 0.8 fusion.35
  78.0 0.7 fusion.5
  78.9 0.8 fusion.52
  79.7 0.8 fusion.33
  81.1 0.8 fusion.31
  81.9 0.8 fusion.29
  82.7 0.9 fusion.11
  83.6 0.8 fusion.27
  84.4 0.8 fusion.25
  85.8 0.8 fusion.23
  86.5 0.8 fusion.21
  87.3 0.7 fusion.6
  88.2 1.6 %collective-permute-start.6 = (bf16[132,8,128]{2,1,0:T(8,128)(2,1)S(1)}, bf16[132,8,128]{2,1,0:T(8,128)(2,1)S(1)}, u32[]{:S(2)}, u32[]{:S(2)}) collective-permute-start(bf16[132,8,128]{2,1,0:T(8,128)(2,1)S(1)} %slice.314), channel_id=1, source_target_pairs={{0,2},{2,0},{1,3},{3,1},{4,6},{6,4},{5,7},{7,5},{8,10},{10,8},{9,1... | collective-permute-start | bytes 811016 | tf_op jit(solution)/shard_map/ppermute | solution.py:167
  90.6 7.1 %collective-permute-done.6 = bf16[132,8,128]{2,1,0:T(8,128)(2,1)S(1)} collective-permute-done((bf16[132,8,128]{2,1,0:T(8,128)(2,1)S(1)}, bf16[132,8,128]{2,1,0:T(8,128)(2,1)S(1)}, u32[]{:S(2)}, u32[]{:S(2)}) %collective-permute-start.6) | collective-permute-done | bytes 270368 | tf_op jit(solution)/shard_map/ppermute | solution.py:167
  97.7 3.2 %collective-permute-done.7 = bf16[132,8,128]{2,1,0:T(8,128)(2,1)S(1)} collective-permute-done((bf16[132,8,128]{2,1,0:T(8,128)(2,1)S(1)}, bf16[132,8,128]{2,1,0:T(8,128)(2,1)S(1)}, u32[]{:S(2)}, u32[]{:S(2)}) %collective-permute-start.7) | collective-permute-done | bytes 270368 | tf_op jit(solution)/shard_map/ppermute | solution.py:167
  101.5 1.8 %fusion.1 = f32[132,4,8,128]{3,2,1,0:T(8,128)} fusion(bf16[132,4,8,128]{3,2,1,0:T(8,128)(2,1)S(1)} %bitcast.144, f32[132,4,8,128]{3,2,1,0:T(8,128)S(1)} %get-tuple-element.7, f32[4,8,128]{2,1,0:T(8,128)S(1)} %compare_convert_fusion, f32[4,8,128]{2,1,0:T(8,128)S(1)} %get-tuple-element.6, f32[132]{0:T(256)S(1)} %get-tuple-element.33), kind=kLoop, calls=%fused_computation.4 | loop fusion | flops 3244032 | bytes 5440016 | tf_op jit(solution)/shard_map/mul | solution.py:226
  (94 shorter events, 9.3 us)
Async XLA Ops:
  0.6 13.2 %copy-start = (bf16[4,33,33]{2,0,1:T(4,128)(2,1)S(1)}, bf16[4,33,33]{2,0,1:T(4,128)(2,1)}, u32[]{:S(2)}) copy-start(bf16[4,33,33]{2,0,1:T(4,128)(2,1)} %param.23) | copy-start | bytes 26140
  0.7 0.9 copy-start.14
  4.7 7.5 %copy-start.16 = (s32[264]{0:T(512)S(1)}, s32[264]{0:T(512)}, u32[]{:S(2)}) copy-start(s32[264]{0:T(512)} %param.21) | copy-start | bytes 3172
  4.7 7.7 %copy-start.11 = (f32[132]{0:T(256)S(1)}, f32[132]{0:T(256)}, u32[]{:S(2)}) copy-start(f32[132]{0:T(256)} %param.19) | copy-start | bytes 1588
  4.7 7.7 %copy-start.17 = (f32[132]{0:T(256)S(1)}, f32[132]{0:T(256)}, u32[]{:S(2)}) copy-start(f32[132]{0:T(256)} %param.20) | copy-start | bytes 1588
  4.7 8.5 %copy-start.8 = (f32[132]{0:T(256)S(1)}, f32[132]{0:T(256)}, u32[]{:S(2)}) copy-start(f32[132]{0:T(256)} %param.18) | copy-start | bytes 1588
  4.7 9.1 %copy-start.7 = (s32[8,8]{1,0:T(8,128)S(1)}, s32[8,8]{1,0:T(8,128)}, u32[]{:S(2)}) copy-start(s32[8,8]{1,0:T(8,128)} %param.22) | copy-start | bytes 772
  4.7 23.2 %collective-permute-start = (bf16[136,3,8,128]{3,2,1,0:T(8,128)(2,1)}, bf16[136,3,8,128]{3,2,1,0:T(8,128)(2,1)S(1)}, u32[]{:S(2)}, u32[]{:S(2)}) collective-permute-start(bf16[136,3,8,128]{3,2,1,0:T(8,128)(2,1)} %pad_maximum_fusion.1), channel_id=1, source_target_pairs={{0,4},{4,8},{8,12},{1,5},{5,9},{9,13},{2,6},{6,10},{10,14},{3,7},{... | collective-permute-start | bytes 2506760 | tf_op jit(solution)/shard_map/ppermute | solution.py:73
  10.9 22.1 %collective-permute-start.1 = (bf16[136,3,8,128]{3,2,1,0:T(8,128)(2,1)}, bf16[136,3,8,128]{3,2,1,0:T(8,128)(2,1)S(1)}, u32[]{:S(2)}, u32[]{:S(2)}) collective-permute-start(bf16[136,3,8,128]{3,2,1,0:T(8,128)(2,1)} %pad_maximum_fusion.2), channel_id=1, source_target_pairs={{4,0},{8,4},{12,8},{5,1},{9,5},{13,9},{6,2},{10,6},{14,10},{7,3},{... | collective-permute-start | bytes 2506760 | tf_op jit(solution)/shard_map/ppermute | solution.py:74
  46.3 4.6 %copy-start.2 = (f32[132,4,8,128]{3,2,1,0:T(8,128)S(1)}, f32[132,4,8,128]{3,2,1,0:T(8,128)}, u32[]{:S(2)}) copy-start(f32[132,4,8,128]{3,2,1,0:T(8,128)} %shard_map.139) | copy-start | bytes 6488068
  46.3 4.9 %collective-permute-start.2 = (f32[132,4,1,128]{3,2,1,0:T(1,128)S(1)}, f32[132,4,1,128]{3,2,1,0:T(1,128)S(1)}, u32[]{:S(2)}, u32[]{:S(2)}) collective-permute-start(f32[132,4,1,128]{3,2,1,0:T(1,128)S(1)} %slice.269), channel_id=1, source_target_pairs={{1,0},{3,2},{5,4},{7,6},{9,8},{11,10},{13,12},{15,14},{17,16},{19,... | collective-permute-start | bytes 811016 | tf_op jit(solution)/shard_map/ppermute | solution.py:95
  50.9 0.7 copy-start.9
  50.9 0.7 copy-start.10
  50.9 0.7 copy-start.12
  50.9 0.7 copy-start.13
  51.6 2.9 %copy-start.6 = (s32[4,128]{1,0:T(4,128)S(1)}, s32[4,128]{1,0:T(4,128)}, u32[]{:S(2)}) copy-start(s32[4,128]{1,0:T(4,128)} %param.17) | copy-start | bytes 6148
  51.6 2.9 %copy-start.15 = (s32[8]{0:T(128)S(1)}, s32[8]{0:T(128)}, u32[]{:S(2)}) copy-start(s32[8]{0:T(128)} %copy-done.14) | copy-start | bytes 100
  51.6 5.5 %copy-start.4 = (f32[4,8,128]{2,1,0:T(8,128)S(1)}, f32[4,8,128]{2,1,0:T(8,128)}, u32[]{:S(2)}) copy-start(f32[4,8,128]{2,1,0:T(8,128)} %param.16) | copy-start | bytes 49156
  51.6 5.5 %copy-start.5 = (f32[4,8,128]{2,1,0:T(8,128)S(1)}, f32[4,8,128]{2,1,0:T(8,128)}, u32[]{:S(2)}) copy-start(f32[4,8,128]{2,1,0:T(8,128)} %param.15) | copy-start | bytes 49156
  52.9 4.2 %collective-permute-start.3 = (f32[2,4,8,128]{3,2,1,0:T(8,128)S(1)}, f32[2,4,8,128]{3,2,1,0:T(8,128)S(1)}, u32[]{:S(2)}, u32[]{:S(2)}) collective-permute-start(f32[2,4,8,128]{3,2,1,0:T(8,128)S(1)} %pad_maximum_fusion.10), channel_id=1, source_target_pairs={{0,2},{2,0},{1,3},{3,1},{4,6},{6,4},{5,7},{7,5},{8,10},{10,8},{9,1... | collective-permute-start | bytes 98312 | tf_op jit(solution)/shard_map/ppermute | solution.py:214
  59.1 9.6 %collective-permute-start.4 = (bf16[132,8,128]{2,1,0:T(8,128)(2,1)}, bf16[132,8,128]{2,1,0:T(8,128)(2,1)}, u32[]{:S(2)}, u32[]{:S(2)}) collective-permute-start(bf16[132,8,128]{2,1,0:T(8,128)(2,1)} %get-tuple-element.18), channel_id=1, source_target_pairs={{0,2},{2,0},{1,3},{3,1},{4,6},{6,4},{5,7},{7,5},{8,10},{10,8},{9,1... | collective-permute-start | bytes 811016 | tf_op jit(solution)/shard_map/ppermute | solution.py:164
  60.7 1.0 copy-start.3
  61.7 17.1 %collective-permute-start.5 = (bf16[132,8,128]{2,1,0:T(8,128)(2,1)S(1)}, bf16[132,8,128]{2,1,0:T(8,128)(2,1)S(1)}, u32[]{:S(2)}, u32[]{:S(2)}) collective-permute-start(bf16[132,8,128]{2,1,0:T(8,128)(2,1)S(1)} %copy-done.3), channel_id=1, source_target_pairs={{0,2},{2,0},{1,3},{3,1},{4,6},{6,4},{5,7},{7,5},{8,10},{10,8},{9,1... | collective-permute-start | bytes 811016 | tf_op jit(solution)/shard_map/ppermute | solution.py:164
  88.2 9.5 %collective-permute-start.6 = (bf16[132,8,128]{2,1,0:T(8,128)(2,1)S(1)}, bf16[132,8,128]{2,1,0:T(8,128)(2,1)S(1)}, u32[]{:S(2)}, u32[]{:S(2)}) collective-permute-start(bf16[132,8,128]{2,1,0:T(8,128)(2,1)S(1)} %slice.314), channel_id=1, source_target_pairs={{0,2},{2,0},{1,3},{3,1},{4,6},{6,4},{5,7},{7,5},{8,10},{10,8},{9,1... | collective-permute-start | bytes 811016 | tf_op jit(solution)/shard_map/ppermute | solution.py:167
  89.9 11.1 %collective-permute-start.7 = (bf16[132,8,128]{2,1,0:T(8,128)(2,1)S(1)}, bf16[132,8,128]{2,1,0:T(8,128)(2,1)S(1)}, u32[]{:S(2)}, u32[]{:S(2)}) collective-permute-start(bf16[132,8,128]{2,1,0:T(8,128)(2,1)S(1)} %slice.315), channel_id=1, source_target_pairs={{0,2},{2,0},{1,3},{3,1},{4,6},{6,4},{5,7},{7,5},{8,10},{10,8},{9,1... | collective-permute-start | bytes 811016 | tf_op jit(solution)/shard_map/ppermute | solution.py:167
  101.4 1.9 %copy-start.1 = (bf16[4,33,33]{2,0,1:T(4,128)(2,1)S(1)}, bf16[4,33,33]{2,0,1:T(4,128)(2,1)}, u32[]{:S(2)}) copy-start(bf16[4,33,33]{2,0,1:T(4,128)(2,1)} %param.23) | copy-start | bytes 26140

commit v5 on v4

--- a/solution.py
+++ b/solution.py
@@ -126,13 +126,16 @@
     return jnp.concatenate([coupling, same_class], axis=0).astype(jnp.bfloat16)
 
 
-def collide(table, first):
+def collide(table, first, tie=None):
     all_bins = table.shape[1]
     iterate = first
     for substep in range(SUB):
+        if tie is not None and substep == SUB // 2:
+            iterate, tie = lax.optimization_barrier((iterate, tie))
         products = jnp.dot(table, iterate.astype(jnp.bfloat16), preferred_element_type=jnp.float32)
         iterate = iterate + collision_rate * products[all_bins:] * products[:all_bins]
-    return (iterate - first).astype(jnp.bfloat16)
+    change = (iterate - first).astype(jnp.bfloat16)
+    return change if tie is None else (change, tie)
 
 
 def spread_collision(grown, bin_order, kernel_index, collision_kernels):
@@ -163,7 +166,11 @@
     for chunk in range(width_x // 2):
         arrived = lax.ppermute(away[:, chunk], "bins", swap)
         first = jnp.concatenate([own[:, chunk], arrived], axis=0).reshape(2 * local_bins, -1).astype(jnp.float32)
-        change = collide(table, first).reshape(2 * local_bins, width_z, width_y)
+        if returned:
+            change, returned[-1] = collide(table, first, returned[-1])
+        else:
+            change = collide(table, first)
+        change = change.reshape(2 * local_bins, width_z, width_y)
         returned.append(lax.ppermute(change[local_bins:], "bins", swap))
         kept.append(change[:local_bins])
     pair = jnp.stack([jnp.stack(kept, axis=1), jnp.stack(returned, axis=1)], axis=1)

time: 104 us -> 99.8 us (0.960)
  waiting for transfers between devices: 38 us -> 33.1 us
    ppermute x2, waiting for transfers between devices: 10.3 us -> 5.41 us  [paired_collision(): returned.append(lax.ppermute(change[local_bins:], 'bins', swap))]
  transfers between devices with their start and end apart: 8 -> 8, of which waited for: 6 -> 6; matrix products, arithmetic and copies ran while one was open for 16% -> 22% of each run, Pallas kernels for 0% -> 0%
where the time goes in v5:
time: 99.8 us; the launch traced here: 99.3 us
  waiting for transfers between devices  33.1 us (33%)
  other arithmetic  17 us (17%)
  matrix products  16.4 us (16%)
  starting transfers between devices  14.5 us (15%)
  local copies, waits for them, and re-layouts  8.9 us (9%)
  Pallas kernels  8.14 us (8%)
  between operations  1.29 us (1%)
    ppermute x1, waiting for transfers between devices, advect_kernel_call(): lax.ppermute(rim(width_x - depth, width_x), 'tiles', up)  13.7 us
    dot_general x16, matrix products, collide(): jnp.dot(table, iterate.astype(jnp.bfloat16), preferred_element_type=jnp.f...  12.6 us
    pallas_call x1, Pallas kernels, advect_kernel_call(): pl.pallas_call(functools.partial(advect_kernel, section_weights), out_sha...  8.14 us
    ppermute x2, waiting for transfers between devices, paired_collision(): arrived = lax.ppermute(away[:, chunk], 'bins', swap)  6.46 us
    ppermute x2, waiting for transfers between devices, paired_collision(): returned.append(lax.ppermute(change[local_bins:], 'bins', swap))  5.41 us
    ppermute x1, starting transfers between devices, advect_kernel_call(): lax.ppermute(rim(width_x - depth, width_x), 'tiles', up)  5.11 us
    ppermute x1, waiting for transfers between devices, advect_kernel_call(): lax.ppermute(rim(0, depth), 'tiles', down)  4.95 us
    add x6, other arithmetic, collide(): iterate + collision_rate * products[all_bins:] * products[:all_bins]  3.85 us
  transfers between devices with their start and end apart: 8, of which 6 were waited for; matrix products, arithmetic and copies ran while one was open for 22% of the time, Pallas kernels for 0%

profile of v5, /device:TPU:0, one launch (start us, length us, event | category | flops | bytes accessed | tf_op | source)
XLA Modules:
  0.0 99.3 jit_solution(17797667287727527469)
XLA Ops:
  0.7 0.8 compare_select_fusion.1
  1.5 1.8 %convert.17 = bf16[132,4,8,128]{3,2,1,0:T(8,128)(2,1)S(1)} convert(f32[132,4,8,128]{3,2,1,0:T(8,128)} %q_ref.1) | non-fusion elementwise | flops 540672 | bytes 3244032 | tf_op jit(solution)/shard_map/convert.6
  3.7 1.0 %pad_maximum_fusion.1 = bf16[136,3,8,128]{3,2,1,0:T(8,128)(2,1)} fusion(bf16[2,3,8,128]{3,2,1,0:T(8,128)(2,1)S(1)} %subtract_convert_fusion.1, bf16[2,3,8,128]{3,2,1,0:T(8,128)(2,1)S(1)} %fusion.61, bf16[132,3,8,128]{3,2,1,0:T(8,128)(2,1)S(1)} %get-tuple-element.15), kind=kLoop, calls=%fused_computation.67 | loop fusion | flops 835584 | bytes 1671168 | tf_op jit(solution)/shard_map/concatenate | solution.py:66
  4.7 5.1 %collective-permute-start = (bf16[136,3,8,128]{3,2,1,0:T(8,128)(2,1)}, bf16[136,3,8,128]{3,2,1,0:T(8,128)(2,1)S(1)}, u32[]{:S(2)}, u32[]{:S(2)}) collective-permute-start(bf16[136,3,8,128]{3,2,1,0:T(8,128)(2,1)} %pad_maximum_fusion.1), channel_id=1, source_target_pairs={{0,4},{4,8},{8,12},{1,5},{5,9},{9,13},{2,6},{6,10},{10,14},{3,7},{... | collective-permute-start | bytes 2506760 | tf_op jit(solution)/shard_map/ppermute | solution.py:73
  9.9 1.0 %pad_maximum_fusion.2 = bf16[136,3,8,128]{3,2,1,0:T(8,128)(2,1)} fusion(bf16[2,3,8,128]{3,2,1,0:T(8,128)(2,1)S(1)} %subtract_convert_fusion, bf16[2,3,8,128]{3,2,1,0:T(8,128)(2,1)S(1)} %fusion.60, bf16[132,3,8,128]{3,2,1,0:T(8,128)(2,1)S(1)} %get-tuple-element.14), kind=kLoop, calls=%fused_computation.68 | loop fusion | flops 835584 | bytes 1671168 | tf_op jit(solution)/shard_map/concatenate | solution.py:66
  10.9 1.3 %collective-permute-start.1 = (bf16[136,3,8,128]{3,2,1,0:T(8,128)(2,1)}, bf16[136,3,8,128]{3,2,1,0:T(8,128)(2,1)S(1)}, u32[]{:S(2)}, u32[]{:S(2)}) collective-permute-start(bf16[136,3,8,128]{3,2,1,0:T(8,128)(2,1)} %pad_maximum_fusion.2), channel_id=1, source_target_pairs={{4,0},{8,4},{12,8},{5,1},{9,5},{13,9},{6,2},{10,6},{14,10},{7,3},{... | collective-permute-start | bytes 2506760 | tf_op jit(solution)/shard_map/ppermute | solution.py:74
  14.2 13.7 %collective-permute-done = bf16[136,3,8,128]{3,2,1,0:T(8,128)(2,1)S(1)} collective-permute-done((bf16[136,3,8,128]{3,2,1,0:T(8,128)(2,1)}, bf16[136,3,8,128]{3,2,1,0:T(8,128)(2,1)S(1)}, u32[]{:S(2)}, u32[]{:S(2)}) %collective-permute-start) | collective-permute-done | bytes 835616 | tf_op jit(solution)/shard_map/ppermute | solution.py:73
  28.1 5.0 %collective-permute-done.1 = bf16[136,3,8,128]{3,2,1,0:T(8,128)(2,1)S(1)} collective-permute-done((bf16[136,3,8,128]{3,2,1,0:T(8,128)(2,1)}, bf16[136,3,8,128]{3,2,1,0:T(8,128)(2,1)S(1)}, u32[]{:S(2)}, u32[]{:S(2)}) %collective-permute-start.1) | collective-permute-done | bytes 835616 | tf_op jit(solution)/shard_map/ppermute | solution.py:74
  33.2 0.6 pad_maximum_fusion.8
  33.8 1.3 %slice.255.left_ref = f32[132,3,8,128]{3,2,1,0:T(8,128)} slice(bf16[136,3,8,128]{3,2,1,0:T(8,128)(2,1)S(1)} %collective-permute-done), slice={[0:132], [0:3], [0:8], [0:128]} | slice | bytes 3244032 | tf_op jit(solution)/shard_map/slice | solution.py:71
  35.1 1.3 %slice.259.right_ref = f32[132,3,8,128]{3,2,1,0:T(8,128)} slice(bf16[136,3,8,128]{3,2,1,0:T(8,128)(2,1)S(1)} %collective-permute-done.1), slice={[0:132], [0:3], [0:8], [0:128]} | slice | bytes 3244032 | tf_op jit(solution)/shard_map/slice | solution.py:71
  36.4 8.1 %shard_map.139 = f32[132,4,8,128]{3,2,1,0:T(8,128)} custom-call(f32[132,4,8,128]{3,2,1,0:T(8,128)} %q_ref.1, f32[132,3,8,128]{3,2,1,0:T(8,128)} %slice.255.left_ref, f32[132,3,8,128]{3,2,1,0:T(8,128)} %slice.259.right_ref, f32[10,8,128]{2,1,0:T(8,128)} %get-tuple-element.39.wx_ref, f32[10,8,128]{2,1,0:T(8,128)} %get-tuple-element.40.wy_ref), custom_call_target="tpu_custom_call" | custom-call | flops 43253760 | bytes 10813440 | tf_op jit(solution)/shard_map/pallas_call | solution.py:82
  44.5 1.8 %slice.269 = f32[132,4,1,128]{3,2,1,0:T(1,128)S(1)} slice(f32[132,4,8,128]{3,2,1,0:T(8,128)} %shard_map.139), slice={[0:132], [0:4], [0:1], [0:128]} | slice | bytes 540672 | tf_op jit(solution)/shard_map/slice | solution.py:209
  46.3 1.4 %collective-permute-start.2 = (f32[132,4,1,128]{3,2,1,0:T(1,128)S(1)}, f32[132,4,1,128]{3,2,1,0:T(1,128)S(1)}, u32[]{:S(2)}, u32[]{:S(2)}) collective-permute-start(f32[132,4,1,128]{3,2,1,0:T(1,128)S(1)} %slice.269), channel_id=1, source_target_pairs={{1,0},{3,2},{5,4},{7,6},{9,8},{11,10},{13,12},{15,14},{17,16},{19,... | collective-permute-start | bytes 811016 | tf_op jit(solution)/shard_map/ppermute | solution.py:95
  47.7 2.0 %multiply_reduce_fusion = f32[264,8,33]{0,2,1:T(8,128)S(1)} fusion(f32[264,8]{0,1:T(8,128)S(1)} %fusion.68, f32[8,8,33,33]{3,1,2,0:T(8,128)S(1)} %fusion.57, s32[264]{0:T(512)S(1)} %get-tuple-element.33), kind=kOutput, calls=%fused_computation | convolution fusion | flops 221851072 | bytes 567072 | tf_op jit(solution)/shard_map/bm,acmn->bacn/dot_general | solution.py:122
  49.7 1.1 %fusion.4 = bf16[264,264]{0,1:T(8,128)(2,1)S(1)} fusion(f32[264,8,33]{0,2,1:T(8,128)S(1)} %multiply_reduce_fusion, f32[264,8]{0,1:T(8,128)S(1)} %fusion.68, f32[264,33]{0,1:T(8,128)S(1)} %fusion.54), kind=kOutput, calls=%fused_computation.17 | convolution fusion | flops 220936320 | bytes 461472 | tf_op jit(solution)/shard_map/bcn,dc,dn->bd/dot_general | solution.py:124
  51.6 1.3 %multiply_reduce_fusion.1 = (f32[4,8,128]{2,1,0:T(8,128)S(1)}, f32[4,8,128]{2,1,0:T(8,128)S(1)}, f32[132,4,8,128]{3,2,1,0:T(8,128)S(1)}) fusion(f32[132]{0:T(256)S(1)} %copy-done.13, f32[132]{0:T(256)S(1)} %copy-done.12, f32[132,4,1,128]{3,2,1,0:T(1,128)S(1)} %collective-permute-done.2, f32[132,4,7,128]{3,2,1,0:T(8,128)S(1)} %slice.268, f32[132]{0:T(256)S(1)} %copy-done.9, ...), kind=kLoop, calls=%fused_computation.6 | loop fusion | flops 4317184 | bytes 6522944 | tf_op jit(solution)/shard_map/reduce_sum | solution.py:216
  52.9 1.6 %collective-permute-start.3 = (f32[2,4,8,128]{3,2,1,0:T(8,128)S(1)}, f32[2,4,8,128]{3,2,1,0:T(8,128)S(1)}, u32[]{:S(2)}, u32[]{:S(2)}) collective-permute-start(f32[2,4,8,128]{3,2,1,0:T(8,128)S(1)} %pad_maximum_fusion.10), channel_id=1, source_target_pairs={{0,2},{2,0},{1,3},{3,1},{4,6},{6,4},{5,7},{7,5},{8,10},{10,8},{9,1... | collective-permute-start | bytes 98312 | tf_op jit(solution)/shard_map/ppermute | solution.py:221
  54.5 2.5 %collective-permute-done.3 = f32[2,4,8,128]{3,2,1,0:T(8,128)S(1)} collective-permute-done((f32[2,4,8,128]{3,2,1,0:T(8,128)S(1)}, f32[2,4,8,128]{3,2,1,0:T(8,128)S(1)}, u32[]{:S(2)}, u32[]{:S(2)}) %collective-permute-start.3) | collective-permute-done | bytes 32800 | tf_op jit(solution)/shard_map/ppermute | solution.py:221
  58.3 0.8 slice_bitcast_fusion.2
  59.1 1.5 %collective-permute-start.4 = (bf16[132,8,128]{2,1,0:T(8,128)(2,1)}, bf16[132,8,128]{2,1,0:T(8,128)(2,1)}, u32[]{:S(2)}, u32[]{:S(2)}) collective-permute-start(bf16[132,8,128]{2,1,0:T(8,128)(2,1)} %get-tuple-element.22), channel_id=1, source_target_pairs={{0,2},{2,0},{1,3},{3,1},{4,6},{6,4},{5,7},{7,5},{8,10},{10,8},{9,1... | collective-permute-start | bytes 811016 | tf_op jit(solution)/shard_map/ppermute | solution.py:167
  60.9 0.8 copy-done.3
  62.3 6.5 %collective-permute-done.4 = bf16[132,8,128]{2,1,0:T(8,128)(2,1)} collective-permute-done((bf16[132,8,128]{2,1,0:T(8,128)(2,1)}, bf16[132,8,128]{2,1,0:T(8,128)(2,1)}, u32[]{:S(2)}, u32[]{:S(2)}) %collective-permute-start.4) | collective-permute-done | bytes 270368 | tf_op jit(solution)/shard_map/ppermute | solution.py:167
  68.8 1.0 pad.35
  69.8 0.8 fusion.53
  70.6 0.8 fusion.47
  72.0 0.8 fusion.45
  72.7 0.8 fusion.43
  73.5 0.7 fusion.18
  74.2 0.8 fusion.41
  75.0 0.8 fusion.39
  76.4 0.8 fusion.37
  77.2 0.8 fusion.35
  78.0 0.7 fusion.5
  78.8 1.6 %collective-permute-start.6 = (bf16[132,8,128]{2,1,0:T(8,128)(2,1)S(1)}, bf16[132,8,128]{2,1,0:T(8,128)(2,1)S(1)}, u32[]{:S(2)}, u32[]{:S(2)}) collective-permute-start(bf16[132,8,128]{2,1,0:T(8,128)(2,1)S(1)} %slice.313), channel_id=1, source_target_pairs={{0,2},{2,0},{1,3},{3,1},{4,6},{6,4},{5,7},{7,5},{8,10},{10,8},{9,1... | collective-permute-start | bytes 811016 | tf_op jit(solution)/shard_map/ppermute | solution.py:174
  80.5 0.8 fusion.52
  81.3 0.8 fusion.33
  82.7 0.8 fusion.31
  83.4 0.8 fusion.29
  84.2 0.9 fusion.11
  85.8 0.8 fusion.27
  86.5 0.8 fusion.25
  87.9 0.8 fusion.23
  88.7 0.8 fusion.21
  89.5 0.7 fusion.6
  90.4 1.5 %collective-permute-start.7 = (bf16[132,8,128]{2,1,0:T(8,128)(2,1)S(1)}, bf16[132,8,128]{2,1,0:T(8,128)(2,1)S(1)}, u32[]{:S(2)}, u32[]{:S(2)}) collective-permute-start(bf16[132,8,128]{2,1,0:T(8,128)(2,1)S(1)} %slice.315), channel_id=1, source_target_pairs={{0,2},{2,0},{1,3},{3,1},{4,6},{6,4},{5,7},{7,5},{8,10},{10,8},{9,1... | collective-permute-start | bytes 811016 | tf_op jit(solution)/shard_map/ppermute | solution.py:174
  92.1 4.9 %collective-permute-done.7 = bf16[132,8,128]{2,1,0:T(8,128)(2,1)S(1)} collective-permute-done((bf16[132,8,128]{2,1,0:T(8,128)(2,1)S(1)}, bf16[132,8,128]{2,1,0:T(8,128)(2,1)S(1)}, u32[]{:S(2)}, u32[]{:S(2)}) %collective-permute-start.7) | collective-permute-done | bytes 270368 | tf_op jit(solution)/shard_map/ppermute | solution.py:174
  97.5 1.8 %fusion.1 = f32[132,4,8,128]{3,2,1,0:T(8,128)} fusion(bf16[132,4,8,128]{3,2,1,0:T(8,128)(2,1)S(1)} %bitcast.144, f32[132,4,8,128]{3,2,1,0:T(8,128)S(1)} %get-tuple-element.11, f32[4,8,128]{2,1,0:T(8,128)S(1)} %compare_convert_fusion, f32[4,8,128]{2,1,0:T(8,128)S(1)} %get-tuple-element.10, f32[132]{0:T(256)S(1)} %get-tuple-element.37), kind=kLoop, calls=%fused_computation.4 | loop fusion | flops 3244032 | bytes 5440016 | tf_op jit(solution)/shard_map/mul | solution.py:233
  (94 shorter events, 9.3 us)
Async XLA Ops:
  0.6 13.2 %copy-start = (bf16[4,33,33]{2,0,1:T(4,128)(2,1)S(1)}, bf16[4,33,33]{2,0,1:T(4,128)(2,1)}, u32[]{:S(2)}) copy-start(bf16[4,33,33]{2,0,1:T(4,128)(2,1)} %param.23) | copy-start | bytes 26140
  0.7 0.9 copy-start.14
  4.7 7.5 %copy-start.16 = (s32[264]{0:T(512)S(1)}, s32[264]{0:T(512)}, u32[]{:S(2)}) copy-start(s32[264]{0:T(512)} %param.21) | copy-start | bytes 3172
  4.7 7.7 %copy-start.11 = (f32[132]{0:T(256)S(1)}, f32[132]{0:T(256)}, u32[]{:S(2)}) copy-start(f32[132]{0:T(256)} %param.19) | copy-start | bytes 1588
  4.7 7.7 %copy-start.17 = (f32[132]{0:T(256)S(1)}, f32[132]{0:T(256)}, u32[]{:S(2)}) copy-start(f32[132]{0:T(256)} %param.20) | copy-start | bytes 1588
  4.7 8.5 %copy-start.8 = (f32[132]{0:T(256)S(1)}, f32[132]{0:T(256)}, u32[]{:S(2)}) copy-start(f32[132]{0:T(256)} %param.18) | copy-start | bytes 1588
  4.7 9.1 %copy-start.7 = (s32[8,8]{1,0:T(8,128)S(1)}, s32[8,8]{1,0:T(8,128)}, u32[]{:S(2)}) copy-start(s32[8,8]{1,0:T(8,128)} %param.22) | copy-start | bytes 772
  4.7 23.2 %collective-permute-start = (bf16[136,3,8,128]{3,2,1,0:T(8,128)(2,1)}, bf16[136,3,8,128]{3,2,1,0:T(8,128)(2,1)S(1)}, u32[]{:S(2)}, u32[]{:S(2)}) collective-permute-start(bf16[136,3,8,128]{3,2,1,0:T(8,128)(2,1)} %pad_maximum_fusion.1), channel_id=1, source_target_pairs={{0,4},{4,8},{8,12},{1,5},{5,9},{9,13},{2,6},{6,10},{10,14},{3,7},{... | collective-permute-start | bytes 2506760 | tf_op jit(solution)/shard_map/ppermute | solution.py:73
  10.9 22.1 %collective-permute-start.1 = (bf16[136,3,8,128]{3,2,1,0:T(8,128)(2,1)}, bf16[136,3,8,128]{3,2,1,0:T(8,128)(2,1)S(1)}, u32[]{:S(2)}, u32[]{:S(2)}) collective-permute-start(bf16[136,3,8,128]{3,2,1,0:T(8,128)(2,1)} %pad_maximum_fusion.2), channel_id=1, source_target_pairs={{4,0},{8,4},{12,8},{5,1},{9,5},{13,9},{6,2},{10,6},{14,10},{7,3},{... | collective-permute-start | bytes 2506760 | tf_op jit(solution)/shard_map/ppermute | solution.py:74
  46.3 4.6 %copy-start.2 = (f32[132,4,8,128]{3,2,1,0:T(8,128)S(1)}, f32[132,4,8,128]{3,2,1,0:T(8,128)}, u32[]{:S(2)}) copy-start(f32[132,4,8,128]{3,2,1,0:T(8,128)} %shard_map.139) | copy-start | bytes 6488068
  46.3 4.9 %collective-permute-start.2 = (f32[132,4,1,128]{3,2,1,0:T(1,128)S(1)}, f32[132,4,1,128]{3,2,1,0:T(1,128)S(1)}, u32[]{:S(2)}, u32[]{:S(2)}) collective-permute-start(f32[132,4,1,128]{3,2,1,0:T(1,128)S(1)} %slice.269), channel_id=1, source_target_pairs={{1,0},{3,2},{5,4},{7,6},{9,8},{11,10},{13,12},{15,14},{17,16},{19,... | collective-permute-start | bytes 811016 | tf_op jit(solution)/shard_map/ppermute | solution.py:95
  50.9 0.7 copy-start.9
  50.9 0.7 copy-start.10
  50.9 0.7 copy-start.12
  50.9 0.7 copy-start.13
  51.6 2.9 %copy-start.6 = (s32[4,128]{1,0:T(4,128)S(1)}, s32[4,128]{1,0:T(4,128)}, u32[]{:S(2)}) copy-start(s32[4,128]{1,0:T(4,128)} %param.17) | copy-start | bytes 6148
  51.6 2.9 %copy-start.15 = (s32[8]{0:T(128)S(1)}, s32[8]{0:T(128)}, u32[]{:S(2)}) copy-start(s32[8]{0:T(128)} %copy-done.14) | copy-start | bytes 100
  51.6 5.5 %copy-start.4 = (f32[4,8,128]{2,1,0:T(8,128)S(1)}, f32[4,8,128]{2,1,0:T(8,128)}, u32[]{:S(2)}) copy-start(f32[4,8,128]{2,1,0:T(8,128)} %param.16) | copy-start | bytes 49156
  51.6 5.5 %copy-start.5 = (f32[4,8,128]{2,1,0:T(8,128)S(1)}, f32[4,8,128]{2,1,0:T(8,128)}, u32[]{:S(2)}) copy-start(f32[4,8,128]{2,1,0:T(8,128)} %param.15) | copy-start | bytes 49156
  52.9 4.2 %collective-permute-start.3 = (f32[2,4,8,128]{3,2,1,0:T(8,128)S(1)}, f32[2,4,8,128]{3,2,1,0:T(8,128)S(1)}, u32[]{:S(2)}, u32[]{:S(2)}) collective-permute-start(f32[2,4,8,128]{3,2,1,0:T(8,128)S(1)} %pad_maximum_fusion.10), channel_id=1, source_target_pairs={{0,2},{2,0},{1,3},{3,1},{4,6},{6,4},{5,7},{7,5},{8,10},{10,8},{9,1... | collective-permute-start | bytes 98312 | tf_op jit(solution)/shard_map/ppermute | solution.py:221
  59.1 9.6 %collective-permute-start.4 = (bf16[132,8,128]{2,1,0:T(8,128)(2,1)}, bf16[132,8,128]{2,1,0:T(8,128)(2,1)}, u32[]{:S(2)}, u32[]{:S(2)}) collective-permute-start(bf16[132,8,128]{2,1,0:T(8,128)(2,1)} %get-tuple-element.22), channel_id=1, source_target_pairs={{0,2},{2,0},{1,3},{3,1},{4,6},{6,4},{5,7},{7,5},{8,10},{10,8},{9,1... | collective-permute-start | bytes 811016 | tf_op jit(solution)/shard_map/ppermute | solution.py:167
  60.7 1.0 copy-start.3
  61.7 18.7 %collective-permute-start.5 = (bf16[132,8,128]{2,1,0:T(8,128)(2,1)S(1)}, bf16[132,8,128]{2,1,0:T(8,128)(2,1)S(1)}, u32[]{:S(2)}, u32[]{:S(2)}) collective-permute-start(bf16[132,8,128]{2,1,0:T(8,128)(2,1)S(1)} %copy-done.3), channel_id=1, source_target_pairs={{0,2},{2,0},{1,3},{3,1},{4,6},{6,4},{5,7},{7,5},{8,10},{10,8},{9,1... | collective-permute-start | bytes 811016 | tf_op jit(solution)/shard_map/ppermute | solution.py:167
  78.8 6.9 %collective-permute-start.6 = (bf16[132,8,128]{2,1,0:T(8,128)(2,1)S(1)}, bf16[132,8,128]{2,1,0:T(8,128)(2,1)S(1)}, u32[]{:S(2)}, u32[]{:S(2)}) collective-permute-start(bf16[132,8,128]{2,1,0:T(8,128)(2,1)S(1)} %slice.313), channel_id=1, source_target_pairs={{0,2},{2,0},{1,3},{3,1},{4,6},{6,4},{5,7},{7,5},{8,10},{10,8},{9,1... | collective-permute-start | bytes 811016 | tf_op jit(solution)/shard_map/ppermute | solution.py:174
  90.4 6.5 %collective-permute-start.7 = (bf16[132,8,128]{2,1,0:T(8,128)(2,1)S(1)}, bf16[132,8,128]{2,1,0:T(8,128)(2,1)S(1)}, u32[]{:S(2)}, u32[]{:S(2)}) collective-permute-start(bf16[132,8,128]{2,1,0:T(8,128)(2,1)S(1)} %slice.315), channel_id=1, source_target_pairs={{0,2},{2,0},{1,3},{3,1},{4,6},{6,4},{5,7},{7,5},{8,10},{10,8},{9,1... | collective-permute-start | bytes 811016 | tf_op jit(solution)/shard_map/ppermute | solution.py:174
  97.4 1.9 %copy-start.1 = (bf16[4,33,33]{2,0,1:T(4,128)(2,1)S(1)}, bf16[4,33,33]{2,0,1:T(4,128)(2,1)}, u32[]{:S(2)}) copy-start(bf16[4,33,33]{2,0,1:T(4,128)(2,1)} %param.23) | copy-start | bytes 26140

commit v6 on v5

--- a/solution.py
+++ b/solution.py
@@ -30,7 +30,7 @@
     return array
 
 
-def advect_kernel(weights, q_ref, left_ref, right_ref, wx_ref, wy_ref, out_ref):
+def advect_kernel(weights, q_ref, left_ref, right_ref, wx_ref, wy_ref, out_ref, bottom_ref):
     depth = len(weights)
     width = q_ref.shape[1]
     field = jnp.concatenate([left_ref[...], q_ref[...], right_ref[...]], axis=1)
@@ -50,6 +50,7 @@
         along_y = jnp.maximum(wind_b, 0.0) * (center - south) + jnp.minimum(wind_b, 0.0) * (north - center)
         section = field[:, stage : stage + span] + weight_now * (-along_x - along_y)
     out_ref[...] = section
+    bottom_ref[...] = section[:, :, :1]
 
 
 def advect_kernel_call(bin_mass, wind_x, wind_y, section_weights):
@@ -81,10 +82,13 @@
     cells = local_bins * width_x * width_z * width_y
     return pl.pallas_call(
         functools.partial(advect_kernel, section_weights),
-        out_shape=jax.ShapeDtypeStruct(bin_mass.shape, bin_mass.dtype),
+        out_shape=(
+            jax.ShapeDtypeStruct(bin_mass.shape, bin_mass.dtype),
+            jax.ShapeDtypeStruct((local_bins, width_x, 1, width_y), bin_mass.dtype),
+        ),
         grid=(local_bins // block,),
         in_specs=[own_spec, rim_spec, rim_spec, wind_spec, wind_spec],
-        out_specs=own_spec,
+        out_specs=(own_spec, pl.BlockSpec((block, width_x, 1, width_y), lambda i: (i, 0, 0, 0))),
         cost_estimate=pl.CostEstimate(flops=80 * cells, bytes_accessed=20 * cells, transcendentals=0),
     )(bin_mass, q_left, q_right, wx, wy)
 
@@ -164,7 +168,10 @@
     away = lax.dynamic_index_in_dim(halves, 1 - me, axis=1, keepdims=False)
     kept, returned = [], []
     for chunk in range(width_x // 2):
-        arrived = lax.ppermute(away[:, chunk], "bins", swap)
+        send = away[:, chunk]
+        if chunk:
+            send, _ = lax.optimization_barrier((send, arrived))
+        arrived = lax.ppermute(send, "bins", swap)
         first = jnp.concatenate([own[:, chunk], arrived], axis=0).reshape(2 * local_bins, -1).astype(jnp.float32)
         if returned:
             change, returned[-1] = collide(table, first, returned[-1])
@@ -198,7 +205,7 @@
     wind_y = wind_north * open_cells
     section_weights = (1.0 / 3.0, 0.5, 1.0)
     if width_x >= len(section_weights):
-        section_field = advect_kernel_call(bin_mass, wind_x, wind_y, section_weights)
+        section_field, bottom = advect_kernel_call(bin_mass, wind_x, wind_y, section_weights)
     else:
         section_field = bin_mass
         for weight_now in section_weights:
@@ -206,7 +213,8 @@
             section_field = bin_mass + weight_now * tendency(
                 extended[:, 1:-1], extended[:, :-2], extended[:, 2:], wind_x, wind_y
             )
-    rim_above = shifted(section_field[:, :, :1, :], "vert", -1)
+        bottom = section_field[:, :, :1, :]
+    rim_above = shifted(bottom, "vert", -1)
     from_above = jnp.concatenate([section_field[:, :, 1:], rim_above], axis=2)
     speed = fall_speed[:, None, None, None]
     settled = (1.0 - speed) * section_field + speed * from_above

time: 99.8 us -> 104 us (1.042)
  waiting for transfers between devices: 33.1 us -> 41.3 us
  local copies, waits for them, and re-layouts: 8.9 us -> 6.17 us
  other arithmetic: 17 us -> 15.8 us
    ppermute x2, waiting for transfers between devices: 6.46 us -> 14.1 us  [paired_collision(): arrived = lax.ppermute(send, 'bins', swap)]
    slice x1 -> x0, local copies, waits for them, and re-layouts: 1.79 us -> none  [body(): rim_above = shifted(section_field[:, :, :1, :], 'vert', -1)]
    ppermute x1, waiting for transfers between devices: 13.7 us -> 14.8 us  [advect_kernel_call(): lax.ppermute(rim(width_x - depth, width_x), 'tiles', up)]
    unnamed x49 -> x37, local copies, waits for them, and re-layouts: 2.73 us -> 1.75 us
  transfers between devices with their start and end apart: 8 -> 8, of which waited for: 6 -> 6; matrix products, arithmetic and copies ran while one was open for 22% -> 10% of each run, Pallas kernels for 0% -> 0%
where the time goes in v6:
time: 104 us
  waiting for transfers between devices  41.3 us (40%)
  matrix products  16.4 us (16%)
  other arithmetic  15.8 us (15%)
  starting transfers between devices  14.5 us (14%)
  Pallas kernels  8.19 us (8%)
  local copies, waits for them, and re-layouts  6.17 us (6%)
  between operations  1.29 us (1%)
    ppermute x1, waiting for transfers between devices, advect_kernel_call(): lax.ppermute(rim(width_x - depth, width_x), 'tiles', up)  14.8 us
    ppermute x2, waiting for transfers between devices, paired_collision(): arrived = lax.ppermute(send, 'bins', swap)  14.1 us
    dot_general x16, matrix products, collide(): jnp.dot(table, iterate.astype(jnp.bfloat16), preferred_element_type=jnp.f...  12.6 us
    pallas_call x1, Pallas kernels, advect_kernel_call(): pl.pallas_call(functools.partial(advect_kernel, section_weights), out_sha...  8.19 us
    ppermute x1, starting transfers between devices, advect_kernel_call(): lax.ppermute(rim(width_x - depth, width_x), 'tiles', up)  5.11 us
    ppermute x1, waiting for transfers between devices, advect_kernel_call(): lax.ppermute(rim(0, depth), 'tiles', down)  4.97 us
    ppermute x2, waiting for transfers between devices, paired_collision(): returned.append(lax.ppermute(change[local_bins:], 'bins', swap))  4.86 us
    add x6, other arithmetic, collide(): iterate + collision_rate * products[all_bins:] * products[:all_bins]  3.85 us
  transfers between devices with their start and end apart: 8, of which 6 were waited for; matrix products, arithmetic and copies ran while one was open for 10% of the time, Pallas kernels for 0%

profile of v6, /device:TPU:0, one launch (start us, length us, event | category | flops | bytes accessed | tf_op | source)
XLA Modules:
  0.0 103.7 jit_solution(14780534403329072950)
XLA Ops:
  0.7 0.8 compare_select_fusion.1
  1.5 1.8 %convert.17 = bf16[132,4,8,128]{3,2,1,0:T(8,128)(2,1)S(1)} convert(f32[132,4,8,128]{3,2,1,0:T(8,128)} %q_ref.1) | non-fusion elementwise | flops 540672 | bytes 3244032 | tf_op jit(solution)/shard_map/convert.6
  3.7 1.0 pad_maximum_fusion.1
  4.7 5.1 %collective-permute-start = (bf16[136,3,8,128]{3,2,1,0:T(8,128)(2,1)}, bf16[136,3,8,128]{3,2,1,0:T(8,128)(2,1)S(1)}, u32[]{:S(2)}, u32[]{:S(2)}) collective-permute-start(bf16[136,3,8,128]{3,2,1,0:T(8,128)(2,1)} %pad_maximum_fusion.1), channel_id=1, source_target_pairs={{0,4},{4,8},{8,12},{1,5},{5,9},{9,13},{2,6},{6,10},{10,14},{3,7},{... | collective-permute-start | bytes 2506760 | tf_op jit(solution)/shard_map/ppermute | solution.py:74
  9.8 1.0 pad_maximum_fusion.2
  10.9 1.3 %collective-permute-start.1 = (bf16[136,3,8,128]{3,2,1,0:T(8,128)(2,1)}, bf16[136,3,8,128]{3,2,1,0:T(8,128)(2,1)S(1)}, u32[]{:S(2)}, u32[]{:S(2)}) collective-permute-start(bf16[136,3,8,128]{3,2,1,0:T(8,128)(2,1)} %pad_maximum_fusion.2), channel_id=1, source_target_pairs={{4,0},{8,4},{12,8},{5,1},{9,5},{13,9},{6,2},{10,6},{14,10},{7,3},{... | collective-permute-start | bytes 2506760 | tf_op jit(solution)/shard_map/ppermute | solution.py:75
  13.1 14.8 %collective-permute-done = bf16[136,3,8,128]{3,2,1,0:T(8,128)(2,1)S(1)} collective-permute-done((bf16[136,3,8,128]{3,2,1,0:T(8,128)(2,1)}, bf16[136,3,8,128]{3,2,1,0:T(8,128)(2,1)S(1)}, u32[]{:S(2)}, u32[]{:S(2)}) %collective-permute-start) | collective-permute-done | bytes 835616 | tf_op jit(solution)/shard_map/ppermute | solution.py:74
  28.0 5.0 %collective-permute-done.1 = bf16[136,3,8,128]{3,2,1,0:T(8,128)(2,1)S(1)} collective-permute-done((bf16[136,3,8,128]{3,2,1,0:T(8,128)(2,1)}, bf16[136,3,8,128]{3,2,1,0:T(8,128)(2,1)S(1)}, u32[]{:S(2)}, u32[]{:S(2)}) %collective-permute-start.1) | collective-permute-done | bytes 835616 | tf_op jit(solution)/shard_map/ppermute | solution.py:75
  33.2 0.6 pad_maximum_fusion.8
  33.8 1.3 %slice.251.left_ref = f32[132,3,8,128]{3,2,1,0:T(8,128)} slice(bf16[136,3,8,128]{3,2,1,0:T(8,128)(2,1)S(1)} %collective-permute-done), slice={[0:132], [0:3], [0:8], [0:128]} | slice | bytes 3244032 | tf_op jit(solution)/shard_map/slice | solution.py:72
  35.1 1.3 %slice.255.right_ref = f32[132,3,8,128]{3,2,1,0:T(8,128)} slice(bf16[136,3,8,128]{3,2,1,0:T(8,128)(2,1)S(1)} %collective-permute-done.1), slice={[0:132], [0:3], [0:8], [0:128]} | slice | bytes 3244032 | tf_op jit(solution)/shard_map/slice | solution.py:72
  36.4 8.2 %shard_map.139 = (f32[132,4,8,128]{3,2,1,0:T(8,128)}, f32[132,4,1,128]{3,2,1,0:T(1,128)}) custom-call(f32[132,4,8,128]{3,2,1,0:T(8,128)} %q_ref.1, f32[132,3,8,128]{3,2,1,0:T(8,128)} %slice.251.left_ref, f32[132,3,8,128]{3,2,1,0:T(8,128)} %slice.255.right_ref, f32[10,8,128]{2,1,0:T(8,128)} %get-tuple-element.45.wx_ref, f32[10,8,128]{2,1,0:T(8,128)} %get-tuple-element.46.wy_ref), custom_call_target="tpu_custom_call" | custom-call | flops 43253760 | bytes 10813440 | tf_op jit(solution)/shard_map/pallas_call | solution.py:83
  44.6 1.4 %collective-permute-start.2 = (f32[132,4,1,128]{3,2,1,0:T(1,128)}, f32[132,4,1,128]{3,2,1,0:T(1,128)S(1)}, u32[]{:S(2)}, u32[]{:S(2)}) collective-permute-start(f32[132,4,1,128]{3,2,1,0:T(1,128)} %get-tuple-element.9), channel_id=1, source_target_pairs={{1,0},{3,2},{5,4},{7,6},{9,8},{11,10},{13,12},{15,14},{17,16},{19,... | collective-permute-start | bytes 811016 | tf_op jit(solution)/shard_map/ppermute | solution.py:99
  46.0 2.0 %multiply_reduce_fusion = f32[264,8,33]{0,2,1:T(8,128)S(1)} fusion(f32[264,8]{0,1:T(8,128)S(1)} %fusion.68, f32[8,8,33,33]{3,1,2,0:T(8,128)S(1)} %fusion.57, s32[264]{0:T(512)S(1)} %get-tuple-element.39), kind=kOutput, calls=%fused_computation | convolution fusion | flops 221851072 | bytes 567072 | tf_op jit(solution)/shard_map/bm,acmn->bacn/dot_general | solution.py:126
  48.0 1.1 %fusion.4 = bf16[264,264]{0,1:T(8,128)(2,1)S(1)} fusion(f32[264,8,33]{0,2,1:T(8,128)S(1)} %multiply_reduce_fusion, f32[264,8]{0,1:T(8,128)S(1)} %fusion.68, f32[264,33]{0,1:T(8,128)S(1)} %fusion.54), kind=kOutput, calls=%fused_computation.17 | convolution fusion | flops 220936320 | bytes 461472 | tf_op jit(solution)/shard_map/bcn,dc,dn->bd/dot_general | solution.py:128
  49.5 1.3 %multiply_reduce_fusion.1 = (f32[4,8,128]{2,1,0:T(8,128)S(1)}, f32[4,8,128]{2,1,0:T(8,128)S(1)}, f32[132,4,8,128]{3,2,1,0:T(8,128)S(1)}) fusion(f32[132]{0:T(256)S(1)} %get-tuple-element.44, f32[132]{0:T(256)S(1)} %copy-done.8, f32[132,4,1,128]{3,2,1,0:T(1,128)S(1)} %collective-permute-done.2, f32[132,4,7,128]{3,2,1,0:T(8,128)S(1)} %slice.203, ...), kind=kLoop, calls=%fused_computation.6 | loop fusion | flops 4317184 | bytes 6522944 | tf_op jit(solution)/shard_map/reduce_sum | solution.py:224
  50.8 1.6 %collective-permute-start.3 = (f32[2,4,8,128]{3,2,1,0:T(8,128)S(1)}, f32[2,4,8,128]{3,2,1,0:T(8,128)S(1)}, u32[]{:S(2)}, u32[]{:S(2)}) collective-permute-start(f32[2,4,8,128]{3,2,1,0:T(8,128)S(1)} %pad_maximum_fusion.10), channel_id=1, source_target_pairs={{0,2},{2,0},{1,3},{3,1},{4,6},{6,4},{5,7},{7,5},{8,10},{10,8},{9,1... | collective-permute-start | bytes 98312 | tf_op jit(solution)/shard_map/ppermute | solution.py:229
  52.4 2.5 %collective-permute-done.3 = f32[2,4,8,128]{3,2,1,0:T(8,128)S(1)} collective-permute-done((f32[2,4,8,128]{3,2,1,0:T(8,128)S(1)}, f32[2,4,8,128]{3,2,1,0:T(8,128)S(1)}, u32[]{:S(2)}, u32[]{:S(2)}) %collective-permute-start.3) | collective-permute-done | bytes 32800 | tf_op jit(solution)/shard_map/ppermute | solution.py:229
  54.9 0.6 fusion.64
  56.1 0.8 slice_bitcast_fusion.2
  57.0 1.5 %collective-permute-start.4 = (bf16[132,8,128]{2,1,0:T(8,128)(2,1)}, bf16[132,8,128]{2,1,0:T(8,128)(2,1)}, u32[]{:S(2)}, u32[]{:S(2)}) collective-permute-start(bf16[132,8,128]{2,1,0:T(8,128)(2,1)} %get-tuple-element.28), channel_id=1, source_target_pairs={{0,2},{2,0},{1,3},{3,1},{4,6},{6,4},{5,7},{7,5},{8,10},{10,8},{9,1... | collective-permute-start | bytes 811016 | tf_op jit(solution)/shard_map/ppermute | solution.py:174
  58.8 7.0 %collective-permute-done.4 = bf16[132,8,128]{2,1,0:T(8,128)(2,1)} collective-permute-done((bf16[132,8,128]{2,1,0:T(8,128)(2,1)}, bf16[132,8,128]{2,1,0:T(8,128)(2,1)}, u32[]{:S(2)}, u32[]{:S(2)}) %collective-permute-start.4) | collective-permute-done | bytes 270368 | tf_op jit(solution)/shard_map/ppermute | solution.py:174
  65.8 1.0 pad.35
  66.8 0.8 fusion.53
  67.6 0.8 fusion.47
  69.0 0.8 fusion.45
  69.8 0.8 fusion.43
  70.6 0.7 fusion.18
  71.3 0.8 fusion.41
  72.0 0.8 fusion.39
  73.4 0.8 fusion.37
  74.2 0.8 fusion.35
  75.0 0.7 fusion.5
  76.0 1.5 %collective-permute-start.5 = (bf16[132,8,128]{2,1,0:T(8,128)(2,1)S(1)}, bf16[132,8,128]{2,1,0:T(8,128)(2,1)S(1)}, u32[]{:S(2)}, u32[]{:S(2)}) collective-permute-start(bf16[132,8,128]{2,1,0:T(8,128)(2,1)S(1)} %copy-done.3), channel_id=1, source_target_pairs={{0,2},{2,0},{1,3},{3,1},{4,6},{6,4},{5,7},{7,5},{8,10},{10,8},{9,1... | collective-permute-start | bytes 811016 | tf_op jit(solution)/shard_map/ppermute | solution.py:174
  78.3 7.1 %collective-permute-done.5 = bf16[132,8,128]{2,1,0:T(8,128)(2,1)S(1)} collective-permute-done((bf16[132,8,128]{2,1,0:T(8,128)(2,1)S(1)}, bf16[132,8,128]{2,1,0:T(8,128)(2,1)S(1)}, u32[]{:S(2)}, u32[]{:S(2)}) %collective-permute-start.5) | collective-permute-done | bytes 270368 | tf_op jit(solution)/shard_map/ppermute | solution.py:174
  85.5 0.8 fusion.52
  86.3 0.8 fusion.33
  87.6 0.8 fusion.31
  88.4 0.8 fusion.29
  89.2 0.9 fusion.11
  90.1 0.8 fusion.27
  90.9 0.8 fusion.25
  92.3 0.8 fusion.23
  93.1 0.8 fusion.21
  93.9 0.7 fusion.6
  94.8 1.5 %collective-permute-start.7 = (bf16[132,8,128]{2,1,0:T(8,128)(2,1)S(1)}, bf16[132,8,128]{2,1,0:T(8,128)(2,1)S(1)}, u32[]{:S(2)}, u32[]{:S(2)}) collective-permute-start(bf16[132,8,128]{2,1,0:T(8,128)(2,1)S(1)} %slice.309), channel_id=1, source_target_pairs={{0,2},{2,0},{1,3},{3,1},{4,6},{6,4},{5,7},{7,5},{8,10},{10,8},{9,1... | collective-permute-start | bytes 811016 | tf_op jit(solution)/shard_map/ppermute | solution.py:181
  96.5 4.9 %collective-permute-done.7 = bf16[132,8,128]{2,1,0:T(8,128)(2,1)S(1)} collective-permute-done((bf16[132,8,128]{2,1,0:T(8,128)(2,1)S(1)}, bf16[132,8,128]{2,1,0:T(8,128)(2,1)S(1)}, u32[]{:S(2)}, u32[]{:S(2)}) %collective-permute-start.7) | collective-permute-done | bytes 270368 | tf_op jit(solution)/shard_map/ppermute | solution.py:181
  101.8 1.8 %fusion.1 = f32[132,4,8,128]{3,2,1,0:T(8,128)} fusion(bf16[132,4,8,128]{3,2,1,0:T(8,128)(2,1)S(1)} %bitcast.144, f32[132,4,8,128]{3,2,1,0:T(8,128)S(1)} %get-tuple-element.17, f32[4,8,128]{2,1,0:T(8,128)S(1)} %compare_convert_fusion, f32[4,8,128]{2,1,0:T(8,128)S(1)} %get-tuple-element.16, f32[132]{0:T(256)S(1)} %get-tuple-element.43), kind=kLoop, calls=%fused_computation.4 | loop fusion | flops 3244032 | bytes 5440016 | tf_op jit(solution)/shard_map/mul | solution.py:241
  (80 shorter events, 6.9 us)
Async XLA Ops:
  0.6 12.1 %copy-start = (bf16[4,33,33]{2,0,1:T(4,128)(2,1)S(1)}, bf16[4,33,33]{2,0,1:T(4,128)(2,1)}, u32[]{:S(2)}) copy-start(bf16[4,33,33]{2,0,1:T(4,128)(2,1)} %param.23) | copy-start | bytes 26140
  4.7 7.5 %copy-start.10 = (s32[264]{0:T(512)S(1)}, s32[264]{0:T(512)}, u32[]{:S(2)}) copy-start(s32[264]{0:T(512)} %param.21) | copy-start | bytes 3172
  4.7 8.0 %copy-start.8 = (f32[132]{0:T(256)S(1)}, f32[132]{0:T(256)}, u32[]{:S(2)}) copy-start(f32[132]{0:T(256)} %param.19) | copy-start | bytes 1588
  4.7 8.0 %copy-start.9 = (f32[132]{0:T(256)S(1)}, f32[132]{0:T(256)}, u32[]{:S(2)}) copy-start(f32[132]{0:T(256)} %param.18) | copy-start | bytes 1588
  4.7 8.0 %copy-start.11 = (f32[132]{0:T(256)S(1)}, f32[132]{0:T(256)}, u32[]{:S(2)}) copy-start(f32[132]{0:T(256)} %param.20) | copy-start | bytes 1588
  4.7 8.0 %copy-start.7 = (s32[8,8]{1,0:T(8,128)S(1)}, s32[8,8]{1,0:T(8,128)}, u32[]{:S(2)}) copy-start(s32[8,8]{1,0:T(8,128)} %param.22) | copy-start | bytes 772
  4.7 23.2 %collective-permute-start = (bf16[136,3,8,128]{3,2,1,0:T(8,128)(2,1)}, bf16[136,3,8,128]{3,2,1,0:T(8,128)(2,1)S(1)}, u32[]{:S(2)}, u32[]{:S(2)}) collective-permute-start(bf16[136,3,8,128]{3,2,1,0:T(8,128)(2,1)} %pad_maximum_fusion.1), channel_id=1, source_target_pairs={{0,4},{4,8},{8,12},{1,5},{5,9},{9,13},{2,6},{6,10},{10,14},{3,7},{... | collective-permute-start | bytes 2506760 | tf_op jit(solution)/shard_map/ppermute | solution.py:74
  10.9 22.1 %collective-permute-start.1 = (bf16[136,3,8,128]{3,2,1,0:T(8,128)(2,1)}, bf16[136,3,8,128]{3,2,1,0:T(8,128)(2,1)S(1)}, u32[]{:S(2)}, u32[]{:S(2)}) collective-permute-start(bf16[136,3,8,128]{3,2,1,0:T(8,128)(2,1)} %pad_maximum_fusion.2), channel_id=1, source_target_pairs={{4,0},{8,4},{12,8},{5,1},{9,5},{13,9},{6,2},{10,6},{14,10},{7,3},{... | collective-permute-start | bytes 2506760 | tf_op jit(solution)/shard_map/ppermute | solution.py:75
  44.6 4.6 %copy-start.2 = (f32[132,4,8,128]{3,2,1,0:T(8,128)S(1)}, f32[132,4,8,128]{3,2,1,0:T(8,128)}, u32[]{:S(2)}) copy-start(f32[132,4,8,128]{3,2,1,0:T(8,128)} %get-tuple-element.8) | copy-start | bytes 6488068
  44.6 4.9 %collective-permute-start.2 = (f32[132,4,1,128]{3,2,1,0:T(1,128)}, f32[132,4,1,128]{3,2,1,0:T(1,128)S(1)}, u32[]{:S(2)}, u32[]{:S(2)}) collective-permute-start(f32[132,4,1,128]{3,2,1,0:T(1,128)} %get-tuple-element.9), channel_id=1, source_target_pairs={{1,0},{3,2},{5,4},{7,6},{9,8},{11,10},{13,12},{15,14},{17,16},{19,... | collective-permute-start | bytes 811016 | tf_op jit(solution)/shard_map/ppermute | solution.py:99
  49.4 2.9 %copy-start.6 = (s32[4,128]{1,0:T(4,128)S(1)}, s32[4,128]{1,0:T(4,128)}, u32[]{:S(2)}) copy-start(s32[4,128]{1,0:T(4,128)} %param.17) | copy-start | bytes 6148
  49.5 5.5 %copy-start.4 = (f32[4,8,128]{2,1,0:T(8,128)S(1)}, f32[4,8,128]{2,1,0:T(8,128)}, u32[]{:S(2)}) copy-start(f32[4,8,128]{2,1,0:T(8,128)} %param.16) | copy-start | bytes 49156
  49.5 5.5 %copy-start.5 = (f32[4,8,128]{2,1,0:T(8,128)S(1)}, f32[4,8,128]{2,1,0:T(8,128)}, u32[]{:S(2)}) copy-start(f32[4,8,128]{2,1,0:T(8,128)} %param.15) | copy-start | bytes 49156
  50.8 4.2 %collective-permute-start.3 = (f32[2,4,8,128]{3,2,1,0:T(8,128)S(1)}, f32[2,4,8,128]{3,2,1,0:T(8,128)S(1)}, u32[]{:S(2)}, u32[]{:S(2)}) collective-permute-start(f32[2,4,8,128]{3,2,1,0:T(8,128)S(1)} %pad_maximum_fusion.10), channel_id=1, source_target_pairs={{0,2},{2,0},{1,3},{3,1},{4,6},{6,4},{5,7},{7,5},{8,10},{10,8},{9,1... | collective-permute-start | bytes 98312 | tf_op jit(solution)/shard_map/ppermute | solution.py:229
  57.0 8.8 %collective-permute-start.4 = (bf16[132,8,128]{2,1,0:T(8,128)(2,1)}, bf16[132,8,128]{2,1,0:T(8,128)(2,1)}, u32[]{:S(2)}, u32[]{:S(2)}) collective-permute-start(bf16[132,8,128]{2,1,0:T(8,128)(2,1)} %get-tuple-element.28), channel_id=1, source_target_pairs={{0,2},{2,0},{1,3},{3,1},{4,6},{6,4},{5,7},{7,5},{8,10},{10,8},{9,1... | collective-permute-start | bytes 811016 | tf_op jit(solution)/shard_map/ppermute | solution.py:174
  75.0 1.0 copy-start.3
  76.0 9.4 %collective-permute-start.5 = (bf16[132,8,128]{2,1,0:T(8,128)(2,1)S(1)}, bf16[132,8,128]{2,1,0:T(8,128)(2,1)S(1)}, u32[]{:S(2)}, u32[]{:S(2)}) collective-permute-start(bf16[132,8,128]{2,1,0:T(8,128)(2,1)S(1)} %copy-done.3), channel_id=1, source_target_pairs={{0,2},{2,0},{1,3},{3,1},{4,6},{6,4},{5,7},{7,5},{8,10},{10,8},{9,1... | collective-permute-start | bytes 811016 | tf_op jit(solution)/shard_map/ppermute | solution.py:174
  77.6 12.5 %collective-permute-start.6 = (bf16[132,8,128]{2,1,0:T(8,128)(2,1)S(1)}, bf16[132,8,128]{2,1,0:T(8,128)(2,1)S(1)}, u32[]{:S(2)}, u32[]{:S(2)}) collective-permute-start(bf16[132,8,128]{2,1,0:T(8,128)(2,1)S(1)} %slice.307), channel_id=1, source_target_pairs={{0,2},{2,0},{1,3},{3,1},{4,6},{6,4},{5,7},{7,5},{8,10},{10,8},{9,1... | collective-permute-start | bytes 811016 | tf_op jit(solution)/shard_map/ppermute | solution.py:181
  94.8 6.5 %collective-permute-start.7 = (bf16[132,8,128]{2,1,0:T(8,128)(2,1)S(1)}, bf16[132,8,128]{2,1,0:T(8,128)(2,1)S(1)}, u32[]{:S(2)}, u32[]{:S(2)}) collective-permute-start(bf16[132,8,128]{2,1,0:T(8,128)(2,1)S(1)} %slice.309), channel_id=1, source_target_pairs={{0,2},{2,0},{1,3},{3,1},{4,6},{6,4},{5,7},{7,5},{8,10},{10,8},{9,1... | collective-permute-start | bytes 811016 | tf_op jit(solution)/shard_map/ppermute | solution.py:181
  101.8 1.9 %copy-start.1 = (bf16[4,33,33]{2,0,1:T(4,128)(2,1)S(1)}, bf16[4,33,33]{2,0,1:T(4,128)(2,1)}, u32[]{:S(2)}) copy-start(bf16[4,33,33]{2,0,1:T(4,128)(2,1)} %param.23) | copy-start | bytes 26140

commit v7 on v6

--- a/solution.py
+++ b/solution.py
@@ -30,12 +30,22 @@
     return array
 
 
-def advect_kernel(weights, q_ref, left_ref, right_ref, wx_ref, wy_ref, out_ref, bottom_ref):
+def advect_kernel(weights, q_ref, left_ref, right_ref, *refs):
+    left_winds, right_winds = refs[0:4], refs[4:8]
+    wx_ref, wy_ref, out_ref, bottom_ref = refs[8:]
     depth = len(weights)
     width = q_ref.shape[1]
-    field = jnp.concatenate([left_ref[...], q_ref[...], right_ref[...]], axis=1)
-    wx = wx_ref[...]
-    wy = wy_ref[...]
+
+    def widened(ref):
+        return ref[...].astype(jnp.float32)
+
+    def winds(rows):
+        return [widened(rows[k])[0] + widened(rows[k + 2])[0] for k in (0, 1)]
+
+    (wx_left, wy_left), (wx_right, wy_right) = winds(left_winds), winds(right_winds)
+    field = jnp.concatenate([widened(left_ref), q_ref[...], widened(right_ref)], axis=1)
+    wx = jnp.concatenate([wx_left, wx_ref[...], wx_right], axis=0)
+    wy = jnp.concatenate([wy_left, wy_ref[...], wy_right], axis=0)
     section = field
     for stage, weight_now in enumerate(weights, start=1):
         span = width + 2 * (depth - stage)
@@ -66,19 +76,16 @@
         low = (winds - high.astype(jnp.float32)).astype(jnp.bfloat16)
         return jnp.concatenate([bin_mass[:, lo:hi].astype(jnp.bfloat16), high, low], axis=0)
 
-    def unpack(message):
-        message = message.astype(jnp.float32)
-        winds = message[local_bins : local_bins + 2] + message[local_bins + 2 :]
-        return message[:local_bins], winds[0], winds[1]
-
-    q_left, wx_left, wy_left = unpack(lax.ppermute(rim(width_x - depth, width_x), "tiles", up))
-    q_right, wx_right, wy_right = unpack(lax.ppermute(rim(0, depth), "tiles", down))
-    wx = jnp.concatenate([wx_left, wind_x, wx_right], axis=0)
-    wy = jnp.concatenate([wy_left, wind_y, wy_right], axis=0)
+    left = lax.ppermute(rim(width_x - depth, width_x), "tiles", up)
+    right = lax.ppermute(rim(0, depth), "tiles", down)
     block = max(d for d in range(1, 34) if local_bins % d == 0)
     rim_spec = pl.BlockSpec((block, depth, width_z, width_y), lambda i: (i, 0, 0, 0))
+    row_specs = [
+        pl.BlockSpec((1, depth, width_z, width_y), lambda i, row=local_bins + k: (row, 0, 0, 0))
+        for k in range(4)
+    ]
     own_spec = pl.BlockSpec((block, width_x, width_z, width_y), lambda i: (i, 0, 0, 0))
-    wind_spec = pl.BlockSpec(wx.shape, lambda i: (0, 0, 0))
+    wind_spec = pl.BlockSpec(wind_x.shape, lambda i: (0, 0, 0))
     cells = local_bins * width_x * width_z * width_y
     return pl.pallas_call(
         functools.partial(advect_kernel, section_weights),
@@ -87,11 +94,10 @@
             jax.ShapeDtypeStruct((local_bins, width_x, 1, width_y), bin_mass.dtype),
         ),
         grid=(local_bins // block,),
-        in_specs=[own_spec, rim_spec, rim_spec, wind_spec, wind_spec],
+        in_specs=[own_spec, rim_spec, rim_spec] + row_specs + row_specs + [wind_spec, wind_spec],
         out_specs=(own_spec, pl.BlockSpec((block, width_x, 1, width_y), lambda i: (i, 0, 0, 0))),
         cost_estimate=pl.CostEstimate(flops=80 * cells, bytes_accessed=20 * cells, transcendentals=0),
-    )(bin_mass, q_left, q_right, wx, wy)
-
+    )(bin_mass, left, right, *([left] * 4), *([right] * 4), wind_x, wind_y)
 
 def shifted(block, axis, distance):
     devices = range(lax.axis_size(axis))
@@ -168,10 +174,7 @@
     away = lax.dynamic_index_in_dim(halves, 1 - me, axis=1, keepdims=False)
     kept, returned = [], []
     for chunk in range(width_x // 2):
-        send = away[:, chunk]
-        if chunk:
-            send, _ = lax.optimization_barrier((send, arrived))
-        arrived = lax.ppermute(send, "bins", swap)
+        arrived = lax.ppermute(away[:, chunk], "bins", swap)
         first = jnp.concatenate([own[:, chunk], arrived], axis=0).reshape(2 * local_bins, -1).astype(jnp.float32)
         if returned:
             change, returned[-1] = collide(table, first, returned[-1])

time: 104 us -> 94.8 us (0.912)
  waiting for transfers between devices: 41.3 us -> 34.3 us
  local copies, waits for them, and re-layouts: 6.17 us -> 5.08 us
    ppermute x4, waiting for transfers between devices: 33.9 us -> 26.4 us  [the longest x1 14.8 us: advect_kernel_call(): left = lax.ppermute(rim(width_x - depth, width_x), 'tiles', up)]
    slice x2 -> x0, local copies, waits for them, and re-layouts: 2.59 us -> none  [unpack(): return (message[:local_bins], winds[0], winds[1])]
    unnamed x37 -> x45, local copies, waits for them, and re-layouts: 1.75 us -> 3.26 us
  transfers between devices with their start and end apart: 8 -> 8, of which waited for: 6 -> 6; matrix products, arithmetic and copies ran while one was open for 10% -> 22% of each run, Pallas kernels for 0% -> 0%
where the time goes in v7:
time: 94.8 us; the launch traced here: 94.4 us
  waiting for transfers between devices  34.3 us (36%)
  matrix products  16.4 us (17%)
  other arithmetic  15 us (16%)
  starting transfers between devices  14.5 us (15%)
  Pallas kernels  7.81 us (8%)
  local copies, waits for them, and re-layouts  5.08 us (5%)
  between operations  1.27 us (1%)
    ppermute x1, waiting for transfers between devices, advect_kernel_call(): left = lax.ppermute(rim(width_x - depth, width_x), 'tiles', up)  14.8 us
    dot_general x16, matrix products, collide(): jnp.dot(table, iterate.astype(jnp.bfloat16), preferred_element_type=jnp.f...  12.7 us
    pallas_call x1, Pallas kernels, advect_kernel_call(): pl.pallas_call(functools.partial(advect_kernel, section_weights), out_sha...  7.81 us
    ppermute x2, waiting for transfers between devices, paired_collision(): arrived = lax.ppermute(away[:, chunk], 'bins', swap)  6.46 us
    ppermute x2, waiting for transfers between devices, paired_collision(): returned.append(lax.ppermute(change[local_bins:], 'bins', swap))  5.38 us
    ppermute x1, waiting for transfers between devices, advect_kernel_call(): right = lax.ppermute(rim(0, depth), 'tiles', down)  5.12 us
    ppermute x1, starting transfers between devices, advect_kernel_call(): left = lax.ppermute(rim(width_x - depth, width_x), 'tiles', up)  5.11 us
    add x6, other arithmetic, collide(): iterate + collision_rate * products[all_bins:] * products[:all_bins]  3.85 us
  transfers between devices with their start and end apart: 8, of which 6 were waited for; matrix products, arithmetic and copies ran while one was open for 22% of the time, Pallas kernels for 0%

profile of v7, /device:TPU:0, one launch (start us, length us, event | category | flops | bytes accessed | tf_op | source)
XLA Modules:
  0.0 94.4 jit_solution(17134268717245538557)
XLA Ops:
  0.7 0.8 compare_select_fusion.1
  1.5 1.8 %convert.17 = bf16[132,4,8,128]{3,2,1,0:T(8,128)(2,1)S(1)} convert(f32[132,4,8,128]{3,2,1,0:T(8,128)} %q_ref.1) | non-fusion elementwise | flops 540672 | bytes 3244032 | tf_op jit(solution)/shard_map/convert.6
  3.7 1.0 %pad_maximum_fusion.1 = bf16[136,3,8,128]{3,2,1,0:T(8,128)(2,1)} fusion(bf16[2,3,8,128]{3,2,1,0:T(8,128)(2,1)S(1)} %subtract_convert_fusion.1, bf16[2,3,8,128]{3,2,1,0:T(8,128)(2,1)S(1)} %fusion.61, bf16[132,3,8,128]{3,2,1,0:T(8,128)(2,1)S(1)} %get-tuple-element.19), kind=kLoop, calls=%fused_computation.67 | loop fusion | flops 835584 | bytes 1671168 | tf_op jit(solution)/shard_map/concatenate | solution.py:77
  4.7 5.1 %collective-permute-start = (bf16[136,3,8,128]{3,2,1,0:T(8,128)(2,1)}, bf16[136,3,8,128]{3,2,1,0:T(8,128)(2,1)S(1)}, u32[]{:S(2)}, u32[]{:S(2)}) collective-permute-start(bf16[136,3,8,128]{3,2,1,0:T(8,128)(2,1)} %pad_maximum_fusion.1), channel_id=1, source_target_pairs={{0,4},{4,8},{8,12},{1,5},{5,9},{9,13},{2,6},{6,10},{10,14},{3,7},{... | collective-permute-start | bytes 2506760 | tf_op jit(solution)/shard_map/ppermute | solution.py:79
  9.9 1.0 %pad_maximum_fusion.2 = bf16[136,3,8,128]{3,2,1,0:T(8,128)(2,1)} fusion(bf16[2,3,8,128]{3,2,1,0:T(8,128)(2,1)S(1)} %subtract_convert_fusion, bf16[2,3,8,128]{3,2,1,0:T(8,128)(2,1)S(1)} %fusion.60, bf16[132,3,8,128]{3,2,1,0:T(8,128)(2,1)S(1)} %get-tuple-element.18), kind=kLoop, calls=%fused_computation.68 | loop fusion | flops 835584 | bytes 1671168 | tf_op jit(solution)/shard_map/concatenate | solution.py:77
  10.9 1.3 %collective-permute-start.1 = (bf16[136,3,8,128]{3,2,1,0:T(8,128)(2,1)}, bf16[136,3,8,128]{3,2,1,0:T(8,128)(2,1)S(1)}, u32[]{:S(2)}, u32[]{:S(2)}) collective-permute-start(bf16[136,3,8,128]{3,2,1,0:T(8,128)(2,1)} %pad_maximum_fusion.2), channel_id=1, source_target_pairs={{4,0},{8,4},{12,8},{5,1},{9,5},{13,9},{6,2},{10,6},{14,10},{7,3},{... | collective-permute-start | bytes 2506760 | tf_op jit(solution)/shard_map/ppermute | solution.py:80
  13.1 14.8 %collective-permute-done.left_ref.refs_0_.refs_1_.refs_2_.refs_3_ = bf16[136,3,8,128]{3,2,1,0:T(8,128)(2,1)S(1)} collective-permute-done((bf16[136,3,8,128]{3,2,1,0:T(8,128)(2,1)}, bf16[136,3,8,128]{3,2,1,0:T(8,128)(2,1)S(1)}, u32[]{:S(2)}, u32[]{:S(2)}) %collective-permute-start) | collective-permute-done | bytes 835616 | tf_op jit(solution)/shard_map/ppermute | solution.py:79
  27.9 5.1 %collective-permute-done.1.right_ref.refs_4_.refs_5_.refs_6_.refs_7_ = bf16[136,3,8,128]{3,2,1,0:T(8,128)(2,1)S(1)} collective-permute-done((bf16[136,3,8,128]{3,2,1,0:T(8,128)(2,1)}, bf16[136,3,8,128]{3,2,1,0:T(8,128)(2,1)S(1)}, u32[]{:S(2)}, u32[]{:S(2)}) %collective-permute-start.1) | collective-permute-done | bytes 835616 | tf_op jit(solution)/shard_map/ppermute | solution.py:80
  33.1 0.9 copy-done.3
  34.0 7.8 %shard_map.139 = (f32[132,4,8,128]{3,2,1,0:T(8,128)}, f32[132,4,1,128]{3,2,1,0:T(1,128)}) custom-call(f32[132,4,8,128]{3,2,1,0:T(8,128)} %q_ref.1, bf16[136,3,8,128]{3,2,1,0:T(8,128)(2,1)} %copy-done.2, bf16[136,3,8,128]{3,2,1,0:T(8,128)(2,1)} %copy-done.3, bf16[136,3,8,128]{3,2,1,0:T(8,128)(2,1)} %copy-done.2, bf16[136,3,8,128]{3,2,1,0:T(8,128)(2,1)} %copy-done.2, ...), custom_call_target="tpu_custom_call" | custom-call | flops 43253760 | bytes 10813440 | tf_op jit(solution)/shard_map/pallas_call | solution.py:90
  41.8 1.4 %collective-permute-start.2 = (f32[132,4,1,128]{3,2,1,0:T(1,128)}, f32[132,4,1,128]{3,2,1,0:T(1,128)S(1)}, u32[]{:S(2)}, u32[]{:S(2)}) collective-permute-start(f32[132,4,1,128]{3,2,1,0:T(1,128)} %get-tuple-element.8), channel_id=1, source_target_pairs={{1,0},{3,2},{5,4},{7,6},{9,8},{11,10},{13,12},{15,14},{17,16},{19,... | collective-permute-start | bytes 811016 | tf_op jit(solution)/shard_map/ppermute | solution.py:105
  43.2 2.0 %multiply_reduce_fusion = f32[264,8,33]{0,2,1:T(8,128)S(1)} fusion(f32[264,8]{0,1:T(8,128)S(1)} %fusion.68, f32[8,8,33,33]{3,1,2,0:T(8,128)S(1)} %fusion.57, s32[264]{0:T(512)S(1)} %get-tuple-element.33), kind=kOutput, calls=%fused_computation | convolution fusion | flops 221851072 | bytes 567072 | tf_op jit(solution)/shard_map/bm,acmn->bacn/dot_general | solution.py:132
  45.2 1.1 %fusion.4 = bf16[264,264]{0,1:T(8,128)(2,1)S(1)} fusion(f32[264,8,33]{0,2,1:T(8,128)S(1)} %multiply_reduce_fusion, f32[264,8]{0,1:T(8,128)S(1)} %fusion.68, f32[264,33]{0,1:T(8,128)S(1)} %fusion.54), kind=kOutput, calls=%fused_computation.17 | convolution fusion | flops 220936320 | bytes 461472 | tf_op jit(solution)/shard_map/bcn,dc,dn->bd/dot_general | solution.py:134
  46.7 1.2 %multiply_reduce_fusion.1 = (f32[4,8,128]{2,1,0:T(8,128)S(1)}, f32[4,8,128]{2,1,0:T(8,128)S(1)}, f32[132,4,8,128]{3,2,1,0:T(8,128)S(1)}) fusion(f32[132]{0:T(256)S(1)} %get-tuple-element.38, f32[132]{0:T(256)S(1)} %copy-done.13, f32[132,4,1,128]{3,2,1,0:T(1,128)S(1)} %collective-permute-done.2, f32[132,4,7,128]{3,2,1,0:T(8,128)S(1)} %slice.163, ...), kind=kLoop, calls=%fused_computation.6 | loop fusion | flops 4317184 | bytes 6522944 | tf_op jit(solution)/shard_map/reduce_sum | solution.py:227
  48.0 1.6 %collective-permute-start.3 = (f32[2,4,8,128]{3,2,1,0:T(8,128)S(1)}, f32[2,4,8,128]{3,2,1,0:T(8,128)S(1)}, u32[]{:S(2)}, u32[]{:S(2)}) collective-permute-start(f32[2,4,8,128]{3,2,1,0:T(8,128)S(1)} %pad_maximum_fusion.8), channel_id=1, source_target_pairs={{0,2},{2,0},{1,3},{3,1},{4,6},{6,4},{5,7},{7,5},{8,10},{10,8},{9,1... | collective-permute-start | bytes 98312 | tf_op jit(solution)/shard_map/ppermute | solution.py:232
  49.6 2.5 %collective-permute-done.3 = f32[2,4,8,128]{3,2,1,0:T(8,128)S(1)} collective-permute-done((f32[2,4,8,128]{3,2,1,0:T(8,128)S(1)}, f32[2,4,8,128]{3,2,1,0:T(8,128)S(1)}, u32[]{:S(2)}, u32[]{:S(2)}) %collective-permute-start.3) | collective-permute-done | bytes 32800 | tf_op jit(solution)/shard_map/ppermute | solution.py:232
  52.1 0.6 fusion.64
  53.4 0.8 slice_bitcast_fusion.2
  54.2 1.5 %collective-permute-start.4 = (bf16[132,8,128]{2,1,0:T(8,128)(2,1)}, bf16[132,8,128]{2,1,0:T(8,128)(2,1)}, u32[]{:S(2)}, u32[]{:S(2)}) collective-permute-start(bf16[132,8,128]{2,1,0:T(8,128)(2,1)} %get-tuple-element.26), channel_id=1, source_target_pairs={{0,2},{2,0},{1,3},{3,1},{4,6},{6,4},{5,7},{7,5},{8,10},{10,8},{9,1... | collective-permute-start | bytes 811016 | tf_op jit(solution)/shard_map/ppermute | solution.py:177
  56.0 0.8 copy-done.5
  57.4 6.5 %collective-permute-done.4 = bf16[132,8,128]{2,1,0:T(8,128)(2,1)} collective-permute-done((bf16[132,8,128]{2,1,0:T(8,128)(2,1)}, bf16[132,8,128]{2,1,0:T(8,128)(2,1)}, u32[]{:S(2)}, u32[]{:S(2)}) %collective-permute-start.4) | collective-permute-done | bytes 270368 | tf_op jit(solution)/shard_map/ppermute | solution.py:177
  63.8 1.0 %pad.29 = bf16[136,8,128]{2,1,0:T(8,128)(2,1)S(1)} pad(bf16[132,8,128]{2,1,0:T(8,128)(2,1)} %collective-permute-done.4, bf16[]{:T(256)} %constant.80), padding=0_4x0_0x0_0 | pad | bytes 548866
  64.9 0.8 fusion.53
  65.7 0.8 fusion.47
  67.0 0.8 fusion.45
  67.8 0.8 fusion.43
  68.6 0.7 fusion.18
  69.3 0.8 fusion.41
  70.1 0.8 fusion.39
  70.9 0.6 fusion.16
  71.5 0.8 fusion.37
  72.3 0.8 fusion.35
  73.1 0.7 fusion.5
  73.9 1.6 %collective-permute-start.6 = (bf16[132,8,128]{2,1,0:T(8,128)(2,1)S(1)}, bf16[132,8,128]{2,1,0:T(8,128)(2,1)S(1)}, u32[]{:S(2)}, u32[]{:S(2)}) collective-permute-start(bf16[132,8,128]{2,1,0:T(8,128)(2,1)S(1)} %slice.257), channel_id=1, source_target_pairs={{0,2},{2,0},{1,3},{3,1},{4,6},{6,4},{5,7},{7,5},{8,10},{10,8},{9,1... | collective-permute-start | bytes 811016 | tf_op jit(solution)/shard_map/ppermute | solution.py:184
  75.6 0.8 fusion.52
  76.3 0.8 fusion.33
  77.7 0.8 fusion.31
  78.5 0.8 fusion.29
  79.3 0.9 fusion.11
  80.8 0.8 fusion.27
  81.6 0.8 fusion.25
  82.4 0.6 fusion.9
  83.0 0.8 fusion.23
  83.8 0.8 fusion.21
  84.6 0.7 fusion.6
  85.5 1.6 %collective-permute-start.7 = (bf16[132,8,128]{2,1,0:T(8,128)(2,1)S(1)}, bf16[132,8,128]{2,1,0:T(8,128)(2,1)S(1)}, u32[]{:S(2)}, u32[]{:S(2)}) collective-permute-start(bf16[132,8,128]{2,1,0:T(8,128)(2,1)S(1)} %slice.259), channel_id=1, source_target_pairs={{0,2},{2,0},{1,3},{3,1},{4,6},{6,4},{5,7},{7,5},{8,10},{10,8},{9,1... | collective-permute-start | bytes 811016 | tf_op jit(solution)/shard_map/ppermute | solution.py:184
  87.2 4.8 %collective-permute-done.7 = bf16[132,8,128]{2,1,0:T(8,128)(2,1)S(1)} collective-permute-done((bf16[132,8,128]{2,1,0:T(8,128)(2,1)S(1)}, bf16[132,8,128]{2,1,0:T(8,128)(2,1)S(1)}, u32[]{:S(2)}, u32[]{:S(2)}) %collective-permute-start.7) | collective-permute-done | bytes 270368 | tf_op jit(solution)/shard_map/ppermute | solution.py:184
  92.5 1.8 %fusion.1 = f32[132,4,8,128]{3,2,1,0:T(8,128)} fusion(bf16[132,4,8,128]{3,2,1,0:T(8,128)(2,1)S(1)} %bitcast.136, f32[132,4,8,128]{3,2,1,0:T(8,128)S(1)} %get-tuple-element.15, f32[4,8,128]{2,1,0:T(8,128)S(1)} %compare_convert_fusion, f32[4,8,128]{2,1,0:T(8,128)S(1)} %get-tuple-element.14, f32[132]{0:T(256)S(1)} %get-tuple-element.37), kind=kLoop, calls=%fused_computation.4 | loop fusion | flops 3244032 | bytes 5440016 | tf_op jit(solution)/shard_map/mul | solution.py:244
  (79 shorter events, 5.7 us)
Async XLA Ops:
  0.6 12.1 %copy-start = (bf16[4,33,33]{2,0,1:T(4,128)(2,1)S(1)}, bf16[4,33,33]{2,0,1:T(4,128)(2,1)}, u32[]{:S(2)}) copy-start(bf16[4,33,33]{2,0,1:T(4,128)(2,1)} %param.23) | copy-start | bytes 26140
  1.5 1.9 %copy-start.6 = (f32[4,8,128]{2,1,0:T(8,128)}, f32[4,8,128]{2,1,0:T(8,128)S(1)}, u32[]{:S(2)}) copy-start(f32[4,8,128]{2,1,0:T(8,128)S(1)} %get-tuple-element.35.refs_8_) | copy-start | bytes 49156
  1.5 1.9 %copy-start.7 = (f32[4,8,128]{2,1,0:T(8,128)}, f32[4,8,128]{2,1,0:T(8,128)S(1)}, u32[]{:S(2)}) copy-start(f32[4,8,128]{2,1,0:T(8,128)S(1)} %get-tuple-element.36.refs_9_) | copy-start | bytes 49156
  4.7 7.5 %copy-start.14 = (s32[264]{0:T(512)S(1)}, s32[264]{0:T(512)}, u32[]{:S(2)}) copy-start(s32[264]{0:T(512)} %param.21) | copy-start | bytes 3172
  4.7 7.7 %copy-start.13 = (f32[132]{0:T(256)S(1)}, f32[132]{0:T(256)}, u32[]{:S(2)}) copy-start(f32[132]{0:T(256)} %param.19) | copy-start | bytes 1588
  4.7 7.7 %copy-start.15 = (f32[132]{0:T(256)S(1)}, f32[132]{0:T(256)}, u32[]{:S(2)}) copy-start(f32[132]{0:T(256)} %param.20) | copy-start | bytes 1588
  4.7 7.7 %copy-start.12 = (f32[132]{0:T(256)S(1)}, f32[132]{0:T(256)}, u32[]{:S(2)}) copy-start(f32[132]{0:T(256)} %param.18) | copy-start | bytes 1588
  4.7 8.1 %copy-start.11 = (s32[8,8]{1,0:T(8,128)S(1)}, s32[8,8]{1,0:T(8,128)}, u32[]{:S(2)}) copy-start(s32[8,8]{1,0:T(8,128)} %param.22) | copy-start | bytes 772
  4.7 23.2 %collective-permute-start = (bf16[136,3,8,128]{3,2,1,0:T(8,128)(2,1)}, bf16[136,3,8,128]{3,2,1,0:T(8,128)(2,1)S(1)}, u32[]{:S(2)}, u32[]{:S(2)}) collective-permute-start(bf16[136,3,8,128]{3,2,1,0:T(8,128)(2,1)} %pad_maximum_fusion.1), channel_id=1, source_target_pairs={{0,4},{4,8},{8,12},{1,5},{5,9},{9,13},{2,6},{6,10},{10,14},{3,7},{... | collective-permute-start | bytes 2506760 | tf_op jit(solution)/shard_map/ppermute | solution.py:79
  10.9 22.1 %collective-permute-start.1 = (bf16[136,3,8,128]{3,2,1,0:T(8,128)(2,1)}, bf16[136,3,8,128]{3,2,1,0:T(8,128)(2,1)S(1)}, u32[]{:S(2)}, u32[]{:S(2)}) collective-permute-start(bf16[136,3,8,128]{3,2,1,0:T(8,128)(2,1)} %pad_maximum_fusion.2), channel_id=1, source_target_pairs={{4,0},{8,4},{12,8},{5,1},{9,5},{13,9},{6,2},{10,6},{14,10},{7,3},{... | collective-permute-start | bytes 2506760 | tf_op jit(solution)/shard_map/ppermute | solution.py:80
  27.9 5.1 %copy-start.2 = (bf16[136,3,8,128]{3,2,1,0:T(8,128)(2,1)}, bf16[136,3,8,128]{3,2,1,0:T(8,128)(2,1)S(1)}, u32[]{:S(2)}) copy-start(bf16[136,3,8,128]{3,2,1,0:T(8,128)(2,1)S(1)} %collective-permute-done.left_ref.refs_0_.refs_1_.refs_2_.refs_3_) | copy-start | bytes 2506756
  33.1 0.9 copy-start.3
  41.8 4.6 %copy-start.4 = (f32[132,4,8,128]{3,2,1,0:T(8,128)S(1)}, f32[132,4,8,128]{3,2,1,0:T(8,128)}, u32[]{:S(2)}) copy-start(f32[132,4,8,128]{3,2,1,0:T(8,128)} %get-tuple-element.7) | copy-start | bytes 6488068
  41.8 4.9 %collective-permute-start.2 = (f32[132,4,1,128]{3,2,1,0:T(1,128)}, f32[132,4,1,128]{3,2,1,0:T(1,128)S(1)}, u32[]{:S(2)}, u32[]{:S(2)}) collective-permute-start(f32[132,4,1,128]{3,2,1,0:T(1,128)} %get-tuple-element.8), channel_id=1, source_target_pairs={{1,0},{3,2},{5,4},{7,6},{9,8},{11,10},{13,12},{15,14},{17,16},{19,... | collective-permute-start | bytes 811016 | tf_op jit(solution)/shard_map/ppermute | solution.py:105
  46.7 2.9 %copy-start.10 = (s32[4,128]{1,0:T(4,128)S(1)}, s32[4,128]{1,0:T(4,128)}, u32[]{:S(2)}) copy-start(s32[4,128]{1,0:T(4,128)} %param.17) | copy-start | bytes 6148
  46.7 5.5 %copy-start.8 = (f32[4,8,128]{2,1,0:T(8,128)S(1)}, f32[4,8,128]{2,1,0:T(8,128)}, u32[]{:S(2)}) copy-start(f32[4,8,128]{2,1,0:T(8,128)} %param.16) | copy-start | bytes 49156
  46.7 5.5 %copy-start.9 = (f32[4,8,128]{2,1,0:T(8,128)S(1)}, f32[4,8,128]{2,1,0:T(8,128)}, u32[]{:S(2)}) copy-start(f32[4,8,128]{2,1,0:T(8,128)} %param.15) | copy-start | bytes 49156
  48.0 4.2 %collective-permute-start.3 = (f32[2,4,8,128]{3,2,1,0:T(8,128)S(1)}, f32[2,4,8,128]{3,2,1,0:T(8,128)S(1)}, u32[]{:S(2)}, u32[]{:S(2)}) collective-permute-start(f32[2,4,8,128]{3,2,1,0:T(8,128)S(1)} %pad_maximum_fusion.8), channel_id=1, source_target_pairs={{0,2},{2,0},{1,3},{3,1},{4,6},{6,4},{5,7},{7,5},{8,10},{10,8},{9,1... | collective-permute-start | bytes 98312 | tf_op jit(solution)/shard_map/ppermute | solution.py:232
  54.2 9.6 %collective-permute-start.4 = (bf16[132,8,128]{2,1,0:T(8,128)(2,1)}, bf16[132,8,128]{2,1,0:T(8,128)(2,1)}, u32[]{:S(2)}, u32[]{:S(2)}) collective-permute-start(bf16[132,8,128]{2,1,0:T(8,128)(2,1)} %get-tuple-element.26), channel_id=1, source_target_pairs={{0,2},{2,0},{1,3},{3,1},{4,6},{6,4},{5,7},{7,5},{8,10},{10,8},{9,1... | collective-permute-start | bytes 811016 | tf_op jit(solution)/shard_map/ppermute | solution.py:177
  55.8 1.0 %copy-start.5 = (bf16[132,8,128]{2,1,0:T(8,128)(2,1)S(1)}, bf16[132,8,128]{2,1,0:T(8,128)(2,1)}, u32[]{:S(2)}) copy-start(bf16[132,8,128]{2,1,0:T(8,128)(2,1)} %get-tuple-element.27) | copy-start | bytes 811012
  56.8 18.7 %collective-permute-start.5 = (bf16[132,8,128]{2,1,0:T(8,128)(2,1)S(1)}, bf16[132,8,128]{2,1,0:T(8,128)(2,1)S(1)}, u32[]{:S(2)}, u32[]{:S(2)}) collective-permute-start(bf16[132,8,128]{2,1,0:T(8,128)(2,1)S(1)} %copy-done.5), channel_id=1, source_target_pairs={{0,2},{2,0},{1,3},{3,1},{4,6},{6,4},{5,7},{7,5},{8,10},{10,8},{9,1... | collective-permute-start | bytes 811016 | tf_op jit(solution)/shard_map/ppermute | solution.py:177
  73.9 6.9 %collective-permute-start.6 = (bf16[132,8,128]{2,1,0:T(8,128)(2,1)S(1)}, bf16[132,8,128]{2,1,0:T(8,128)(2,1)S(1)}, u32[]{:S(2)}, u32[]{:S(2)}) collective-permute-start(bf16[132,8,128]{2,1,0:T(8,128)(2,1)S(1)} %slice.257), channel_id=1, source_target_pairs={{0,2},{2,0},{1,3},{3,1},{4,6},{6,4},{5,7},{7,5},{8,10},{10,8},{9,1... | collective-permute-start | bytes 811016 | tf_op jit(solution)/shard_map/ppermute | solution.py:184
  85.5 6.5 %collective-permute-start.7 = (bf16[132,8,128]{2,1,0:T(8,128)(2,1)S(1)}, bf16[132,8,128]{2,1,0:T(8,128)(2,1)S(1)}, u32[]{:S(2)}, u32[]{:S(2)}) collective-permute-start(bf16[132,8,128]{2,1,0:T(8,128)(2,1)S(1)} %slice.259), channel_id=1, source_target_pairs={{0,2},{2,0},{1,3},{3,1},{4,6},{6,4},{5,7},{7,5},{8,10},{10,8},{9,1... | collective-permute-start | bytes 811016 | tf_op jit(solution)/shard_map/ppermute | solution.py:184
  92.5 1.9 %copy-start.1 = (bf16[4,33,33]{2,0,1:T(4,128)(2,1)S(1)}, bf16[4,33,33]{2,0,1:T(4,128)(2,1)}, u32[]{:S(2)}) copy-start(bf16[4,33,33]{2,0,1:T(4,128)(2,1)} %param.23) | copy-start | bytes 26140

commit v8 on v7

--- a/solution.py
+++ b/solution.py
@@ -28,6 +28,27 @@
         after = lax.ppermute(first.astype(link), axis, down).astype(array.dtype)
         array = jnp.concatenate([before, array, after], axis=dim)
     return array
+
+
+def rim_kernel(depth, q_ref, wx_ref, wy_ref, left_ref, right_ref):
+    local_bins, width_x = q_ref.shape[:2]
+    for out_ref, lo in ((left_ref, width_x - depth), (right_ref, 0)):
+        out_ref[0:local_bins] = q_ref[:, lo : lo + depth].astype(out_ref.dtype)
+        for k, wind_ref in enumerate((wx_ref, wy_ref)):
+            wind = wind_ref[lo : lo + depth]
+            high = wind.astype(out_ref.dtype)
+            low = (wind - high.astype(jnp.float32)).astype(out_ref.dtype)
+            out_ref[local_bins + k] = high
+            out_ref[local_bins + 2 + k] = low
+
+
+def rims(bin_mass, wind_x, wind_y, depth):
+    local_bins, width_x, width_z, width_y = bin_mass.shape
+    shape = jax.ShapeDtypeStruct((local_bins + 4, depth, width_z, width_y), jnp.bfloat16)
+    return pl.pallas_call(
+        functools.partial(rim_kernel, depth),
+        out_shape=(shape, shape),
+    )(bin_mass, wind_x, wind_y)
 
 
 def advect_kernel(weights, q_ref, left_ref, right_ref, *refs):
@@ -70,14 +91,10 @@
     up = [(i, i + 1) for i in range(tiles - 1)]
     down = [(j, i) for i, j in up]
 
-    def rim(lo, hi):
-        winds = jnp.stack([wind_x[lo:hi], wind_y[lo:hi]])
-        high = winds.astype(jnp.bfloat16)
-        low = (winds - high.astype(jnp.float32)).astype(jnp.bfloat16)
-        return jnp.concatenate([bin_mass[:, lo:hi].astype(jnp.bfloat16), high, low], axis=0)
-
-    left = lax.ppermute(rim(width_x - depth, width_x), "tiles", up)
-    right = lax.ppermute(rim(0, depth), "tiles", down)
+    left, right = (
+        lax.ppermute(message, "tiles", pairs)
+        for message, pairs in zip(rims(bin_mass, wind_x, wind_y, depth), (up, down))
+    )
     block = max(d for d in range(1, 34) if local_bins % d == 0)
     rim_spec = pl.BlockSpec((block, depth, width_z, width_y), lambda i: (i, 0, 0, 0))
     row_specs = [

time: 94.8 us -> 93.9 us (level)
  other arithmetic: 15 us -> 11.7 us
  Pallas kernels: 7.81 us -> 10.8 us
    pallas_call x0 -> x1, Pallas kernels: none -> 2.98 us  [rims(): pl.pallas_call(functools.partial(rim_kernel, depth), out_shape=(shape, sh...]
    concatenate x2 -> x0, other arithmetic: 2.05 us -> none  [rim(): jnp.concatenate([bin_mass[:, lo:hi].astype(jnp.bfloat16), high, low], axi...]
    another operation x2 -> x1, other arithmetic: 1.85 us -> 0.01 us
    unnamed x45 -> x41, local copies, waits for them, and re-layouts: 3.26 us -> 3.28 us
  transfers between devices with their start and end apart: 8 -> 8, of which waited for: 6 -> 6; matrix products, arithmetic and copies ran while one was open for 22% -> 21% of each run, Pallas kernels for 0% -> 0%
where the time goes in v8:
time: 93.9 us; the launch traced here: 93.6 us
  waiting for transfers between devices  34.3 us (37%)
  matrix products  16.4 us (17%)
  starting transfers between devices  14.4 us (15%)
  other arithmetic  11.7 us (12%)
  Pallas kernels  10.8 us (12%)
  local copies, waits for them, and re-layouts  4.79 us (5%)
  between operations  1.2 us (1%)
    ppermute x2, waiting for transfers between devices, advect_kernel_call(): lax.ppermute(message, 'tiles', pairs)  19.9 us
    dot_general x16, matrix products, collide(): jnp.dot(table, iterate.astype(jnp.bfloat16), preferred_element_type=jnp.f...  12.7 us
    pallas_call x1, Pallas kernels, advect_kernel_call(): pl.pallas_call(functools.partial(advect_kernel, section_weights), out_sha...  7.8 us
    ppermute x2, waiting for transfers between devices, paired_collision(): arrived = lax.ppermute(away[:, chunk], 'bins', swap)  6.46 us
    ppermute x2, starting transfers between devices, advect_kernel_call(): lax.ppermute(message, 'tiles', pairs)  6.26 us
    ppermute x2, waiting for transfers between devices, paired_collision(): returned.append(lax.ppermute(change[local_bins:], 'bins', swap))  5.4 us
    add x6, other arithmetic, collide(): iterate + collision_rate * products[all_bins:] * products[:all_bins]  3.85 us
    unnamed x41, local copies, waits for them, and re-layouts  3.28 us
  transfers between devices with their start and end apart: 8, of which 6 were waited for; matrix products, arithmetic and copies ran while one was open for 21% of the time, Pallas kernels for 0%

profile of v8, /device:TPU:0, one launch (start us, length us, event | category | flops | bytes accessed | tf_op | source)
XLA Modules:
  0.0 93.6 jit_solution(17156146013547946419)
XLA Ops:
  0.7 1.4 %compare_select_fusion = (f32[4,8,128]{2,1,0:T(8,128)}, f32[4,8,128]{2,1,0:T(8,128)}) fusion(f32[4,8,128]{2,1,0:T(8,128)} %param.14, s32[4,128]{1,0:T(4,128)} %param.17, s32[8]{0:T(128)S(1)} %iota_add_fusion, f32[4,8,128]{2,1,0:T(8,128)} %param.13), kind=kLoop, calls=%fused_computation.121 | loop fusion | flops 12288 | bytes 67616 | tf_op jit(solution)/shard_map/mul | solution.py:225
  2.1 3.0 %shard_map.139 = (bf16[136,3,8,128]{3,2,1,0:T(8,128)(2,1)}, bf16[136,3,8,128]{3,2,1,0:T(8,128)(2,1)}) custom-call(f32[132,4,8,128]{3,2,1,0:T(8,128)} %q_ref.3, f32[4,8,128]{2,1,0:T(8,128)} %get-tuple-element.34.wx_ref.refs_8_, f32[4,8,128]{2,1,0:T(8,128)} %get-tuple-element.33.wy_ref.refs_9_), custom_call_target="tpu_custom_call" | custom-call | tf_op jit(solution)/shard_map/pallas_call | solution.py:48
  5.1 5.0 %collective-permute-start = (bf16[136,3,8,128]{3,2,1,0:T(8,128)(2,1)}, bf16[136,3,8,128]{3,2,1,0:T(8,128)(2,1)S(1)}, u32[]{:S(2)}, u32[]{:S(2)}) collective-permute-start(bf16[136,3,8,128]{3,2,1,0:T(8,128)(2,1)} %get-tuple-element.9), channel_id=1, source_target_pairs={{0,4},{4,8},{8,12},{1,5},{5,9},{9,13},{2,6},{6,10},{10,14},{3,7},{... | collective-permute-start | bytes 2506760 | tf_op jit(solution)/shard_map/ppermute | solution.py:95
  10.1 1.3 %collective-permute-start.1 = (bf16[136,3,8,128]{3,2,1,0:T(8,128)(2,1)}, bf16[136,3,8,128]{3,2,1,0:T(8,128)(2,1)S(1)}, u32[]{:S(2)}, u32[]{:S(2)}) collective-permute-start(bf16[136,3,8,128]{3,2,1,0:T(8,128)(2,1)} %get-tuple-element.10), channel_id=1, source_target_pairs={{4,0},{8,4},{12,8},{5,1},{9,5},{13,9},{6,2},{10,6},{14,10},{7,3},{... | collective-permute-start | bytes 2506760 | tf_op jit(solution)/shard_map/ppermute | solution.py:95
  12.3 15.9 %collective-permute-done.left_ref.refs_0_.refs_1_.refs_2_.refs_3_ = bf16[136,3,8,128]{3,2,1,0:T(8,128)(2,1)S(1)} collective-permute-done((bf16[136,3,8,128]{3,2,1,0:T(8,128)(2,1)}, bf16[136,3,8,128]{3,2,1,0:T(8,128)(2,1)S(1)}, u32[]{:S(2)}, u32[]{:S(2)}) %collective-permute-start) | collective-permute-done | bytes 835616 | tf_op jit(solution)/shard_map/ppermute | solution.py:95
  28.2 4.1 %collective-permute-done.1.right_ref.refs_4_.refs_5_.refs_6_.refs_7_ = bf16[136,3,8,128]{3,2,1,0:T(8,128)(2,1)S(1)} collective-permute-done((bf16[136,3,8,128]{3,2,1,0:T(8,128)(2,1)}, bf16[136,3,8,128]{3,2,1,0:T(8,128)(2,1)S(1)}, u32[]{:S(2)}, u32[]{:S(2)}) %collective-permute-start.1) | collective-permute-done | bytes 835616 | tf_op jit(solution)/shard_map/ppermute | solution.py:95
  32.2 1.0 %copy-done.3 = bf16[136,3,8,128]{3,2,1,0:T(8,128)(2,1)} copy-done((bf16[136,3,8,128]{3,2,1,0:T(8,128)(2,1)}, bf16[136,3,8,128]{3,2,1,0:T(8,128)(2,1)S(1)}, u32[]{:S(2)}) %copy-start.3) | copy-done | bytes 835608
  33.2 7.8 %shard_map.140 = (f32[132,4,8,128]{3,2,1,0:T(8,128)}, f32[132,4,1,128]{3,2,1,0:T(1,128)}) custom-call(f32[132,4,8,128]{3,2,1,0:T(8,128)} %q_ref.3, bf16[136,3,8,128]{3,2,1,0:T(8,128)(2,1)} %copy-done.2, bf16[136,3,8,128]{3,2,1,0:T(8,128)(2,1)} %copy-done.3, bf16[136,3,8,128]{3,2,1,0:T(8,128)(2,1)} %copy-done.2, bf16[136,3,8,128]{3,2,1,0:T(8,128)(2,1)} %copy-done.2, ...), custom_call_target="tpu_custom_call" | custom-call | flops 43253760 | bytes 10813440 | tf_op jit(solution)/shard_map/pallas_call | solution.py:107
  41.0 1.4 %collective-permute-start.2 = (f32[132,4,1,128]{3,2,1,0:T(1,128)}, f32[132,4,1,128]{3,2,1,0:T(1,128)S(1)}, u32[]{:S(2)}, u32[]{:S(2)}) collective-permute-start(f32[132,4,1,128]{3,2,1,0:T(1,128)} %get-tuple-element.12), channel_id=1, source_target_pairs={{1,0},{3,2},{5,4},{7,6},{9,8},{11,10},{13,12},{15,14},{17,16},{19,... | collective-permute-start | bytes 811016 | tf_op jit(solution)/shard_map/ppermute | solution.py:122
  42.4 2.0 %multiply_reduce_fusion = f32[264,8,33]{0,2,1:T(8,128)S(1)} fusion(f32[264,8]{0,1:T(8,128)S(1)} %fusion.66, f32[8,8,33,33]{3,1,2,0:T(8,128)S(1)} %fusion.57, s32[264]{0:T(512)S(1)} %get-tuple-element.31), kind=kOutput, calls=%fused_computation | convolution fusion | flops 221851072 | bytes 567072 | tf_op jit(solution)/shard_map/bm,acmn->bacn/dot_general | solution.py:149
  44.4 1.1 %fusion.4 = bf16[264,264]{0,1:T(8,128)(2,1)S(1)} fusion(f32[264,8,33]{0,2,1:T(8,128)S(1)} %multiply_reduce_fusion, f32[264,8]{0,1:T(8,128)S(1)} %fusion.66, f32[264,33]{0,1:T(8,128)S(1)} %fusion.54), kind=kOutput, calls=%fused_computation.17 | convolution fusion | flops 220936320 | bytes 461472 | tf_op jit(solution)/shard_map/bcn,dc,dn->bd/dot_general | solution.py:151
  45.9 1.2 %multiply_reduce_fusion.1 = (f32[4,8,128]{2,1,0:T(8,128)S(1)}, f32[4,8,128]{2,1,0:T(8,128)S(1)}, f32[132,4,8,128]{3,2,1,0:T(8,128)S(1)}) fusion(f32[132]{0:T(256)S(1)} %get-tuple-element.36, f32[132]{0:T(256)S(1)} %copy-done.11, f32[132,4,1,128]{3,2,1,0:T(1,128)S(1)} %collective-permute-done.2, f32[132,4,7,128]{3,2,1,0:T(8,128)S(1)} %slice.137, ...), kind=kLoop, calls=%fused_computation.6 | loop fusion | flops 4317184 | bytes 6522944 | tf_op jit(solution)/shard_map/reduce_sum | solution.py:244
  47.2 1.6 %collective-permute-start.3 = (f32[2,4,8,128]{3,2,1,0:T(8,128)S(1)}, f32[2,4,8,128]{3,2,1,0:T(8,128)S(1)}, u32[]{:S(2)}, u32[]{:S(2)}) collective-permute-start(f32[2,4,8,128]{3,2,1,0:T(8,128)S(1)} %pad_maximum_fusion.6), channel_id=1, source_target_pairs={{0,2},{2,0},{1,3},{3,1},{4,6},{6,4},{5,7},{7,5},{8,10},{10,8},{9,1... | collective-permute-start | bytes 98312 | tf_op jit(solution)/shard_map/ppermute | solution.py:249
  48.8 2.5 %collective-permute-done.3 = f32[2,4,8,128]{3,2,1,0:T(8,128)S(1)} collective-permute-done((f32[2,4,8,128]{3,2,1,0:T(8,128)S(1)}, f32[2,4,8,128]{3,2,1,0:T(8,128)S(1)}, u32[]{:S(2)}, u32[]{:S(2)}) %collective-permute-start.3) | collective-permute-done | bytes 32800 | tf_op jit(solution)/shard_map/ppermute | solution.py:249
  51.3 0.6 fusion.62
  52.6 0.8 slice_bitcast_fusion.2
  53.4 1.5 %collective-permute-start.4 = (bf16[132,8,128]{2,1,0:T(8,128)(2,1)}, bf16[132,8,128]{2,1,0:T(8,128)(2,1)}, u32[]{:S(2)}, u32[]{:S(2)}) collective-permute-start(bf16[132,8,128]{2,1,0:T(8,128)(2,1)} %get-tuple-element.28), channel_id=1, source_target_pairs={{0,2},{2,0},{1,3},{3,1},{4,6},{6,4},{5,7},{7,5},{8,10},{10,8},{9,1... | collective-permute-start | bytes 811016 | tf_op jit(solution)/shard_map/ppermute | solution.py:194
  55.1 0.8 copy-done.5
  56.6 6.5 %collective-permute-done.4 = bf16[132,8,128]{2,1,0:T(8,128)(2,1)} collective-permute-done((bf16[132,8,128]{2,1,0:T(8,128)(2,1)}, bf16[132,8,128]{2,1,0:T(8,128)(2,1)}, u32[]{:S(2)}, u32[]{:S(2)}) %collective-permute-start.4) | collective-permute-done | bytes 270368 | tf_op jit(solution)/shard_map/ppermute | solution.py:194
  63.0 1.0 %pad.19 = bf16[136,8,128]{2,1,0:T(8,128)(2,1)S(1)} pad(bf16[132,8,128]{2,1,0:T(8,128)(2,1)} %collective-permute-done.4, bf16[]{:T(256)} %constant.76), padding=0_4x0_0x0_0 | pad | bytes 548866
  64.1 0.8 fusion.53
  64.8 0.8 fusion.47
  65.7 0.5 fusion.20
  66.2 0.8 fusion.45
  67.0 0.8 fusion.43
  67.8 0.7 fusion.18
  68.5 0.8 fusion.41
  69.3 0.8 fusion.39
  70.1 0.6 fusion.16
  70.7 0.8 fusion.37
  71.5 0.8 fusion.35
  72.3 0.7 fusion.5
  73.1 1.6 %collective-permute-start.6 = (bf16[132,8,128]{2,1,0:T(8,128)(2,1)S(1)}, bf16[132,8,128]{2,1,0:T(8,128)(2,1)S(1)}, u32[]{:S(2)}, u32[]{:S(2)}) collective-permute-start(bf16[132,8,128]{2,1,0:T(8,128)(2,1)S(1)} %slice.225), channel_id=1, source_target_pairs={{0,2},{2,0},{1,3},{3,1},{4,6},{6,4},{5,7},{7,5},{8,10},{10,8},{9,1... | collective-permute-start | bytes 811016 | tf_op jit(solution)/shard_map/ppermute | solution.py:201
  74.7 0.8 fusion.52
  75.5 0.8 fusion.33
  76.9 0.8 fusion.31
  77.7 0.8 fusion.29
  78.6 0.9 fusion.11
  79.5 0.6 collective-permute-done.6
  80.0 0.8 fusion.27
  80.8 0.8 fusion.25
  81.6 0.6 fusion.9
  82.2 0.8 fusion.23
  83.0 0.8 fusion.21
  83.8 0.7 fusion.6
  84.7 1.6 %collective-permute-start.7 = (bf16[132,8,128]{2,1,0:T(8,128)(2,1)S(1)}, bf16[132,8,128]{2,1,0:T(8,128)(2,1)S(1)}, u32[]{:S(2)}, u32[]{:S(2)}) collective-permute-start(bf16[132,8,128]{2,1,0:T(8,128)(2,1)S(1)} %slice.227), channel_id=1, source_target_pairs={{0,2},{2,0},{1,3},{3,1},{4,6},{6,4},{5,7},{7,5},{8,10},{10,8},{9,1... | collective-permute-start | bytes 811016 | tf_op jit(solution)/shard_map/ppermute | solution.py:201
  86.4 4.8 %collective-permute-done.7 = bf16[132,8,128]{2,1,0:T(8,128)(2,1)S(1)} collective-permute-done((bf16[132,8,128]{2,1,0:T(8,128)(2,1)S(1)}, bf16[132,8,128]{2,1,0:T(8,128)(2,1)S(1)}, u32[]{:S(2)}, u32[]{:S(2)}) %collective-permute-start.7) | collective-permute-done | bytes 270368 | tf_op jit(solution)/shard_map/ppermute | solution.py:201
  91.7 1.8 %fusion.1 = f32[132,4,8,128]{3,2,1,0:T(8,128)} fusion(bf16[132,4,8,128]{3,2,1,0:T(8,128)(2,1)S(1)} %bitcast.128, f32[132,4,8,128]{3,2,1,0:T(8,128)S(1)} %get-tuple-element.19, f32[4,8,128]{2,1,0:T(8,128)S(1)} %compare_convert_fusion, f32[4,8,128]{2,1,0:T(8,128)S(1)} %get-tuple-element.18, f32[132]{0:T(256)S(1)} %get-tuple-element.35), kind=kLoop, calls=%fused_computation.4 | loop fusion | flops 3244032 | bytes 5440016 | tf_op jit(solution)/shard_map/mul | solution.py:261
  (66 shorter events, 4.3 us)
Async XLA Ops:
  0.6 11.3 %copy-start = (bf16[4,33,33]{2,0,1:T(4,128)(2,1)S(1)}, bf16[4,33,33]{2,0,1:T(4,128)(2,1)}, u32[]{:S(2)}) copy-start(bf16[4,33,33]{2,0,1:T(4,128)(2,1)} %param.23) | copy-start | bytes 26140
  2.1 9.3 %copy-start.12 = (s32[264]{0:T(512)S(1)}, s32[264]{0:T(512)}, u32[]{:S(2)}) copy-start(s32[264]{0:T(512)} %param.21) | copy-start | bytes 3172
  2.1 9.5 %copy-start.11 = (f32[132]{0:T(256)S(1)}, f32[132]{0:T(256)}, u32[]{:S(2)}) copy-start(f32[132]{0:T(256)} %param.19) | copy-start | bytes 1588
  2.1 9.5 %copy-start.13 = (f32[132]{0:T(256)S(1)}, f32[132]{0:T(256)}, u32[]{:S(2)}) copy-start(f32[132]{0:T(256)} %param.20) | copy-start | bytes 1588
  2.1 9.5 %copy-start.10 = (f32[132]{0:T(256)S(1)}, f32[132]{0:T(256)}, u32[]{:S(2)}) copy-start(f32[132]{0:T(256)} %param.18) | copy-start | bytes 1588
  2.1 9.8 %copy-start.9 = (s32[8,8]{1,0:T(8,128)S(1)}, s32[8,8]{1,0:T(8,128)}, u32[]{:S(2)}) copy-start(s32[8,8]{1,0:T(8,128)} %param.22) | copy-start | bytes 772
  5.1 23.1 %collective-permute-start = (bf16[136,3,8,128]{3,2,1,0:T(8,128)(2,1)}, bf16[136,3,8,128]{3,2,1,0:T(8,128)(2,1)S(1)}, u32[]{:S(2)}, u32[]{:S(2)}) collective-permute-start(bf16[136,3,8,128]{3,2,1,0:T(8,128)(2,1)} %get-tuple-element.9), channel_id=1, source_target_pairs={{0,4},{4,8},{8,12},{1,5},{5,9},{9,13},{2,6},{6,10},{10,14},{3,7},{... | collective-permute-start | bytes 2506760 | tf_op jit(solution)/shard_map/ppermute | solution.py:95
  10.1 22.2 %collective-permute-start.1 = (bf16[136,3,8,128]{3,2,1,0:T(8,128)(2,1)}, bf16[136,3,8,128]{3,2,1,0:T(8,128)(2,1)S(1)}, u32[]{:S(2)}, u32[]{:S(2)}) collective-permute-start(bf16[136,3,8,128]{3,2,1,0:T(8,128)(2,1)} %get-tuple-element.10), channel_id=1, source_target_pairs={{4,0},{8,4},{12,8},{5,1},{9,5},{13,9},{6,2},{10,6},{14,10},{7,3},{... | collective-permute-start | bytes 2506760 | tf_op jit(solution)/shard_map/ppermute | solution.py:95
  28.2 4.1 %copy-start.2 = (bf16[136,3,8,128]{3,2,1,0:T(8,128)(2,1)}, bf16[136,3,8,128]{3,2,1,0:T(8,128)(2,1)S(1)}, u32[]{:S(2)}) copy-start(bf16[136,3,8,128]{3,2,1,0:T(8,128)(2,1)S(1)} %collective-permute-done.left_ref.refs_0_.refs_1_.refs_2_.refs_3_) | copy-start | bytes 2506756
  32.2 1.0 %copy-start.3 = (bf16[136,3,8,128]{3,2,1,0:T(8,128)(2,1)}, bf16[136,3,8,128]{3,2,1,0:T(8,128)(2,1)S(1)}, u32[]{:S(2)}) copy-start(bf16[136,3,8,128]{3,2,1,0:T(8,128)(2,1)S(1)} %collective-permute-done.1.right_ref.refs_4_.refs_5_.refs_6_.refs_7_) | copy-start | bytes 2506756
  41.0 4.6 %copy-start.4 = (f32[132,4,8,128]{3,2,1,0:T(8,128)S(1)}, f32[132,4,8,128]{3,2,1,0:T(8,128)}, u32[]{:S(2)}) copy-start(f32[132,4,8,128]{3,2,1,0:T(8,128)} %get-tuple-element.11) | copy-start | bytes 6488068
  41.0 4.9 %collective-permute-start.2 = (f32[132,4,1,128]{3,2,1,0:T(1,128)}, f32[132,4,1,128]{3,2,1,0:T(1,128)S(1)}, u32[]{:S(2)}, u32[]{:S(2)}) collective-permute-start(f32[132,4,1,128]{3,2,1,0:T(1,128)} %get-tuple-element.12), channel_id=1, source_target_pairs={{1,0},{3,2},{5,4},{7,6},{9,8},{11,10},{13,12},{15,14},{17,16},{19,... | collective-permute-start | bytes 811016 | tf_op jit(solution)/shard_map/ppermute | solution.py:122
  45.9 2.9 %copy-start.8 = (s32[4,128]{1,0:T(4,128)S(1)}, s32[4,128]{1,0:T(4,128)}, u32[]{:S(2)}) copy-start(s32[4,128]{1,0:T(4,128)} %param.17) | copy-start | bytes 6148
  45.9 5.5 %copy-start.6 = (f32[4,8,128]{2,1,0:T(8,128)S(1)}, f32[4,8,128]{2,1,0:T(8,128)}, u32[]{:S(2)}) copy-start(f32[4,8,128]{2,1,0:T(8,128)} %param.16) | copy-start | bytes 49156
  45.9 5.4 %copy-start.7 = (f32[4,8,128]{2,1,0:T(8,128)S(1)}, f32[4,8,128]{2,1,0:T(8,128)}, u32[]{:S(2)}) copy-start(f32[4,8,128]{2,1,0:T(8,128)} %param.15) | copy-start | bytes 49156
  47.2 4.2 %collective-permute-start.3 = (f32[2,4,8,128]{3,2,1,0:T(8,128)S(1)}, f32[2,4,8,128]{3,2,1,0:T(8,128)S(1)}, u32[]{:S(2)}, u32[]{:S(2)}) collective-permute-start(f32[2,4,8,128]{3,2,1,0:T(8,128)S(1)} %pad_maximum_fusion.6), channel_id=1, source_target_pairs={{0,2},{2,0},{1,3},{3,1},{4,6},{6,4},{5,7},{7,5},{8,10},{10,8},{9,1... | collective-permute-start | bytes 98312 | tf_op jit(solution)/shard_map/ppermute | solution.py:249
  53.4 9.6 %collective-permute-start.4 = (bf16[132,8,128]{2,1,0:T(8,128)(2,1)}, bf16[132,8,128]{2,1,0:T(8,128)(2,1)}, u32[]{:S(2)}, u32[]{:S(2)}) collective-permute-start(bf16[132,8,128]{2,1,0:T(8,128)(2,1)} %get-tuple-element.28), channel_id=1, source_target_pairs={{0,2},{2,0},{1,3},{3,1},{4,6},{6,4},{5,7},{7,5},{8,10},{10,8},{9,1... | collective-permute-start | bytes 811016 | tf_op jit(solution)/shard_map/ppermute | solution.py:194
  55.0 1.0 %copy-start.5 = (bf16[132,8,128]{2,1,0:T(8,128)(2,1)S(1)}, bf16[132,8,128]{2,1,0:T(8,128)(2,1)}, u32[]{:S(2)}) copy-start(bf16[132,8,128]{2,1,0:T(8,128)(2,1)} %get-tuple-element.29) | copy-start | bytes 811012
  56.0 18.7 %collective-permute-start.5 = (bf16[132,8,128]{2,1,0:T(8,128)(2,1)S(1)}, bf16[132,8,128]{2,1,0:T(8,128)(2,1)S(1)}, u32[]{:S(2)}, u32[]{:S(2)}) collective-permute-start(bf16[132,8,128]{2,1,0:T(8,128)(2,1)S(1)} %copy-done.5), channel_id=1, source_target_pairs={{0,2},{2,0},{1,3},{3,1},{4,6},{6,4},{5,7},{7,5},{8,10},{10,8},{9,1... | collective-permute-start | bytes 811016 | tf_op jit(solution)/shard_map/ppermute | solution.py:194
  73.1 6.9 %collective-permute-start.6 = (bf16[132,8,128]{2,1,0:T(8,128)(2,1)S(1)}, bf16[132,8,128]{2,1,0:T(8,128)(2,1)S(1)}, u32[]{:S(2)}, u32[]{:S(2)}) collective-permute-start(bf16[132,8,128]{2,1,0:T(8,128)(2,1)S(1)} %slice.225), channel_id=1, source_target_pairs={{0,2},{2,0},{1,3},{3,1},{4,6},{6,4},{5,7},{7,5},{8,10},{10,8},{9,1... | collective-permute-start | bytes 811016 | tf_op jit(solution)/shard_map/ppermute | solution.py:201
  84.7 6.5 %collective-permute-start.7 = (bf16[132,8,128]{2,1,0:T(8,128)(2,1)S(1)}, bf16[132,8,128]{2,1,0:T(8,128)(2,1)S(1)}, u32[]{:S(2)}, u32[]{:S(2)}) collective-permute-start(bf16[132,8,128]{2,1,0:T(8,128)(2,1)S(1)} %slice.227), channel_id=1, source_target_pairs={{0,2},{2,0},{1,3},{3,1},{4,6},{6,4},{5,7},{7,5},{8,10},{10,8},{9,1... | collective-permute-start | bytes 811016 | tf_op jit(solution)/shard_map/ppermute | solution.py:201
  91.7 1.9 %copy-start.1 = (bf16[4,33,33]{2,0,1:T(4,128)(2,1)S(1)}, bf16[4,33,33]{2,0,1:T(4,128)(2,1)}, u32[]{:S(2)}) copy-start(bf16[4,33,33]{2,0,1:T(4,128)(2,1)} %param.23) | copy-start | bytes 26140

commit v9 on v8

--- a/solution.py
+++ b/solution.py
@@ -115,6 +115,58 @@
         out_specs=(own_spec, pl.BlockSpec((block, width_x, 1, width_y), lambda i: (i, 0, 0, 0))),
         cost_estimate=pl.CostEstimate(flops=80 * cells, bytes_accessed=20 * cells, transcendentals=0),
     )(bin_mass, left, right, *([left] * 4), *([right] * 4), wind_x, wind_y)
+
+def settle_kernel(fall_ref, growth_ref, latent_ref, adv_ref, above_ref, settled_ref, partial_ref):
+    block = adv_ref.shape[0]
+    first = pl.program_id(0) * block
+    levels = adv_ref.shape[2]
+    top = lax.broadcasted_iota(jnp.int32, adv_ref.shape[1:], 1) == levels - 1
+
+    @pl.when(pl.program_id(0) == 0)
+    def _():
+        partial_ref[...] = jnp.zeros_like(partial_ref)
+
+    def one_bin(b, sums):
+        uptake, heating = sums
+        speed = fall_ref[first + b]
+        growth = growth_ref[first + b]
+        latent = latent_ref[first + b]
+        field = adv_ref[b]
+        from_above = jnp.where(
+            top, jnp.broadcast_to(above_ref[b], field.shape), pltpu.roll(field, levels - 1, 1)
+        )
+        settled = (1.0 - speed) * field + speed * from_above
+        settled_ref[b] = settled
+        return uptake + growth * settled, heating + latent * growth * settled
+
+    zeros = jnp.zeros(adv_ref.shape[1:], jnp.float32)
+    uptake, heating = lax.fori_loop(0, block, one_bin, (zeros, zeros))
+    partial_ref[0] += uptake
+    partial_ref[1] += heating
+
+
+def settle_call(advected, above, fall_speed, growth_rate, latent_factor):
+    local_bins, width_x, width_z, width_y = advected.shape
+    block = max(d for d in range(1, 34) if local_bins % d == 0)
+    field_spec = pl.BlockSpec((block, width_x, width_z, width_y), lambda i: (i, 0, 0, 0))
+    scalar_spec = pl.BlockSpec(memory_space=pltpu.SMEM)
+    return pl.pallas_call(
+        settle_kernel,
+        out_shape=(
+            jax.ShapeDtypeStruct(advected.shape, advected.dtype),
+            jax.ShapeDtypeStruct((2, width_x, width_z, width_y), jnp.float32),
+        ),
+        grid=(local_bins // block,),
+        in_specs=[
+            scalar_spec,
+            scalar_spec,
+            scalar_spec,
+            field_spec,
+            pl.BlockSpec((block, width_x, 1, width_y), lambda i: (i, 0, 0, 0)),
+        ],
+        out_specs=(field_spec, pl.BlockSpec((2, width_x, width_z, width_y), lambda i: (0, 0, 0, 0))),
+    )(fall_speed, growth_rate, latent_factor, advected, above)
+
 
 def shifted(block, axis, distance):
     devices = range(lax.axis_size(axis))
@@ -235,14 +287,8 @@
             )
         bottom = section_field[:, :, :1, :]
     rim_above = shifted(bottom, "vert", -1)
-    from_above = jnp.concatenate([section_field[:, :, 1:], rim_above], axis=2)
-    speed = fall_speed[:, None, None, None]
-    settled = (1.0 - speed) * section_field + speed * from_above
     growth = growth_rate[:, None, None, None]
-    partial = (
-        jnp.sum(growth * settled, axis=0),
-        jnp.sum(latent_factor[:, None, None, None] * growth * settled, axis=0),
-    )
+    settled, partial = settle_call(section_field, rim_above, fall_speed, growth_rate, latent_factor)
     bin_devices = lax.axis_size("bins")
     if bin_devices == 2:
         swap = [(0, 1), (1, 0)]

time: 93.9 us -> 99.4 us (1.059)
  Pallas kernels: 10.8 us -> 15.4 us
  other arithmetic: 11.7 us -> 12.8 us
    pallas_call x0 -> x1, Pallas kernels: none -> 4.65 us  [settle_call(): pl.pallas_call(settle_kernel, out_shape=(jax.ShapeDtypeStruct(advected.sh...]
    convert_element_type x1, other arithmetic: 0.37 us -> 1.98 us  [paired_collision(): grown.astype(jnp.bfloat16)]
    reduce_sum x1 -> x0, other arithmetic: 1.25 us -> none  [body(): jnp.sum(latent_factor[:, None, None, None] * growth * settled, axis=0)]
    unnamed x41 -> x37, local copies, waits for them, and re-layouts: 3.28 us -> 3.47 us
  transfers between devices with their start and end apart: 8 -> 8, of which waited for: 6 -> 6; matrix products, arithmetic and copies ran while one was open for 21% -> 18% of each run, Pallas kernels for 0% -> 0%
where the time goes in v9:
time: 99.4 us; the launch traced here: 98.9 us
  waiting for transfers between devices  35 us (35%)
  matrix products  16.4 us (16%)
  Pallas kernels  15.4 us (15%)
  starting transfers between devices  14.4 us (14%)
  other arithmetic  12.8 us (13%)
  local copies, waits for them, and re-layouts  3.94 us (4%)
  between operations  1.09 us (1%)
    ppermute x2, waiting for transfers between devices, advect_kernel_call(): lax.ppermute(message, 'tiles', pairs)  19.9 us
    dot_general x16, matrix products, collide(): jnp.dot(table, iterate.astype(jnp.bfloat16), preferred_element_type=jnp.f...  12.7 us
    pallas_call x1, Pallas kernels, advect_kernel_call(): pl.pallas_call(functools.partial(advect_kernel, section_weights), out_sha...  7.8 us
    ppermute x2, waiting for transfers between devices, paired_collision(): arrived = lax.ppermute(away[:, chunk], 'bins', swap)  6.9 us
    ppermute x2, starting transfers between devices, advect_kernel_call(): lax.ppermute(message, 'tiles', pairs)  6.26 us
    ppermute x2, waiting for transfers between devices, paired_collision(): returned.append(lax.ppermute(change[local_bins:], 'bins', swap))  5.35 us
    pallas_call x1, Pallas kernels, settle_call(): pl.pallas_call(settle_kernel, out_shape=(jax.ShapeDtypeStruct(advected.sh...  4.65 us
    add x6, other arithmetic, collide(): iterate + collision_rate * products[all_bins:] * products[:all_bins]  3.85 us
  transfers between devices with their start and end apart: 8, of which 6 were waited for; matrix products, arithmetic and copies ran while one was open for 18% of the time, Pallas kernels for 0%

profile of v9, /device:TPU:0, one launch (start us, length us, event | category | flops | bytes accessed | tf_op | source)
XLA Modules:
  0.0 98.9 jit_solution(7233636431982578302)
XLA Ops:
  0.7 1.4 %compare_select_fusion = (f32[4,8,128]{2,1,0:T(8,128)}, f32[4,8,128]{2,1,0:T(8,128)}) fusion(f32[4,8,128]{2,1,0:T(8,128)} %param.14, s32[4,128]{1,0:T(4,128)} %param.17, s32[8]{0:T(128)S(1)} %iota_add_fusion, f32[4,8,128]{2,1,0:T(8,128)} %param.13), kind=kLoop, calls=%fused_computation.116 | loop fusion | flops 12288 | bytes 67616 | tf_op jit(solution)/shard_map/mul | solution.py:277
  2.1 2.9 %shard_map.139 = (bf16[136,3,8,128]{3,2,1,0:T(8,128)(2,1)}, bf16[136,3,8,128]{3,2,1,0:T(8,128)(2,1)}) custom-call(f32[132,4,8,128]{3,2,1,0:T(8,128)} %q_ref.3, f32[4,8,128]{2,1,0:T(8,128)} %get-tuple-element.35.wx_ref.refs_8_, f32[4,8,128]{2,1,0:T(8,128)} %get-tuple-element.34.wy_ref.refs_9_), custom_call_target="tpu_custom_call" | custom-call | tf_op jit(solution)/shard_map/pallas_call | solution.py:48
  5.1 5.0 %collective-permute-start = (bf16[136,3,8,128]{3,2,1,0:T(8,128)(2,1)}, bf16[136,3,8,128]{3,2,1,0:T(8,128)(2,1)S(1)}, u32[]{:S(2)}, u32[]{:S(2)}) collective-permute-start(bf16[136,3,8,128]{3,2,1,0:T(8,128)(2,1)} %get-tuple-element.11), channel_id=1, source_target_pairs={{0,4},{4,8},{8,12},{1,5},{5,9},{9,13},{2,6},{6,10},{10,14},{3,7},{... | collective-permute-start | bytes 2506760 | tf_op jit(solution)/shard_map/ppermute | solution.py:95
  10.0 1.3 %collective-permute-start.1 = (bf16[136,3,8,128]{3,2,1,0:T(8,128)(2,1)}, bf16[136,3,8,128]{3,2,1,0:T(8,128)(2,1)S(1)}, u32[]{:S(2)}, u32[]{:S(2)}) collective-permute-start(bf16[136,3,8,128]{3,2,1,0:T(8,128)(2,1)} %get-tuple-element.12), channel_id=1, source_target_pairs={{4,0},{8,4},{12,8},{5,1},{9,5},{13,9},{6,2},{10,6},{14,10},{7,3},{... | collective-permute-start | bytes 2506760 | tf_op jit(solution)/shard_map/ppermute | solution.py:95
  12.3 15.9 %collective-permute-done.left_ref.refs_0_.refs_1_.refs_2_.refs_3_ = bf16[136,3,8,128]{3,2,1,0:T(8,128)(2,1)S(1)} collective-permute-done((bf16[136,3,8,128]{3,2,1,0:T(8,128)(2,1)}, bf16[136,3,8,128]{3,2,1,0:T(8,128)(2,1)S(1)}, u32[]{:S(2)}, u32[]{:S(2)}) %collective-permute-start) | collective-permute-done | bytes 835616 | tf_op jit(solution)/shard_map/ppermute | solution.py:95
  28.1 4.1 %collective-permute-done.1.right_ref.refs_4_.refs_5_.refs_6_.refs_7_ = bf16[136,3,8,128]{3,2,1,0:T(8,128)(2,1)S(1)} collective-permute-done((bf16[136,3,8,128]{3,2,1,0:T(8,128)(2,1)}, bf16[136,3,8,128]{3,2,1,0:T(8,128)(2,1)S(1)}, u32[]{:S(2)}, u32[]{:S(2)}) %collective-permute-start.1) | collective-permute-done | bytes 835616 | tf_op jit(solution)/shard_map/ppermute | solution.py:95
  32.2 0.9 copy-done.3
  33.1 7.8 %shard_map.140 = (f32[132,4,8,128]{3,2,1,0:T(8,128)}, f32[132,4,1,128]{3,2,1,0:T(1,128)}) custom-call(f32[132,4,8,128]{3,2,1,0:T(8,128)} %q_ref.3, bf16[136,3,8,128]{3,2,1,0:T(8,128)(2,1)} %copy-done.2, bf16[136,3,8,128]{3,2,1,0:T(8,128)(2,1)} %copy-done.3, bf16[136,3,8,128]{3,2,1,0:T(8,128)(2,1)} %copy-done.2, bf16[136,3,8,128]{3,2,1,0:T(8,128)(2,1)} %copy-done.2, ...), custom_call_target="tpu_custom_call" | custom-call | flops 43253760 | bytes 10813440 | tf_op jit(solution)/shard_map/pallas_call | solution.py:107
  40.9 1.3 %collective-permute-start.2 = (f32[132,4,1,128]{3,2,1,0:T(1,128)}, f32[132,4,1,128]{3,2,1,0:T(1,128)S(1)}, u32[]{:S(2)}, u32[]{:S(2)}) collective-permute-start(f32[132,4,1,128]{3,2,1,0:T(1,128)} %get-tuple-element.14), channel_id=1, source_target_pairs={{1,0},{3,2},{5,4},{7,6},{9,8},{11,10},{13,12},{15,14},{17,16},{19,... | collective-permute-start | bytes 811016 | tf_op jit(solution)/shard_map/ppermute | solution.py:174
  42.2 2.0 %multiply_reduce_fusion = f32[264,8,33]{0,2,1:T(8,128)S(1)} fusion(f32[264,8]{0,1:T(8,128)S(1)} %fusion.64, f32[8,8,33,33]{3,1,2,0:T(8,128)S(1)} %fusion.56, s32[264]{0:T(512)S(1)} %get-tuple-element.32), kind=kOutput, calls=%fused_computation | convolution fusion | flops 221851072 | bytes 567072 | tf_op jit(solution)/shard_map/bm,acmn->bacn/dot_general | solution.py:201
  44.2 1.1 %fusion.3 = bf16[264,264]{0,1:T(8,128)(2,1)S(1)} fusion(f32[264,8,33]{0,2,1:T(8,128)S(1)} %multiply_reduce_fusion, f32[264,8]{0,1:T(8,128)S(1)} %fusion.64, f32[264,33]{0,1:T(8,128)S(1)} %fusion.53), kind=kOutput, calls=%fused_computation.13 | convolution fusion | flops 220936320 | bytes 461472 | tf_op jit(solution)/shard_map/bcn,dc,dn->bd/dot_general | solution.py:203
  45.4 0.7 copy-done.5
  46.1 4.6 %shard_map.141 = (f32[132,4,8,128]{3,2,1,0:T(8,128)}, f32[2,4,8,128]{3,2,1,0:T(8,128)}) custom-call(f32[132]{0:T(256)} %fall_ref.1, f32[132]{0:T(256)} %growth_ref.1, f32[132]{0:T(256)} %latent_ref.1, f32[132,4,8,128]{3,2,1,0:T(8,128)} %get-tuple-element.13.adv_ref, f32[132,4,1,128]{3,2,1,0:T(1,128)} %copy-done.5), custom_call_target="tpu_custom_call" | custom-call | tf_op jit(solution)/shard_map/pallas_call | solution.py:153
  50.7 1.5 %collective-permute-start.3 = (f32[2,4,8,128]{3,2,1,0:T(8,128)}, f32[2,4,8,128]{3,2,1,0:T(8,128)S(1)}, u32[]{:S(2)}, u32[]{:S(2)}) collective-permute-start(f32[2,4,8,128]{3,2,1,0:T(8,128)} %get-tuple-element.16), channel_id=1, source_target_pairs={{0,2},{2,0},{1,3},{3,1},{4,6},{6,4},{5,7},{7,5},{8,10},{10,8},{9,1... | collective-permute-start | bytes 98312 | tf_op jit(solution)/shard_map/ppermute | solution.py:295
  52.2 2.8 %collective-permute-done.3 = f32[2,4,8,128]{3,2,1,0:T(8,128)S(1)} collective-permute-done((f32[2,4,8,128]{3,2,1,0:T(8,128)}, f32[2,4,8,128]{3,2,1,0:T(8,128)S(1)}, u32[]{:S(2)}, u32[]{:S(2)}) %collective-permute-start.3) | collective-permute-done | bytes 32800 | tf_op jit(solution)/shard_map/ppermute | solution.py:295
  55.1 1.4 %fusion.61 = (f32[4,8,128]{2,1,0:T(8,128)}, f32[4,8,128]{2,1,0:T(8,128)S(1)}, f32[4,8,128]{2,1,0:T(8,128)}) fusion(f32[4,8,128]{2,1,0:T(8,128)S(1)} %copy-done.6, f32[2,4,8,128]{3,2,1,0:T(8,128)S(1)} %collective-permute-done.3, f32[2,4,8,128]{3,2,1,0:T(8,128)} %get-tuple-element.16, f32[4,8,128]{2,1,0:T(8,128)S(1)} %copy-done.7), kind=kLoop, calls=%fused_computation.121 | loop fusion | flops 36864 | bytes 147456 | tf_op jit(solution)/shard_map/add | solution.py:301
  56.4 2.0 %fusion.1 = bf16[132,4,8,128]{3,2,1,0:T(8,128)(2,1)S(1)} fusion(f32[132,4,8,128]{3,2,1,0:T(8,128)} %get-tuple-element.15, f32[4,8,128]{2,1,0:T(8,128)S(1)} %get-tuple-element.20, f32[132]{0:T(256)S(1)} %broadcast_multiply_fusion), kind=kLoop, calls=%fused_computation.4 | loop fusion | flops 2162688 | bytes 3260944 | tf_op jit(solution)/shard_map/convert_element_type | solution.py:241
  58.7 1.6 %collective-permute-start.4 = (bf16[132,8,128]{2,1,0:T(8,128)(2,1)S(1)}, bf16[132,8,128]{2,1,0:T(8,128)(2,1)S(1)}, u32[]{:S(2)}, u32[]{:S(2)}) collective-permute-start(bf16[132,8,128]{2,1,0:T(8,128)(2,1)S(1)} %get-tuple-element.29), channel_id=1, source_target_pairs={{0,2},{2,0},{1,3},{3,1},{4,6},{6,4},{5,7},{7,5},{8,10},{10,8},{9,1... | collective-permute-start | bytes 811016 | tf_op jit(solution)/shard_map/ppermute | solution.py:246
  60.5 0.6 collective-permute-start.5
  61.2 6.9 %collective-permute-done.4 = bf16[132,8,128]{2,1,0:T(8,128)(2,1)S(1)} collective-permute-done((bf16[132,8,128]{2,1,0:T(8,128)(2,1)S(1)}, bf16[132,8,128]{2,1,0:T(8,128)(2,1)S(1)}, u32[]{:S(2)}, u32[]{:S(2)}) %collective-permute-start.4) | collective-permute-done | bytes 270368 | tf_op jit(solution)/shard_map/ppermute | solution.py:246
  68.1 0.8 fusion.52
  68.9 0.8 fusion.46
  70.3 0.8 fusion.44
  71.1 0.8 fusion.42
  71.9 0.7 fusion.17
  72.6 0.8 fusion.40
  73.3 0.8 fusion.38
  74.2 0.6 fusion.15
  74.8 0.8 fusion.36
  75.5 0.8 fusion.34
  76.3 0.7 fusion.4
  77.2 1.6 %collective-permute-start.6 = (bf16[132,8,128]{2,1,0:T(8,128)(2,1)S(1)}, bf16[132,8,128]{2,1,0:T(8,128)(2,1)S(1)}, u32[]{:S(2)}, u32[]{:S(2)}) collective-permute-start(bf16[132,8,128]{2,1,0:T(8,128)(2,1)S(1)} %slice.229), channel_id=1, source_target_pairs={{0,2},{2,0},{1,3},{3,1},{4,6},{6,4},{5,7},{7,5},{8,10},{10,8},{9,1... | collective-permute-start | bytes 811016 | tf_op jit(solution)/shard_map/ppermute | solution.py:253
  78.8 0.8 fusion.51
  79.6 0.8 fusion.32
  81.0 0.8 fusion.30
  81.8 0.8 fusion.28
  82.6 0.9 fusion.10
  83.5 0.5 collective-permute-done.6
  84.1 0.8 fusion.26
  84.9 0.8 fusion.24
  85.7 0.6 fusion.8
  86.3 0.8 fusion.22
  87.0 0.8 fusion.20
  87.9 0.7 fusion.5
  88.8 1.6 %collective-permute-start.7 = (bf16[132,8,128]{2,1,0:T(8,128)(2,1)S(1)}, bf16[132,8,128]{2,1,0:T(8,128)(2,1)S(1)}, u32[]{:S(2)}, u32[]{:S(2)}) collective-permute-start(bf16[132,8,128]{2,1,0:T(8,128)(2,1)S(1)} %slice.231), channel_id=1, source_target_pairs={{0,2},{2,0},{1,3},{3,1},{4,6},{6,4},{5,7},{7,5},{8,10},{10,8},{9,1... | collective-permute-start | bytes 811016 | tf_op jit(solution)/shard_map/ppermute | solution.py:253
  90.5 4.8 %collective-permute-done.7 = bf16[132,8,128]{2,1,0:T(8,128)(2,1)S(1)} collective-permute-done((bf16[132,8,128]{2,1,0:T(8,128)(2,1)S(1)}, bf16[132,8,128]{2,1,0:T(8,128)(2,1)S(1)}, u32[]{:S(2)}, u32[]{:S(2)}) %collective-permute-start.7) | collective-permute-done | bytes 270368 | tf_op jit(solution)/shard_map/ppermute | solution.py:253
  95.8 1.3 %copy-done.4 = f32[132,4,8,128]{3,2,1,0:T(8,128)S(1)} copy-done((f32[132,4,8,128]{3,2,1,0:T(8,128)S(1)}, f32[132,4,8,128]{3,2,1,0:T(8,128)}, u32[]{:S(2)}) %copy-start.4) | copy-done | bytes 2162712
  97.1 1.8 %fusion = f32[132,4,8,128]{3,2,1,0:T(8,128)} fusion(bf16[132,4,8,128]{3,2,1,0:T(8,128)(2,1)S(1)} %bitcast.120, f32[132,4,8,128]{3,2,1,0:T(8,128)S(1)} %copy-done.4, f32[4,8,128]{2,1,0:T(8,128)S(1)} %compare_convert_fusion, f32[4,8,128]{2,1,0:T(8,128)S(1)} %get-tuple-element.20, f32[132]{0:T(256)S(1)} %broadcast_multiply_fusion), kind=kLoop, calls=%fused_computation.2 | loop fusion | flops 3244032 | bytes 5440016 | tf_op jit(solution)/shard_map/mul | solution.py:307
  (59 shorter events, 3.7 us)
Async XLA Ops:
  0.6 11.3 %copy-start = (bf16[4,33,33]{2,0,1:T(4,128)(2,1)S(1)}, bf16[4,33,33]{2,0,1:T(4,128)(2,1)}, u32[]{:S(2)}) copy-start(bf16[4,33,33]{2,0,1:T(4,128)(2,1)} %param.23) | copy-start | bytes 26140
  2.1 9.2 %copy-start.8 = (s32[4,128]{1,0:T(4,128)S(1)}, s32[4,128]{1,0:T(4,128)}, u32[]{:S(2)}) copy-start(s32[4,128]{1,0:T(4,128)} %param.17) | copy-start | bytes 6148
  2.1 9.3 %copy-start.11 = (s32[264]{0:T(512)S(1)}, s32[264]{0:T(512)}, u32[]{:S(2)}) copy-start(s32[264]{0:T(512)} %param.21) | copy-start | bytes 3172
  2.1 9.8 %copy-start.10 = (s32[8,8]{1,0:T(8,128)S(1)}, s32[8,8]{1,0:T(8,128)}, u32[]{:S(2)}) copy-start(s32[8,8]{1,0:T(8,128)} %param.22) | copy-start | bytes 772
  5.1 23.1 %collective-permute-start = (bf16[136,3,8,128]{3,2,1,0:T(8,128)(2,1)}, bf16[136,3,8,128]{3,2,1,0:T(8,128)(2,1)S(1)}, u32[]{:S(2)}, u32[]{:S(2)}) collective-permute-start(bf16[136,3,8,128]{3,2,1,0:T(8,128)(2,1)} %get-tuple-element.11), channel_id=1, source_target_pairs={{0,4},{4,8},{8,12},{1,5},{5,9},{9,13},{2,6},{6,10},{10,14},{3,7},{... | collective-permute-start | bytes 2506760 | tf_op jit(solution)/shard_map/ppermute | solution.py:95
  10.0 22.2 %collective-permute-start.1 = (bf16[136,3,8,128]{3,2,1,0:T(8,128)(2,1)}, bf16[136,3,8,128]{3,2,1,0:T(8,128)(2,1)S(1)}, u32[]{:S(2)}, u32[]{:S(2)}) collective-permute-start(bf16[136,3,8,128]{3,2,1,0:T(8,128)(2,1)} %get-tuple-element.12), channel_id=1, source_target_pairs={{4,0},{8,4},{12,8},{5,1},{9,5},{13,9},{6,2},{10,6},{14,10},{7,3},{... | collective-permute-start | bytes 2506760 | tf_op jit(solution)/shard_map/ppermute | solution.py:95
  28.1 4.1 %copy-start.2 = (bf16[136,3,8,128]{3,2,1,0:T(8,128)(2,1)}, bf16[136,3,8,128]{3,2,1,0:T(8,128)(2,1)S(1)}, u32[]{:S(2)}) copy-start(bf16[136,3,8,128]{3,2,1,0:T(8,128)(2,1)S(1)} %collective-permute-done.left_ref.refs_0_.refs_1_.refs_2_.refs_3_) | copy-start | bytes 2506756
  32.2 0.9 copy-start.3
  40.9 4.4 %collective-permute-start.2 = (f32[132,4,1,128]{3,2,1,0:T(1,128)}, f32[132,4,1,128]{3,2,1,0:T(1,128)S(1)}, u32[]{:S(2)}, u32[]{:S(2)}) collective-permute-start(f32[132,4,1,128]{3,2,1,0:T(1,128)} %get-tuple-element.14), channel_id=1, source_target_pairs={{1,0},{3,2},{5,4},{7,6},{9,8},{11,10},{13,12},{15,14},{17,16},{19,... | collective-permute-start | bytes 811016 | tf_op jit(solution)/shard_map/ppermute | solution.py:174
  45.4 0.7 copy-start.5
  46.1 6.2 %copy-start.9 = (f32[132]{0:T(256)S(1)}, f32[132]{0:T(256)}, u32[]{:S(2)}) copy-start(f32[132]{0:T(256)} %growth_ref.1) | copy-start | bytes 1588
  46.1 9.0 %copy-start.6 = (f32[4,8,128]{2,1,0:T(8,128)S(1)}, f32[4,8,128]{2,1,0:T(8,128)}, u32[]{:S(2)}) copy-start(f32[4,8,128]{2,1,0:T(8,128)} %param.16) | copy-start | bytes 49156
  46.1 9.0 %copy-start.7 = (f32[4,8,128]{2,1,0:T(8,128)S(1)}, f32[4,8,128]{2,1,0:T(8,128)}, u32[]{:S(2)}) copy-start(f32[4,8,128]{2,1,0:T(8,128)} %param.15) | copy-start | bytes 49156
  50.7 4.3 %collective-permute-start.3 = (f32[2,4,8,128]{3,2,1,0:T(8,128)}, f32[2,4,8,128]{3,2,1,0:T(8,128)S(1)}, u32[]{:S(2)}, u32[]{:S(2)}) collective-permute-start(f32[2,4,8,128]{3,2,1,0:T(8,128)} %get-tuple-element.16), channel_id=1, source_target_pairs={{0,2},{2,0},{1,3},{3,1},{4,6},{6,4},{5,7},{7,5},{8,10},{10,8},{9,1... | collective-permute-start | bytes 98312 | tf_op jit(solution)/shard_map/ppermute | solution.py:295
  58.7 9.4 %collective-permute-start.4 = (bf16[132,8,128]{2,1,0:T(8,128)(2,1)S(1)}, bf16[132,8,128]{2,1,0:T(8,128)(2,1)S(1)}, u32[]{:S(2)}, u32[]{:S(2)}) collective-permute-start(bf16[132,8,128]{2,1,0:T(8,128)(2,1)S(1)} %get-tuple-element.29), channel_id=1, source_target_pairs={{0,2},{2,0},{1,3},{3,1},{4,6},{6,4},{5,7},{7,5},{8,10},{10,8},{9,1... | collective-permute-start | bytes 811016 | tf_op jit(solution)/shard_map/ppermute | solution.py:246
  60.5 18.3 %collective-permute-start.5 = (bf16[132,8,128]{2,1,0:T(8,128)(2,1)S(1)}, bf16[132,8,128]{2,1,0:T(8,128)(2,1)S(1)}, u32[]{:S(2)}, u32[]{:S(2)}) collective-permute-start(bf16[132,8,128]{2,1,0:T(8,128)(2,1)S(1)} %get-tuple-element.30), channel_id=1, source_target_pairs={{0,2},{2,0},{1,3},{3,1},{4,6},{6,4},{5,7},{7,5},{8,10},{10,8},{9,1... | collective-permute-start | bytes 811016 | tf_op jit(solution)/shard_map/ppermute | solution.py:246
  77.2 6.9 %collective-permute-start.6 = (bf16[132,8,128]{2,1,0:T(8,128)(2,1)S(1)}, bf16[132,8,128]{2,1,0:T(8,128)(2,1)S(1)}, u32[]{:S(2)}, u32[]{:S(2)}) collective-permute-start(bf16[132,8,128]{2,1,0:T(8,128)(2,1)S(1)} %slice.229), channel_id=1, source_target_pairs={{0,2},{2,0},{1,3},{3,1},{4,6},{6,4},{5,7},{7,5},{8,10},{10,8},{9,1... | collective-permute-start | bytes 811016 | tf_op jit(solution)/shard_map/ppermute | solution.py:253
  88.8 6.5 %collective-permute-start.7 = (bf16[132,8,128]{2,1,0:T(8,128)(2,1)S(1)}, bf16[132,8,128]{2,1,0:T(8,128)(2,1)S(1)}, u32[]{:S(2)}, u32[]{:S(2)}) collective-permute-start(bf16[132,8,128]{2,1,0:T(8,128)(2,1)S(1)} %slice.231), channel_id=1, source_target_pairs={{0,2},{2,0},{1,3},{3,1},{4,6},{6,4},{5,7},{7,5},{8,10},{10,8},{9,1... | collective-permute-start | bytes 811016 | tf_op jit(solution)/shard_map/ppermute | solution.py:253
  95.5 1.6 %copy-start.4 = (f32[132,4,8,128]{3,2,1,0:T(8,128)S(1)}, f32[132,4,8,128]{3,2,1,0:T(8,128)}, u32[]{:S(2)}) copy-start(f32[132,4,8,128]{3,2,1,0:T(8,128)} %get-tuple-element.15) | copy-start | bytes 6488068
  97.1 1.8 %copy-start.1 = (bf16[4,33,33]{2,0,1:T(4,128)(2,1)S(1)}, bf16[4,33,33]{2,0,1:T(4,128)(2,1)}, u32[]{:S(2)}) copy-start(bf16[4,33,33]{2,0,1:T(4,128)(2,1)} %param.23) | copy-start | bytes 26140

commit v10 on v8

--- a/solution.py
+++ b/solution.py
@@ -84,7 +84,7 @@
     bottom_ref[...] = section[:, :, :1]
 
 
-def advect_kernel_call(bin_mass, wind_x, wind_y, section_weights):
+def advect_kernel_call(bin_mass, wind_x, wind_y, section_weights, tie):
     local_bins, width_x, width_z, width_y = bin_mass.shape
     depth = len(section_weights)
     tiles = lax.axis_size("tiles")
@@ -95,6 +95,7 @@
         lax.ppermute(message, "tiles", pairs)
         for message, pairs in zip(rims(bin_mass, wind_x, wind_y, depth), (up, down))
     )
+    left, tie = lax.optimization_barrier((left, tie))
     block = max(d for d in range(1, 34) if local_bins % d == 0)
     rim_spec = pl.BlockSpec((block, depth, width_z, width_y), lambda i: (i, 0, 0, 0))
     row_specs = [
@@ -104,7 +105,7 @@
     own_spec = pl.BlockSpec((block, width_x, width_z, width_y), lambda i: (i, 0, 0, 0))
     wind_spec = pl.BlockSpec(wind_x.shape, lambda i: (0, 0, 0))
     cells = local_bins * width_x * width_z * width_y
-    return pl.pallas_call(
+    return tie, pl.pallas_call(
         functools.partial(advect_kernel, section_weights),
         out_shape=(
             jax.ShapeDtypeStruct(bin_mass.shape, bin_mass.dtype),
@@ -178,14 +179,19 @@
     return change.reshape(local_bins, width_x, width_z, width_y).astype(jnp.float32)
 
 
-def paired_collision(grown, bin_order, kernel_index, collision_kernels):
+def paired_table(bin_order, kernel_index, collision_kernels):
+    local_bins = bin_order.shape[0] // 2
+    me = lax.axis_index("bins")
+    order = lax.dynamic_slice_in_dim(
+        jnp.concatenate([bin_order, bin_order]), me * local_bins, 2 * local_bins
+    )
+    return coupling_table(order, kernel_index, collision_kernels)
+
+
+def paired_collision(grown, table):
     local_bins, width_x, width_z, width_y = grown.shape
     swap = [(0, 1), (1, 0)]
     me = lax.axis_index("bins")
-    order = lax.dynamic_slice_in_dim(
-        jnp.concatenate([bin_order, bin_order]), me * local_bins, 2 * local_bins
-    )
-    table = coupling_table(order, kernel_index, collision_kernels)
     halves = grown.astype(jnp.bfloat16).reshape(local_bins, 2, width_x // 2, width_z, width_y)
     own = lax.dynamic_index_in_dim(halves, me, axis=1, keepdims=False)
     away = lax.dynamic_index_in_dim(halves, 1 - me, axis=1, keepdims=False)
@@ -203,6 +209,7 @@
     pair = jnp.stack([jnp.stack(kept, axis=1), jnp.stack(returned, axis=1)], axis=1)
     pair = jnp.where(me == 0, pair, pair[:, ::-1])
     return pair.reshape(local_bins, width_x, width_z, width_y).astype(jnp.float32)
+
 
 def body(
     bin_mass,
@@ -224,8 +231,12 @@
     wind_x = wind_east * open_cells
     wind_y = wind_north * open_cells
     section_weights = (1.0 / 3.0, 0.5, 1.0)
+    paired = lax.axis_size("bins") == 2 and width_x % 2 == 0
+    table = paired_table(bin_order, kernel_index, collision_kernels) if paired else None
     if width_x >= len(section_weights):
-        section_field, bottom = advect_kernel_call(bin_mass, wind_x, wind_y, section_weights)
+        table, (section_field, bottom) = advect_kernel_call(
+            bin_mass, wind_x, wind_y, section_weights, table
+        )
     else:
         section_field = bin_mass
         for weight_now in section_weights:
@@ -254,8 +265,8 @@
     grown = settled * (1.0 + growth_gain * growth * midway)
     temp_next = potential_temp + heating_gain * midway * heating
     vapor_next = supersaturation * jnp.exp(-condense_rate * uptake)
-    if bin_devices == 2 and width_x % 2 == 0:
-        change = paired_collision(grown, bin_order, kernel_index, collision_kernels)
+    if paired:
+        change = paired_collision(grown, table)
     else:
         change = spread_collision(grown, bin_order, kernel_index, collision_kernels)
     mass_next = (grown + change) * open_cells

time: 93.9 us -> 91.6 us (0.976)
  waiting for transfers between devices: 34.3 us -> 31.4 us
    ppermute x2, waiting for transfers between devices: 19.9 us -> 16.7 us  [advect_kernel_call(): lax.ppermute(message, 'tiles', pairs)]
    slice x1, local copies, waits for them, and re-layouts: 0.26 us -> 2.02 us  [body(): from_above = jnp.concatenate([section_field[:, :, 1:], rim_above], axis=2)]
    unnamed x41, local copies, waits for them, and re-layouts: 3.28 us -> 2.34 us
  transfers between devices with their start and end apart: 8 -> 8, of which waited for: 6 -> 7; matrix products, arithmetic and copies ran while one was open for 21% -> 22% of each run, Pallas kernels for 0% -> 0%
where the time goes in v10:
time: 91.6 us; the launch traced here: 91.3 us
  waiting for transfers between devices  31.4 us (34%)
  matrix products  16.4 us (18%)
  starting transfers between devices  14.2 us (16%)
  other arithmetic  11.7 us (13%)
  Pallas kernels  10.8 us (12%)
  local copies, waits for them, and re-layouts  5.61 us (6%)
  between operations  1.17 us (1%)
    ppermute x2, waiting for transfers between devices, advect_kernel_call(): lax.ppermute(message, 'tiles', pairs)  16.7 us
    dot_general x16, matrix products, collide(): jnp.dot(table, iterate.astype(jnp.bfloat16), preferred_element_type=jnp.f...  12.7 us
    pallas_call x1, Pallas kernels, advect_kernel_call(): pl.pallas_call(functools.partial(advect_kernel, section_weights), out_sha...  7.8 us
    ppermute x2, waiting for transfers between devices, paired_collision(): arrived = lax.ppermute(away[:, chunk], 'bins', swap)  6.41 us
    ppermute x2, starting transfers between devices, advect_kernel_call(): lax.ppermute(message, 'tiles', pairs)  6.26 us
    ppermute x2, waiting for transfers between devices, paired_collision(): returned.append(lax.ppermute(change[local_bins:], 'bins', swap))  5.41 us
    add x6, other arithmetic, collide(): iterate + collision_rate * products[all_bins:] * products[:all_bins]  3.85 us
    ppermute x2, starting transfers between devices, paired_collision(): returned.append(lax.ppermute(change[local_bins:], 'bins', swap))  3.09 us
  transfers between devices with their start and end apart: 8, of which 7 were waited for; matrix products, arithmetic and copies ran while one was open for 22% of the time, Pallas kernels for 0%

profile of v10, /device:TPU:0, one launch (start us, length us, event | category | flops | bytes accessed | tf_op | source)
XLA Modules:
  0.0 91.3 jit_solution(16732587760736670704)
XLA Ops:
  0.7 1.4 %compare_select_fusion = (f32[4,8,128]{2,1,0:T(8,128)}, f32[4,8,128]{2,1,0:T(8,128)}) fusion(f32[4,8,128]{2,1,0:T(8,128)} %param.14, s32[4,128]{1,0:T(4,128)} %param.17, s32[8]{0:T(128)S(1)} %iota_add_fusion, f32[4,8,128]{2,1,0:T(8,128)} %param.13), kind=kLoop, calls=%fused_computation.121 | loop fusion | flops 12288 | bytes 67616 | tf_op jit(solution)/shard_map/mul | solution.py:232
  2.1 3.0 %shard_map.139 = (bf16[136,3,8,128]{3,2,1,0:T(8,128)(2,1)}, bf16[136,3,8,128]{3,2,1,0:T(8,128)(2,1)}) custom-call(f32[132,4,8,128]{3,2,1,0:T(8,128)} %q_ref.3, f32[4,8,128]{2,1,0:T(8,128)} %get-tuple-element.38.wx_ref.refs_8_, f32[4,8,128]{2,1,0:T(8,128)} %get-tuple-element.37.wy_ref.refs_9_), custom_call_target="tpu_custom_call" | custom-call | tf_op jit(solution)/shard_map/pallas_call | solution.py:48
  5.1 5.0 %collective-permute-start = (bf16[136,3,8,128]{3,2,1,0:T(8,128)(2,1)}, bf16[136,3,8,128]{3,2,1,0:T(8,128)(2,1)S(1)}, u32[]{:S(2)}, u32[]{:S(2)}) collective-permute-start(bf16[136,3,8,128]{3,2,1,0:T(8,128)(2,1)} %get-tuple-element.11), channel_id=1, source_target_pairs={{0,4},{4,8},{8,12},{1,5},{5,9},{9,13},{2,6},{6,10},{10,14},{3,7},{... | collective-permute-start | bytes 2506760 | tf_op jit(solution)/shard_map/ppermute | solution.py:95
  10.0 1.3 %collective-permute-start.1 = (bf16[136,3,8,128]{3,2,1,0:T(8,128)(2,1)}, bf16[136,3,8,128]{3,2,1,0:T(8,128)(2,1)S(1)}, u32[]{:S(2)}, u32[]{:S(2)}) collective-permute-start(bf16[136,3,8,128]{3,2,1,0:T(8,128)(2,1)} %get-tuple-element.13), channel_id=1, source_target_pairs={{4,0},{8,4},{12,8},{5,1},{9,5},{13,9},{6,2},{10,6},{14,10},{7,3},{... | collective-permute-start | bytes 2506760 | tf_op jit(solution)/shard_map/ppermute | solution.py:95
  11.9 2.0 %multiply_reduce_fusion = f32[264,8,33]{0,2,1:T(8,128)S(1)} fusion(f32[264,8]{0,1:T(8,128)S(1)} %fusion.66, f32[8,8,33,33]{3,1,2,0:T(8,128)S(1)} %fusion.57, s32[264]{0:T(512)S(1)} %get-tuple-element.35), kind=kOutput, calls=%fused_computation | convolution fusion | flops 221851072 | bytes 567072 | tf_op jit(solution)/shard_map/bm,acmn->bacn/dot_general | solution.py:150
  14.2 1.1 %fusion.4 = bf16[264,264]{0,1:T(8,128)(2,1)S(1)} fusion(f32[264,8,33]{0,2,1:T(8,128)S(1)} %multiply_reduce_fusion, f32[264,8]{0,1:T(8,128)S(1)} %fusion.66, f32[264,33]{0,1:T(8,128)S(1)} %fusion.54), kind=kOutput, calls=%fused_computation.17 | convolution fusion | flops 220936320 | bytes 461472 | tf_op jit(solution)/shard_map/bcn,dc,dn->bd/dot_general | solution.py:152
  15.5 12.6 %collective-permute-done.left_ref.refs_0_.refs_1_.refs_2_.refs_3_ = bf16[136,3,8,128]{3,2,1,0:T(8,128)(2,1)S(1)} collective-permute-done((bf16[136,3,8,128]{3,2,1,0:T(8,128)(2,1)}, bf16[136,3,8,128]{3,2,1,0:T(8,128)(2,1)S(1)}, u32[]{:S(2)}, u32[]{:S(2)}) %collective-permute-start) | collective-permute-done | bytes 835616 | tf_op jit(solution)/shard_map/ppermute | solution.py:95
  28.1 4.1 %collective-permute-done.1.right_ref.refs_4_.refs_5_.refs_6_.refs_7_ = bf16[136,3,8,128]{3,2,1,0:T(8,128)(2,1)S(1)} collective-permute-done((bf16[136,3,8,128]{3,2,1,0:T(8,128)(2,1)}, bf16[136,3,8,128]{3,2,1,0:T(8,128)(2,1)S(1)}, u32[]{:S(2)}, u32[]{:S(2)}) %collective-permute-start.1) | collective-permute-done | bytes 835616 | tf_op jit(solution)/shard_map/ppermute | solution.py:95
  32.2 1.0 %copy-done.3 = bf16[136,3,8,128]{3,2,1,0:T(8,128)(2,1)} copy-done((bf16[136,3,8,128]{3,2,1,0:T(8,128)(2,1)}, bf16[136,3,8,128]{3,2,1,0:T(8,128)(2,1)S(1)}, u32[]{:S(2)}) %copy-start.3) | copy-done | bytes 835608
  33.2 7.8 %shard_map.140 = (f32[132,4,8,128]{3,2,1,0:T(8,128)}, f32[132,4,1,128]{3,2,1,0:T(1,128)}) custom-call(f32[132,4,8,128]{3,2,1,0:T(8,128)} %q_ref.3, bf16[136,3,8,128]{3,2,1,0:T(8,128)(2,1)} %copy-done.2, bf16[136,3,8,128]{3,2,1,0:T(8,128)(2,1)} %copy-done.3, bf16[136,3,8,128]{3,2,1,0:T(8,128)(2,1)} %copy-done.2, bf16[136,3,8,128]{3,2,1,0:T(8,128)(2,1)} %copy-done.2, ...), custom_call_target="tpu_custom_call" | custom-call | flops 43253760 | bytes 10813440 | tf_op jit(solution)/shard_map/pallas_call | solution.py:108
  41.0 1.3 %collective-permute-start.2 = (f32[132,4,1,128]{3,2,1,0:T(1,128)}, f32[132,4,1,128]{3,2,1,0:T(1,128)S(1)}, u32[]{:S(2)}, u32[]{:S(2)}) collective-permute-start(f32[132,4,1,128]{3,2,1,0:T(1,128)} %get-tuple-element.15), channel_id=1, source_target_pairs={{1,0},{3,2},{5,4},{7,6},{9,8},{11,10},{13,12},{15,14},{17,16},{19,... | collective-permute-start | bytes 811016 | tf_op jit(solution)/shard_map/ppermute | solution.py:123
  42.3 2.0 %slice.137 = f32[132,4,7,128]{3,2,1,0:T(8,128)S(1)} slice(f32[132,4,8,128]{3,2,1,0:T(8,128)} %get-tuple-element.14), slice={[0:132], [0:4], [1:8], [0:128]} | slice | bytes 3784704 | tf_op jit(solution)/shard_map/slice | solution.py:249
  44.6 1.3 %multiply_reduce_fusion.1 = (f32[4,8,128]{2,1,0:T(8,128)S(1)}, f32[4,8,128]{2,1,0:T(8,128)S(1)}, f32[132,4,8,128]{3,2,1,0:T(8,128)S(1)}) fusion(f32[132]{0:T(256)S(1)} %get-tuple-element.40, f32[132]{0:T(256)S(1)} %copy-done.11, f32[132,4,1,128]{3,2,1,0:T(1,128)S(1)} %collective-permute-done.2, f32[132,4,7,128]{3,2,1,0:T(8,128)S(1)} %slice.137, ...), kind=kLoop, calls=%fused_computation.6 | loop fusion | flops 4317184 | bytes 6522944 | tf_op jit(solution)/shard_map/reduce_sum | solution.py:255
  45.9 1.6 %collective-permute-start.3 = (f32[2,4,8,128]{3,2,1,0:T(8,128)S(1)}, f32[2,4,8,128]{3,2,1,0:T(8,128)S(1)}, u32[]{:S(2)}, u32[]{:S(2)}) collective-permute-start(f32[2,4,8,128]{3,2,1,0:T(8,128)S(1)} %pad_maximum_fusion.6), channel_id=1, source_target_pairs={{0,2},{2,0},{1,3},{3,1},{4,6},{6,4},{5,7},{7,5},{8,10},{10,8},{9,1... | collective-permute-start | bytes 98312 | tf_op jit(solution)/shard_map/ppermute | solution.py:260
  47.4 2.7 %collective-permute-done.3 = f32[2,4,8,128]{3,2,1,0:T(8,128)S(1)} collective-permute-done((f32[2,4,8,128]{3,2,1,0:T(8,128)S(1)}, f32[2,4,8,128]{3,2,1,0:T(8,128)S(1)}, u32[]{:S(2)}, u32[]{:S(2)}) %collective-permute-start.3) | collective-permute-done | bytes 32800 | tf_op jit(solution)/shard_map/ppermute | solution.py:260
  50.1 0.6 fusion.62
  51.3 0.8 slice_bitcast_fusion.2
  52.2 1.5 %collective-permute-start.4 = (bf16[132,8,128]{2,1,0:T(8,128)(2,1)}, bf16[132,8,128]{2,1,0:T(8,128)(2,1)S(1)}, u32[]{:S(2)}, u32[]{:S(2)}) collective-permute-start(bf16[132,8,128]{2,1,0:T(8,128)(2,1)} %get-tuple-element.32), channel_id=1, source_target_pairs={{0,2},{2,0},{1,3},{3,1},{4,6},{6,4},{5,7},{7,5},{8,10},{10,8},{9,1... | collective-permute-start | bytes 811016 | tf_op jit(solution)/shard_map/ppermute | solution.py:200
  53.9 0.8 copy-done.5
  55.3 6.4 %collective-permute-done.4 = bf16[132,8,128]{2,1,0:T(8,128)(2,1)S(1)} collective-permute-done((bf16[132,8,128]{2,1,0:T(8,128)(2,1)}, bf16[132,8,128]{2,1,0:T(8,128)(2,1)S(1)}, u32[]{:S(2)}, u32[]{:S(2)}) %collective-permute-start.4) | collective-permute-done | bytes 270368 | tf_op jit(solution)/shard_map/ppermute | solution.py:200
  61.8 0.8 fusion.53
  62.6 0.8 fusion.47
  63.9 0.8 fusion.45
  64.7 0.8 fusion.43
  65.5 0.7 fusion.18
  66.2 0.8 fusion.41
  67.0 0.8 fusion.39
  67.8 0.6 fusion.16
  68.4 0.8 fusion.37
  69.2 0.8 fusion.35
  70.0 0.7 fusion.5
  70.8 1.5 %collective-permute-start.6 = (bf16[132,8,128]{2,1,0:T(8,128)(2,1)S(1)}, bf16[132,8,128]{2,1,0:T(8,128)(2,1)S(1)}, u32[]{:S(2)}, u32[]{:S(2)}) collective-permute-start(bf16[132,8,128]{2,1,0:T(8,128)(2,1)S(1)} %slice.225), channel_id=1, source_target_pairs={{0,2},{2,0},{1,3},{3,1},{4,6},{6,4},{5,7},{7,5},{8,10},{10,8},{9,1... | collective-permute-start | bytes 811016 | tf_op jit(solution)/shard_map/ppermute | solution.py:207
  72.5 0.8 fusion.52
  73.2 0.8 fusion.33
  74.1 0.5 fusion.13
  74.6 0.8 fusion.31
  75.4 0.8 fusion.29
  76.3 0.9 fusion.11
  77.2 0.6 collective-permute-done.6
  77.7 0.8 fusion.27
  78.5 0.8 fusion.25
  79.3 0.6 fusion.9
  79.9 0.8 fusion.23
  80.7 0.8 fusion.21
  81.5 0.7 fusion.6
  82.4 1.5 %collective-permute-start.7 = (bf16[132,8,128]{2,1,0:T(8,128)(2,1)S(1)}, bf16[132,8,128]{2,1,0:T(8,128)(2,1)S(1)}, u32[]{:S(2)}, u32[]{:S(2)}) collective-permute-start(bf16[132,8,128]{2,1,0:T(8,128)(2,1)S(1)} %slice.227), channel_id=1, source_target_pairs={{0,2},{2,0},{1,3},{3,1},{4,6},{6,4},{5,7},{7,5},{8,10},{10,8},{9,1... | collective-permute-start | bytes 811016 | tf_op jit(solution)/shard_map/ppermute | solution.py:207
  84.1 4.8 %collective-permute-done.7 = bf16[132,8,128]{2,1,0:T(8,128)(2,1)S(1)} collective-permute-done((bf16[132,8,128]{2,1,0:T(8,128)(2,1)S(1)}, bf16[132,8,128]{2,1,0:T(8,128)(2,1)S(1)}, u32[]{:S(2)}, u32[]{:S(2)}) %collective-permute-start.7) | collective-permute-done | bytes 270368 | tf_op jit(solution)/shard_map/ppermute | solution.py:207
  89.4 1.8 %fusion.1 = f32[132,4,8,128]{3,2,1,0:T(8,128)} fusion(bf16[132,4,8,128]{3,2,1,0:T(8,128)(2,1)S(1)} %bitcast.128, f32[132,4,8,128]{3,2,1,0:T(8,128)S(1)} %get-tuple-element.23, f32[4,8,128]{2,1,0:T(8,128)S(1)} %compare_convert_fusion, f32[4,8,128]{2,1,0:T(8,128)S(1)} %get-tuple-element.22, f32[132]{0:T(256)S(1)} %get-tuple-element.39), kind=kLoop, calls=%fused_computation.4 | loop fusion | flops 3244032 | bytes 5440016 | tf_op jit(solution)/shard_map/mul | solution.py:272
  (66 shorter events, 4.3 us)
Async XLA Ops:
  0.6 10.9 %copy-start = (bf16[4,33,33]{2,0,1:T(4,128)(2,1)S(1)}, bf16[4,33,33]{2,0,1:T(4,128)(2,1)}, u32[]{:S(2)}) copy-start(bf16[4,33,33]{2,0,1:T(4,128)(2,1)} %param.23) | copy-start | bytes 26140
  2.1 9.2 %copy-start.12 = (s32[264]{0:T(512)S(1)}, s32[264]{0:T(512)}, u32[]{:S(2)}) copy-start(s32[264]{0:T(512)} %param.21) | copy-start | bytes 3172
  2.1 9.4 %copy-start.9 = (s32[8,8]{1,0:T(8,128)S(1)}, s32[8,8]{1,0:T(8,128)}, u32[]{:S(2)}) copy-start(s32[8,8]{1,0:T(8,128)} %param.22) | copy-start | bytes 772
  5.1 23.1 %collective-permute-start = (bf16[136,3,8,128]{3,2,1,0:T(8,128)(2,1)}, bf16[136,3,8,128]{3,2,1,0:T(8,128)(2,1)S(1)}, u32[]{:S(2)}, u32[]{:S(2)}) collective-permute-start(bf16[136,3,8,128]{3,2,1,0:T(8,128)(2,1)} %get-tuple-element.11), channel_id=1, source_target_pairs={{0,4},{4,8},{8,12},{1,5},{5,9},{9,13},{2,6},{6,10},{10,14},{3,7},{... | collective-permute-start | bytes 2506760 | tf_op jit(solution)/shard_map/ppermute | solution.py:95
  10.0 22.2 %collective-permute-start.1 = (bf16[136,3,8,128]{3,2,1,0:T(8,128)(2,1)}, bf16[136,3,8,128]{3,2,1,0:T(8,128)(2,1)S(1)}, u32[]{:S(2)}, u32[]{:S(2)}) collective-permute-start(bf16[136,3,8,128]{3,2,1,0:T(8,128)(2,1)} %get-tuple-element.13), channel_id=1, source_target_pairs={{4,0},{8,4},{12,8},{5,1},{9,5},{13,9},{6,2},{10,6},{14,10},{7,3},{... | collective-permute-start | bytes 2506760 | tf_op jit(solution)/shard_map/ppermute | solution.py:95
  15.5 26.8 %copy-start.10 = (f32[132]{0:T(256)S(1)}, f32[132]{0:T(256)}, u32[]{:S(2)}) copy-start(f32[132]{0:T(256)} %param.18) | copy-start | bytes 1588
  15.5 26.8 %copy-start.11 = (f32[132]{0:T(256)S(1)}, f32[132]{0:T(256)}, u32[]{:S(2)}) copy-start(f32[132]{0:T(256)} %param.19) | copy-start | bytes 1588
  15.5 26.8 %copy-start.13 = (f32[132]{0:T(256)S(1)}, f32[132]{0:T(256)}, u32[]{:S(2)}) copy-start(f32[132]{0:T(256)} %param.20) | copy-start | bytes 1588
  28.1 4.1 %copy-start.2 = (bf16[136,3,8,128]{3,2,1,0:T(8,128)(2,1)}, bf16[136,3,8,128]{3,2,1,0:T(8,128)(2,1)S(1)}, u32[]{:S(2)}) copy-start(bf16[136,3,8,128]{3,2,1,0:T(8,128)(2,1)S(1)} %collective-permute-done.left_ref.refs_0_.refs_1_.refs_2_.refs_3_) | copy-start | bytes 2506756
  32.2 1.0 %copy-start.3 = (bf16[136,3,8,128]{3,2,1,0:T(8,128)(2,1)}, bf16[136,3,8,128]{3,2,1,0:T(8,128)(2,1)S(1)}, u32[]{:S(2)}) copy-start(bf16[136,3,8,128]{3,2,1,0:T(8,128)(2,1)S(1)} %collective-permute-done.1.right_ref.refs_4_.refs_5_.refs_6_.refs_7_) | copy-start | bytes 2506756
  41.0 3.6 %collective-permute-start.2 = (f32[132,4,1,128]{3,2,1,0:T(1,128)}, f32[132,4,1,128]{3,2,1,0:T(1,128)S(1)}, u32[]{:S(2)}, u32[]{:S(2)}) collective-permute-start(f32[132,4,1,128]{3,2,1,0:T(1,128)} %get-tuple-element.15), channel_id=1, source_target_pairs={{1,0},{3,2},{5,4},{7,6},{9,8},{11,10},{13,12},{15,14},{17,16},{19,... | collective-permute-start | bytes 811016 | tf_op jit(solution)/shard_map/ppermute | solution.py:123
  42.3 2.3 %copy-start.4 = (f32[132,4,8,128]{3,2,1,0:T(8,128)S(1)}, f32[132,4,8,128]{3,2,1,0:T(8,128)}, u32[]{:S(2)}) copy-start(f32[132,4,8,128]{3,2,1,0:T(8,128)} %get-tuple-element.14) | copy-start | bytes 6488068
  44.6 5.5 %copy-start.6 = (f32[4,8,128]{2,1,0:T(8,128)S(1)}, f32[4,8,128]{2,1,0:T(8,128)}, u32[]{:S(2)}) copy-start(f32[4,8,128]{2,1,0:T(8,128)} %param.16) | copy-start | bytes 49156
  44.6 5.5 %copy-start.7 = (f32[4,8,128]{2,1,0:T(8,128)S(1)}, f32[4,8,128]{2,1,0:T(8,128)}, u32[]{:S(2)}) copy-start(f32[4,8,128]{2,1,0:T(8,128)} %param.15) | copy-start | bytes 49156
  45.9 4.2 %collective-permute-start.3 = (f32[2,4,8,128]{3,2,1,0:T(8,128)S(1)}, f32[2,4,8,128]{3,2,1,0:T(8,128)S(1)}, u32[]{:S(2)}, u32[]{:S(2)}) collective-permute-start(f32[2,4,8,128]{3,2,1,0:T(8,128)S(1)} %pad_maximum_fusion.6), channel_id=1, source_target_pairs={{0,2},{2,0},{1,3},{3,1},{4,6},{6,4},{5,7},{7,5},{8,10},{10,8},{9,1... | collective-permute-start | bytes 98312 | tf_op jit(solution)/shard_map/ppermute | solution.py:260
  51.3 2.3 %copy-start.8 = (s32[4,128]{1,0:T(4,128)S(1)}, s32[4,128]{1,0:T(4,128)}, u32[]{:S(2)}) copy-start(s32[4,128]{1,0:T(4,128)} %param.17) | copy-start | bytes 6148
  52.2 9.5 %collective-permute-start.4 = (bf16[132,8,128]{2,1,0:T(8,128)(2,1)}, bf16[132,8,128]{2,1,0:T(8,128)(2,1)S(1)}, u32[]{:S(2)}, u32[]{:S(2)}) collective-permute-start(bf16[132,8,128]{2,1,0:T(8,128)(2,1)} %get-tuple-element.32), channel_id=1, source_target_pairs={{0,2},{2,0},{1,3},{3,1},{4,6},{6,4},{5,7},{7,5},{8,10},{10,8},{9,1... | collective-permute-start | bytes 811016 | tf_op jit(solution)/shard_map/ppermute | solution.py:200
  53.7 1.0 %copy-start.5 = (bf16[132,8,128]{2,1,0:T(8,128)(2,1)S(1)}, bf16[132,8,128]{2,1,0:T(8,128)(2,1)}, u32[]{:S(2)}) copy-start(bf16[132,8,128]{2,1,0:T(8,128)(2,1)} %get-tuple-element.33) | copy-start | bytes 811012
  54.7 17.7 %collective-permute-start.5 = (bf16[132,8,128]{2,1,0:T(8,128)(2,1)S(1)}, bf16[132,8,128]{2,1,0:T(8,128)(2,1)S(1)}, u32[]{:S(2)}, u32[]{:S(2)}) collective-permute-start(bf16[132,8,128]{2,1,0:T(8,128)(2,1)S(1)} %copy-done.5), channel_id=1, source_target_pairs={{0,2},{2,0},{1,3},{3,1},{4,6},{6,4},{5,7},{7,5},{8,10},{10,8},{9,1... | collective-permute-start | bytes 811016 | tf_op jit(solution)/shard_map/ppermute | solution.py:200
  70.8 6.9 %collective-permute-start.6 = (bf16[132,8,128]{2,1,0:T(8,128)(2,1)S(1)}, bf16[132,8,128]{2,1,0:T(8,128)(2,1)S(1)}, u32[]{:S(2)}, u32[]{:S(2)}) collective-permute-start(bf16[132,8,128]{2,1,0:T(8,128)(2,1)S(1)} %slice.225), channel_id=1, source_target_pairs={{0,2},{2,0},{1,3},{3,1},{4,6},{6,4},{5,7},{7,5},{8,10},{10,8},{9,1... | collective-permute-start | bytes 811016 | tf_op jit(solution)/shard_map/ppermute | solution.py:207
  82.4 6.5 %collective-permute-start.7 = (bf16[132,8,128]{2,1,0:T(8,128)(2,1)S(1)}, bf16[132,8,128]{2,1,0:T(8,128)(2,1)S(1)}, u32[]{:S(2)}, u32[]{:S(2)}) collective-permute-start(bf16[132,8,128]{2,1,0:T(8,128)(2,1)S(1)} %slice.227), channel_id=1, source_target_pairs={{0,2},{2,0},{1,3},{3,1},{4,6},{6,4},{5,7},{7,5},{8,10},{10,8},{9,1... | collective-permute-start | bytes 811016 | tf_op jit(solution)/shard_map/ppermute | solution.py:207
  89.4 1.9 %copy-start.1 = (bf16[4,33,33]{2,0,1:T(4,128)(2,1)S(1)}, bf16[4,33,33]{2,0,1:T(4,128)(2,1)}, u32[]{:S(2)}) copy-start(bf16[4,33,33]{2,0,1:T(4,128)(2,1)} %param.23) | copy-start | bytes 26140

commit v11 on v10

--- a/solution.py
+++ b/solution.py
@@ -53,7 +53,7 @@
 
 def advect_kernel(weights, q_ref, left_ref, right_ref, *refs):
     left_winds, right_winds = refs[0:4], refs[4:8]
-    wx_ref, wy_ref, out_ref, bottom_ref = refs[8:]
+    wx_ref, wy_ref, out_ref, bottom_ref, lifted_ref = refs[8:]
     depth = len(weights)
     width = q_ref.shape[1]
 
@@ -82,6 +82,7 @@
         section = field[:, stage : stage + span] + weight_now * (-along_x - along_y)
     out_ref[...] = section
     bottom_ref[...] = section[:, :, :1]
+    lifted_ref[...] = pltpu.roll(section, section.shape[2] - 1, 2)
 
 
 def advect_kernel_call(bin_mass, wind_x, wind_y, section_weights, tie):
@@ -110,10 +111,11 @@
         out_shape=(
             jax.ShapeDtypeStruct(bin_mass.shape, bin_mass.dtype),
             jax.ShapeDtypeStruct((local_bins, width_x, 1, width_y), bin_mass.dtype),
+            jax.ShapeDtypeStruct(bin_mass.shape, bin_mass.dtype),
         ),
         grid=(local_bins // block,),
         in_specs=[own_spec, rim_spec, rim_spec] + row_specs + row_specs + [wind_spec, wind_spec],
-        out_specs=(own_spec, pl.BlockSpec((block, width_x, 1, width_y), lambda i: (i, 0, 0, 0))),
+        out_specs=(own_spec, pl.BlockSpec((block, width_x, 1, width_y), lambda i: (i, 0, 0, 0)), own_spec),
         cost_estimate=pl.CostEstimate(flops=80 * cells, bytes_accessed=20 * cells, transcendentals=0),
     )(bin_mass, left, right, *([left] * 4), *([right] * 4), wind_x, wind_y)
 
@@ -234,7 +236,7 @@
     paired = lax.axis_size("bins") == 2 and width_x % 2 == 0
     table = paired_table(bin_order, kernel_index, collision_kernels) if paired else None
     if width_x >= len(section_weights):
-        table, (section_field, bottom) = advect_kernel_call(
+        table, (section_field, bottom, lifted) = advect_kernel_call(
             bin_mass, wind_x, wind_y, section_weights, table
         )
     else:
@@ -245,8 +247,10 @@
                 extended[:, 1:-1], extended[:, :-2], extended[:, 2:], wind_x, wind_y
             )
         bottom = section_field[:, :, :1, :]
+        lifted = jnp.roll(section_field, -1, axis=2)
     rim_above = shifted(bottom, "vert", -1)
-    from_above = jnp.concatenate([section_field[:, :, 1:], rim_above], axis=2)
+    top = lax.broadcasted_iota(jnp.int32, section_field.shape, 2) == width_z - 1
+    from_above = jnp.where(top, rim_above, lifted)
     speed = fall_speed[:, None, None, None]
     settled = (1.0 - speed) * section_field + speed * from_above
     growth = growth_rate[:, None, None, None]

time: 91.6 us -> 93 us (1.015)
  local copies, waits for them, and re-layouts: 5.61 us -> 3.55 us
  other arithmetic: 11.7 us -> 13.3 us
  waiting for transfers between devices: 31.4 us -> 32.9 us
    ppermute x1, waiting for transfers between devices: 0.26 us -> 2.31 us  [shifted(): return lax.ppermute(block, axis, route)]
    slice x1 -> x0, local copies, waits for them, and re-layouts: 2.02 us -> none  [body(): from_above = jnp.concatenate([section_field[:, :, 1:], rim_above], axis=2)]
    reduce_sum x1, other arithmetic: 1.25 us -> 2.83 us  [body(): jnp.sum(latent_factor[:, None, None, None] * growth * settled, axis=0)]
    unnamed x41 -> x39, local copies, waits for them, and re-layouts: 2.34 us -> 2.3 us
  transfers between devices with their start and end apart: 8 -> 8, of which waited for: 7 -> 7; matrix products, arithmetic and copies ran while one was open for 22% -> 20% of each run, Pallas kernels for 0% -> 0%
where the time goes in v11:
time: 93 us; the launch traced here: 92.6 us
  waiting for transfers between devices  32.9 us (35%)
  matrix products  16.4 us (18%)
  starting transfers between devices  14.2 us (15%)
  other arithmetic  13.3 us (14%)
  Pallas kernels  11 us (12%)
  local copies, waits for them, and re-layouts  3.55 us (4%)
  between operations  1.16 us (1%)
    ppermute x2, waiting for transfers between devices, advect_kernel_call(): lax.ppermute(message, 'tiles', pairs)  16.7 us
    dot_general x16, matrix products, collide(): jnp.dot(table, iterate.astype(jnp.bfloat16), preferred_element_type=jnp.f...  12.6 us
    pallas_call x1, Pallas kernels, advect_kernel_call(): pl.pallas_call(functools.partial(advect_kernel, section_weights), out_sha...  8.13 us
    ppermute x2, waiting for transfers between devices, paired_collision(): arrived = lax.ppermute(away[:, chunk], 'bins', swap)  6.5 us
    ppermute x2, starting transfers between devices, advect_kernel_call(): lax.ppermute(message, 'tiles', pairs)  6.26 us
    ppermute x2, waiting for transfers between devices, paired_collision(): returned.append(lax.ppermute(change[local_bins:], 'bins', swap))  5.02 us
    add x6, other arithmetic, collide(): iterate + collision_rate * products[all_bins:] * products[:all_bins]  3.85 us
    ppermute x2, starting transfers between devices, paired_collision(): returned.append(lax.ppermute(change[local_bins:], 'bins', swap))  3.1 us
  transfers between devices with their start and end apart: 8, of which 7 were waited for; matrix products, arithmetic and copies ran while one was open for 20% of the time, Pallas kernels for 0%

profile of v11, /device:TPU:0, one launch (start us, length us, event | category | flops | bytes accessed | tf_op | source)
XLA Modules:
  0.0 92.6 jit_solution(12767812921830488621)
XLA Ops:
  0.7 1.4 %compare_select_fusion = (f32[4,8,128]{2,1,0:T(8,128)}, f32[4,8,128]{2,1,0:T(8,128)}) fusion(f32[4,8,128]{2,1,0:T(8,128)} %param.14, s32[4,128]{1,0:T(4,128)} %param.17, s32[8]{0:T(128)S(1)} %iota_add_fusion, f32[4,8,128]{2,1,0:T(8,128)} %param.13), kind=kLoop, calls=%fused_computation.120 | loop fusion | flops 12288 | bytes 67616 | tf_op jit(solution)/shard_map/mul | solution.py:234
  2.1 2.9 %shard_map.139 = (bf16[136,3,8,128]{3,2,1,0:T(8,128)(2,1)}, bf16[136,3,8,128]{3,2,1,0:T(8,128)(2,1)}) custom-call(f32[132,4,8,128]{3,2,1,0:T(8,128)} %q_ref.3, f32[4,8,128]{2,1,0:T(8,128)} %get-tuple-element.40.wx_ref.refs_8_, f32[4,8,128]{2,1,0:T(8,128)} %get-tuple-element.39.wy_ref.refs_9_), custom_call_target="tpu_custom_call" | custom-call | tf_op jit(solution)/shard_map/pallas_call | solution.py:48
  5.0 5.0 %collective-permute-start = (bf16[136,3,8,128]{3,2,1,0:T(8,128)(2,1)}, bf16[136,3,8,128]{3,2,1,0:T(8,128)(2,1)S(1)}, u32[]{:S(2)}, u32[]{:S(2)}) collective-permute-start(bf16[136,3,8,128]{3,2,1,0:T(8,128)(2,1)} %get-tuple-element.12), channel_id=1, source_target_pairs={{0,4},{4,8},{8,12},{1,5},{5,9},{9,13},{2,6},{6,10},{10,14},{3,7},{... | collective-permute-start | bytes 2506760 | tf_op jit(solution)/shard_map/ppermute | solution.py:96
  10.0 1.3 %collective-permute-start.1 = (bf16[136,3,8,128]{3,2,1,0:T(8,128)(2,1)}, bf16[136,3,8,128]{3,2,1,0:T(8,128)(2,1)S(1)}, u32[]{:S(2)}, u32[]{:S(2)}) collective-permute-start(bf16[136,3,8,128]{3,2,1,0:T(8,128)(2,1)} %get-tuple-element.14), channel_id=1, source_target_pairs={{4,0},{8,4},{12,8},{5,1},{9,5},{13,9},{6,2},{10,6},{14,10},{7,3},{... | collective-permute-start | bytes 2506760 | tf_op jit(solution)/shard_map/ppermute | solution.py:96
  11.9 2.0 %multiply_reduce_fusion = f32[264,8,33]{0,2,1:T(8,128)S(1)} fusion(f32[264,8]{0,1:T(8,128)S(1)} %fusion.65, f32[8,8,33,33]{3,1,2,0:T(8,128)S(1)} %fusion.56, s32[264]{0:T(512)S(1)} %get-tuple-element.37), kind=kOutput, calls=%fused_computation | convolution fusion | flops 221851072 | bytes 567072 | tf_op jit(solution)/shard_map/bm,acmn->bacn/dot_general | solution.py:152
  14.2 1.1 %fusion.3 = bf16[264,264]{0,1:T(8,128)(2,1)S(1)} fusion(f32[264,8,33]{0,2,1:T(8,128)S(1)} %multiply_reduce_fusion, f32[264,8]{0,1:T(8,128)S(1)} %fusion.65, f32[264,33]{0,1:T(8,128)S(1)} %fusion.53), kind=kOutput, calls=%fused_computation.16 | convolution fusion | flops 220936320 | bytes 461472 | tf_op jit(solution)/shard_map/bcn,dc,dn->bd/dot_general | solution.py:154
  15.5 12.6 %collective-permute-done.left_ref.refs_0_.refs_1_.refs_2_.refs_3_ = bf16[136,3,8,128]{3,2,1,0:T(8,128)(2,1)S(1)} collective-permute-done((bf16[136,3,8,128]{3,2,1,0:T(8,128)(2,1)}, bf16[136,3,8,128]{3,2,1,0:T(8,128)(2,1)S(1)}, u32[]{:S(2)}, u32[]{:S(2)}) %collective-permute-start) | collective-permute-done | bytes 835616 | tf_op jit(solution)/shard_map/ppermute | solution.py:96
  28.1 4.1 %collective-permute-done.1.right_ref.refs_4_.refs_5_.refs_6_.refs_7_ = bf16[136,3,8,128]{3,2,1,0:T(8,128)(2,1)S(1)} collective-permute-done((bf16[136,3,8,128]{3,2,1,0:T(8,128)(2,1)}, bf16[136,3,8,128]{3,2,1,0:T(8,128)(2,1)S(1)}, u32[]{:S(2)}, u32[]{:S(2)}) %collective-permute-start.1) | collective-permute-done | bytes 835616 | tf_op jit(solution)/shard_map/ppermute | solution.py:96
  32.2 0.9 copy-done.3
  33.1 8.1 %shard_map.140 = (f32[132,4,8,128]{3,2,1,0:T(8,128)}, f32[132,4,1,128]{3,2,1,0:T(1,128)}, f32[132,4,8,128]{3,2,1,0:T(8,128)}) custom-call(f32[132,4,8,128]{3,2,1,0:T(8,128)} %q_ref.3, bf16[136,3,8,128]{3,2,1,0:T(8,128)(2,1)} %copy-done.2, bf16[136,3,8,128]{3,2,1,0:T(8,128)(2,1)} %copy-done.3, bf16[136,3,8,128]{3,2,1,0:T(8,128)(2,1)} %copy-done.2, ...), custom_call_target="tpu_custom_call" | custom-call | flops 43253760 | bytes 10813440 | tf_op jit(solution)/shard_map/pallas_call | solution.py:109
  41.2 1.3 %collective-permute-start.2 = (f32[132,4,1,128]{3,2,1,0:T(1,128)}, f32[132,4,1,128]{3,2,1,0:T(1,128)S(1)}, u32[]{:S(2)}, u32[]{:S(2)}) collective-permute-start(f32[132,4,1,128]{3,2,1,0:T(1,128)} %get-tuple-element.16), channel_id=1, source_target_pairs={{1,0},{3,2},{5,4},{7,6},{9,8},{11,10},{13,12},{15,14},{17,16},{19,... | collective-permute-start | bytes 811016 | tf_op jit(solution)/shard_map/ppermute | solution.py:125
  42.5 2.3 %collective-permute-done.2 = f32[132,4,1,128]{3,2,1,0:T(1,128)S(1)} collective-permute-done((f32[132,4,1,128]{3,2,1,0:T(1,128)}, f32[132,4,1,128]{3,2,1,0:T(1,128)S(1)}, u32[]{:S(2)}, u32[]{:S(2)}) %collective-permute-start.2) | collective-permute-done | bytes 270368 | tf_op jit(solution)/shard_map/ppermute | solution.py:125
  44.8 2.8 %multiply_reduce_fusion.1 = (f32[4,8,128]{2,1,0:T(8,128)S(1)}, f32[4,8,128]{2,1,0:T(8,128)S(1)}, f32[132,4,8,128]{3,2,1,0:T(8,128)S(1)}) fusion(f32[132]{0:T(256)S(1)} %get-tuple-element.42, f32[132]{0:T(256)S(1)} %copy-done.10, f32[132,4,8,128]{3,2,1,0:T(8,128)} %get-tuple-element.17, f32[132,4,128]{2,1,0:T(4,128)S(1)} %bitcast.143, ...), kind=kLoop, calls=%fused_computation.4 | loop fusion | flops 4317184 | bytes 6793288 | tf_op jit(solution)/shard_map/reduce_sum | solution.py:259
  47.7 1.6 %collective-permute-start.3 = (f32[2,4,8,128]{3,2,1,0:T(8,128)S(1)}, f32[2,4,8,128]{3,2,1,0:T(8,128)S(1)}, u32[]{:S(2)}, u32[]{:S(2)}) collective-permute-start(f32[2,4,8,128]{3,2,1,0:T(8,128)S(1)} %pad_maximum_fusion.6), channel_id=1, source_target_pairs={{0,2},{2,0},{1,3},{3,1},{4,6},{6,4},{5,7},{7,5},{8,10},{10,8},{9,1... | collective-permute-start | bytes 98312 | tf_op jit(solution)/shard_map/ppermute | solution.py:264
  49.3 2.4 %collective-permute-done.3 = f32[2,4,8,128]{3,2,1,0:T(8,128)S(1)} collective-permute-done((f32[2,4,8,128]{3,2,1,0:T(8,128)S(1)}, f32[2,4,8,128]{3,2,1,0:T(8,128)S(1)}, u32[]{:S(2)}, u32[]{:S(2)}) %collective-permute-start.3) | collective-permute-done | bytes 32800 | tf_op jit(solution)/shard_map/ppermute | solution.py:264
  51.7 0.6 fusion.61
  52.9 0.8 slice_bitcast_fusion.2
  53.7 1.5 %collective-permute-start.4 = (bf16[132,8,128]{2,1,0:T(8,128)(2,1)}, bf16[132,8,128]{2,1,0:T(8,128)(2,1)S(1)}, u32[]{:S(2)}, u32[]{:S(2)}) collective-permute-start(bf16[132,8,128]{2,1,0:T(8,128)(2,1)} %get-tuple-element.34), channel_id=1, source_target_pairs={{0,2},{2,0},{1,3},{3,1},{4,6},{6,4},{5,7},{7,5},{8,10},{10,8},{9,1... | collective-permute-start | bytes 811016 | tf_op jit(solution)/shard_map/ppermute | solution.py:202
  55.4 0.8 copy-done.4
  56.9 6.5 %collective-permute-done.4 = bf16[132,8,128]{2,1,0:T(8,128)(2,1)S(1)} collective-permute-done((bf16[132,8,128]{2,1,0:T(8,128)(2,1)}, bf16[132,8,128]{2,1,0:T(8,128)(2,1)S(1)}, u32[]{:S(2)}, u32[]{:S(2)}) %collective-permute-start.4) | collective-permute-done | bytes 270368 | tf_op jit(solution)/shard_map/ppermute | solution.py:202
  63.4 0.8 fusion.52
  64.2 0.8 fusion.46
  65.1 0.5 fusion.19
  65.6 0.8 fusion.44
  66.4 0.8 fusion.42
  67.2 0.7 fusion.17
  67.9 0.8 fusion.40
  68.7 0.8 fusion.38
  69.5 0.6 fusion.15
  70.1 0.8 fusion.36
  70.8 0.8 fusion.34
  71.7 0.7 fusion.4
  72.5 1.5 %collective-permute-start.6 = (bf16[132,8,128]{2,1,0:T(8,128)(2,1)S(1)}, bf16[132,8,128]{2,1,0:T(8,128)(2,1)S(1)}, u32[]{:S(2)}, u32[]{:S(2)}) collective-permute-start(bf16[132,8,128]{2,1,0:T(8,128)(2,1)S(1)} %slice.221), channel_id=1, source_target_pairs={{0,2},{2,0},{1,3},{3,1},{4,6},{6,4},{5,7},{7,5},{8,10},{10,8},{9,1... | collective-permute-start | bytes 811016 | tf_op jit(solution)/shard_map/ppermute | solution.py:209
  74.1 0.8 fusion.51
  74.9 0.8 fusion.32
  75.8 0.5 fusion.12
  76.3 0.8 fusion.30
  77.1 0.8 fusion.28
  77.9 0.9 fusion.10
  79.0 0.8 fusion.26
  79.8 0.8 fusion.24
  80.6 0.6 fusion.8
  81.2 0.8 fusion.22
  82.0 0.8 fusion.20
  82.8 0.7 fusion.5
  83.7 1.6 %collective-permute-start.7 = (bf16[132,8,128]{2,1,0:T(8,128)(2,1)S(1)}, bf16[132,8,128]{2,1,0:T(8,128)(2,1)S(1)}, u32[]{:S(2)}, u32[]{:S(2)}) collective-permute-start(bf16[132,8,128]{2,1,0:T(8,128)(2,1)S(1)} %slice.223), channel_id=1, source_target_pairs={{0,2},{2,0},{1,3},{3,1},{4,6},{6,4},{5,7},{7,5},{8,10},{10,8},{9,1... | collective-permute-start | bytes 811016 | tf_op jit(solution)/shard_map/ppermute | solution.py:209
  85.4 4.8 %collective-permute-done.7 = bf16[132,8,128]{2,1,0:T(8,128)(2,1)S(1)} collective-permute-done((bf16[132,8,128]{2,1,0:T(8,128)(2,1)S(1)}, bf16[132,8,128]{2,1,0:T(8,128)(2,1)S(1)}, u32[]{:S(2)}, u32[]{:S(2)}) %collective-permute-start.7) | collective-permute-done | bytes 270368 | tf_op jit(solution)/shard_map/ppermute | solution.py:209
  90.7 1.8 %fusion = f32[132,4,8,128]{3,2,1,0:T(8,128)} fusion(bf16[132,4,8,128]{3,2,1,0:T(8,128)(2,1)S(1)} %bitcast.129, f32[132,4,8,128]{3,2,1,0:T(8,128)S(1)} %get-tuple-element.25, f32[4,8,128]{2,1,0:T(8,128)S(1)} %compare_convert_fusion, f32[4,8,128]{2,1,0:T(8,128)S(1)} %get-tuple-element.24, f32[132]{0:T(256)S(1)} %get-tuple-element.41), kind=kLoop, calls=%fused_computation.2 | loop fusion | flops 3244032 | bytes 5440016 | tf_op jit(solution)/shard_map/mul | solution.py:276
  (64 shorter events, 3.7 us)
Async XLA Ops:
  0.6 10.9 %copy-start = (bf16[4,33,33]{2,0,1:T(4,128)(2,1)S(1)}, bf16[4,33,33]{2,0,1:T(4,128)(2,1)}, u32[]{:S(2)}) copy-start(bf16[4,33,33]{2,0,1:T(4,128)(2,1)} %param.23) | copy-start | bytes 26140
  2.1 9.2 %copy-start.11 = (s32[264]{0:T(512)S(1)}, s32[264]{0:T(512)}, u32[]{:S(2)}) copy-start(s32[264]{0:T(512)} %param.21) | copy-start | bytes 3172
  2.1 9.4 %copy-start.8 = (s32[8,8]{1,0:T(8,128)S(1)}, s32[8,8]{1,0:T(8,128)}, u32[]{:S(2)}) copy-start(s32[8,8]{1,0:T(8,128)} %param.22) | copy-start | bytes 772
  5.0 23.1 %collective-permute-start = (bf16[136,3,8,128]{3,2,1,0:T(8,128)(2,1)}, bf16[136,3,8,128]{3,2,1,0:T(8,128)(2,1)S(1)}, u32[]{:S(2)}, u32[]{:S(2)}) collective-permute-start(bf16[136,3,8,128]{3,2,1,0:T(8,128)(2,1)} %get-tuple-element.12), channel_id=1, source_target_pairs={{0,4},{4,8},{8,12},{1,5},{5,9},{9,13},{2,6},{6,10},{10,14},{3,7},{... | collective-permute-start | bytes 2506760 | tf_op jit(solution)/shard_map/ppermute | solution.py:96
  10.0 22.2 %collective-permute-start.1 = (bf16[136,3,8,128]{3,2,1,0:T(8,128)(2,1)}, bf16[136,3,8,128]{3,2,1,0:T(8,128)(2,1)S(1)}, u32[]{:S(2)}, u32[]{:S(2)}) collective-permute-start(bf16[136,3,8,128]{3,2,1,0:T(8,128)(2,1)} %get-tuple-element.14), channel_id=1, source_target_pairs={{4,0},{8,4},{12,8},{5,1},{9,5},{13,9},{6,2},{10,6},{14,10},{7,3},{... | collective-permute-start | bytes 2506760 | tf_op jit(solution)/shard_map/ppermute | solution.py:96
  13.9 1.6 %copy-start.9 = (f32[132]{0:T(256)S(1)}, f32[132]{0:T(256)}, u32[]{:S(2)}) copy-start(f32[132]{0:T(256)} %param.18) | copy-start | bytes 1588
  15.5 27.0 %copy-start.10 = (f32[132]{0:T(256)S(1)}, f32[132]{0:T(256)}, u32[]{:S(2)}) copy-start(f32[132]{0:T(256)} %param.19) | copy-start | bytes 1588
  15.5 27.0 %copy-start.12 = (f32[132]{0:T(256)S(1)}, f32[132]{0:T(256)}, u32[]{:S(2)}) copy-start(f32[132]{0:T(256)} %param.20) | copy-start | bytes 1588
  28.1 4.1 %copy-start.2 = (bf16[136,3,8,128]{3,2,1,0:T(8,128)(2,1)}, bf16[136,3,8,128]{3,2,1,0:T(8,128)(2,1)S(1)}, u32[]{:S(2)}) copy-start(bf16[136,3,8,128]{3,2,1,0:T(8,128)(2,1)S(1)} %collective-permute-done.left_ref.refs_0_.refs_1_.refs_2_.refs_3_) | copy-start | bytes 2506756
  32.1 0.9 copy-start.3
  41.2 3.6 %collective-permute-start.2 = (f32[132,4,1,128]{3,2,1,0:T(1,128)}, f32[132,4,1,128]{3,2,1,0:T(1,128)S(1)}, u32[]{:S(2)}, u32[]{:S(2)}) collective-permute-start(f32[132,4,1,128]{3,2,1,0:T(1,128)} %get-tuple-element.16), channel_id=1, source_target_pairs={{1,0},{3,2},{5,4},{7,6},{9,8},{11,10},{13,12},{15,14},{17,16},{19,... | collective-permute-start | bytes 811016 | tf_op jit(solution)/shard_map/ppermute | solution.py:125
  44.8 6.8 %copy-start.5 = (f32[4,8,128]{2,1,0:T(8,128)S(1)}, f32[4,8,128]{2,1,0:T(8,128)}, u32[]{:S(2)}) copy-start(f32[4,8,128]{2,1,0:T(8,128)} %param.16) | copy-start | bytes 49156
  44.8 6.8 %copy-start.6 = (f32[4,8,128]{2,1,0:T(8,128)S(1)}, f32[4,8,128]{2,1,0:T(8,128)}, u32[]{:S(2)}) copy-start(f32[4,8,128]{2,1,0:T(8,128)} %param.15) | copy-start | bytes 49156
  47.7 4.0 %collective-permute-start.3 = (f32[2,4,8,128]{3,2,1,0:T(8,128)S(1)}, f32[2,4,8,128]{3,2,1,0:T(8,128)S(1)}, u32[]{:S(2)}, u32[]{:S(2)}) collective-permute-start(f32[2,4,8,128]{3,2,1,0:T(8,128)S(1)} %pad_maximum_fusion.6), channel_id=1, source_target_pairs={{0,2},{2,0},{1,3},{3,1},{4,6},{6,4},{5,7},{7,5},{8,10},{10,8},{9,1... | collective-permute-start | bytes 98312 | tf_op jit(solution)/shard_map/ppermute | solution.py:264
  52.9 2.3 %copy-start.7 = (s32[4,128]{1,0:T(4,128)S(1)}, s32[4,128]{1,0:T(4,128)}, u32[]{:S(2)}) copy-start(s32[4,128]{1,0:T(4,128)} %param.17) | copy-start | bytes 6148
  53.7 9.6 %collective-permute-start.4 = (bf16[132,8,128]{2,1,0:T(8,128)(2,1)}, bf16[132,8,128]{2,1,0:T(8,128)(2,1)S(1)}, u32[]{:S(2)}, u32[]{:S(2)}) collective-permute-start(bf16[132,8,128]{2,1,0:T(8,128)(2,1)} %get-tuple-element.34), channel_id=1, source_target_pairs={{0,2},{2,0},{1,3},{3,1},{4,6},{6,4},{5,7},{7,5},{8,10},{10,8},{9,1... | collective-permute-start | bytes 811016 | tf_op jit(solution)/shard_map/ppermute | solution.py:202
  55.3 1.0 %copy-start.4 = (bf16[132,8,128]{2,1,0:T(8,128)(2,1)S(1)}, bf16[132,8,128]{2,1,0:T(8,128)(2,1)}, u32[]{:S(2)}) copy-start(bf16[132,8,128]{2,1,0:T(8,128)(2,1)} %get-tuple-element.35) | copy-start | bytes 811012
  56.3 17.8 %collective-permute-start.5 = (bf16[132,8,128]{2,1,0:T(8,128)(2,1)S(1)}, bf16[132,8,128]{2,1,0:T(8,128)(2,1)S(1)}, u32[]{:S(2)}, u32[]{:S(2)}) collective-permute-start(bf16[132,8,128]{2,1,0:T(8,128)(2,1)S(1)} %copy-done.4), channel_id=1, source_target_pairs={{0,2},{2,0},{1,3},{3,1},{4,6},{6,4},{5,7},{7,5},{8,10},{10,8},{9,1... | collective-permute-start | bytes 811016 | tf_op jit(solution)/shard_map/ppermute | solution.py:202
  72.5 6.5 %collective-permute-start.6 = (bf16[132,8,128]{2,1,0:T(8,128)(2,1)S(1)}, bf16[132,8,128]{2,1,0:T(8,128)(2,1)S(1)}, u32[]{:S(2)}, u32[]{:S(2)}) collective-permute-start(bf16[132,8,128]{2,1,0:T(8,128)(2,1)S(1)} %slice.221), channel_id=1, source_target_pairs={{0,2},{2,0},{1,3},{3,1},{4,6},{6,4},{5,7},{7,5},{8,10},{10,8},{9,1... | collective-permute-start | bytes 811016 | tf_op jit(solution)/shard_map/ppermute | solution.py:209
  83.7 6.5 %collective-permute-start.7 = (bf16[132,8,128]{2,1,0:T(8,128)(2,1)S(1)}, bf16[132,8,128]{2,1,0:T(8,128)(2,1)S(1)}, u32[]{:S(2)}, u32[]{:S(2)}) collective-permute-start(bf16[132,8,128]{2,1,0:T(8,128)(2,1)S(1)} %slice.223), channel_id=1, source_target_pairs={{0,2},{2,0},{1,3},{3,1},{4,6},{6,4},{5,7},{7,5},{8,10},{10,8},{9,1... | collective-permute-start | bytes 811016 | tf_op jit(solution)/shard_map/ppermute | solution.py:209
  90.7 1.9 %copy-start.1 = (bf16[4,33,33]{2,0,1:T(4,128)(2,1)S(1)}, bf16[4,33,33]{2,0,1:T(4,128)(2,1)}, u32[]{:S(2)}) copy-start(bf16[4,33,33]{2,0,1:T(4,128)(2,1)} %param.23) | copy-start | bytes 26140

commit v12 on v10

--- a/solution.py
+++ b/solution.py
@@ -77,8 +77,8 @@
         north = pltpu.roll(center, center.shape[3] - 1, 3)
         wind_a = wx[stage : stage + span]
         wind_b = wy[stage : stage + span]
-        along_x = jnp.maximum(wind_a, 0.0) * (center - west) + jnp.minimum(wind_a, 0.0) * (east - center)
-        along_y = jnp.maximum(wind_b, 0.0) * (center - south) + jnp.minimum(wind_b, 0.0) * (north - center)
+        along_x = wind_a * jnp.where(wind_a > 0.0, center - west, east - center)
+        along_y = wind_b * jnp.where(wind_b > 0.0, center - south, north - center)
         section = field[:, stage : stage + span] + weight_now * (-along_x - along_y)
     out_ref[...] = section
     bottom_ref[...] = section[:, :, :1]

time: 91.6 us -> 91.7 us (level)
  no operation moved by 1% of the time
where the time goes in v12:
time: 91.7 us; the launch traced here: 91.4 us
  waiting for transfers between devices  31.4 us (34%)
  matrix products  16.4 us (18%)
  starting transfers between devices  14.3 us (16%)
  other arithmetic  11.7 us (13%)
  Pallas kernels  10.8 us (12%)
  local copies, waits for them, and re-layouts  5.61 us (6%)
  between operations  1.17 us (1%)
    ppermute x2, waiting for transfers between devices, advect_kernel_call(): lax.ppermute(message, 'tiles', pairs)  16.7 us
    dot_general x16, matrix products, collide(): jnp.dot(table, iterate.astype(jnp.bfloat16), preferred_element_type=jnp.f...  12.7 us
    pallas_call x1, Pallas kernels, advect_kernel_call(): pl.pallas_call(functools.partial(advect_kernel, section_weights), out_sha...  7.89 us
    ppermute x2, waiting for transfers between devices, paired_collision(): arrived = lax.ppermute(away[:, chunk], 'bins', swap)  6.41 us
    ppermute x2, starting transfers between devices, advect_kernel_call(): lax.ppermute(message, 'tiles', pairs)  6.26 us
    ppermute x2, waiting for transfers between devices, paired_collision(): returned.append(lax.ppermute(change[local_bins:], 'bins', swap))  5.38 us
    add x6, other arithmetic, collide(): iterate + collision_rate * products[all_bins:] * products[:all_bins]  3.85 us
    ppermute x2, starting transfers between devices, paired_collision(): returned.append(lax.ppermute(change[local_bins:], 'bins', swap))  3.12 us
  transfers between devices with their start and end apart: 8, of which 7 were waited for; matrix products, arithmetic and copies ran while one was open for 22% of the time, Pallas kernels for 0%

profile of v12, /device:TPU:0, one launch (start us, length us, event | category | flops | bytes accessed | tf_op | source)
XLA Modules:
  0.0 91.4 jit_solution(202398968901253664)
XLA Ops:
  0.7 1.4 %compare_select_fusion = (f32[4,8,128]{2,1,0:T(8,128)}, f32[4,8,128]{2,1,0:T(8,128)}) fusion(f32[4,8,128]{2,1,0:T(8,128)} %param.14, s32[4,128]{1,0:T(4,128)} %param.17, s32[8]{0:T(128)S(1)} %iota_add_fusion, f32[4,8,128]{2,1,0:T(8,128)} %param.13), kind=kLoop, calls=%fused_computation.121 | loop fusion | flops 12288 | bytes 67616 | tf_op jit(solution)/shard_map/mul | solution.py:232
  2.1 3.0 %shard_map.139 = (bf16[136,3,8,128]{3,2,1,0:T(8,128)(2,1)}, bf16[136,3,8,128]{3,2,1,0:T(8,128)(2,1)}) custom-call(f32[132,4,8,128]{3,2,1,0:T(8,128)} %q_ref.3, f32[4,8,128]{2,1,0:T(8,128)} %get-tuple-element.38.wx_ref.refs_8_, f32[4,8,128]{2,1,0:T(8,128)} %get-tuple-element.37.wy_ref.refs_9_), custom_call_target="tpu_custom_call" | custom-call | tf_op jit(solution)/shard_map/pallas_call | solution.py:48
  5.1 5.0 %collective-permute-start = (bf16[136,3,8,128]{3,2,1,0:T(8,128)(2,1)}, bf16[136,3,8,128]{3,2,1,0:T(8,128)(2,1)S(1)}, u32[]{:S(2)}, u32[]{:S(2)}) collective-permute-start(bf16[136,3,8,128]{3,2,1,0:T(8,128)(2,1)} %get-tuple-element.11), channel_id=1, source_target_pairs={{0,4},{4,8},{8,12},{1,5},{5,9},{9,13},{2,6},{6,10},{10,14},{3,7},{... | collective-permute-start | bytes 2506760 | tf_op jit(solution)/shard_map/ppermute | solution.py:95
  10.0 1.3 %collective-permute-start.1 = (bf16[136,3,8,128]{3,2,1,0:T(8,128)(2,1)}, bf16[136,3,8,128]{3,2,1,0:T(8,128)(2,1)S(1)}, u32[]{:S(2)}, u32[]{:S(2)}) collective-permute-start(bf16[136,3,8,128]{3,2,1,0:T(8,128)(2,1)} %get-tuple-element.13), channel_id=1, source_target_pairs={{4,0},{8,4},{12,8},{5,1},{9,5},{13,9},{6,2},{10,6},{14,10},{7,3},{... | collective-permute-start | bytes 2506760 | tf_op jit(solution)/shard_map/ppermute | solution.py:95
  11.9 2.0 %multiply_reduce_fusion = f32[264,8,33]{0,2,1:T(8,128)S(1)} fusion(f32[264,8]{0,1:T(8,128)S(1)} %fusion.66, f32[8,8,33,33]{3,1,2,0:T(8,128)S(1)} %fusion.57, s32[264]{0:T(512)S(1)} %get-tuple-element.35), kind=kOutput, calls=%fused_computation | convolution fusion | flops 221851072 | bytes 567072 | tf_op jit(solution)/shard_map/bm,acmn->bacn/dot_general | solution.py:150
  14.2 1.1 %fusion.4 = bf16[264,264]{0,1:T(8,128)(2,1)S(1)} fusion(f32[264,8,33]{0,2,1:T(8,128)S(1)} %multiply_reduce_fusion, f32[264,8]{0,1:T(8,128)S(1)} %fusion.66, f32[264,33]{0,1:T(8,128)S(1)} %fusion.54), kind=kOutput, calls=%fused_computation.17 | convolution fusion | flops 220936320 | bytes 461472 | tf_op jit(solution)/shard_map/bcn,dc,dn->bd/dot_general | solution.py:152
  15.5 12.6 %collective-permute-done.left_ref.refs_0_.refs_1_.refs_2_.refs_3_ = bf16[136,3,8,128]{3,2,1,0:T(8,128)(2,1)S(1)} collective-permute-done((bf16[136,3,8,128]{3,2,1,0:T(8,128)(2,1)}, bf16[136,3,8,128]{3,2,1,0:T(8,128)(2,1)S(1)}, u32[]{:S(2)}, u32[]{:S(2)}) %collective-permute-start) | collective-permute-done | bytes 835616 | tf_op jit(solution)/shard_map/ppermute | solution.py:95
  28.1 4.1 %collective-permute-done.1.right_ref.refs_4_.refs_5_.refs_6_.refs_7_ = bf16[136,3,8,128]{3,2,1,0:T(8,128)(2,1)S(1)} collective-permute-done((bf16[136,3,8,128]{3,2,1,0:T(8,128)(2,1)}, bf16[136,3,8,128]{3,2,1,0:T(8,128)(2,1)S(1)}, u32[]{:S(2)}, u32[]{:S(2)}) %collective-permute-start.1) | collective-permute-done | bytes 835616 | tf_op jit(solution)/shard_map/ppermute | solution.py:95
  32.2 1.0 %copy-done.3 = bf16[136,3,8,128]{3,2,1,0:T(8,128)(2,1)} copy-done((bf16[136,3,8,128]{3,2,1,0:T(8,128)(2,1)}, bf16[136,3,8,128]{3,2,1,0:T(8,128)(2,1)S(1)}, u32[]{:S(2)}) %copy-start.3) | copy-done | bytes 835608
  33.2 7.9 %shard_map.140 = (f32[132,4,8,128]{3,2,1,0:T(8,128)}, f32[132,4,1,128]{3,2,1,0:T(1,128)}) custom-call(f32[132,4,8,128]{3,2,1,0:T(8,128)} %q_ref.3, bf16[136,3,8,128]{3,2,1,0:T(8,128)(2,1)} %copy-done.2, bf16[136,3,8,128]{3,2,1,0:T(8,128)(2,1)} %copy-done.3, bf16[136,3,8,128]{3,2,1,0:T(8,128)(2,1)} %copy-done.2, bf16[136,3,8,128]{3,2,1,0:T(8,128)(2,1)} %copy-done.2, ...), custom_call_target="tpu_custom_call" | custom-call | flops 43253760 | bytes 10813440 | tf_op jit(solution)/shard_map/pallas_call | solution.py:108
  41.0 1.3 %collective-permute-start.2 = (f32[132,4,1,128]{3,2,1,0:T(1,128)}, f32[132,4,1,128]{3,2,1,0:T(1,128)S(1)}, u32[]{:S(2)}, u32[]{:S(2)}) collective-permute-start(f32[132,4,1,128]{3,2,1,0:T(1,128)} %get-tuple-element.15), channel_id=1, source_target_pairs={{1,0},{3,2},{5,4},{7,6},{9,8},{11,10},{13,12},{15,14},{17,16},{19,... | collective-permute-start | bytes 811016 | tf_op jit(solution)/shard_map/ppermute | solution.py:123
  42.4 2.0 %slice.137 = f32[132,4,7,128]{3,2,1,0:T(8,128)S(1)} slice(f32[132,4,8,128]{3,2,1,0:T(8,128)} %get-tuple-element.14), slice={[0:132], [0:4], [1:8], [0:128]} | slice | bytes 3784704 | tf_op jit(solution)/shard_map/slice | solution.py:249
  44.7 1.3 %multiply_reduce_fusion.1 = (f32[4,8,128]{2,1,0:T(8,128)S(1)}, f32[4,8,128]{2,1,0:T(8,128)S(1)}, f32[132,4,8,128]{3,2,1,0:T(8,128)S(1)}) fusion(f32[132]{0:T(256)S(1)} %get-tuple-element.40, f32[132]{0:T(256)S(1)} %copy-done.11, f32[132,4,1,128]{3,2,1,0:T(1,128)S(1)} %collective-permute-done.2, f32[132,4,7,128]{3,2,1,0:T(8,128)S(1)} %slice.137, ...), kind=kLoop, calls=%fused_computation.6 | loop fusion | flops 4317184 | bytes 6522944 | tf_op jit(solution)/shard_map/reduce_sum | solution.py:255
  46.0 1.6 %collective-permute-start.3 = (f32[2,4,8,128]{3,2,1,0:T(8,128)S(1)}, f32[2,4,8,128]{3,2,1,0:T(8,128)S(1)}, u32[]{:S(2)}, u32[]{:S(2)}) collective-permute-start(f32[2,4,8,128]{3,2,1,0:T(8,128)S(1)} %pad_maximum_fusion.6), channel_id=1, source_target_pairs={{0,2},{2,0},{1,3},{3,1},{4,6},{6,4},{5,7},{7,5},{8,10},{10,8},{9,1... | collective-permute-start | bytes 98312 | tf_op jit(solution)/shard_map/ppermute | solution.py:260
  47.5 2.7 %collective-permute-done.3 = f32[2,4,8,128]{3,2,1,0:T(8,128)S(1)} collective-permute-done((f32[2,4,8,128]{3,2,1,0:T(8,128)S(1)}, f32[2,4,8,128]{3,2,1,0:T(8,128)S(1)}, u32[]{:S(2)}, u32[]{:S(2)}) %collective-permute-start.3) | collective-permute-done | bytes 32800 | tf_op jit(solution)/shard_map/ppermute | solution.py:260
  50.2 0.6 fusion.62
  51.4 0.8 slice_bitcast_fusion.2
  52.2 1.5 %collective-permute-start.4 = (bf16[132,8,128]{2,1,0:T(8,128)(2,1)}, bf16[132,8,128]{2,1,0:T(8,128)(2,1)S(1)}, u32[]{:S(2)}, u32[]{:S(2)}) collective-permute-start(bf16[132,8,128]{2,1,0:T(8,128)(2,1)} %get-tuple-element.32), channel_id=1, source_target_pairs={{0,2},{2,0},{1,3},{3,1},{4,6},{6,4},{5,7},{7,5},{8,10},{10,8},{9,1... | collective-permute-start | bytes 811016 | tf_op jit(solution)/shard_map/ppermute | solution.py:200
  53.9 0.8 copy-done.5
  55.4 6.4 %collective-permute-done.4 = bf16[132,8,128]{2,1,0:T(8,128)(2,1)S(1)} collective-permute-done((bf16[132,8,128]{2,1,0:T(8,128)(2,1)}, bf16[132,8,128]{2,1,0:T(8,128)(2,1)S(1)}, u32[]{:S(2)}, u32[]{:S(2)}) %collective-permute-start.4) | collective-permute-done | bytes 270368 | tf_op jit(solution)/shard_map/ppermute | solution.py:200
  61.9 0.8 fusion.53
  62.6 0.8 fusion.47
  63.5 0.5 fusion.20
  64.0 0.8 fusion.45
  64.8 0.8 fusion.43
  65.6 0.7 fusion.18
  66.3 0.8 fusion.41
  67.1 0.8 fusion.39
  67.9 0.6 fusion.16
  68.5 0.8 fusion.37
  69.3 0.8 fusion.35
  70.1 0.7 fusion.5
  70.9 1.6 %collective-permute-start.6 = (bf16[132,8,128]{2,1,0:T(8,128)(2,1)S(1)}, bf16[132,8,128]{2,1,0:T(8,128)(2,1)S(1)}, u32[]{:S(2)}, u32[]{:S(2)}) collective-permute-start(bf16[132,8,128]{2,1,0:T(8,128)(2,1)S(1)} %slice.225), channel_id=1, source_target_pairs={{0,2},{2,0},{1,3},{3,1},{4,6},{6,4},{5,7},{7,5},{8,10},{10,8},{9,1... | collective-permute-start | bytes 811016 | tf_op jit(solution)/shard_map/ppermute | solution.py:207
  72.6 0.8 fusion.52
  73.3 0.8 fusion.33
  74.7 0.8 fusion.31
  75.5 0.8 fusion.29
  76.4 0.9 fusion.11
  77.3 0.6 collective-permute-done.6
  77.8 0.8 fusion.27
  78.6 0.8 fusion.25
  79.4 0.6 fusion.9
  80.0 0.8 fusion.23
  80.8 0.8 fusion.21
  81.6 0.7 fusion.6
  82.5 1.6 %collective-permute-start.7 = (bf16[132,8,128]{2,1,0:T(8,128)(2,1)S(1)}, bf16[132,8,128]{2,1,0:T(8,128)(2,1)S(1)}, u32[]{:S(2)}, u32[]{:S(2)}) collective-permute-start(bf16[132,8,128]{2,1,0:T(8,128)(2,1)S(1)} %slice.227), channel_id=1, source_target_pairs={{0,2},{2,0},{1,3},{3,1},{4,6},{6,4},{5,7},{7,5},{8,10},{10,8},{9,1... | collective-permute-start | bytes 811016 | tf_op jit(solution)/shard_map/ppermute | solution.py:207
  84.2 4.8 %collective-permute-done.7 = bf16[132,8,128]{2,1,0:T(8,128)(2,1)S(1)} collective-permute-done((bf16[132,8,128]{2,1,0:T(8,128)(2,1)S(1)}, bf16[132,8,128]{2,1,0:T(8,128)(2,1)S(1)}, u32[]{:S(2)}, u32[]{:S(2)}) %collective-permute-start.7) | collective-permute-done | bytes 270368 | tf_op jit(solution)/shard_map/ppermute | solution.py:207
  89.5 1.8 %fusion.1 = f32[132,4,8,128]{3,2,1,0:T(8,128)} fusion(bf16[132,4,8,128]{3,2,1,0:T(8,128)(2,1)S(1)} %bitcast.128, f32[132,4,8,128]{3,2,1,0:T(8,128)S(1)} %get-tuple-element.23, f32[4,8,128]{2,1,0:T(8,128)S(1)} %compare_convert_fusion, f32[4,8,128]{2,1,0:T(8,128)S(1)} %get-tuple-element.22, f32[132]{0:T(256)S(1)} %get-tuple-element.39), kind=kLoop, calls=%fused_computation.4 | loop fusion | flops 3244032 | bytes 5440016 | tf_op jit(solution)/shard_map/mul | solution.py:272
  (66 shorter events, 4.3 us)
Async XLA Ops:
  0.6 10.9 %copy-start = (bf16[4,33,33]{2,0,1:T(4,128)(2,1)S(1)}, bf16[4,33,33]{2,0,1:T(4,128)(2,1)}, u32[]{:S(2)}) copy-start(bf16[4,33,33]{2,0,1:T(4,128)(2,1)} %param.23) | copy-start | bytes 26140
  2.1 9.2 %copy-start.12 = (s32[264]{0:T(512)S(1)}, s32[264]{0:T(512)}, u32[]{:S(2)}) copy-start(s32[264]{0:T(512)} %param.21) | copy-start | bytes 3172
  2.1 9.4 %copy-start.9 = (s32[8,8]{1,0:T(8,128)S(1)}, s32[8,8]{1,0:T(8,128)}, u32[]{:S(2)}) copy-start(s32[8,8]{1,0:T(8,128)} %param.22) | copy-start | bytes 772
  5.1 23.1 %collective-permute-start = (bf16[136,3,8,128]{3,2,1,0:T(8,128)(2,1)}, bf16[136,3,8,128]{3,2,1,0:T(8,128)(2,1)S(1)}, u32[]{:S(2)}, u32[]{:S(2)}) collective-permute-start(bf16[136,3,8,128]{3,2,1,0:T(8,128)(2,1)} %get-tuple-element.11), channel_id=1, source_target_pairs={{0,4},{4,8},{8,12},{1,5},{5,9},{9,13},{2,6},{6,10},{10,14},{3,7},{... | collective-permute-start | bytes 2506760 | tf_op jit(solution)/shard_map/ppermute | solution.py:95
  10.0 22.2 %collective-permute-start.1 = (bf16[136,3,8,128]{3,2,1,0:T(8,128)(2,1)}, bf16[136,3,8,128]{3,2,1,0:T(8,128)(2,1)S(1)}, u32[]{:S(2)}, u32[]{:S(2)}) collective-permute-start(bf16[136,3,8,128]{3,2,1,0:T(8,128)(2,1)} %get-tuple-element.13), channel_id=1, source_target_pairs={{4,0},{8,4},{12,8},{5,1},{9,5},{13,9},{6,2},{10,6},{14,10},{7,3},{... | collective-permute-start | bytes 2506760 | tf_op jit(solution)/shard_map/ppermute | solution.py:95
  15.5 26.9 %copy-start.10 = (f32[132]{0:T(256)S(1)}, f32[132]{0:T(256)}, u32[]{:S(2)}) copy-start(f32[132]{0:T(256)} %param.18) | copy-start | bytes 1588
  15.5 26.9 %copy-start.11 = (f32[132]{0:T(256)S(1)}, f32[132]{0:T(256)}, u32[]{:S(2)}) copy-start(f32[132]{0:T(256)} %param.19) | copy-start | bytes 1588
  15.5 26.9 %copy-start.13 = (f32[132]{0:T(256)S(1)}, f32[132]{0:T(256)}, u32[]{:S(2)}) copy-start(f32[132]{0:T(256)} %param.20) | copy-start | bytes 1588
  28.1 4.1 %copy-start.2 = (bf16[136,3,8,128]{3,2,1,0:T(8,128)(2,1)}, bf16[136,3,8,128]{3,2,1,0:T(8,128)(2,1)S(1)}, u32[]{:S(2)}) copy-start(bf16[136,3,8,128]{3,2,1,0:T(8,128)(2,1)S(1)} %collective-permute-done.left_ref.refs_0_.refs_1_.refs_2_.refs_3_) | copy-start | bytes 2506756
  32.2 1.0 %copy-start.3 = (bf16[136,3,8,128]{3,2,1,0:T(8,128)(2,1)}, bf16[136,3,8,128]{3,2,1,0:T(8,128)(2,1)S(1)}, u32[]{:S(2)}) copy-start(bf16[136,3,8,128]{3,2,1,0:T(8,128)(2,1)S(1)} %collective-permute-done.1.right_ref.refs_4_.refs_5_.refs_6_.refs_7_) | copy-start | bytes 2506756
  41.0 3.6 %collective-permute-start.2 = (f32[132,4,1,128]{3,2,1,0:T(1,128)}, f32[132,4,1,128]{3,2,1,0:T(1,128)S(1)}, u32[]{:S(2)}, u32[]{:S(2)}) collective-permute-start(f32[132,4,1,128]{3,2,1,0:T(1,128)} %get-tuple-element.15), channel_id=1, source_target_pairs={{1,0},{3,2},{5,4},{7,6},{9,8},{11,10},{13,12},{15,14},{17,16},{19,... | collective-permute-start | bytes 811016 | tf_op jit(solution)/shard_map/ppermute | solution.py:123
  42.4 2.3 %copy-start.4 = (f32[132,4,8,128]{3,2,1,0:T(8,128)S(1)}, f32[132,4,8,128]{3,2,1,0:T(8,128)}, u32[]{:S(2)}) copy-start(f32[132,4,8,128]{3,2,1,0:T(8,128)} %get-tuple-element.14) | copy-start | bytes 6488068
  44.7 5.5 %copy-start.6 = (f32[4,8,128]{2,1,0:T(8,128)S(1)}, f32[4,8,128]{2,1,0:T(8,128)}, u32[]{:S(2)}) copy-start(f32[4,8,128]{2,1,0:T(8,128)} %param.16) | copy-start | bytes 49156
  44.7 5.5 %copy-start.7 = (f32[4,8,128]{2,1,0:T(8,128)S(1)}, f32[4,8,128]{2,1,0:T(8,128)}, u32[]{:S(2)}) copy-start(f32[4,8,128]{2,1,0:T(8,128)} %param.15) | copy-start | bytes 49156
  46.0 4.2 %collective-permute-start.3 = (f32[2,4,8,128]{3,2,1,0:T(8,128)S(1)}, f32[2,4,8,128]{3,2,1,0:T(8,128)S(1)}, u32[]{:S(2)}, u32[]{:S(2)}) collective-permute-start(f32[2,4,8,128]{3,2,1,0:T(8,128)S(1)} %pad_maximum_fusion.6), channel_id=1, source_target_pairs={{0,2},{2,0},{1,3},{3,1},{4,6},{6,4},{5,7},{7,5},{8,10},{10,8},{9,1... | collective-permute-start | bytes 98312 | tf_op jit(solution)/shard_map/ppermute | solution.py:260
  51.4 2.3 %copy-start.8 = (s32[4,128]{1,0:T(4,128)S(1)}, s32[4,128]{1,0:T(4,128)}, u32[]{:S(2)}) copy-start(s32[4,128]{1,0:T(4,128)} %param.17) | copy-start | bytes 6148
  52.2 9.5 %collective-permute-start.4 = (bf16[132,8,128]{2,1,0:T(8,128)(2,1)}, bf16[132,8,128]{2,1,0:T(8,128)(2,1)S(1)}, u32[]{:S(2)}, u32[]{:S(2)}) collective-permute-start(bf16[132,8,128]{2,1,0:T(8,128)(2,1)} %get-tuple-element.32), channel_id=1, source_target_pairs={{0,2},{2,0},{1,3},{3,1},{4,6},{6,4},{5,7},{7,5},{8,10},{10,8},{9,1... | collective-permute-start | bytes 811016 | tf_op jit(solution)/shard_map/ppermute | solution.py:200
  53.8 1.0 %copy-start.5 = (bf16[132,8,128]{2,1,0:T(8,128)(2,1)S(1)}, bf16[132,8,128]{2,1,0:T(8,128)(2,1)}, u32[]{:S(2)}) copy-start(bf16[132,8,128]{2,1,0:T(8,128)(2,1)} %get-tuple-element.33) | copy-start | bytes 811012
  54.8 17.7 %collective-permute-start.5 = (bf16[132,8,128]{2,1,0:T(8,128)(2,1)S(1)}, bf16[132,8,128]{2,1,0:T(8,128)(2,1)S(1)}, u32[]{:S(2)}, u32[]{:S(2)}) collective-permute-start(bf16[132,8,128]{2,1,0:T(8,128)(2,1)S(1)} %copy-done.5), channel_id=1, source_target_pairs={{0,2},{2,0},{1,3},{3,1},{4,6},{6,4},{5,7},{7,5},{8,10},{10,8},{9,1... | collective-permute-start | bytes 811016 | tf_op jit(solution)/shard_map/ppermute | solution.py:200
  70.9 6.9 %collective-permute-start.6 = (bf16[132,8,128]{2,1,0:T(8,128)(2,1)S(1)}, bf16[132,8,128]{2,1,0:T(8,128)(2,1)S(1)}, u32[]{:S(2)}, u32[]{:S(2)}) collective-permute-start(bf16[132,8,128]{2,1,0:T(8,128)(2,1)S(1)} %slice.225), channel_id=1, source_target_pairs={{0,2},{2,0},{1,3},{3,1},{4,6},{6,4},{5,7},{7,5},{8,10},{10,8},{9,1... | collective-permute-start | bytes 811016 | tf_op jit(solution)/shard_map/ppermute | solution.py:207
  82.5 6.5 %collective-permute-start.7 = (bf16[132,8,128]{2,1,0:T(8,128)(2,1)S(1)}, bf16[132,8,128]{2,1,0:T(8,128)(2,1)S(1)}, u32[]{:S(2)}, u32[]{:S(2)}) collective-permute-start(bf16[132,8,128]{2,1,0:T(8,128)(2,1)S(1)} %slice.227), channel_id=1, source_target_pairs={{0,2},{2,0},{1,3},{3,1},{4,6},{6,4},{5,7},{7,5},{8,10},{10,8},{9,1... | collective-permute-start | bytes 811016 | tf_op jit(solution)/shard_map/ppermute | solution.py:207
  89.5 1.9 %copy-start.1 = (bf16[4,33,33]{2,0,1:T(4,128)(2,1)S(1)}, bf16[4,33,33]{2,0,1:T(4,128)(2,1)}, u32[]{:S(2)}) copy-start(bf16[4,33,33]{2,0,1:T(4,128)(2,1)} %param.23) | copy-start | bytes 26140

commit v13 on v12

--- a/solution.py
+++ b/solution.py
@@ -64,24 +64,31 @@
         return [widened(rows[k])[0] + widened(rows[k + 2])[0] for k in (0, 1)]
 
     (wx_left, wy_left), (wx_right, wy_right) = winds(left_winds), winds(right_winds)
-    field = jnp.concatenate([widened(left_ref), q_ref[...], widened(right_ref)], axis=1)
     wx = jnp.concatenate([wx_left, wx_ref[...], wx_right], axis=0)
     wy = jnp.concatenate([wy_left, wy_ref[...], wy_right], axis=0)
-    section = field
-    for stage, weight_now in enumerate(weights, start=1):
-        span = width + 2 * (depth - stage)
-        center = section[:, 1 : 1 + span]
-        west = section[:, 0:span]
-        east = section[:, 2 : 2 + span]
-        south = pltpu.roll(center, 1, 3)
-        north = pltpu.roll(center, center.shape[3] - 1, 3)
-        wind_a = wx[stage : stage + span]
-        wind_b = wy[stage : stage + span]
-        along_x = wind_a * jnp.where(wind_a > 0.0, center - west, east - center)
-        along_y = wind_b * jnp.where(wind_b > 0.0, center - south, north - center)
-        section = field[:, stage : stage + span] + weight_now * (-along_x - along_y)
-    out_ref[...] = section
-    bottom_ref[...] = section[:, :, :1]
+
+    def one_bin(b, carry):
+        field = jnp.concatenate(
+            [left_ref[b].astype(jnp.float32), q_ref[b], right_ref[b].astype(jnp.float32)], axis=0
+        )
+        section = field
+        for stage, weight_now in enumerate(weights, start=1):
+            span = width + 2 * (depth - stage)
+            center = section[1 : 1 + span]
+            west = section[0:span]
+            east = section[2 : 2 + span]
+            south = pltpu.roll(center, 1, 2)
+            north = pltpu.roll(center, center.shape[2] - 1, 2)
+            wind_a = wx[stage : stage + span]
+            wind_b = wy[stage : stage + span]
+            along_x = wind_a * jnp.where(wind_a > 0.0, center - west, east - center)
+            along_y = wind_b * jnp.where(wind_b > 0.0, center - south, north - center)
+            section = field[stage : stage + span] + weight_now * (-along_x - along_y)
+        out_ref[b] = section
+        bottom_ref[b] = section[:, :1]
+        return carry
+
+    lax.fori_loop(0, q_ref.shape[0], one_bin, 0)
 
 
 def advect_kernel_call(bin_mass, wind_x, wind_y, section_weights, tie):

time: 91.7 us -> 117 us (1.28)
  Pallas kernels: 10.8 us -> 36.3 us
    pallas_call x1, Pallas kernels: 7.89 us -> 33.3 us  [advect_kernel_call(): pl.pallas_call(functools.partial(advect_kernel, section_weights), out_sha...]
  transfers between devices with their start and end apart: 8 -> 8, of which waited for: 7 -> 7; matrix products, arithmetic and copies ran while one was open for 22% -> 17% of each run, Pallas kernels for 0% -> 0%
where the time goes in v13:
time: 117 us
  Pallas kernels  36.3 us (31%)
  waiting for transfers between devices  31.4 us (27%)
  matrix products  16.4 us (14%)
  starting transfers between devices  14.2 us (12%)
  other arithmetic  11.7 us (10%)
  local copies, waits for them, and re-layouts  5.61 us (5%)
  between operations  1.17 us (1%)
    pallas_call x1, Pallas kernels, advect_kernel_call(): pl.pallas_call(functools.partial(advect_kernel, section_weights), out_sha...  33.3 us
    ppermute x2, waiting for transfers between devices, advect_kernel_call(): lax.ppermute(message, 'tiles', pairs)  16.7 us
    dot_general x16, matrix products, collide(): jnp.dot(table, iterate.astype(jnp.bfloat16), preferred_element_type=jnp.f...  12.6 us
    ppermute x2, waiting for transfers between devices, paired_collision(): arrived = lax.ppermute(away[:, chunk], 'bins', swap)  6.41 us
    ppermute x2, starting transfers between devices, advect_kernel_call(): lax.ppermute(message, 'tiles', pairs)  6.26 us
    ppermute x2, waiting for transfers between devices, paired_collision(): returned.append(lax.ppermute(change[local_bins:], 'bins', swap))  5.41 us
    add x6, other arithmetic, collide(): iterate + collision_rate * products[all_bins:] * products[:all_bins]  3.85 us
    ppermute x2, starting transfers between devices, paired_collision(): returned.append(lax.ppermute(change[local_bins:], 'bins', swap))  3.11 us
  transfers between devices with their start and end apart: 8, of which 7 were waited for; matrix products, arithmetic and copies ran while one was open for 17% of the time, Pallas kernels for 0%

profile of v13, /device:TPU:0, one launch (start us, length us, event | category | flops | bytes accessed | tf_op | source)
XLA Modules:
  0.0 116.8 jit_solution(15048498734293419149)
XLA Ops:
  0.7 1.4 %compare_select_fusion = (f32[4,8,128]{2,1,0:T(8,128)}, f32[4,8,128]{2,1,0:T(8,128)}) fusion(f32[4,8,128]{2,1,0:T(8,128)} %param.14, s32[4,128]{1,0:T(4,128)} %param.17, s32[8]{0:T(128)S(1)} %iota_add_fusion, f32[4,8,128]{2,1,0:T(8,128)} %param.13), kind=kLoop, calls=%fused_computation.121 | loop fusion | flops 12288 | bytes 67616 | tf_op jit(solution)/shard_map/mul | solution.py:239
  2.1 3.0 %shard_map.139 = (bf16[136,3,8,128]{3,2,1,0:T(8,128)(2,1)}, bf16[136,3,8,128]{3,2,1,0:T(8,128)(2,1)}) custom-call(f32[132,4,8,128]{3,2,1,0:T(8,128)} %q_ref.3, f32[4,8,128]{2,1,0:T(8,128)} %get-tuple-element.38.wx_ref.refs_8_, f32[4,8,128]{2,1,0:T(8,128)} %get-tuple-element.37.wy_ref.refs_9_), custom_call_target="tpu_custom_call" | custom-call | tf_op jit(solution)/shard_map/pallas_call | solution.py:48
  5.1 5.0 %collective-permute-start = (bf16[136,3,8,128]{3,2,1,0:T(8,128)(2,1)}, bf16[136,3,8,128]{3,2,1,0:T(8,128)(2,1)S(1)}, u32[]{:S(2)}, u32[]{:S(2)}) collective-permute-start(bf16[136,3,8,128]{3,2,1,0:T(8,128)(2,1)} %get-tuple-element.11), channel_id=1, source_target_pairs={{0,4},{4,8},{8,12},{1,5},{5,9},{9,13},{2,6},{6,10},{10,14},{3,7},{... | collective-permute-start | bytes 2506760 | tf_op jit(solution)/shard_map/ppermute | solution.py:102
  10.0 1.3 %collective-permute-start.1 = (bf16[136,3,8,128]{3,2,1,0:T(8,128)(2,1)}, bf16[136,3,8,128]{3,2,1,0:T(8,128)(2,1)S(1)}, u32[]{:S(2)}, u32[]{:S(2)}) collective-permute-start(bf16[136,3,8,128]{3,2,1,0:T(8,128)(2,1)} %get-tuple-element.13), channel_id=1, source_target_pairs={{4,0},{8,4},{12,8},{5,1},{9,5},{13,9},{6,2},{10,6},{14,10},{7,3},{... | collective-permute-start | bytes 2506760 | tf_op jit(solution)/shard_map/ppermute | solution.py:102
  11.9 2.0 %multiply_reduce_fusion = f32[264,8,33]{0,2,1:T(8,128)S(1)} fusion(f32[264,8]{0,1:T(8,128)S(1)} %fusion.66, f32[8,8,33,33]{3,1,2,0:T(8,128)S(1)} %fusion.57, s32[264]{0:T(512)S(1)} %get-tuple-element.35), kind=kOutput, calls=%fused_computation | convolution fusion | flops 221851072 | bytes 567072 | tf_op jit(solution)/shard_map/bm,acmn->bacn/dot_general | solution.py:157
  14.2 1.1 fusion.4
  15.5 12.6 %collective-permute-done.left_ref.refs_0_.refs_1_.refs_2_.refs_3_ = bf16[136,3,8,128]{3,2,1,0:T(8,128)(2,1)S(1)} collective-permute-done((bf16[136,3,8,128]{3,2,1,0:T(8,128)(2,1)}, bf16[136,3,8,128]{3,2,1,0:T(8,128)(2,1)S(1)}, u32[]{:S(2)}, u32[]{:S(2)}) %collective-permute-start) | collective-permute-done | bytes 835616 | tf_op jit(solution)/shard_map/ppermute | solution.py:102
  28.1 4.1 %collective-permute-done.1.right_ref.refs_4_.refs_5_.refs_6_.refs_7_ = bf16[136,3,8,128]{3,2,1,0:T(8,128)(2,1)S(1)} collective-permute-done((bf16[136,3,8,128]{3,2,1,0:T(8,128)(2,1)}, bf16[136,3,8,128]{3,2,1,0:T(8,128)(2,1)S(1)}, u32[]{:S(2)}, u32[]{:S(2)}) %collective-permute-start.1) | collective-permute-done | bytes 835616 | tf_op jit(solution)/shard_map/ppermute | solution.py:102
  32.2 1.0 copy-done.3
  33.2 33.3 %shard_map.140 = (f32[132,4,8,128]{3,2,1,0:T(8,128)}, f32[132,4,1,128]{3,2,1,0:T(1,128)}) custom-call(f32[132,4,8,128]{3,2,1,0:T(8,128)} %q_ref.3, bf16[136,3,8,128]{3,2,1,0:T(8,128)(2,1)} %copy-done.2, bf16[136,3,8,128]{3,2,1,0:T(8,128)(2,1)} %copy-done.3, bf16[136,3,8,128]{3,2,1,0:T(8,128)(2,1)} %copy-done.2, bf16[136,3,8,128]{3,2,1,0:T(8,128)(2,1)} %copy-done.2, ...), custom_call_target="tpu_custom_call" | custom-call | flops 43253760 | bytes 10813440 | tf_op jit(solution)/shard_map/pallas_call | solution.py:115
  66.5 1.3 %collective-permute-start.2 = (f32[132,4,1,128]{3,2,1,0:T(1,128)}, f32[132,4,1,128]{3,2,1,0:T(1,128)S(1)}, u32[]{:S(2)}, u32[]{:S(2)}) collective-permute-start(f32[132,4,1,128]{3,2,1,0:T(1,128)} %get-tuple-element.15), channel_id=1, source_target_pairs={{1,0},{3,2},{5,4},{7,6},{9,8},{11,10},{13,12},{15,14},{17,16},{19,... | collective-permute-start | bytes 811016 | tf_op jit(solution)/shard_map/ppermute | solution.py:130
  67.8 2.0 %slice.137 = f32[132,4,7,128]{3,2,1,0:T(8,128)S(1)} slice(f32[132,4,8,128]{3,2,1,0:T(8,128)} %get-tuple-element.14), slice={[0:132], [0:4], [1:8], [0:128]} | slice | bytes 3784704 | tf_op jit(solution)/shard_map/slice | solution.py:256
  70.1 1.3 %multiply_reduce_fusion.1 = (f32[4,8,128]{2,1,0:T(8,128)S(1)}, f32[4,8,128]{2,1,0:T(8,128)S(1)}, f32[132,4,8,128]{3,2,1,0:T(8,128)S(1)}) fusion(f32[132]{0:T(256)S(1)} %get-tuple-element.40, f32[132]{0:T(256)S(1)} %copy-done.11, f32[132,4,1,128]{3,2,1,0:T(1,128)S(1)} %collective-permute-done.2, f32[132,4,7,128]{3,2,1,0:T(8,128)S(1)} %slice.137, ...), kind=kLoop, calls=%fused_computation.6 | loop fusion | flops 4317184 | bytes 6522944 | tf_op jit(solution)/shard_map/reduce_sum | solution.py:262
  71.4 1.6 %collective-permute-start.3 = (f32[2,4,8,128]{3,2,1,0:T(8,128)S(1)}, f32[2,4,8,128]{3,2,1,0:T(8,128)S(1)}, u32[]{:S(2)}, u32[]{:S(2)}) collective-permute-start(f32[2,4,8,128]{3,2,1,0:T(8,128)S(1)} %pad_maximum_fusion.6), channel_id=1, source_target_pairs={{0,2},{2,0},{1,3},{3,1},{4,6},{6,4},{5,7},{7,5},{8,10},{10,8},{9,1... | collective-permute-start | bytes 98312 | tf_op jit(solution)/shard_map/ppermute | solution.py:267
  73.0 2.7 %collective-permute-done.3 = f32[2,4,8,128]{3,2,1,0:T(8,128)S(1)} collective-permute-done((f32[2,4,8,128]{3,2,1,0:T(8,128)S(1)}, f32[2,4,8,128]{3,2,1,0:T(8,128)S(1)}, u32[]{:S(2)}, u32[]{:S(2)}) %collective-permute-start.3) | collective-permute-done | bytes 32800 | tf_op jit(solution)/shard_map/ppermute | solution.py:267
  75.6 0.6 fusion.62
  76.8 0.8 slice_bitcast_fusion.2
  77.7 1.5 %collective-permute-start.4 = (bf16[132,8,128]{2,1,0:T(8,128)(2,1)}, bf16[132,8,128]{2,1,0:T(8,128)(2,1)S(1)}, u32[]{:S(2)}, u32[]{:S(2)}) collective-permute-start(bf16[132,8,128]{2,1,0:T(8,128)(2,1)} %get-tuple-element.32), channel_id=1, source_target_pairs={{0,2},{2,0},{1,3},{3,1},{4,6},{6,4},{5,7},{7,5},{8,10},{10,8},{9,1... | collective-permute-start | bytes 811016 | tf_op jit(solution)/shard_map/ppermute | solution.py:207
  79.4 0.8 copy-done.5
  80.8 6.4 %collective-permute-done.4 = bf16[132,8,128]{2,1,0:T(8,128)(2,1)S(1)} collective-permute-done((bf16[132,8,128]{2,1,0:T(8,128)(2,1)}, bf16[132,8,128]{2,1,0:T(8,128)(2,1)S(1)}, u32[]{:S(2)}, u32[]{:S(2)}) %collective-permute-start.4) | collective-permute-done | bytes 270368 | tf_op jit(solution)/shard_map/ppermute | solution.py:207
  87.3 0.8 fusion.53
  88.1 0.8 fusion.47
  89.5 0.8 fusion.45
  90.2 0.8 fusion.43
  91.0 0.7 fusion.18
  91.7 0.8 fusion.41
  92.5 0.8 fusion.39
  93.3 0.6 fusion.16
  93.9 0.8 fusion.37
  94.7 0.8 fusion.35
  95.5 0.7 fusion.5
  96.3 1.6 %collective-permute-start.6 = (bf16[132,8,128]{2,1,0:T(8,128)(2,1)S(1)}, bf16[132,8,128]{2,1,0:T(8,128)(2,1)S(1)}, u32[]{:S(2)}, u32[]{:S(2)}) collective-permute-start(bf16[132,8,128]{2,1,0:T(8,128)(2,1)S(1)} %slice.225), channel_id=1, source_target_pairs={{0,2},{2,0},{1,3},{3,1},{4,6},{6,4},{5,7},{7,5},{8,10},{10,8},{9,1... | collective-permute-start | bytes 811016 | tf_op jit(solution)/shard_map/ppermute | solution.py:214
  98.0 0.8 fusion.52
  98.8 0.8 fusion.33
  99.6 0.5 fusion.13
  100.2 0.8 fusion.31
  100.9 0.8 fusion.29
  101.8 0.9 fusion.11
  102.7 0.6 collective-permute-done.6
  103.3 0.8 fusion.27
  104.0 0.8 fusion.25
  104.8 0.6 fusion.9
  105.4 0.8 fusion.23
  106.2 0.8 fusion.21
  107.0 0.7 fusion.6
  107.9 1.6 %collective-permute-start.7 = (bf16[132,8,128]{2,1,0:T(8,128)(2,1)S(1)}, bf16[132,8,128]{2,1,0:T(8,128)(2,1)S(1)}, u32[]{:S(2)}, u32[]{:S(2)}) collective-permute-start(bf16[132,8,128]{2,1,0:T(8,128)(2,1)S(1)} %slice.227), channel_id=1, source_target_pairs={{0,2},{2,0},{1,3},{3,1},{4,6},{6,4},{5,7},{7,5},{8,10},{10,8},{9,1... | collective-permute-start | bytes 811016 | tf_op jit(solution)/shard_map/ppermute | solution.py:214
  109.6 4.8 %collective-permute-done.7 = bf16[132,8,128]{2,1,0:T(8,128)(2,1)S(1)} collective-permute-done((bf16[132,8,128]{2,1,0:T(8,128)(2,1)S(1)}, bf16[132,8,128]{2,1,0:T(8,128)(2,1)S(1)}, u32[]{:S(2)}, u32[]{:S(2)}) %collective-permute-start.7) | collective-permute-done | bytes 270368 | tf_op jit(solution)/shard_map/ppermute | solution.py:214
  115.0 1.8 %fusion.1 = f32[132,4,8,128]{3,2,1,0:T(8,128)} fusion(bf16[132,4,8,128]{3,2,1,0:T(8,128)(2,1)S(1)} %bitcast.128, f32[132,4,8,128]{3,2,1,0:T(8,128)S(1)} %get-tuple-element.23, f32[4,8,128]{2,1,0:T(8,128)S(1)} %compare_convert_fusion, f32[4,8,128]{2,1,0:T(8,128)S(1)} %get-tuple-element.22, f32[132]{0:T(256)S(1)} %get-tuple-element.39), kind=kLoop, calls=%fused_computation.4 | loop fusion | flops 3244032 | bytes 5440016 | tf_op jit(solution)/shard_map/mul | solution.py:279
  (66 shorter events, 4.3 us)
Async XLA Ops:
  0.6 10.9 %copy-start = (bf16[4,33,33]{2,0,1:T(4,128)(2,1)S(1)}, bf16[4,33,33]{2,0,1:T(4,128)(2,1)}, u32[]{:S(2)}) copy-start(bf16[4,33,33]{2,0,1:T(4,128)(2,1)} %param.23) | copy-start | bytes 26140
  2.1 9.2 %copy-start.12 = (s32[264]{0:T(512)S(1)}, s32[264]{0:T(512)}, u32[]{:S(2)}) copy-start(s32[264]{0:T(512)} %param.21) | copy-start | bytes 3172
  2.1 9.4 %copy-start.9 = (s32[8,8]{1,0:T(8,128)S(1)}, s32[8,8]{1,0:T(8,128)}, u32[]{:S(2)}) copy-start(s32[8,8]{1,0:T(8,128)} %param.22) | copy-start | bytes 772
  5.1 23.1 %collective-permute-start = (bf16[136,3,8,128]{3,2,1,0:T(8,128)(2,1)}, bf16[136,3,8,128]{3,2,1,0:T(8,128)(2,1)S(1)}, u32[]{:S(2)}, u32[]{:S(2)}) collective-permute-start(bf16[136,3,8,128]{3,2,1,0:T(8,128)(2,1)} %get-tuple-element.11), channel_id=1, source_target_pairs={{0,4},{4,8},{8,12},{1,5},{5,9},{9,13},{2,6},{6,10},{10,14},{3,7},{... | collective-permute-start | bytes 2506760 | tf_op jit(solution)/shard_map/ppermute | solution.py:102
  10.0 22.2 %collective-permute-start.1 = (bf16[136,3,8,128]{3,2,1,0:T(8,128)(2,1)}, bf16[136,3,8,128]{3,2,1,0:T(8,128)(2,1)S(1)}, u32[]{:S(2)}, u32[]{:S(2)}) collective-permute-start(bf16[136,3,8,128]{3,2,1,0:T(8,128)(2,1)} %get-tuple-element.13), channel_id=1, source_target_pairs={{4,0},{8,4},{12,8},{5,1},{9,5},{13,9},{6,2},{10,6},{14,10},{7,3},{... | collective-permute-start | bytes 2506760 | tf_op jit(solution)/shard_map/ppermute | solution.py:102
  15.5 52.3 %copy-start.10 = (f32[132]{0:T(256)S(1)}, f32[132]{0:T(256)}, u32[]{:S(2)}) copy-start(f32[132]{0:T(256)} %param.18) | copy-start | bytes 1588
  15.5 52.3 %copy-start.11 = (f32[132]{0:T(256)S(1)}, f32[132]{0:T(256)}, u32[]{:S(2)}) copy-start(f32[132]{0:T(256)} %param.19) | copy-start | bytes 1588
  15.5 52.3 %copy-start.13 = (f32[132]{0:T(256)S(1)}, f32[132]{0:T(256)}, u32[]{:S(2)}) copy-start(f32[132]{0:T(256)} %param.20) | copy-start | bytes 1588
  28.1 4.1 %copy-start.2 = (bf16[136,3,8,128]{3,2,1,0:T(8,128)(2,1)}, bf16[136,3,8,128]{3,2,1,0:T(8,128)(2,1)S(1)}, u32[]{:S(2)}) copy-start(bf16[136,3,8,128]{3,2,1,0:T(8,128)(2,1)S(1)} %collective-permute-done.left_ref.refs_0_.refs_1_.refs_2_.refs_3_) | copy-start | bytes 2506756
  32.2 1.0 copy-start.3
  66.5 3.6 %collective-permute-start.2 = (f32[132,4,1,128]{3,2,1,0:T(1,128)}, f32[132,4,1,128]{3,2,1,0:T(1,128)S(1)}, u32[]{:S(2)}, u32[]{:S(2)}) collective-permute-start(f32[132,4,1,128]{3,2,1,0:T(1,128)} %get-tuple-element.15), channel_id=1, source_target_pairs={{1,0},{3,2},{5,4},{7,6},{9,8},{11,10},{13,12},{15,14},{17,16},{19,... | collective-permute-start | bytes 811016 | tf_op jit(solution)/shard_map/ppermute | solution.py:130
  67.8 2.3 %copy-start.4 = (f32[132,4,8,128]{3,2,1,0:T(8,128)S(1)}, f32[132,4,8,128]{3,2,1,0:T(8,128)}, u32[]{:S(2)}) copy-start(f32[132,4,8,128]{3,2,1,0:T(8,128)} %get-tuple-element.14) | copy-start | bytes 6488068
  70.1 5.5 %copy-start.6 = (f32[4,8,128]{2,1,0:T(8,128)S(1)}, f32[4,8,128]{2,1,0:T(8,128)}, u32[]{:S(2)}) copy-start(f32[4,8,128]{2,1,0:T(8,128)} %param.16) | copy-start | bytes 49156
  70.1 5.5 %copy-start.7 = (f32[4,8,128]{2,1,0:T(8,128)S(1)}, f32[4,8,128]{2,1,0:T(8,128)}, u32[]{:S(2)}) copy-start(f32[4,8,128]{2,1,0:T(8,128)} %param.15) | copy-start | bytes 49156
  71.4 4.2 %collective-permute-start.3 = (f32[2,4,8,128]{3,2,1,0:T(8,128)S(1)}, f32[2,4,8,128]{3,2,1,0:T(8,128)S(1)}, u32[]{:S(2)}, u32[]{:S(2)}) collective-permute-start(f32[2,4,8,128]{3,2,1,0:T(8,128)S(1)} %pad_maximum_fusion.6), channel_id=1, source_target_pairs={{0,2},{2,0},{1,3},{3,1},{4,6},{6,4},{5,7},{7,5},{8,10},{10,8},{9,1... | collective-permute-start | bytes 98312 | tf_op jit(solution)/shard_map/ppermute | solution.py:267
  76.8 2.3 %copy-start.8 = (s32[4,128]{1,0:T(4,128)S(1)}, s32[4,128]{1,0:T(4,128)}, u32[]{:S(2)}) copy-start(s32[4,128]{1,0:T(4,128)} %param.17) | copy-start | bytes 6148
  77.7 9.5 %collective-permute-start.4 = (bf16[132,8,128]{2,1,0:T(8,128)(2,1)}, bf16[132,8,128]{2,1,0:T(8,128)(2,1)S(1)}, u32[]{:S(2)}, u32[]{:S(2)}) collective-permute-start(bf16[132,8,128]{2,1,0:T(8,128)(2,1)} %get-tuple-element.32), channel_id=1, source_target_pairs={{0,2},{2,0},{1,3},{3,1},{4,6},{6,4},{5,7},{7,5},{8,10},{10,8},{9,1... | collective-permute-start | bytes 811016 | tf_op jit(solution)/shard_map/ppermute | solution.py:207
  79.2 1.0 copy-start.5
  80.2 17.7 %collective-permute-start.5 = (bf16[132,8,128]{2,1,0:T(8,128)(2,1)S(1)}, bf16[132,8,128]{2,1,0:T(8,128)(2,1)S(1)}, u32[]{:S(2)}, u32[]{:S(2)}) collective-permute-start(bf16[132,8,128]{2,1,0:T(8,128)(2,1)S(1)} %copy-done.5), channel_id=1, source_target_pairs={{0,2},{2,0},{1,3},{3,1},{4,6},{6,4},{5,7},{7,5},{8,10},{10,8},{9,1... | collective-permute-start | bytes 811016 | tf_op jit(solution)/shard_map/ppermute | solution.py:207
  96.3 6.9 %collective-permute-start.6 = (bf16[132,8,128]{2,1,0:T(8,128)(2,1)S(1)}, bf16[132,8,128]{2,1,0:T(8,128)(2,1)S(1)}, u32[]{:S(2)}, u32[]{:S(2)}) collective-permute-start(bf16[132,8,128]{2,1,0:T(8,128)(2,1)S(1)} %slice.225), channel_id=1, source_target_pairs={{0,2},{2,0},{1,3},{3,1},{4,6},{6,4},{5,7},{7,5},{8,10},{10,8},{9,1... | collective-permute-start | bytes 811016 | tf_op jit(solution)/shard_map/ppermute | solution.py:214
  107.9 6.5 %collective-permute-start.7 = (bf16[132,8,128]{2,1,0:T(8,128)(2,1)S(1)}, bf16[132,8,128]{2,1,0:T(8,128)(2,1)S(1)}, u32[]{:S(2)}, u32[]{:S(2)}) collective-permute-start(bf16[132,8,128]{2,1,0:T(8,128)(2,1)S(1)} %slice.227), channel_id=1, source_target_pairs={{0,2},{2,0},{1,3},{3,1},{4,6},{6,4},{5,7},{7,5},{8,10},{10,8},{9,1... | collective-permute-start | bytes 811016 | tf_op jit(solution)/shard_map/ppermute | solution.py:214
  114.9 1.9 %copy-start.1 = (bf16[4,33,33]{2,0,1:T(4,128)(2,1)S(1)}, bf16[4,33,33]{2,0,1:T(4,128)(2,1)}, u32[]{:S(2)}) copy-start(bf16[4,33,33]{2,0,1:T(4,128)(2,1)} %param.23) | copy-start | bytes 26140

commit v14 on v10

--- a/solution.py
+++ b/solution.py
@@ -96,7 +96,7 @@
         for message, pairs in zip(rims(bin_mass, wind_x, wind_y, depth), (up, down))
     )
     left, tie = lax.optimization_barrier((left, tie))
-    block = max(d for d in range(1, 34) if local_bins % d == 0)
+    block = max(d for d in range(1, 13) if local_bins % d == 0)
     rim_spec = pl.BlockSpec((block, depth, width_z, width_y), lambda i: (i, 0, 0, 0))
     row_specs = [
         pl.BlockSpec((1, depth, width_z, width_y), lambda i, row=local_bins + k: (row, 0, 0, 0))

time: 91.6 us -> 94.6 us (1.033)
  Pallas kernels: 10.8 us -> 13.6 us
    pallas_call x1, Pallas kernels: 7.8 us -> 10.6 us  [advect_kernel_call(): pl.pallas_call(functools.partial(advect_kernel, section_weights), out_sha...]
  transfers between devices with their start and end apart: 8 -> 8, of which waited for: 7 -> 7; matrix products, arithmetic and copies ran while one was open for 22% -> 21% of each run, Pallas kernels for 0% -> 0%
where the time goes in v14:
time: 94.6 us; the launch traced here: 94.1 us
  waiting for transfers between devices  31.4 us (33%)
  matrix products  16.4 us (17%)
  starting transfers between devices  14.2 us (15%)
  Pallas kernels  13.6 us (14%)
  other arithmetic  11.7 us (12%)
  local copies, waits for them, and re-layouts  5.61 us (6%)
  between operations  1.17 us (1%)
    ppermute x2, waiting for transfers between devices, advect_kernel_call(): lax.ppermute(message, 'tiles', pairs)  16.7 us
    dot_general x16, matrix products, collide(): jnp.dot(table, iterate.astype(jnp.bfloat16), preferred_element_type=jnp.f...  12.6 us
    pallas_call x1, Pallas kernels, advect_kernel_call(): pl.pallas_call(functools.partial(advect_kernel, section_weights), out_sha...  10.6 us
    ppermute x2, waiting for transfers between devices, paired_collision(): arrived = lax.ppermute(away[:, chunk], 'bins', swap)  6.41 us
    ppermute x2, starting transfers between devices, advect_kernel_call(): lax.ppermute(message, 'tiles', pairs)  6.26 us
    ppermute x2, waiting for transfers between devices, paired_collision(): returned.append(lax.ppermute(change[local_bins:], 'bins', swap))  5.4 us
    add x6, other arithmetic, collide(): iterate + collision_rate * products[all_bins:] * products[:all_bins]  3.85 us
    ppermute x2, starting transfers between devices, paired_collision(): returned.append(lax.ppermute(change[local_bins:], 'bins', swap))  3.12 us
  transfers between devices with their start and end apart: 8, of which 7 were waited for; matrix products, arithmetic and copies ran while one was open for 21% of the time, Pallas kernels for 0%

profile of v14, /device:TPU:0, one launch (start us, length us, event | category | flops | bytes accessed | tf_op | source)
XLA Modules:
  0.0 94.1 jit_solution(14218053440838130635)
XLA Ops:
  0.7 1.4 %compare_select_fusion = (f32[4,8,128]{2,1,0:T(8,128)}, f32[4,8,128]{2,1,0:T(8,128)}) fusion(f32[4,8,128]{2,1,0:T(8,128)} %param.14, s32[4,128]{1,0:T(4,128)} %param.17, s32[8]{0:T(128)S(1)} %iota_add_fusion, f32[4,8,128]{2,1,0:T(8,128)} %param.13), kind=kLoop, calls=%fused_computation.121 | loop fusion | flops 12288 | bytes 67616 | tf_op jit(solution)/shard_map/mul | solution.py:232
  2.1 3.0 %shard_map.139 = (bf16[136,3,8,128]{3,2,1,0:T(8,128)(2,1)}, bf16[136,3,8,128]{3,2,1,0:T(8,128)(2,1)}) custom-call(f32[132,4,8,128]{3,2,1,0:T(8,128)} %q_ref.3, f32[4,8,128]{2,1,0:T(8,128)} %get-tuple-element.38.wx_ref.refs_8_, f32[4,8,128]{2,1,0:T(8,128)} %get-tuple-element.37.wy_ref.refs_9_), custom_call_target="tpu_custom_call" | custom-call | tf_op jit(solution)/shard_map/pallas_call | solution.py:48
  5.1 5.0 %collective-permute-start = (bf16[136,3,8,128]{3,2,1,0:T(8,128)(2,1)}, bf16[136,3,8,128]{3,2,1,0:T(8,128)(2,1)S(1)}, u32[]{:S(2)}, u32[]{:S(2)}) collective-permute-start(bf16[136,3,8,128]{3,2,1,0:T(8,128)(2,1)} %get-tuple-element.11), channel_id=1, source_target_pairs={{0,4},{4,8},{8,12},{1,5},{5,9},{9,13},{2,6},{6,10},{10,14},{3,7},{... | collective-permute-start | bytes 2506760 | tf_op jit(solution)/shard_map/ppermute | solution.py:95
  10.0 1.3 %collective-permute-start.1 = (bf16[136,3,8,128]{3,2,1,0:T(8,128)(2,1)}, bf16[136,3,8,128]{3,2,1,0:T(8,128)(2,1)S(1)}, u32[]{:S(2)}, u32[]{:S(2)}) collective-permute-start(bf16[136,3,8,128]{3,2,1,0:T(8,128)(2,1)} %get-tuple-element.13), channel_id=1, source_target_pairs={{4,0},{8,4},{12,8},{5,1},{9,5},{13,9},{6,2},{10,6},{14,10},{7,3},{... | collective-permute-start | bytes 2506760 | tf_op jit(solution)/shard_map/ppermute | solution.py:95
  11.9 2.0 %multiply_reduce_fusion = f32[264,8,33]{0,2,1:T(8,128)S(1)} fusion(f32[264,8]{0,1:T(8,128)S(1)} %fusion.66, f32[8,8,33,33]{3,1,2,0:T(8,128)S(1)} %fusion.57, s32[264]{0:T(512)S(1)} %get-tuple-element.35), kind=kOutput, calls=%fused_computation | convolution fusion | flops 221851072 | bytes 567072 | tf_op jit(solution)/shard_map/bm,acmn->bacn/dot_general | solution.py:150
  14.2 1.1 %fusion.4 = bf16[264,264]{0,1:T(8,128)(2,1)S(1)} fusion(f32[264,8,33]{0,2,1:T(8,128)S(1)} %multiply_reduce_fusion, f32[264,8]{0,1:T(8,128)S(1)} %fusion.66, f32[264,33]{0,1:T(8,128)S(1)} %fusion.54), kind=kOutput, calls=%fused_computation.17 | convolution fusion | flops 220936320 | bytes 461472 | tf_op jit(solution)/shard_map/bcn,dc,dn->bd/dot_general | solution.py:152
  15.5 12.6 %collective-permute-done.left_ref.refs_0_.refs_1_.refs_2_.refs_3_ = bf16[136,3,8,128]{3,2,1,0:T(8,128)(2,1)S(1)} collective-permute-done((bf16[136,3,8,128]{3,2,1,0:T(8,128)(2,1)}, bf16[136,3,8,128]{3,2,1,0:T(8,128)(2,1)S(1)}, u32[]{:S(2)}, u32[]{:S(2)}) %collective-permute-start) | collective-permute-done | bytes 835616 | tf_op jit(solution)/shard_map/ppermute | solution.py:95
  28.1 4.1 %collective-permute-done.1.right_ref.refs_4_.refs_5_.refs_6_.refs_7_ = bf16[136,3,8,128]{3,2,1,0:T(8,128)(2,1)S(1)} collective-permute-done((bf16[136,3,8,128]{3,2,1,0:T(8,128)(2,1)}, bf16[136,3,8,128]{3,2,1,0:T(8,128)(2,1)S(1)}, u32[]{:S(2)}, u32[]{:S(2)}) %collective-permute-start.1) | collective-permute-done | bytes 835616 | tf_op jit(solution)/shard_map/ppermute | solution.py:95
  32.2 1.0 %copy-done.3 = bf16[136,3,8,128]{3,2,1,0:T(8,128)(2,1)} copy-done((bf16[136,3,8,128]{3,2,1,0:T(8,128)(2,1)}, bf16[136,3,8,128]{3,2,1,0:T(8,128)(2,1)S(1)}, u32[]{:S(2)}) %copy-start.3) | copy-done | bytes 835608
  33.2 10.6 %shard_map.140 = (f32[132,4,8,128]{3,2,1,0:T(8,128)}, f32[132,4,1,128]{3,2,1,0:T(1,128)}) custom-call(f32[132,4,8,128]{3,2,1,0:T(8,128)} %q_ref.3, bf16[136,3,8,128]{3,2,1,0:T(8,128)(2,1)} %copy-done.2, bf16[136,3,8,128]{3,2,1,0:T(8,128)(2,1)} %copy-done.3, bf16[136,3,8,128]{3,2,1,0:T(8,128)(2,1)} %copy-done.2, bf16[136,3,8,128]{3,2,1,0:T(8,128)(2,1)} %copy-done.2, ...), custom_call_target="tpu_custom_call" | custom-call | flops 43253760 | bytes 10813440 | tf_op jit(solution)/shard_map/pallas_call | solution.py:108
  43.8 1.3 %collective-permute-start.2 = (f32[132,4,1,128]{3,2,1,0:T(1,128)}, f32[132,4,1,128]{3,2,1,0:T(1,128)S(1)}, u32[]{:S(2)}, u32[]{:S(2)}) collective-permute-start(f32[132,4,1,128]{3,2,1,0:T(1,128)} %get-tuple-element.15), channel_id=1, source_target_pairs={{1,0},{3,2},{5,4},{7,6},{9,8},{11,10},{13,12},{15,14},{17,16},{19,... | collective-permute-start | bytes 811016 | tf_op jit(solution)/shard_map/ppermute | solution.py:123
  45.1 2.0 %slice.137 = f32[132,4,7,128]{3,2,1,0:T(8,128)S(1)} slice(f32[132,4,8,128]{3,2,1,0:T(8,128)} %get-tuple-element.14), slice={[0:132], [0:4], [1:8], [0:128]} | slice | bytes 3784704 | tf_op jit(solution)/shard_map/slice | solution.py:249
  47.4 1.3 %multiply_reduce_fusion.1 = (f32[4,8,128]{2,1,0:T(8,128)S(1)}, f32[4,8,128]{2,1,0:T(8,128)S(1)}, f32[132,4,8,128]{3,2,1,0:T(8,128)S(1)}) fusion(f32[132]{0:T(256)S(1)} %get-tuple-element.40, f32[132]{0:T(256)S(1)} %copy-done.11, f32[132,4,1,128]{3,2,1,0:T(1,128)S(1)} %collective-permute-done.2, f32[132,4,7,128]{3,2,1,0:T(8,128)S(1)} %slice.137, ...), kind=kLoop, calls=%fused_computation.6 | loop fusion | flops 4317184 | bytes 6522944 | tf_op jit(solution)/shard_map/reduce_sum | solution.py:255
  48.7 1.6 %collective-permute-start.3 = (f32[2,4,8,128]{3,2,1,0:T(8,128)S(1)}, f32[2,4,8,128]{3,2,1,0:T(8,128)S(1)}, u32[]{:S(2)}, u32[]{:S(2)}) collective-permute-start(f32[2,4,8,128]{3,2,1,0:T(8,128)S(1)} %pad_maximum_fusion.6), channel_id=1, source_target_pairs={{0,2},{2,0},{1,3},{3,1},{4,6},{6,4},{5,7},{7,5},{8,10},{10,8},{9,1... | collective-permute-start | bytes 98312 | tf_op jit(solution)/shard_map/ppermute | solution.py:260
  50.2 2.7 %collective-permute-done.3 = f32[2,4,8,128]{3,2,1,0:T(8,128)S(1)} collective-permute-done((f32[2,4,8,128]{3,2,1,0:T(8,128)S(1)}, f32[2,4,8,128]{3,2,1,0:T(8,128)S(1)}, u32[]{:S(2)}, u32[]{:S(2)}) %collective-permute-start.3) | collective-permute-done | bytes 32800 | tf_op jit(solution)/shard_map/ppermute | solution.py:260
  52.9 0.6 fusion.62
  54.1 0.8 slice_bitcast_fusion.2
  55.0 1.5 %collective-permute-start.4 = (bf16[132,8,128]{2,1,0:T(8,128)(2,1)}, bf16[132,8,128]{2,1,0:T(8,128)(2,1)S(1)}, u32[]{:S(2)}, u32[]{:S(2)}) collective-permute-start(bf16[132,8,128]{2,1,0:T(8,128)(2,1)} %get-tuple-element.32), channel_id=1, source_target_pairs={{0,2},{2,0},{1,3},{3,1},{4,6},{6,4},{5,7},{7,5},{8,10},{10,8},{9,1... | collective-permute-start | bytes 811016 | tf_op jit(solution)/shard_map/ppermute | solution.py:200
  56.6 0.8 copy-done.5
  58.1 6.4 %collective-permute-done.4 = bf16[132,8,128]{2,1,0:T(8,128)(2,1)S(1)} collective-permute-done((bf16[132,8,128]{2,1,0:T(8,128)(2,1)}, bf16[132,8,128]{2,1,0:T(8,128)(2,1)S(1)}, u32[]{:S(2)}, u32[]{:S(2)}) %collective-permute-start.4) | collective-permute-done | bytes 270368 | tf_op jit(solution)/shard_map/ppermute | solution.py:200
  64.6 0.8 fusion.53
  65.3 0.8 fusion.47
  66.2 0.5 fusion.20
  66.7 0.8 fusion.45
  67.5 0.8 fusion.43
  68.3 0.7 fusion.18
  69.0 0.8 fusion.41
  69.8 0.8 fusion.39
  70.6 0.6 fusion.16
  71.2 0.8 fusion.37
  72.0 0.8 fusion.35
  72.8 0.7 fusion.5
  73.6 1.6 %collective-permute-start.6 = (bf16[132,8,128]{2,1,0:T(8,128)(2,1)S(1)}, bf16[132,8,128]{2,1,0:T(8,128)(2,1)S(1)}, u32[]{:S(2)}, u32[]{:S(2)}) collective-permute-start(bf16[132,8,128]{2,1,0:T(8,128)(2,1)S(1)} %slice.225), channel_id=1, source_target_pairs={{0,2},{2,0},{1,3},{3,1},{4,6},{6,4},{5,7},{7,5},{8,10},{10,8},{9,1... | collective-permute-start | bytes 811016 | tf_op jit(solution)/shard_map/ppermute | solution.py:207
  75.3 0.8 fusion.52
  76.0 0.8 fusion.33
  77.4 0.8 fusion.31
  78.2 0.8 fusion.29
  79.1 0.9 fusion.11
  80.0 0.6 collective-permute-done.6
  80.5 0.8 fusion.27
  81.3 0.8 fusion.25
  82.1 0.6 fusion.9
  82.7 0.8 fusion.23
  83.5 0.8 fusion.21
  84.3 0.7 fusion.6
  85.2 1.6 %collective-permute-start.7 = (bf16[132,8,128]{2,1,0:T(8,128)(2,1)S(1)}, bf16[132,8,128]{2,1,0:T(8,128)(2,1)S(1)}, u32[]{:S(2)}, u32[]{:S(2)}) collective-permute-start(bf16[132,8,128]{2,1,0:T(8,128)(2,1)S(1)} %slice.227), channel_id=1, source_target_pairs={{0,2},{2,0},{1,3},{3,1},{4,6},{6,4},{5,7},{7,5},{8,10},{10,8},{9,1... | collective-permute-start | bytes 811016 | tf_op jit(solution)/shard_map/ppermute | solution.py:207
  86.9 4.8 %collective-permute-done.7 = bf16[132,8,128]{2,1,0:T(8,128)(2,1)S(1)} collective-permute-done((bf16[132,8,128]{2,1,0:T(8,128)(2,1)S(1)}, bf16[132,8,128]{2,1,0:T(8,128)(2,1)S(1)}, u32[]{:S(2)}, u32[]{:S(2)}) %collective-permute-start.7) | collective-permute-done | bytes 270368 | tf_op jit(solution)/shard_map/ppermute | solution.py:207
  92.2 1.8 %fusion.1 = f32[132,4,8,128]{3,2,1,0:T(8,128)} fusion(bf16[132,4,8,128]{3,2,1,0:T(8,128)(2,1)S(1)} %bitcast.128, f32[132,4,8,128]{3,2,1,0:T(8,128)S(1)} %get-tuple-element.23, f32[4,8,128]{2,1,0:T(8,128)S(1)} %compare_convert_fusion, f32[4,8,128]{2,1,0:T(8,128)S(1)} %get-tuple-element.22, f32[132]{0:T(256)S(1)} %get-tuple-element.39), kind=kLoop, calls=%fused_computation.4 | loop fusion | flops 3244032 | bytes 5440016 | tf_op jit(solution)/shard_map/mul | solution.py:272
  (66 shorter events, 4.3 us)
Async XLA Ops:
  0.6 10.9 %copy-start = (bf16[4,33,33]{2,0,1:T(4,128)(2,1)S(1)}, bf16[4,33,33]{2,0,1:T(4,128)(2,1)}, u32[]{:S(2)}) copy-start(bf16[4,33,33]{2,0,1:T(4,128)(2,1)} %param.23) | copy-start | bytes 26140
  2.1 9.2 %copy-start.12 = (s32[264]{0:T(512)S(1)}, s32[264]{0:T(512)}, u32[]{:S(2)}) copy-start(s32[264]{0:T(512)} %param.21) | copy-start | bytes 3172
  2.1 9.4 %copy-start.9 = (s32[8,8]{1,0:T(8,128)S(1)}, s32[8,8]{1,0:T(8,128)}, u32[]{:S(2)}) copy-start(s32[8,8]{1,0:T(8,128)} %param.22) | copy-start | bytes 772
  5.1 23.1 %collective-permute-start = (bf16[136,3,8,128]{3,2,1,0:T(8,128)(2,1)}, bf16[136,3,8,128]{3,2,1,0:T(8,128)(2,1)S(1)}, u32[]{:S(2)}, u32[]{:S(2)}) collective-permute-start(bf16[136,3,8,128]{3,2,1,0:T(8,128)(2,1)} %get-tuple-element.11), channel_id=1, source_target_pairs={{0,4},{4,8},{8,12},{1,5},{5,9},{9,13},{2,6},{6,10},{10,14},{3,7},{... | collective-permute-start | bytes 2506760 | tf_op jit(solution)/shard_map/ppermute | solution.py:95
  10.0 22.2 %collective-permute-start.1 = (bf16[136,3,8,128]{3,2,1,0:T(8,128)(2,1)}, bf16[136,3,8,128]{3,2,1,0:T(8,128)(2,1)S(1)}, u32[]{:S(2)}, u32[]{:S(2)}) collective-permute-start(bf16[136,3,8,128]{3,2,1,0:T(8,128)(2,1)} %get-tuple-element.13), channel_id=1, source_target_pairs={{4,0},{8,4},{12,8},{5,1},{9,5},{13,9},{6,2},{10,6},{14,10},{7,3},{... | collective-permute-start | bytes 2506760 | tf_op jit(solution)/shard_map/ppermute | solution.py:95
  15.5 29.6 %copy-start.10 = (f32[132]{0:T(256)S(1)}, f32[132]{0:T(256)}, u32[]{:S(2)}) copy-start(f32[132]{0:T(256)} %param.18) | copy-start | bytes 1588
  15.5 29.6 %copy-start.11 = (f32[132]{0:T(256)S(1)}, f32[132]{0:T(256)}, u32[]{:S(2)}) copy-start(f32[132]{0:T(256)} %param.19) | copy-start | bytes 1588
  15.5 29.6 %copy-start.13 = (f32[132]{0:T(256)S(1)}, f32[132]{0:T(256)}, u32[]{:S(2)}) copy-start(f32[132]{0:T(256)} %param.20) | copy-start | bytes 1588
  28.1 4.1 %copy-start.2 = (bf16[136,3,8,128]{3,2,1,0:T(8,128)(2,1)}, bf16[136,3,8,128]{3,2,1,0:T(8,128)(2,1)S(1)}, u32[]{:S(2)}) copy-start(bf16[136,3,8,128]{3,2,1,0:T(8,128)(2,1)S(1)} %collective-permute-done.left_ref.refs_0_.refs_1_.refs_2_.refs_3_) | copy-start | bytes 2506756
  32.2 1.0 %copy-start.3 = (bf16[136,3,8,128]{3,2,1,0:T(8,128)(2,1)}, bf16[136,3,8,128]{3,2,1,0:T(8,128)(2,1)S(1)}, u32[]{:S(2)}) copy-start(bf16[136,3,8,128]{3,2,1,0:T(8,128)(2,1)S(1)} %collective-permute-done.1.right_ref.refs_4_.refs_5_.refs_6_.refs_7_) | copy-start | bytes 2506756
  43.8 3.6 %collective-permute-start.2 = (f32[132,4,1,128]{3,2,1,0:T(1,128)}, f32[132,4,1,128]{3,2,1,0:T(1,128)S(1)}, u32[]{:S(2)}, u32[]{:S(2)}) collective-permute-start(f32[132,4,1,128]{3,2,1,0:T(1,128)} %get-tuple-element.15), channel_id=1, source_target_pairs={{1,0},{3,2},{5,4},{7,6},{9,8},{11,10},{13,12},{15,14},{17,16},{19,... | collective-permute-start | bytes 811016 | tf_op jit(solution)/shard_map/ppermute | solution.py:123
  45.1 2.3 %copy-start.4 = (f32[132,4,8,128]{3,2,1,0:T(8,128)S(1)}, f32[132,4,8,128]{3,2,1,0:T(8,128)}, u32[]{:S(2)}) copy-start(f32[132,4,8,128]{3,2,1,0:T(8,128)} %get-tuple-element.14) | copy-start | bytes 6488068
  47.4 5.5 %copy-start.6 = (f32[4,8,128]{2,1,0:T(8,128)S(1)}, f32[4,8,128]{2,1,0:T(8,128)}, u32[]{:S(2)}) copy-start(f32[4,8,128]{2,1,0:T(8,128)} %param.16) | copy-start | bytes 49156
  47.4 5.5 %copy-start.7 = (f32[4,8,128]{2,1,0:T(8,128)S(1)}, f32[4,8,128]{2,1,0:T(8,128)}, u32[]{:S(2)}) copy-start(f32[4,8,128]{2,1,0:T(8,128)} %param.15) | copy-start | bytes 49156
  48.7 4.2 %collective-permute-start.3 = (f32[2,4,8,128]{3,2,1,0:T(8,128)S(1)}, f32[2,4,8,128]{3,2,1,0:T(8,128)S(1)}, u32[]{:S(2)}, u32[]{:S(2)}) collective-permute-start(f32[2,4,8,128]{3,2,1,0:T(8,128)S(1)} %pad_maximum_fusion.6), channel_id=1, source_target_pairs={{0,2},{2,0},{1,3},{3,1},{4,6},{6,4},{5,7},{7,5},{8,10},{10,8},{9,1... | collective-permute-start | bytes 98312 | tf_op jit(solution)/shard_map/ppermute | solution.py:260
  54.1 2.3 %copy-start.8 = (s32[4,128]{1,0:T(4,128)S(1)}, s32[4,128]{1,0:T(4,128)}, u32[]{:S(2)}) copy-start(s32[4,128]{1,0:T(4,128)} %param.17) | copy-start | bytes 6148
  55.0 9.5 %collective-permute-start.4 = (bf16[132,8,128]{2,1,0:T(8,128)(2,1)}, bf16[132,8,128]{2,1,0:T(8,128)(2,1)S(1)}, u32[]{:S(2)}, u32[]{:S(2)}) collective-permute-start(bf16[132,8,128]{2,1,0:T(8,128)(2,1)} %get-tuple-element.32), channel_id=1, source_target_pairs={{0,2},{2,0},{1,3},{3,1},{4,6},{6,4},{5,7},{7,5},{8,10},{10,8},{9,1... | collective-permute-start | bytes 811016 | tf_op jit(solution)/shard_map/ppermute | solution.py:200
  56.5 1.0 %copy-start.5 = (bf16[132,8,128]{2,1,0:T(8,128)(2,1)S(1)}, bf16[132,8,128]{2,1,0:T(8,128)(2,1)}, u32[]{:S(2)}) copy-start(bf16[132,8,128]{2,1,0:T(8,128)(2,1)} %get-tuple-element.33) | copy-start | bytes 811012
  57.5 17.7 %collective-permute-start.5 = (bf16[132,8,128]{2,1,0:T(8,128)(2,1)S(1)}, bf16[132,8,128]{2,1,0:T(8,128)(2,1)S(1)}, u32[]{:S(2)}, u32[]{:S(2)}) collective-permute-start(bf16[132,8,128]{2,1,0:T(8,128)(2,1)S(1)} %copy-done.5), channel_id=1, source_target_pairs={{0,2},{2,0},{1,3},{3,1},{4,6},{6,4},{5,7},{7,5},{8,10},{10,8},{9,1... | collective-permute-start | bytes 811016 | tf_op jit(solution)/shard_map/ppermute | solution.py:200
  73.6 6.9 %collective-permute-start.6 = (bf16[132,8,128]{2,1,0:T(8,128)(2,1)S(1)}, bf16[132,8,128]{2,1,0:T(8,128)(2,1)S(1)}, u32[]{:S(2)}, u32[]{:S(2)}) collective-permute-start(bf16[132,8,128]{2,1,0:T(8,128)(2,1)S(1)} %slice.225), channel_id=1, source_target_pairs={{0,2},{2,0},{1,3},{3,1},{4,6},{6,4},{5,7},{7,5},{8,10},{10,8},{9,1... | collective-permute-start | bytes 811016 | tf_op jit(solution)/shard_map/ppermute | solution.py:207
  85.2 6.5 %collective-permute-start.7 = (bf16[132,8,128]{2,1,0:T(8,128)(2,1)S(1)}, bf16[132,8,128]{2,1,0:T(8,128)(2,1)S(1)}, u32[]{:S(2)}, u32[]{:S(2)}) collective-permute-start(bf16[132,8,128]{2,1,0:T(8,128)(2,1)S(1)} %slice.227), channel_id=1, source_target_pairs={{0,2},{2,0},{1,3},{3,1},{4,6},{6,4},{5,7},{7,5},{8,10},{10,8},{9,1... | collective-permute-start | bytes 811016 | tf_op jit(solution)/shard_map/ppermute | solution.py:207
  92.2 1.9 %copy-start.1 = (bf16[4,33,33]{2,0,1:T(4,128)(2,1)S(1)}, bf16[4,33,33]{2,0,1:T(4,128)(2,1)}, u32[]{:S(2)}) copy-start(bf16[4,33,33]{2,0,1:T(4,128)(2,1)} %param.23) | copy-start | bytes 26140

commit v15 on v14

--- a/solution.py
+++ b/solution.py
@@ -96,7 +96,7 @@
         for message, pairs in zip(rims(bin_mass, wind_x, wind_y, depth), (up, down))
     )
     left, tie = lax.optimization_barrier((left, tie))
-    block = max(d for d in range(1, 13) if local_bins % d == 0)
+    block = max(d for d in range(1, 67) if local_bins % d == 0)
     rim_spec = pl.BlockSpec((block, depth, width_z, width_y), lambda i: (i, 0, 0, 0))
     row_specs = [
         pl.BlockSpec((1, depth, width_z, width_y), lambda i, row=local_bins + k: (row, 0, 0, 0))

time: 94.6 us -> 92.1 us (0.974)
  Pallas kernels: 13.6 us -> 11.2 us
    pallas_call x1, Pallas kernels: 10.6 us -> 8.28 us  [advect_kernel_call(): pl.pallas_call(functools.partial(advect_kernel, section_weights), out_sha...]
  transfers between devices with their start and end apart: 8 -> 8, of which waited for: 7 -> 7; matrix products, arithmetic and copies ran while one was open for 21% -> 22% of each run, Pallas kernels for 0% -> 0%
where the time goes in v15:
time: 92.1 us; the launch traced here: 91.8 us
  waiting for transfers between devices  31.4 us (34%)
  matrix products  16.4 us (18%)
  starting transfers between devices  14.2 us (15%)
  other arithmetic  11.7 us (13%)
  Pallas kernels  11.2 us (12%)
  local copies, waits for them, and re-layouts  5.61 us (6%)
  between operations  1.17 us (1%)
    ppermute x2, waiting for transfers between devices, advect_kernel_call(): lax.ppermute(message, 'tiles', pairs)  16.7 us
    dot_general x16, matrix products, collide(): jnp.dot(table, iterate.astype(jnp.bfloat16), preferred_element_type=jnp.f...  12.7 us
    pallas_call x1, Pallas kernels, advect_kernel_call(): pl.pallas_call(functools.partial(advect_kernel, section_weights), out_sha...  8.28 us
    ppermute x2, waiting for transfers between devices, paired_collision(): arrived = lax.ppermute(away[:, chunk], 'bins', swap)  6.41 us
    ppermute x2, starting transfers between devices, advect_kernel_call(): lax.ppermute(message, 'tiles', pairs)  6.26 us
    ppermute x2, waiting for transfers between devices, paired_collision(): returned.append(lax.ppermute(change[local_bins:], 'bins', swap))  5.38 us
    add x6, other arithmetic, collide(): iterate + collision_rate * products[all_bins:] * products[:all_bins]  3.85 us
    ppermute x2, starting transfers between devices, paired_collision(): returned.append(lax.ppermute(change[local_bins:], 'bins', swap))  3.12 us
  transfers between devices with their start and end apart: 8, of which 7 were waited for; matrix products, arithmetic and copies ran while one was open for 22% of the time, Pallas kernels for 0%

profile of v15, /device:TPU:0, one launch (start us, length us, event | category | flops | bytes accessed | tf_op | source)
XLA Modules:
  0.0 91.8 jit_solution(411534052327279695)
XLA Ops:
  0.7 1.4 %compare_select_fusion = (f32[4,8,128]{2,1,0:T(8,128)}, f32[4,8,128]{2,1,0:T(8,128)}) fusion(f32[4,8,128]{2,1,0:T(8,128)} %param.14, s32[4,128]{1,0:T(4,128)} %param.17, s32[8]{0:T(128)S(1)} %iota_add_fusion, f32[4,8,128]{2,1,0:T(8,128)} %param.13), kind=kLoop, calls=%fused_computation.121 | loop fusion | flops 12288 | bytes 67616 | tf_op jit(solution)/shard_map/mul | solution.py:232
  2.1 3.0 %shard_map.139 = (bf16[136,3,8,128]{3,2,1,0:T(8,128)(2,1)}, bf16[136,3,8,128]{3,2,1,0:T(8,128)(2,1)}) custom-call(f32[132,4,8,128]{3,2,1,0:T(8,128)} %q_ref.3, f32[4,8,128]{2,1,0:T(8,128)} %get-tuple-element.38.wx_ref.refs_8_, f32[4,8,128]{2,1,0:T(8,128)} %get-tuple-element.37.wy_ref.refs_9_), custom_call_target="tpu_custom_call" | custom-call | tf_op jit(solution)/shard_map/pallas_call | solution.py:48
  5.1 5.0 %collective-permute-start = (bf16[136,3,8,128]{3,2,1,0:T(8,128)(2,1)}, bf16[136,3,8,128]{3,2,1,0:T(8,128)(2,1)S(1)}, u32[]{:S(2)}, u32[]{:S(2)}) collective-permute-start(bf16[136,3,8,128]{3,2,1,0:T(8,128)(2,1)} %get-tuple-element.11), channel_id=1, source_target_pairs={{0,4},{4,8},{8,12},{1,5},{5,9},{9,13},{2,6},{6,10},{10,14},{3,7},{... | collective-permute-start | bytes 2506760 | tf_op jit(solution)/shard_map/ppermute | solution.py:95
  10.0 1.3 %collective-permute-start.1 = (bf16[136,3,8,128]{3,2,1,0:T(8,128)(2,1)}, bf16[136,3,8,128]{3,2,1,0:T(8,128)(2,1)S(1)}, u32[]{:S(2)}, u32[]{:S(2)}) collective-permute-start(bf16[136,3,8,128]{3,2,1,0:T(8,128)(2,1)} %get-tuple-element.13), channel_id=1, source_target_pairs={{4,0},{8,4},{12,8},{5,1},{9,5},{13,9},{6,2},{10,6},{14,10},{7,3},{... | collective-permute-start | bytes 2506760 | tf_op jit(solution)/shard_map/ppermute | solution.py:95
  11.9 2.0 %multiply_reduce_fusion = f32[264,8,33]{0,2,1:T(8,128)S(1)} fusion(f32[264,8]{0,1:T(8,128)S(1)} %fusion.66, f32[8,8,33,33]{3,1,2,0:T(8,128)S(1)} %fusion.57, s32[264]{0:T(512)S(1)} %get-tuple-element.35), kind=kOutput, calls=%fused_computation | convolution fusion | flops 221851072 | bytes 567072 | tf_op jit(solution)/shard_map/bm,acmn->bacn/dot_general | solution.py:150
  14.2 1.1 %fusion.4 = bf16[264,264]{0,1:T(8,128)(2,1)S(1)} fusion(f32[264,8,33]{0,2,1:T(8,128)S(1)} %multiply_reduce_fusion, f32[264,8]{0,1:T(8,128)S(1)} %fusion.66, f32[264,33]{0,1:T(8,128)S(1)} %fusion.54), kind=kOutput, calls=%fused_computation.17 | convolution fusion | flops 220936320 | bytes 461472 | tf_op jit(solution)/shard_map/bcn,dc,dn->bd/dot_general | solution.py:152
  15.5 12.6 %collective-permute-done.left_ref.refs_0_.refs_1_.refs_2_.refs_3_ = bf16[136,3,8,128]{3,2,1,0:T(8,128)(2,1)S(1)} collective-permute-done((bf16[136,3,8,128]{3,2,1,0:T(8,128)(2,1)}, bf16[136,3,8,128]{3,2,1,0:T(8,128)(2,1)S(1)}, u32[]{:S(2)}, u32[]{:S(2)}) %collective-permute-start) | collective-permute-done | bytes 835616 | tf_op jit(solution)/shard_map/ppermute | solution.py:95
  28.1 4.1 %collective-permute-done.1.right_ref.refs_4_.refs_5_.refs_6_.refs_7_ = bf16[136,3,8,128]{3,2,1,0:T(8,128)(2,1)S(1)} collective-permute-done((bf16[136,3,8,128]{3,2,1,0:T(8,128)(2,1)}, bf16[136,3,8,128]{3,2,1,0:T(8,128)(2,1)S(1)}, u32[]{:S(2)}, u32[]{:S(2)}) %collective-permute-start.1) | collective-permute-done | bytes 835616 | tf_op jit(solution)/shard_map/ppermute | solution.py:95
  32.2 1.0 %copy-done.3 = bf16[136,3,8,128]{3,2,1,0:T(8,128)(2,1)} copy-done((bf16[136,3,8,128]{3,2,1,0:T(8,128)(2,1)}, bf16[136,3,8,128]{3,2,1,0:T(8,128)(2,1)S(1)}, u32[]{:S(2)}) %copy-start.3) | copy-done | bytes 835608
  33.2 8.3 %shard_map.140 = (f32[132,4,8,128]{3,2,1,0:T(8,128)}, f32[132,4,1,128]{3,2,1,0:T(1,128)}) custom-call(f32[132,4,8,128]{3,2,1,0:T(8,128)} %q_ref.3, bf16[136,3,8,128]{3,2,1,0:T(8,128)(2,1)} %copy-done.2, bf16[136,3,8,128]{3,2,1,0:T(8,128)(2,1)} %copy-done.3, bf16[136,3,8,128]{3,2,1,0:T(8,128)(2,1)} %copy-done.2, bf16[136,3,8,128]{3,2,1,0:T(8,128)(2,1)} %copy-done.2, ...), custom_call_target="tpu_custom_call" | custom-call | flops 43253760 | bytes 10813440 | tf_op jit(solution)/shard_map/pallas_call | solution.py:108
  41.4 1.3 %collective-permute-start.2 = (f32[132,4,1,128]{3,2,1,0:T(1,128)}, f32[132,4,1,128]{3,2,1,0:T(1,128)S(1)}, u32[]{:S(2)}, u32[]{:S(2)}) collective-permute-start(f32[132,4,1,128]{3,2,1,0:T(1,128)} %get-tuple-element.15), channel_id=1, source_target_pairs={{1,0},{3,2},{5,4},{7,6},{9,8},{11,10},{13,12},{15,14},{17,16},{19,... | collective-permute-start | bytes 811016 | tf_op jit(solution)/shard_map/ppermute | solution.py:123
  42.8 2.0 %slice.137 = f32[132,4,7,128]{3,2,1,0:T(8,128)S(1)} slice(f32[132,4,8,128]{3,2,1,0:T(8,128)} %get-tuple-element.14), slice={[0:132], [0:4], [1:8], [0:128]} | slice | bytes 3784704 | tf_op jit(solution)/shard_map/slice | solution.py:249
  45.1 1.3 %multiply_reduce_fusion.1 = (f32[4,8,128]{2,1,0:T(8,128)S(1)}, f32[4,8,128]{2,1,0:T(8,128)S(1)}, f32[132,4,8,128]{3,2,1,0:T(8,128)S(1)}) fusion(f32[132]{0:T(256)S(1)} %get-tuple-element.40, f32[132]{0:T(256)S(1)} %copy-done.11, f32[132,4,1,128]{3,2,1,0:T(1,128)S(1)} %collective-permute-done.2, f32[132,4,7,128]{3,2,1,0:T(8,128)S(1)} %slice.137, ...), kind=kLoop, calls=%fused_computation.6 | loop fusion | flops 4317184 | bytes 6522944 | tf_op jit(solution)/shard_map/reduce_sum | solution.py:255
  46.4 1.6 %collective-permute-start.3 = (f32[2,4,8,128]{3,2,1,0:T(8,128)S(1)}, f32[2,4,8,128]{3,2,1,0:T(8,128)S(1)}, u32[]{:S(2)}, u32[]{:S(2)}) collective-permute-start(f32[2,4,8,128]{3,2,1,0:T(8,128)S(1)} %pad_maximum_fusion.6), channel_id=1, source_target_pairs={{0,2},{2,0},{1,3},{3,1},{4,6},{6,4},{5,7},{7,5},{8,10},{10,8},{9,1... | collective-permute-start | bytes 98312 | tf_op jit(solution)/shard_map/ppermute | solution.py:260
  47.9 2.7 %collective-permute-done.3 = f32[2,4,8,128]{3,2,1,0:T(8,128)S(1)} collective-permute-done((f32[2,4,8,128]{3,2,1,0:T(8,128)S(1)}, f32[2,4,8,128]{3,2,1,0:T(8,128)S(1)}, u32[]{:S(2)}, u32[]{:S(2)}) %collective-permute-start.3) | collective-permute-done | bytes 32800 | tf_op jit(solution)/shard_map/ppermute | solution.py:260
  50.6 0.6 fusion.62
  51.8 0.8 slice_bitcast_fusion.2
  52.6 1.5 %collective-permute-start.4 = (bf16[132,8,128]{2,1,0:T(8,128)(2,1)}, bf16[132,8,128]{2,1,0:T(8,128)(2,1)S(1)}, u32[]{:S(2)}, u32[]{:S(2)}) collective-permute-start(bf16[132,8,128]{2,1,0:T(8,128)(2,1)} %get-tuple-element.32), channel_id=1, source_target_pairs={{0,2},{2,0},{1,3},{3,1},{4,6},{6,4},{5,7},{7,5},{8,10},{10,8},{9,1... | collective-permute-start | bytes 811016 | tf_op jit(solution)/shard_map/ppermute | solution.py:200
  54.3 0.8 copy-done.5
  55.8 6.4 %collective-permute-done.4 = bf16[132,8,128]{2,1,0:T(8,128)(2,1)S(1)} collective-permute-done((bf16[132,8,128]{2,1,0:T(8,128)(2,1)}, bf16[132,8,128]{2,1,0:T(8,128)(2,1)S(1)}, u32[]{:S(2)}, u32[]{:S(2)}) %collective-permute-start.4) | collective-permute-done | bytes 270368 | tf_op jit(solution)/shard_map/ppermute | solution.py:200
  62.2 0.8 fusion.53
  63.0 0.8 fusion.47
  63.9 0.5 fusion.20
  64.4 0.8 fusion.45
  65.2 0.8 fusion.43
  66.0 0.7 fusion.18
  66.7 0.8 fusion.41
  67.4 0.8 fusion.39
  68.3 0.6 fusion.16
  68.9 0.8 fusion.37
  69.6 0.8 fusion.35
  70.4 0.7 fusion.5
  71.3 1.6 %collective-permute-start.6 = (bf16[132,8,128]{2,1,0:T(8,128)(2,1)S(1)}, bf16[132,8,128]{2,1,0:T(8,128)(2,1)S(1)}, u32[]{:S(2)}, u32[]{:S(2)}) collective-permute-start(bf16[132,8,128]{2,1,0:T(8,128)(2,1)S(1)} %slice.225), channel_id=1, source_target_pairs={{0,2},{2,0},{1,3},{3,1},{4,6},{6,4},{5,7},{7,5},{8,10},{10,8},{9,1... | collective-permute-start | bytes 811016 | tf_op jit(solution)/shard_map/ppermute | solution.py:207
  72.9 0.8 fusion.52
  73.7 0.8 fusion.33
  75.1 0.8 fusion.31
  75.9 0.8 fusion.29
  76.8 0.9 fusion.11
  77.7 0.5 collective-permute-done.6
  78.2 0.8 fusion.27
  79.0 0.8 fusion.25
  79.8 0.6 fusion.9
  80.4 0.8 fusion.23
  81.2 0.8 fusion.21
  82.0 0.7 fusion.6
  82.9 1.6 %collective-permute-start.7 = (bf16[132,8,128]{2,1,0:T(8,128)(2,1)S(1)}, bf16[132,8,128]{2,1,0:T(8,128)(2,1)S(1)}, u32[]{:S(2)}, u32[]{:S(2)}) collective-permute-start(bf16[132,8,128]{2,1,0:T(8,128)(2,1)S(1)} %slice.227), channel_id=1, source_target_pairs={{0,2},{2,0},{1,3},{3,1},{4,6},{6,4},{5,7},{7,5},{8,10},{10,8},{9,1... | collective-permute-start | bytes 811016 | tf_op jit(solution)/shard_map/ppermute | solution.py:207
  84.6 4.8 %collective-permute-done.7 = bf16[132,8,128]{2,1,0:T(8,128)(2,1)S(1)} collective-permute-done((bf16[132,8,128]{2,1,0:T(8,128)(2,1)S(1)}, bf16[132,8,128]{2,1,0:T(8,128)(2,1)S(1)}, u32[]{:S(2)}, u32[]{:S(2)}) %collective-permute-start.7) | collective-permute-done | bytes 270368 | tf_op jit(solution)/shard_map/ppermute | solution.py:207
  89.9 1.8 %fusion.1 = f32[132,4,8,128]{3,2,1,0:T(8,128)} fusion(bf16[132,4,8,128]{3,2,1,0:T(8,128)(2,1)S(1)} %bitcast.128, f32[132,4,8,128]{3,2,1,0:T(8,128)S(1)} %get-tuple-element.23, f32[4,8,128]{2,1,0:T(8,128)S(1)} %compare_convert_fusion, f32[4,8,128]{2,1,0:T(8,128)S(1)} %get-tuple-element.22, f32[132]{0:T(256)S(1)} %get-tuple-element.39), kind=kLoop, calls=%fused_computation.4 | loop fusion | flops 3244032 | bytes 5440016 | tf_op jit(solution)/shard_map/mul | solution.py:272
  (66 shorter events, 4.3 us)
Async XLA Ops:
  0.6 10.9 %copy-start = (bf16[4,33,33]{2,0,1:T(4,128)(2,1)S(1)}, bf16[4,33,33]{2,0,1:T(4,128)(2,1)}, u32[]{:S(2)}) copy-start(bf16[4,33,33]{2,0,1:T(4,128)(2,1)} %param.23) | copy-start | bytes 26140
  2.1 9.2 %copy-start.12 = (s32[264]{0:T(512)S(1)}, s32[264]{0:T(512)}, u32[]{:S(2)}) copy-start(s32[264]{0:T(512)} %param.21) | copy-start | bytes 3172
  2.1 9.4 %copy-start.9 = (s32[8,8]{1,0:T(8,128)S(1)}, s32[8,8]{1,0:T(8,128)}, u32[]{:S(2)}) copy-start(s32[8,8]{1,0:T(8,128)} %param.22) | copy-start | bytes 772
  5.1 23.1 %collective-permute-start = (bf16[136,3,8,128]{3,2,1,0:T(8,128)(2,1)}, bf16[136,3,8,128]{3,2,1,0:T(8,128)(2,1)S(1)}, u32[]{:S(2)}, u32[]{:S(2)}) collective-permute-start(bf16[136,3,8,128]{3,2,1,0:T(8,128)(2,1)} %get-tuple-element.11), channel_id=1, source_target_pairs={{0,4},{4,8},{8,12},{1,5},{5,9},{9,13},{2,6},{6,10},{10,14},{3,7},{... | collective-permute-start | bytes 2506760 | tf_op jit(solution)/shard_map/ppermute | solution.py:95
  10.0 22.2 %collective-permute-start.1 = (bf16[136,3,8,128]{3,2,1,0:T(8,128)(2,1)}, bf16[136,3,8,128]{3,2,1,0:T(8,128)(2,1)S(1)}, u32[]{:S(2)}, u32[]{:S(2)}) collective-permute-start(bf16[136,3,8,128]{3,2,1,0:T(8,128)(2,1)} %get-tuple-element.13), channel_id=1, source_target_pairs={{4,0},{8,4},{12,8},{5,1},{9,5},{13,9},{6,2},{10,6},{14,10},{7,3},{... | collective-permute-start | bytes 2506760 | tf_op jit(solution)/shard_map/ppermute | solution.py:95
  15.5 27.2 %copy-start.10 = (f32[132]{0:T(256)S(1)}, f32[132]{0:T(256)}, u32[]{:S(2)}) copy-start(f32[132]{0:T(256)} %param.18) | copy-start | bytes 1588
  15.5 27.3 %copy-start.11 = (f32[132]{0:T(256)S(1)}, f32[132]{0:T(256)}, u32[]{:S(2)}) copy-start(f32[132]{0:T(256)} %param.19) | copy-start | bytes 1588
  15.5 27.3 %copy-start.13 = (f32[132]{0:T(256)S(1)}, f32[132]{0:T(256)}, u32[]{:S(2)}) copy-start(f32[132]{0:T(256)} %param.20) | copy-start | bytes 1588
  28.1 4.1 %copy-start.2 = (bf16[136,3,8,128]{3,2,1,0:T(8,128)(2,1)}, bf16[136,3,8,128]{3,2,1,0:T(8,128)(2,1)S(1)}, u32[]{:S(2)}) copy-start(bf16[136,3,8,128]{3,2,1,0:T(8,128)(2,1)S(1)} %collective-permute-done.left_ref.refs_0_.refs_1_.refs_2_.refs_3_) | copy-start | bytes 2506756
  32.2 1.0 %copy-start.3 = (bf16[136,3,8,128]{3,2,1,0:T(8,128)(2,1)}, bf16[136,3,8,128]{3,2,1,0:T(8,128)(2,1)S(1)}, u32[]{:S(2)}) copy-start(bf16[136,3,8,128]{3,2,1,0:T(8,128)(2,1)S(1)} %collective-permute-done.1.right_ref.refs_4_.refs_5_.refs_6_.refs_7_) | copy-start | bytes 2506756
  41.4 3.6 %collective-permute-start.2 = (f32[132,4,1,128]{3,2,1,0:T(1,128)}, f32[132,4,1,128]{3,2,1,0:T(1,128)S(1)}, u32[]{:S(2)}, u32[]{:S(2)}) collective-permute-start(f32[132,4,1,128]{3,2,1,0:T(1,128)} %get-tuple-element.15), channel_id=1, source_target_pairs={{1,0},{3,2},{5,4},{7,6},{9,8},{11,10},{13,12},{15,14},{17,16},{19,... | collective-permute-start | bytes 811016 | tf_op jit(solution)/shard_map/ppermute | solution.py:123
  42.8 2.3 %copy-start.4 = (f32[132,4,8,128]{3,2,1,0:T(8,128)S(1)}, f32[132,4,8,128]{3,2,1,0:T(8,128)}, u32[]{:S(2)}) copy-start(f32[132,4,8,128]{3,2,1,0:T(8,128)} %get-tuple-element.14) | copy-start | bytes 6488068
  45.1 5.5 %copy-start.6 = (f32[4,8,128]{2,1,0:T(8,128)S(1)}, f32[4,8,128]{2,1,0:T(8,128)}, u32[]{:S(2)}) copy-start(f32[4,8,128]{2,1,0:T(8,128)} %param.16) | copy-start | bytes 49156
  45.1 5.5 %copy-start.7 = (f32[4,8,128]{2,1,0:T(8,128)S(1)}, f32[4,8,128]{2,1,0:T(8,128)}, u32[]{:S(2)}) copy-start(f32[4,8,128]{2,1,0:T(8,128)} %param.15) | copy-start | bytes 49156
  46.4 4.2 %collective-permute-start.3 = (f32[2,4,8,128]{3,2,1,0:T(8,128)S(1)}, f32[2,4,8,128]{3,2,1,0:T(8,128)S(1)}, u32[]{:S(2)}, u32[]{:S(2)}) collective-permute-start(f32[2,4,8,128]{3,2,1,0:T(8,128)S(1)} %pad_maximum_fusion.6), channel_id=1, source_target_pairs={{0,2},{2,0},{1,3},{3,1},{4,6},{6,4},{5,7},{7,5},{8,10},{10,8},{9,1... | collective-permute-start | bytes 98312 | tf_op jit(solution)/shard_map/ppermute | solution.py:260
  51.8 2.3 %copy-start.8 = (s32[4,128]{1,0:T(4,128)S(1)}, s32[4,128]{1,0:T(4,128)}, u32[]{:S(2)}) copy-start(s32[4,128]{1,0:T(4,128)} %param.17) | copy-start | bytes 6148
  52.6 9.5 %collective-permute-start.4 = (bf16[132,8,128]{2,1,0:T(8,128)(2,1)}, bf16[132,8,128]{2,1,0:T(8,128)(2,1)S(1)}, u32[]{:S(2)}, u32[]{:S(2)}) collective-permute-start(bf16[132,8,128]{2,1,0:T(8,128)(2,1)} %get-tuple-element.32), channel_id=1, source_target_pairs={{0,2},{2,0},{1,3},{3,1},{4,6},{6,4},{5,7},{7,5},{8,10},{10,8},{9,1... | collective-permute-start | bytes 811016 | tf_op jit(solution)/shard_map/ppermute | solution.py:200
  54.2 1.0 %copy-start.5 = (bf16[132,8,128]{2,1,0:T(8,128)(2,1)S(1)}, bf16[132,8,128]{2,1,0:T(8,128)(2,1)}, u32[]{:S(2)}) copy-start(bf16[132,8,128]{2,1,0:T(8,128)(2,1)} %get-tuple-element.33) | copy-start | bytes 811012
  55.1 17.7 %collective-permute-start.5 = (bf16[132,8,128]{2,1,0:T(8,128)(2,1)S(1)}, bf16[132,8,128]{2,1,0:T(8,128)(2,1)S(1)}, u32[]{:S(2)}, u32[]{:S(2)}) collective-permute-start(bf16[132,8,128]{2,1,0:T(8,128)(2,1)S(1)} %copy-done.5), channel_id=1, source_target_pairs={{0,2},{2,0},{1,3},{3,1},{4,6},{6,4},{5,7},{7,5},{8,10},{10,8},{9,1... | collective-permute-start | bytes 811016 | tf_op jit(solution)/shard_map/ppermute | solution.py:200
  71.3 6.9 %collective-permute-start.6 = (bf16[132,8,128]{2,1,0:T(8,128)(2,1)S(1)}, bf16[132,8,128]{2,1,0:T(8,128)(2,1)S(1)}, u32[]{:S(2)}, u32[]{:S(2)}) collective-permute-start(bf16[132,8,128]{2,1,0:T(8,128)(2,1)S(1)} %slice.225), channel_id=1, source_target_pairs={{0,2},{2,0},{1,3},{3,1},{4,6},{6,4},{5,7},{7,5},{8,10},{10,8},{9,1... | collective-permute-start | bytes 811016 | tf_op jit(solution)/shard_map/ppermute | solution.py:207
  82.9 6.5 %collective-permute-start.7 = (bf16[132,8,128]{2,1,0:T(8,128)(2,1)S(1)}, bf16[132,8,128]{2,1,0:T(8,128)(2,1)S(1)}, u32[]{:S(2)}, u32[]{:S(2)}) collective-permute-start(bf16[132,8,128]{2,1,0:T(8,128)(2,1)S(1)} %slice.227), channel_id=1, source_target_pairs={{0,2},{2,0},{1,3},{3,1},{4,6},{6,4},{5,7},{7,5},{8,10},{10,8},{9,1... | collective-permute-start | bytes 811016 | tf_op jit(solution)/shard_map/ppermute | solution.py:207
  89.9 1.9 %copy-start.1 = (bf16[4,33,33]{2,0,1:T(4,128)(2,1)S(1)}, bf16[4,33,33]{2,0,1:T(4,128)(2,1)}, u32[]{:S(2)}) copy-start(bf16[4,33,33]{2,0,1:T(4,128)(2,1)} %param.23) | copy-start | bytes 26140

commit v16 on v10

--- a/solution.py
+++ b/solution.py
@@ -31,23 +31,41 @@
 
 
 def rim_kernel(depth, q_ref, wx_ref, wy_ref, left_ref, right_ref):
-    local_bins, width_x = q_ref.shape[:2]
-    for out_ref, lo in ((left_ref, width_x - depth), (right_ref, 0)):
-        out_ref[0:local_bins] = q_ref[:, lo : lo + depth].astype(out_ref.dtype)
+    local_bins = q_ref.shape[0]
+    plane = pl.program_id(0)
+    width_x = pl.num_programs(0)
+
+    def fill(out_ref):
+        out_ref[0:local_bins] = q_ref[...].astype(out_ref.dtype)
         for k, wind_ref in enumerate((wx_ref, wy_ref)):
-            wind = wind_ref[lo : lo + depth]
+            wind = wind_ref[...]
             high = wind.astype(out_ref.dtype)
             low = (wind - high.astype(jnp.float32)).astype(out_ref.dtype)
             out_ref[local_bins + k] = high
             out_ref[local_bins + 2 + k] = low
 
+    pl.when(plane >= width_x - depth)(lambda: fill(left_ref))
+    pl.when(plane < depth)(lambda: fill(right_ref))
+
 
 def rims(bin_mass, wind_x, wind_y, depth):
     local_bins, width_x, width_z, width_y = bin_mass.shape
     shape = jax.ShapeDtypeStruct((local_bins + 4, depth, width_z, width_y), jnp.bfloat16)
+    out_block = (local_bins + 4, 1, width_z, width_y)
+    wind_spec = pl.BlockSpec((1, width_z, width_y), lambda x: (x, 0, 0))
     return pl.pallas_call(
         functools.partial(rim_kernel, depth),
         out_shape=(shape, shape),
+        grid=(width_x,),
+        in_specs=[
+            pl.BlockSpec((local_bins, 1, width_z, width_y), lambda x: (0, x, 0, 0)),
+            wind_spec,
+            wind_spec,
+        ],
+        out_specs=(
+            pl.BlockSpec(out_block, lambda x: (0, jnp.maximum(x - (width_x - depth), 0), 0, 0)),
+            pl.BlockSpec(out_block, lambda x: (0, jnp.minimum(x, depth - 1), 0, 0)),
+        ),
     )(bin_mass, wind_x, wind_y)
 
 

time: 91.6 us -> 92.5 us (level)
  no operation moved by 1% of the time
where the time goes in v16:
time: 92.5 us; the launch traced here: 92.2 us
  waiting for transfers between devices  31.4 us (34%)
  matrix products  16.4 us (18%)
  starting transfers between devices  14.2 us (15%)
  other arithmetic  11.7 us (13%)
  Pallas kernels  11.6 us (13%)
  local copies, waits for them, and re-layouts  5.61 us (6%)
  between operations  1.17 us (1%)
    ppermute x2, waiting for transfers between devices, advect_kernel_call(): lax.ppermute(message, 'tiles', pairs)  16.7 us
    dot_general x16, matrix products, collide(): jnp.dot(table, iterate.astype(jnp.bfloat16), preferred_element_type=jnp.f...  12.6 us
    pallas_call x1, Pallas kernels, advect_kernel_call(): pl.pallas_call(functools.partial(advect_kernel, section_weights), out_sha...  7.8 us
    ppermute x2, waiting for transfers between devices, paired_collision(): arrived = lax.ppermute(away[:, chunk], 'bins', swap)  6.41 us
    ppermute x2, starting transfers between devices, advect_kernel_call(): lax.ppermute(message, 'tiles', pairs)  6.26 us
    ppermute x2, waiting for transfers between devices, paired_collision(): returned.append(lax.ppermute(change[local_bins:], 'bins', swap))  5.4 us
    add x6, other arithmetic, collide(): iterate + collision_rate * products[all_bins:] * products[:all_bins]  3.85 us
    pallas_call x1, Pallas kernels, rims(): pl.pallas_call(functools.partial(rim_kernel, depth), out_shape=(shape, sh...  3.82 us
  transfers between devices with their start and end apart: 8, of which 7 were waited for; matrix products, arithmetic and copies ran while one was open for 22% of the time, Pallas kernels for 0%

profile of v16, /device:TPU:0, one launch (start us, length us, event | category | flops | bytes accessed | tf_op | source)
XLA Modules:
  0.0 92.2 jit_solution(8566174576802689192)
XLA Ops:
  0.7 1.4 %compare_select_fusion = (f32[4,8,128]{2,1,0:T(8,128)}, f32[4,8,128]{2,1,0:T(8,128)}) fusion(f32[4,8,128]{2,1,0:T(8,128)} %param.14, s32[4,128]{1,0:T(4,128)} %param.17, s32[8]{0:T(128)S(1)} %iota_add_fusion, f32[4,8,128]{2,1,0:T(8,128)} %param.13), kind=kLoop, calls=%fused_computation.121 | loop fusion | flops 12288 | bytes 67616 | tf_op jit(solution)/shard_map/mul | solution.py:250
  2.1 3.8 %shard_map.139 = (bf16[136,3,8,128]{3,2,1,0:T(8,128)(2,1)}, bf16[136,3,8,128]{3,2,1,0:T(8,128)(2,1)}) custom-call(f32[132,4,8,128]{3,2,1,0:T(8,128)} %q_ref.3, f32[4,8,128]{2,1,0:T(8,128)} %get-tuple-element.38.wx_ref.refs_8_, f32[4,8,128]{2,1,0:T(8,128)} %get-tuple-element.37.wy_ref.refs_9_), custom_call_target="tpu_custom_call" | custom-call | tf_op jit(solution)/shard_map/pallas_call | solution.py:56
  5.9 5.0 %collective-permute-start = (bf16[136,3,8,128]{3,2,1,0:T(8,128)(2,1)}, bf16[136,3,8,128]{3,2,1,0:T(8,128)(2,1)S(1)}, u32[]{:S(2)}, u32[]{:S(2)}) collective-permute-start(bf16[136,3,8,128]{3,2,1,0:T(8,128)(2,1)} %get-tuple-element.11), channel_id=1, source_target_pairs={{0,4},{4,8},{8,12},{1,5},{5,9},{9,13},{2,6},{6,10},{10,14},{3,7},{... | collective-permute-start | bytes 2506760 | tf_op jit(solution)/shard_map/ppermute | solution.py:113
  10.9 1.3 %collective-permute-start.1 = (bf16[136,3,8,128]{3,2,1,0:T(8,128)(2,1)}, bf16[136,3,8,128]{3,2,1,0:T(8,128)(2,1)S(1)}, u32[]{:S(2)}, u32[]{:S(2)}) collective-permute-start(bf16[136,3,8,128]{3,2,1,0:T(8,128)(2,1)} %get-tuple-element.13), channel_id=1, source_target_pairs={{4,0},{8,4},{12,8},{5,1},{9,5},{13,9},{6,2},{10,6},{14,10},{7,3},{... | collective-permute-start | bytes 2506760 | tf_op jit(solution)/shard_map/ppermute | solution.py:113
  12.8 2.0 %multiply_reduce_fusion = f32[264,8,33]{0,2,1:T(8,128)S(1)} fusion(f32[264,8]{0,1:T(8,128)S(1)} %fusion.66, f32[8,8,33,33]{3,1,2,0:T(8,128)S(1)} %fusion.57, s32[264]{0:T(512)S(1)} %get-tuple-element.35), kind=kOutput, calls=%fused_computation | convolution fusion | flops 221851072 | bytes 567072 | tf_op jit(solution)/shard_map/bm,acmn->bacn/dot_general | solution.py:168
  15.1 1.1 %fusion.4 = bf16[264,264]{0,1:T(8,128)(2,1)S(1)} fusion(f32[264,8,33]{0,2,1:T(8,128)S(1)} %multiply_reduce_fusion, f32[264,8]{0,1:T(8,128)S(1)} %fusion.66, f32[264,33]{0,1:T(8,128)S(1)} %fusion.54), kind=kOutput, calls=%fused_computation.17 | convolution fusion | flops 220936320 | bytes 461472 | tf_op jit(solution)/shard_map/bcn,dc,dn->bd/dot_general | solution.py:170
  16.4 12.6 %collective-permute-done.left_ref.refs_0_.refs_1_.refs_2_.refs_3_ = bf16[136,3,8,128]{3,2,1,0:T(8,128)(2,1)S(1)} collective-permute-done((bf16[136,3,8,128]{3,2,1,0:T(8,128)(2,1)}, bf16[136,3,8,128]{3,2,1,0:T(8,128)(2,1)S(1)}, u32[]{:S(2)}, u32[]{:S(2)}) %collective-permute-start) | collective-permute-done | bytes 835616 | tf_op jit(solution)/shard_map/ppermute | solution.py:113
  29.0 4.1 %collective-permute-done.1.right_ref.refs_4_.refs_5_.refs_6_.refs_7_ = bf16[136,3,8,128]{3,2,1,0:T(8,128)(2,1)S(1)} collective-permute-done((bf16[136,3,8,128]{3,2,1,0:T(8,128)(2,1)}, bf16[136,3,8,128]{3,2,1,0:T(8,128)(2,1)S(1)}, u32[]{:S(2)}, u32[]{:S(2)}) %collective-permute-start.1) | collective-permute-done | bytes 835616 | tf_op jit(solution)/shard_map/ppermute | solution.py:113
  33.1 1.0 %copy-done.3 = bf16[136,3,8,128]{3,2,1,0:T(8,128)(2,1)} copy-done((bf16[136,3,8,128]{3,2,1,0:T(8,128)(2,1)}, bf16[136,3,8,128]{3,2,1,0:T(8,128)(2,1)S(1)}, u32[]{:S(2)}) %copy-start.3) | copy-done | bytes 835608
  34.0 7.8 %shard_map.140 = (f32[132,4,8,128]{3,2,1,0:T(8,128)}, f32[132,4,1,128]{3,2,1,0:T(1,128)}) custom-call(f32[132,4,8,128]{3,2,1,0:T(8,128)} %q_ref.3, bf16[136,3,8,128]{3,2,1,0:T(8,128)(2,1)} %copy-done.2, bf16[136,3,8,128]{3,2,1,0:T(8,128)(2,1)} %copy-done.3, bf16[136,3,8,128]{3,2,1,0:T(8,128)(2,1)} %copy-done.2, bf16[136,3,8,128]{3,2,1,0:T(8,128)(2,1)} %copy-done.2, ...), custom_call_target="tpu_custom_call" | custom-call | flops 43253760 | bytes 10813440 | tf_op jit(solution)/shard_map/pallas_call | solution.py:126
  41.8 1.3 %collective-permute-start.2 = (f32[132,4,1,128]{3,2,1,0:T(1,128)}, f32[132,4,1,128]{3,2,1,0:T(1,128)S(1)}, u32[]{:S(2)}, u32[]{:S(2)}) collective-permute-start(f32[132,4,1,128]{3,2,1,0:T(1,128)} %get-tuple-element.15), channel_id=1, source_target_pairs={{1,0},{3,2},{5,4},{7,6},{9,8},{11,10},{13,12},{15,14},{17,16},{19,... | collective-permute-start | bytes 811016 | tf_op jit(solution)/shard_map/ppermute | solution.py:141
  43.2 2.0 %slice.137 = f32[132,4,7,128]{3,2,1,0:T(8,128)S(1)} slice(f32[132,4,8,128]{3,2,1,0:T(8,128)} %get-tuple-element.14), slice={[0:132], [0:4], [1:8], [0:128]} | slice | bytes 3784704 | tf_op jit(solution)/shard_map/slice | solution.py:267
  45.5 1.3 %multiply_reduce_fusion.1 = (f32[4,8,128]{2,1,0:T(8,128)S(1)}, f32[4,8,128]{2,1,0:T(8,128)S(1)}, f32[132,4,8,128]{3,2,1,0:T(8,128)S(1)}) fusion(f32[132]{0:T(256)S(1)} %get-tuple-element.40, f32[132]{0:T(256)S(1)} %copy-done.11, f32[132,4,1,128]{3,2,1,0:T(1,128)S(1)} %collective-permute-done.2, f32[132,4,7,128]{3,2,1,0:T(8,128)S(1)} %slice.137, ...), kind=kLoop, calls=%fused_computation.6 | loop fusion | flops 4317184 | bytes 6522944 | tf_op jit(solution)/shard_map/reduce_sum | solution.py:273
  46.8 1.6 %collective-permute-start.3 = (f32[2,4,8,128]{3,2,1,0:T(8,128)S(1)}, f32[2,4,8,128]{3,2,1,0:T(8,128)S(1)}, u32[]{:S(2)}, u32[]{:S(2)}) collective-permute-start(f32[2,4,8,128]{3,2,1,0:T(8,128)S(1)} %pad_maximum_fusion.6), channel_id=1, source_target_pairs={{0,2},{2,0},{1,3},{3,1},{4,6},{6,4},{5,7},{7,5},{8,10},{10,8},{9,1... | collective-permute-start | bytes 98312 | tf_op jit(solution)/shard_map/ppermute | solution.py:278
  48.3 2.7 %collective-permute-done.3 = f32[2,4,8,128]{3,2,1,0:T(8,128)S(1)} collective-permute-done((f32[2,4,8,128]{3,2,1,0:T(8,128)S(1)}, f32[2,4,8,128]{3,2,1,0:T(8,128)S(1)}, u32[]{:S(2)}, u32[]{:S(2)}) %collective-permute-start.3) | collective-permute-done | bytes 32800 | tf_op jit(solution)/shard_map/ppermute | solution.py:278
  51.0 0.6 fusion.62
  52.2 0.8 slice_bitcast_fusion.2
  53.0 1.5 %collective-permute-start.4 = (bf16[132,8,128]{2,1,0:T(8,128)(2,1)}, bf16[132,8,128]{2,1,0:T(8,128)(2,1)S(1)}, u32[]{:S(2)}, u32[]{:S(2)}) collective-permute-start(bf16[132,8,128]{2,1,0:T(8,128)(2,1)} %get-tuple-element.32), channel_id=1, source_target_pairs={{0,2},{2,0},{1,3},{3,1},{4,6},{6,4},{5,7},{7,5},{8,10},{10,8},{9,1... | collective-permute-start | bytes 811016 | tf_op jit(solution)/shard_map/ppermute | solution.py:218
  54.7 0.8 copy-done.5
  56.2 6.4 %collective-permute-done.4 = bf16[132,8,128]{2,1,0:T(8,128)(2,1)S(1)} collective-permute-done((bf16[132,8,128]{2,1,0:T(8,128)(2,1)}, bf16[132,8,128]{2,1,0:T(8,128)(2,1)S(1)}, u32[]{:S(2)}, u32[]{:S(2)}) %collective-permute-start.4) | collective-permute-done | bytes 270368 | tf_op jit(solution)/shard_map/ppermute | solution.py:218
  62.6 0.8 fusion.53
  63.4 0.8 fusion.47
  64.3 0.5 fusion.20
  64.8 0.8 fusion.45
  65.6 0.8 fusion.43
  66.4 0.7 fusion.18
  67.1 0.8 fusion.41
  67.8 0.8 fusion.39
  68.7 0.6 fusion.16
  69.3 0.8 fusion.37
  70.0 0.8 fusion.35
  70.8 0.7 fusion.5
  71.7 1.6 %collective-permute-start.6 = (bf16[132,8,128]{2,1,0:T(8,128)(2,1)S(1)}, bf16[132,8,128]{2,1,0:T(8,128)(2,1)S(1)}, u32[]{:S(2)}, u32[]{:S(2)}) collective-permute-start(bf16[132,8,128]{2,1,0:T(8,128)(2,1)S(1)} %slice.225), channel_id=1, source_target_pairs={{0,2},{2,0},{1,3},{3,1},{4,6},{6,4},{5,7},{7,5},{8,10},{10,8},{9,1... | collective-permute-start | bytes 811016 | tf_op jit(solution)/shard_map/ppermute | solution.py:225
  73.3 0.8 fusion.52
  74.1 0.8 fusion.33
  75.5 0.8 fusion.31
  76.3 0.8 fusion.29
  77.1 0.9 fusion.11
  78.0 0.6 collective-permute-done.6
  78.6 0.8 fusion.27
  79.4 0.8 fusion.25
  80.2 0.6 fusion.9
  80.8 0.8 fusion.23
  81.6 0.8 fusion.21
  82.4 0.7 fusion.6
  83.3 1.6 %collective-permute-start.7 = (bf16[132,8,128]{2,1,0:T(8,128)(2,1)S(1)}, bf16[132,8,128]{2,1,0:T(8,128)(2,1)S(1)}, u32[]{:S(2)}, u32[]{:S(2)}) collective-permute-start(bf16[132,8,128]{2,1,0:T(8,128)(2,1)S(1)} %slice.227), channel_id=1, source_target_pairs={{0,2},{2,0},{1,3},{3,1},{4,6},{6,4},{5,7},{7,5},{8,10},{10,8},{9,1... | collective-permute-start | bytes 811016 | tf_op jit(solution)/shard_map/ppermute | solution.py:225
  85.0 4.8 %collective-permute-done.7 = bf16[132,8,128]{2,1,0:T(8,128)(2,1)S(1)} collective-permute-done((bf16[132,8,128]{2,1,0:T(8,128)(2,1)S(1)}, bf16[132,8,128]{2,1,0:T(8,128)(2,1)S(1)}, u32[]{:S(2)}, u32[]{:S(2)}) %collective-permute-start.7) | collective-permute-done | bytes 270368 | tf_op jit(solution)/shard_map/ppermute | solution.py:225
  90.3 1.8 %fusion.1 = f32[132,4,8,128]{3,2,1,0:T(8,128)} fusion(bf16[132,4,8,128]{3,2,1,0:T(8,128)(2,1)S(1)} %bitcast.128, f32[132,4,8,128]{3,2,1,0:T(8,128)S(1)} %get-tuple-element.23, f32[4,8,128]{2,1,0:T(8,128)S(1)} %compare_convert_fusion, f32[4,8,128]{2,1,0:T(8,128)S(1)} %get-tuple-element.22, f32[132]{0:T(256)S(1)} %get-tuple-element.39), kind=kLoop, calls=%fused_computation.4 | loop fusion | flops 3244032 | bytes 5440016 | tf_op jit(solution)/shard_map/mul | solution.py:290
  (66 shorter events, 4.3 us)
Async XLA Ops:
  0.6 11.8 %copy-start = (bf16[4,33,33]{2,0,1:T(4,128)(2,1)S(1)}, bf16[4,33,33]{2,0,1:T(4,128)(2,1)}, u32[]{:S(2)}) copy-start(bf16[4,33,33]{2,0,1:T(4,128)(2,1)} %param.23) | copy-start | bytes 26140
  2.1 10.1 %copy-start.12 = (s32[264]{0:T(512)S(1)}, s32[264]{0:T(512)}, u32[]{:S(2)}) copy-start(s32[264]{0:T(512)} %param.21) | copy-start | bytes 3172
  2.1 10.3 %copy-start.9 = (s32[8,8]{1,0:T(8,128)S(1)}, s32[8,8]{1,0:T(8,128)}, u32[]{:S(2)}) copy-start(s32[8,8]{1,0:T(8,128)} %param.22) | copy-start | bytes 772
  5.9 23.1 %collective-permute-start = (bf16[136,3,8,128]{3,2,1,0:T(8,128)(2,1)}, bf16[136,3,8,128]{3,2,1,0:T(8,128)(2,1)S(1)}, u32[]{:S(2)}, u32[]{:S(2)}) collective-permute-start(bf16[136,3,8,128]{3,2,1,0:T(8,128)(2,1)} %get-tuple-element.11), channel_id=1, source_target_pairs={{0,4},{4,8},{8,12},{1,5},{5,9},{9,13},{2,6},{6,10},{10,14},{3,7},{... | collective-permute-start | bytes 2506760 | tf_op jit(solution)/shard_map/ppermute | solution.py:113
  10.9 22.2 %collective-permute-start.1 = (bf16[136,3,8,128]{3,2,1,0:T(8,128)(2,1)}, bf16[136,3,8,128]{3,2,1,0:T(8,128)(2,1)S(1)}, u32[]{:S(2)}, u32[]{:S(2)}) collective-permute-start(bf16[136,3,8,128]{3,2,1,0:T(8,128)(2,1)} %get-tuple-element.13), channel_id=1, source_target_pairs={{4,0},{8,4},{12,8},{5,1},{9,5},{13,9},{6,2},{10,6},{14,10},{7,3},{... | collective-permute-start | bytes 2506760 | tf_op jit(solution)/shard_map/ppermute | solution.py:113
  16.4 26.8 %copy-start.10 = (f32[132]{0:T(256)S(1)}, f32[132]{0:T(256)}, u32[]{:S(2)}) copy-start(f32[132]{0:T(256)} %param.18) | copy-start | bytes 1588
  16.4 26.8 %copy-start.11 = (f32[132]{0:T(256)S(1)}, f32[132]{0:T(256)}, u32[]{:S(2)}) copy-start(f32[132]{0:T(256)} %param.19) | copy-start | bytes 1588
  16.4 26.8 %copy-start.13 = (f32[132]{0:T(256)S(1)}, f32[132]{0:T(256)}, u32[]{:S(2)}) copy-start(f32[132]{0:T(256)} %param.20) | copy-start | bytes 1588
  29.0 4.1 %copy-start.2 = (bf16[136,3,8,128]{3,2,1,0:T(8,128)(2,1)}, bf16[136,3,8,128]{3,2,1,0:T(8,128)(2,1)S(1)}, u32[]{:S(2)}) copy-start(bf16[136,3,8,128]{3,2,1,0:T(8,128)(2,1)S(1)} %collective-permute-done.left_ref.refs_0_.refs_1_.refs_2_.refs_3_) | copy-start | bytes 2506756
  33.1 1.0 %copy-start.3 = (bf16[136,3,8,128]{3,2,1,0:T(8,128)(2,1)}, bf16[136,3,8,128]{3,2,1,0:T(8,128)(2,1)S(1)}, u32[]{:S(2)}) copy-start(bf16[136,3,8,128]{3,2,1,0:T(8,128)(2,1)S(1)} %collective-permute-done.1.right_ref.refs_4_.refs_5_.refs_6_.refs_7_) | copy-start | bytes 2506756
  41.8 3.6 %collective-permute-start.2 = (f32[132,4,1,128]{3,2,1,0:T(1,128)}, f32[132,4,1,128]{3,2,1,0:T(1,128)S(1)}, u32[]{:S(2)}, u32[]{:S(2)}) collective-permute-start(f32[132,4,1,128]{3,2,1,0:T(1,128)} %get-tuple-element.15), channel_id=1, source_target_pairs={{1,0},{3,2},{5,4},{7,6},{9,8},{11,10},{13,12},{15,14},{17,16},{19,... | collective-permute-start | bytes 811016 | tf_op jit(solution)/shard_map/ppermute | solution.py:141
  43.2 2.3 %copy-start.4 = (f32[132,4,8,128]{3,2,1,0:T(8,128)S(1)}, f32[132,4,8,128]{3,2,1,0:T(8,128)}, u32[]{:S(2)}) copy-start(f32[132,4,8,128]{3,2,1,0:T(8,128)} %get-tuple-element.14) | copy-start | bytes 6488068
  45.5 5.5 %copy-start.6 = (f32[4,8,128]{2,1,0:T(8,128)S(1)}, f32[4,8,128]{2,1,0:T(8,128)}, u32[]{:S(2)}) copy-start(f32[4,8,128]{2,1,0:T(8,128)} %param.16) | copy-start | bytes 49156
  45.5 5.5 %copy-start.7 = (f32[4,8,128]{2,1,0:T(8,128)S(1)}, f32[4,8,128]{2,1,0:T(8,128)}, u32[]{:S(2)}) copy-start(f32[4,8,128]{2,1,0:T(8,128)} %param.15) | copy-start | bytes 49156
  46.8 4.2 %collective-permute-start.3 = (f32[2,4,8,128]{3,2,1,0:T(8,128)S(1)}, f32[2,4,8,128]{3,2,1,0:T(8,128)S(1)}, u32[]{:S(2)}, u32[]{:S(2)}) collective-permute-start(f32[2,4,8,128]{3,2,1,0:T(8,128)S(1)} %pad_maximum_fusion.6), channel_id=1, source_target_pairs={{0,2},{2,0},{1,3},{3,1},{4,6},{6,4},{5,7},{7,5},{8,10},{10,8},{9,1... | collective-permute-start | bytes 98312 | tf_op jit(solution)/shard_map/ppermute | solution.py:278
  52.2 2.3 %copy-start.8 = (s32[4,128]{1,0:T(4,128)S(1)}, s32[4,128]{1,0:T(4,128)}, u32[]{:S(2)}) copy-start(s32[4,128]{1,0:T(4,128)} %param.17) | copy-start | bytes 6148
  53.0 9.5 %collective-permute-start.4 = (bf16[132,8,128]{2,1,0:T(8,128)(2,1)}, bf16[132,8,128]{2,1,0:T(8,128)(2,1)S(1)}, u32[]{:S(2)}, u32[]{:S(2)}) collective-permute-start(bf16[132,8,128]{2,1,0:T(8,128)(2,1)} %get-tuple-element.32), channel_id=1, source_target_pairs={{0,2},{2,0},{1,3},{3,1},{4,6},{6,4},{5,7},{7,5},{8,10},{10,8},{9,1... | collective-permute-start | bytes 811016 | tf_op jit(solution)/shard_map/ppermute | solution.py:218
  54.6 1.0 %copy-start.5 = (bf16[132,8,128]{2,1,0:T(8,128)(2,1)S(1)}, bf16[132,8,128]{2,1,0:T(8,128)(2,1)}, u32[]{:S(2)}) copy-start(bf16[132,8,128]{2,1,0:T(8,128)(2,1)} %get-tuple-element.33) | copy-start | bytes 811012
  55.5 17.7 %collective-permute-start.5 = (bf16[132,8,128]{2,1,0:T(8,128)(2,1)S(1)}, bf16[132,8,128]{2,1,0:T(8,128)(2,1)S(1)}, u32[]{:S(2)}, u32[]{:S(2)}) collective-permute-start(bf16[132,8,128]{2,1,0:T(8,128)(2,1)S(1)} %copy-done.5), channel_id=1, source_target_pairs={{0,2},{2,0},{1,3},{3,1},{4,6},{6,4},{5,7},{7,5},{8,10},{10,8},{9,1... | collective-permute-start | bytes 811016 | tf_op jit(solution)/shard_map/ppermute | solution.py:218
  71.7 6.9 %collective-permute-start.6 = (bf16[132,8,128]{2,1,0:T(8,128)(2,1)S(1)}, bf16[132,8,128]{2,1,0:T(8,128)(2,1)S(1)}, u32[]{:S(2)}, u32[]{:S(2)}) collective-permute-start(bf16[132,8,128]{2,1,0:T(8,128)(2,1)S(1)} %slice.225), channel_id=1, source_target_pairs={{0,2},{2,0},{1,3},{3,1},{4,6},{6,4},{5,7},{7,5},{8,10},{10,8},{9,1... | collective-permute-start | bytes 811016 | tf_op jit(solution)/shard_map/ppermute | solution.py:225
  83.3 6.5 %collective-permute-start.7 = (bf16[132,8,128]{2,1,0:T(8,128)(2,1)S(1)}, bf16[132,8,128]{2,1,0:T(8,128)(2,1)S(1)}, u32[]{:S(2)}, u32[]{:S(2)}) collective-permute-start(bf16[132,8,128]{2,1,0:T(8,128)(2,1)S(1)} %slice.227), channel_id=1, source_target_pairs={{0,2},{2,0},{1,3},{3,1},{4,6},{6,4},{5,7},{7,5},{8,10},{10,8},{9,1... | collective-permute-start | bytes 811016 | tf_op jit(solution)/shard_map/ppermute | solution.py:225
  90.3 1.9 %copy-start.1 = (bf16[4,33,33]{2,0,1:T(4,128)(2,1)S(1)}, bf16[4,33,33]{2,0,1:T(4,128)(2,1)}, u32[]{:S(2)}) copy-start(bf16[4,33,33]{2,0,1:T(4,128)(2,1)} %param.23) | copy-start | bytes 26140

commit v17 on v10

--- a/solution.py
+++ b/solution.py
@@ -30,25 +30,28 @@
     return array
 
 
-def rim_kernel(depth, q_ref, wx_ref, wy_ref, left_ref, right_ref):
-    local_bins, width_x = q_ref.shape[:2]
+def rim_kernel(depth, q_ref, east_ref, north_ref, terrain_ref, left_ref, right_ref):
+    local_bins, width_x, width_z = q_ref.shape[:3]
+    levels = lax.axis_index("vert") * width_z + lax.broadcasted_iota(jnp.int32, east_ref.shape, 1)
+    open_cells = (levels >= terrain_ref[...][:, None, :]).astype(jnp.float32)
+    winds = (east_ref[...] * open_cells, north_ref[...] * open_cells)
     for out_ref, lo in ((left_ref, width_x - depth), (right_ref, 0)):
         out_ref[0:local_bins] = q_ref[:, lo : lo + depth].astype(out_ref.dtype)
-        for k, wind_ref in enumerate((wx_ref, wy_ref)):
-            wind = wind_ref[lo : lo + depth]
+        for k, wind_all in enumerate(winds):
+            wind = wind_all[lo : lo + depth]
             high = wind.astype(out_ref.dtype)
             low = (wind - high.astype(jnp.float32)).astype(out_ref.dtype)
             out_ref[local_bins + k] = high
             out_ref[local_bins + 2 + k] = low
 
 
-def rims(bin_mass, wind_x, wind_y, depth):
+def rims(bin_mass, wind_east, wind_north, terrain_height, depth):
     local_bins, width_x, width_z, width_y = bin_mass.shape
     shape = jax.ShapeDtypeStruct((local_bins + 4, depth, width_z, width_y), jnp.bfloat16)
     return pl.pallas_call(
         functools.partial(rim_kernel, depth),
         out_shape=(shape, shape),
-    )(bin_mass, wind_x, wind_y)
+    )(bin_mass, wind_east, wind_north, terrain_height)
 
 
 def advect_kernel(weights, q_ref, left_ref, right_ref, *refs):
@@ -84,7 +87,7 @@
     bottom_ref[...] = section[:, :, :1]
 
 
-def advect_kernel_call(bin_mass, wind_x, wind_y, section_weights, tie):
+def advect_kernel_call(bin_mass, wind_x, wind_y, section_weights, tie, raw_winds):
     local_bins, width_x, width_z, width_y = bin_mass.shape
     depth = len(section_weights)
     tiles = lax.axis_size("tiles")
@@ -93,7 +96,7 @@
 
     left, right = (
         lax.ppermute(message, "tiles", pairs)
-        for message, pairs in zip(rims(bin_mass, wind_x, wind_y, depth), (up, down))
+        for message, pairs in zip(rims(bin_mass, *raw_winds, depth), (up, down))
     )
     left, tie = lax.optimization_barrier((left, tie))
     block = max(d for d in range(1, 34) if local_bins % d == 0)
@@ -235,7 +238,7 @@
     table = paired_table(bin_order, kernel_index, collision_kernels) if paired else None
     if width_x >= len(section_weights):
         table, (section_field, bottom) = advect_kernel_call(
-            bin_mass, wind_x, wind_y, section_weights, table
+            bin_mass, wind_x, wind_y, section_weights, table, (wind_east, wind_north, terrain_height)
         )
     else:
         section_field = bin_mass

time: 91.6 us -> 90.1 us (0.984)
    unnamed x41 -> x45, local copies, waits for them, and re-layouts: 2.34 us -> 2.32 us
  transfers between devices with their start and end apart: 8 -> 8, of which waited for: 7 -> 7; matrix products, arithmetic and copies ran while one was open for 22% -> 23% of each run, Pallas kernels for 0% -> 0%
where the time goes in v17:
time: 90.1 us; the launch traced here: 89.9 us
  waiting for transfers between devices  30.7 us (34%)
  matrix products  16.4 us (18%)
  starting transfers between devices  14.2 us (16%)
  other arithmetic  10.9 us (12%)
  Pallas kernels  10.8 us (12%)
  local copies, waits for them, and re-layouts  5.61 us (6%)
  between operations  1.2 us (1%)
    ppermute x2, waiting for transfers between devices, advect_kernel_call(): lax.ppermute(message, 'tiles', pairs)  16 us
    dot_general x16, matrix products, collide(): jnp.dot(table, iterate.astype(jnp.bfloat16), preferred_element_type=jnp.f...  12.6 us
    pallas_call x1, Pallas kernels, advect_kernel_call(): pl.pallas_call(functools.partial(advect_kernel, section_weights), out_sha...  7.84 us
    ppermute x2, waiting for transfers between devices, paired_collision(): arrived = lax.ppermute(away[:, chunk], 'bins', swap)  6.42 us
    ppermute x2, starting transfers between devices, advect_kernel_call(): lax.ppermute(message, 'tiles', pairs)  6.26 us
    ppermute x2, waiting for transfers between devices, paired_collision(): returned.append(lax.ppermute(change[local_bins:], 'bins', swap))  5.41 us
    add x6, other arithmetic, collide(): iterate + collision_rate * products[all_bins:] * products[:all_bins]  3.85 us
    ppermute x2, starting transfers between devices, paired_collision(): returned.append(lax.ppermute(change[local_bins:], 'bins', swap))  3.11 us
  transfers between devices with their start and end apart: 8, of which 7 were waited for; matrix products, arithmetic and copies ran while one was open for 23% of the time, Pallas kernels for 0%

profile of v17, /device:TPU:0, one launch (start us, length us, event | category | flops | bytes accessed | tf_op | source)
XLA Modules:
  0.0 89.9 jit_solution(2037843927826855965)
XLA Ops:
  0.7 3.0 %shard_map.139 = (bf16[136,3,8,128]{3,2,1,0:T(8,128)(2,1)}, bf16[136,3,8,128]{3,2,1,0:T(8,128)(2,1)}) custom-call(f32[132,4,8,128]{3,2,1,0:T(8,128)} %q_ref.3, f32[4,8,128]{2,1,0:T(8,128)} %east_ref.1, f32[4,8,128]{2,1,0:T(8,128)} %north_ref.1, s32[4,128]{1,0:T(4,128)} %terrain_ref.1), custom_call_target="tpu_custom_call" | custom-call | tf_op jit(solution)/shard_map/pallas_call | solution.py:51
  3.6 5.0 %collective-permute-start = (bf16[136,3,8,128]{3,2,1,0:T(8,128)(2,1)}, bf16[136,3,8,128]{3,2,1,0:T(8,128)(2,1)S(1)}, u32[]{:S(2)}, u32[]{:S(2)}) collective-permute-start(bf16[136,3,8,128]{3,2,1,0:T(8,128)(2,1)} %get-tuple-element.11), channel_id=1, source_target_pairs={{0,4},{4,8},{8,12},{1,5},{5,9},{9,13},{2,6},{6,10},{10,14},{3,7},{... | collective-permute-start | bytes 2506760 | tf_op jit(solution)/shard_map/ppermute | solution.py:98
  8.6 1.3 %collective-permute-start.1 = (bf16[136,3,8,128]{3,2,1,0:T(8,128)(2,1)}, bf16[136,3,8,128]{3,2,1,0:T(8,128)(2,1)S(1)}, u32[]{:S(2)}, u32[]{:S(2)}) collective-permute-start(bf16[136,3,8,128]{3,2,1,0:T(8,128)(2,1)} %get-tuple-element.13), channel_id=1, source_target_pairs={{4,0},{8,4},{12,8},{5,1},{9,5},{13,9},{6,2},{10,6},{14,10},{7,3},{... | collective-permute-start | bytes 2506760 | tf_op jit(solution)/shard_map/ppermute | solution.py:98
  10.5 2.0 %multiply_reduce_fusion = f32[264,8,33]{0,2,1:T(8,128)S(1)} fusion(f32[264,8]{0,1:T(8,128)S(1)} %fusion.66, f32[8,8,33,33]{3,1,2,0:T(8,128)S(1)} %fusion.57, s32[264]{0:T(512)S(1)} %get-tuple-element.35), kind=kOutput, calls=%fused_computation | convolution fusion | flops 221851072 | bytes 567072 | tf_op jit(solution)/shard_map/bm,acmn->bacn/dot_general | solution.py:153
  12.8 1.1 %fusion.4 = bf16[264,264]{0,1:T(8,128)(2,1)S(1)} fusion(f32[264,8,33]{0,2,1:T(8,128)S(1)} %multiply_reduce_fusion, f32[264,8]{0,1:T(8,128)S(1)} %fusion.66, f32[264,33]{0,1:T(8,128)S(1)} %fusion.54), kind=kOutput, calls=%fused_computation.17 | convolution fusion | flops 220936320 | bytes 461472 | tf_op jit(solution)/shard_map/bcn,dc,dn->bd/dot_general | solution.py:155
  14.1 0.7 compare_select_fusion
  14.8 11.9 %collective-permute-done.left_ref.refs_0_.refs_1_.refs_2_.refs_3_ = bf16[136,3,8,128]{3,2,1,0:T(8,128)(2,1)S(1)} collective-permute-done((bf16[136,3,8,128]{3,2,1,0:T(8,128)(2,1)}, bf16[136,3,8,128]{3,2,1,0:T(8,128)(2,1)S(1)}, u32[]{:S(2)}, u32[]{:S(2)}) %collective-permute-start) | collective-permute-done | bytes 835616 | tf_op jit(solution)/shard_map/ppermute | solution.py:98
  26.7 4.1 %collective-permute-done.1.right_ref.refs_4_.refs_5_.refs_6_.refs_7_ = bf16[136,3,8,128]{3,2,1,0:T(8,128)(2,1)S(1)} collective-permute-done((bf16[136,3,8,128]{3,2,1,0:T(8,128)(2,1)}, bf16[136,3,8,128]{3,2,1,0:T(8,128)(2,1)S(1)}, u32[]{:S(2)}, u32[]{:S(2)}) %collective-permute-start.1) | collective-permute-done | bytes 835616 | tf_op jit(solution)/shard_map/ppermute | solution.py:98
  30.8 0.9 %copy-done.3 = bf16[136,3,8,128]{3,2,1,0:T(8,128)(2,1)} copy-done((bf16[136,3,8,128]{3,2,1,0:T(8,128)(2,1)}, bf16[136,3,8,128]{3,2,1,0:T(8,128)(2,1)S(1)}, u32[]{:S(2)}) %copy-start.3) | copy-done | bytes 835608
  31.7 7.8 %shard_map.140 = (f32[132,4,8,128]{3,2,1,0:T(8,128)}, f32[132,4,1,128]{3,2,1,0:T(1,128)}) custom-call(f32[132,4,8,128]{3,2,1,0:T(8,128)} %q_ref.3, bf16[136,3,8,128]{3,2,1,0:T(8,128)(2,1)} %copy-done.2, bf16[136,3,8,128]{3,2,1,0:T(8,128)(2,1)} %copy-done.3, bf16[136,3,8,128]{3,2,1,0:T(8,128)(2,1)} %copy-done.2, bf16[136,3,8,128]{3,2,1,0:T(8,128)(2,1)} %copy-done.2, ...), custom_call_target="tpu_custom_call" | custom-call | flops 43253760 | bytes 10813440 | tf_op jit(solution)/shard_map/pallas_call | solution.py:111
  39.5 1.3 %collective-permute-start.2 = (f32[132,4,1,128]{3,2,1,0:T(1,128)}, f32[132,4,1,128]{3,2,1,0:T(1,128)S(1)}, u32[]{:S(2)}, u32[]{:S(2)}) collective-permute-start(f32[132,4,1,128]{3,2,1,0:T(1,128)} %get-tuple-element.15), channel_id=1, source_target_pairs={{1,0},{3,2},{5,4},{7,6},{9,8},{11,10},{13,12},{15,14},{17,16},{19,... | collective-permute-start | bytes 811016 | tf_op jit(solution)/shard_map/ppermute | solution.py:126
  40.9 2.0 %slice.137 = f32[132,4,7,128]{3,2,1,0:T(8,128)S(1)} slice(f32[132,4,8,128]{3,2,1,0:T(8,128)} %get-tuple-element.14), slice={[0:132], [0:4], [1:8], [0:128]} | slice | bytes 3784704 | tf_op jit(solution)/shard_map/slice | solution.py:252
  43.2 1.3 %multiply_reduce_fusion.1 = (f32[4,8,128]{2,1,0:T(8,128)S(1)}, f32[4,8,128]{2,1,0:T(8,128)S(1)}, f32[132,4,8,128]{3,2,1,0:T(8,128)S(1)}) fusion(f32[132]{0:T(256)S(1)} %get-tuple-element.40, f32[132]{0:T(256)S(1)} %copy-done.13, f32[132,4,1,128]{3,2,1,0:T(1,128)S(1)} %collective-permute-done.2, f32[132,4,7,128]{3,2,1,0:T(8,128)S(1)} %slice.137, ...), kind=kLoop, calls=%fused_computation.6 | loop fusion | flops 4317184 | bytes 6522944 | tf_op jit(solution)/shard_map/reduce_sum | solution.py:258
  44.5 1.6 %collective-permute-start.3 = (f32[2,4,8,128]{3,2,1,0:T(8,128)S(1)}, f32[2,4,8,128]{3,2,1,0:T(8,128)S(1)}, u32[]{:S(2)}, u32[]{:S(2)}) collective-permute-start(f32[2,4,8,128]{3,2,1,0:T(8,128)S(1)} %pad_maximum_fusion.6), channel_id=1, source_target_pairs={{0,2},{2,0},{1,3},{3,1},{4,6},{6,4},{5,7},{7,5},{8,10},{10,8},{9,1... | collective-permute-start | bytes 98312 | tf_op jit(solution)/shard_map/ppermute | solution.py:263
  46.0 2.7 %collective-permute-done.3 = f32[2,4,8,128]{3,2,1,0:T(8,128)S(1)} collective-permute-done((f32[2,4,8,128]{3,2,1,0:T(8,128)S(1)}, f32[2,4,8,128]{3,2,1,0:T(8,128)S(1)}, u32[]{:S(2)}, u32[]{:S(2)}) %collective-permute-start.3) | collective-permute-done | bytes 32800 | tf_op jit(solution)/shard_map/ppermute | solution.py:263
  48.7 0.6 fusion.62
  49.9 0.8 slice_bitcast_fusion.2
  50.7 1.5 %collective-permute-start.4 = (bf16[132,8,128]{2,1,0:T(8,128)(2,1)}, bf16[132,8,128]{2,1,0:T(8,128)(2,1)S(1)}, u32[]{:S(2)}, u32[]{:S(2)}) collective-permute-start(bf16[132,8,128]{2,1,0:T(8,128)(2,1)} %get-tuple-element.32), channel_id=1, source_target_pairs={{0,2},{2,0},{1,3},{3,1},{4,6},{6,4},{5,7},{7,5},{8,10},{10,8},{9,1... | collective-permute-start | bytes 811016 | tf_op jit(solution)/shard_map/ppermute | solution.py:203
  52.4 0.8 copy-done.5
  53.9 6.4 %collective-permute-done.4 = bf16[132,8,128]{2,1,0:T(8,128)(2,1)S(1)} collective-permute-done((bf16[132,8,128]{2,1,0:T(8,128)(2,1)}, bf16[132,8,128]{2,1,0:T(8,128)(2,1)S(1)}, u32[]{:S(2)}, u32[]{:S(2)}) %collective-permute-start.4) | collective-permute-done | bytes 270368 | tf_op jit(solution)/shard_map/ppermute | solution.py:203
  60.4 0.8 fusion.53
  61.1 0.8 fusion.47
  62.0 0.5 fusion.20
  62.5 0.8 fusion.45
  63.3 0.8 fusion.43
  64.1 0.7 fusion.18
  64.8 0.8 fusion.41
  65.6 0.8 fusion.39
  66.4 0.6 fusion.16
  67.0 0.8 fusion.37
  67.7 0.8 fusion.35
  68.6 0.7 fusion.5
  69.4 1.6 %collective-permute-start.6 = (bf16[132,8,128]{2,1,0:T(8,128)(2,1)S(1)}, bf16[132,8,128]{2,1,0:T(8,128)(2,1)S(1)}, u32[]{:S(2)}, u32[]{:S(2)}) collective-permute-start(bf16[132,8,128]{2,1,0:T(8,128)(2,1)S(1)} %slice.225), channel_id=1, source_target_pairs={{0,2},{2,0},{1,3},{3,1},{4,6},{6,4},{5,7},{7,5},{8,10},{10,8},{9,1... | collective-permute-start | bytes 811016 | tf_op jit(solution)/shard_map/ppermute | solution.py:210
  71.0 0.8 fusion.52
  71.8 0.8 fusion.33
  73.2 0.8 fusion.31
  74.0 0.8 fusion.29
  74.8 0.9 fusion.11
  75.7 0.6 collective-permute-done.6
  76.3 0.8 fusion.27
  77.1 0.8 fusion.25
  77.9 0.6 fusion.9
  78.5 0.8 fusion.23
  79.3 0.8 fusion.21
  80.1 0.7 fusion.6
  81.0 1.6 %collective-permute-start.7 = (bf16[132,8,128]{2,1,0:T(8,128)(2,1)S(1)}, bf16[132,8,128]{2,1,0:T(8,128)(2,1)S(1)}, u32[]{:S(2)}, u32[]{:S(2)}) collective-permute-start(bf16[132,8,128]{2,1,0:T(8,128)(2,1)S(1)} %slice.227), channel_id=1, source_target_pairs={{0,2},{2,0},{1,3},{3,1},{4,6},{6,4},{5,7},{7,5},{8,10},{10,8},{9,1... | collective-permute-start | bytes 811016 | tf_op jit(solution)/shard_map/ppermute | solution.py:210
  82.7 4.8 %collective-permute-done.7 = bf16[132,8,128]{2,1,0:T(8,128)(2,1)S(1)} collective-permute-done((bf16[132,8,128]{2,1,0:T(8,128)(2,1)S(1)}, bf16[132,8,128]{2,1,0:T(8,128)(2,1)S(1)}, u32[]{:S(2)}, u32[]{:S(2)}) %collective-permute-start.7) | collective-permute-done | bytes 270368 | tf_op jit(solution)/shard_map/ppermute | solution.py:210
  88.0 1.8 %fusion.1 = f32[132,4,8,128]{3,2,1,0:T(8,128)} fusion(bf16[132,4,8,128]{3,2,1,0:T(8,128)(2,1)S(1)} %bitcast.128, f32[132,4,8,128]{3,2,1,0:T(8,128)S(1)} %get-tuple-element.23, f32[4,8,128]{2,1,0:T(8,128)S(1)} %compare_convert_fusion, f32[4,8,128]{2,1,0:T(8,128)S(1)} %get-tuple-element.22, f32[132]{0:T(256)S(1)} %get-tuple-element.39), kind=kLoop, calls=%fused_computation.4 | loop fusion | flops 3244032 | bytes 5440016 | tf_op jit(solution)/shard_map/mul | solution.py:275
  (70 shorter events, 4.3 us)
Async XLA Ops:
  0.6 9.5 %copy-start = (bf16[4,33,33]{2,0,1:T(4,128)(2,1)S(1)}, bf16[4,33,33]{2,0,1:T(4,128)(2,1)}, u32[]{:S(2)}) copy-start(bf16[4,33,33]{2,0,1:T(4,128)(2,1)} %param.23) | copy-start | bytes 26140
  0.6 9.3 %copy-start.14 = (s32[264]{0:T(512)S(1)}, s32[264]{0:T(512)}, u32[]{:S(2)}) copy-start(s32[264]{0:T(512)} %param.21) | copy-start | bytes 3172
  0.7 9.5 %copy-start.11 = (s32[8,8]{1,0:T(8,128)S(1)}, s32[8,8]{1,0:T(8,128)}, u32[]{:S(2)}) copy-start(s32[8,8]{1,0:T(8,128)} %param.22) | copy-start | bytes 772
  3.6 23.1 %collective-permute-start = (bf16[136,3,8,128]{3,2,1,0:T(8,128)(2,1)}, bf16[136,3,8,128]{3,2,1,0:T(8,128)(2,1)S(1)}, u32[]{:S(2)}, u32[]{:S(2)}) collective-permute-start(bf16[136,3,8,128]{3,2,1,0:T(8,128)(2,1)} %get-tuple-element.11), channel_id=1, source_target_pairs={{0,4},{4,8},{8,12},{1,5},{5,9},{9,13},{2,6},{6,10},{10,14},{3,7},{... | collective-permute-start | bytes 2506760 | tf_op jit(solution)/shard_map/ppermute | solution.py:98
  8.6 22.2 %collective-permute-start.1 = (bf16[136,3,8,128]{3,2,1,0:T(8,128)(2,1)}, bf16[136,3,8,128]{3,2,1,0:T(8,128)(2,1)S(1)}, u32[]{:S(2)}, u32[]{:S(2)}) collective-permute-start(bf16[136,3,8,128]{3,2,1,0:T(8,128)(2,1)} %get-tuple-element.13), channel_id=1, source_target_pairs={{4,0},{8,4},{12,8},{5,1},{9,5},{13,9},{6,2},{10,6},{14,10},{7,3},{... | collective-permute-start | bytes 2506760 | tf_op jit(solution)/shard_map/ppermute | solution.py:98
  12.5 1.6 %copy-start.6 = (f32[4,8,128]{2,1,0:T(8,128)S(1)}, f32[4,8,128]{2,1,0:T(8,128)}, u32[]{:S(2)}) copy-start(f32[4,8,128]{2,1,0:T(8,128)} %east_ref.1) | copy-start | bytes 49156
  12.5 1.6 %copy-start.7 = (f32[4,8,128]{2,1,0:T(8,128)S(1)}, f32[4,8,128]{2,1,0:T(8,128)}, u32[]{:S(2)}) copy-start(f32[4,8,128]{2,1,0:T(8,128)} %north_ref.1) | copy-start | bytes 49156
  12.5 1.6 %copy-start.8 = (s32[4,128]{1,0:T(4,128)S(1)}, s32[4,128]{1,0:T(4,128)}, u32[]{:S(2)}) copy-start(s32[4,128]{1,0:T(4,128)} %terrain_ref.1) | copy-start | bytes 6148
  26.7 4.1 %copy-start.2 = (bf16[136,3,8,128]{3,2,1,0:T(8,128)(2,1)}, bf16[136,3,8,128]{3,2,1,0:T(8,128)(2,1)S(1)}, u32[]{:S(2)}) copy-start(bf16[136,3,8,128]{3,2,1,0:T(8,128)(2,1)S(1)} %collective-permute-done.left_ref.refs_0_.refs_1_.refs_2_.refs_3_) | copy-start | bytes 2506756
  30.8 0.9 %copy-start.3 = (bf16[136,3,8,128]{3,2,1,0:T(8,128)(2,1)}, bf16[136,3,8,128]{3,2,1,0:T(8,128)(2,1)S(1)}, u32[]{:S(2)}) copy-start(bf16[136,3,8,128]{3,2,1,0:T(8,128)(2,1)S(1)} %collective-permute-done.1.right_ref.refs_4_.refs_5_.refs_6_.refs_7_) | copy-start | bytes 2506756
  31.7 9.1 %copy-start.12 = (f32[132]{0:T(256)S(1)}, f32[132]{0:T(256)}, u32[]{:S(2)}) copy-start(f32[132]{0:T(256)} %param.18) | copy-start | bytes 1588
  31.7 9.2 %copy-start.13 = (f32[132]{0:T(256)S(1)}, f32[132]{0:T(256)}, u32[]{:S(2)}) copy-start(f32[132]{0:T(256)} %param.19) | copy-start | bytes 1588
  31.7 9.2 %copy-start.15 = (f32[132]{0:T(256)S(1)}, f32[132]{0:T(256)}, u32[]{:S(2)}) copy-start(f32[132]{0:T(256)} %param.20) | copy-start | bytes 1588
  39.5 3.6 %collective-permute-start.2 = (f32[132,4,1,128]{3,2,1,0:T(1,128)}, f32[132,4,1,128]{3,2,1,0:T(1,128)S(1)}, u32[]{:S(2)}, u32[]{:S(2)}) collective-permute-start(f32[132,4,1,128]{3,2,1,0:T(1,128)} %get-tuple-element.15), channel_id=1, source_target_pairs={{1,0},{3,2},{5,4},{7,6},{9,8},{11,10},{13,12},{15,14},{17,16},{19,... | collective-permute-start | bytes 811016 | tf_op jit(solution)/shard_map/ppermute | solution.py:126
  40.9 2.3 %copy-start.4 = (f32[132,4,8,128]{3,2,1,0:T(8,128)S(1)}, f32[132,4,8,128]{3,2,1,0:T(8,128)}, u32[]{:S(2)}) copy-start(f32[132,4,8,128]{3,2,1,0:T(8,128)} %get-tuple-element.14) | copy-start | bytes 6488068
  43.2 5.5 %copy-start.9 = (f32[4,8,128]{2,1,0:T(8,128)S(1)}, f32[4,8,128]{2,1,0:T(8,128)}, u32[]{:S(2)}) copy-start(f32[4,8,128]{2,1,0:T(8,128)} %param.16) | copy-start | bytes 49156
  43.2 5.5 %copy-start.10 = (f32[4,8,128]{2,1,0:T(8,128)S(1)}, f32[4,8,128]{2,1,0:T(8,128)}, u32[]{:S(2)}) copy-start(f32[4,8,128]{2,1,0:T(8,128)} %param.15) | copy-start | bytes 49156
  44.5 4.2 %collective-permute-start.3 = (f32[2,4,8,128]{3,2,1,0:T(8,128)S(1)}, f32[2,4,8,128]{3,2,1,0:T(8,128)S(1)}, u32[]{:S(2)}, u32[]{:S(2)}) collective-permute-start(f32[2,4,8,128]{3,2,1,0:T(8,128)S(1)} %pad_maximum_fusion.6), channel_id=1, source_target_pairs={{0,2},{2,0},{1,3},{3,1},{4,6},{6,4},{5,7},{7,5},{8,10},{10,8},{9,1... | collective-permute-start | bytes 98312 | tf_op jit(solution)/shard_map/ppermute | solution.py:263
  50.7 9.5 %collective-permute-start.4 = (bf16[132,8,128]{2,1,0:T(8,128)(2,1)}, bf16[132,8,128]{2,1,0:T(8,128)(2,1)S(1)}, u32[]{:S(2)}, u32[]{:S(2)}) collective-permute-start(bf16[132,8,128]{2,1,0:T(8,128)(2,1)} %get-tuple-element.32), channel_id=1, source_target_pairs={{0,2},{2,0},{1,3},{3,1},{4,6},{6,4},{5,7},{7,5},{8,10},{10,8},{9,1... | collective-permute-start | bytes 811016 | tf_op jit(solution)/shard_map/ppermute | solution.py:203
  52.3 1.0 %copy-start.5 = (bf16[132,8,128]{2,1,0:T(8,128)(2,1)S(1)}, bf16[132,8,128]{2,1,0:T(8,128)(2,1)}, u32[]{:S(2)}) copy-start(bf16[132,8,128]{2,1,0:T(8,128)(2,1)} %get-tuple-element.33) | copy-start | bytes 811012
  53.3 17.7 %collective-permute-start.5 = (bf16[132,8,128]{2,1,0:T(8,128)(2,1)S(1)}, bf16[132,8,128]{2,1,0:T(8,128)(2,1)S(1)}, u32[]{:S(2)}, u32[]{:S(2)}) collective-permute-start(bf16[132,8,128]{2,1,0:T(8,128)(2,1)S(1)} %copy-done.5), channel_id=1, source_target_pairs={{0,2},{2,0},{1,3},{3,1},{4,6},{6,4},{5,7},{7,5},{8,10},{10,8},{9,1... | collective-permute-start | bytes 811016 | tf_op jit(solution)/shard_map/ppermute | solution.py:203
  69.4 6.9 %collective-permute-start.6 = (bf16[132,8,128]{2,1,0:T(8,128)(2,1)S(1)}, bf16[132,8,128]{2,1,0:T(8,128)(2,1)S(1)}, u32[]{:S(2)}, u32[]{:S(2)}) collective-permute-start(bf16[132,8,128]{2,1,0:T(8,128)(2,1)S(1)} %slice.225), channel_id=1, source_target_pairs={{0,2},{2,0},{1,3},{3,1},{4,6},{6,4},{5,7},{7,5},{8,10},{10,8},{9,1... | collective-permute-start | bytes 811016 | tf_op jit(solution)/shard_map/ppermute | solution.py:210
  81.0 6.5 %collective-permute-start.7 = (bf16[132,8,128]{2,1,0:T(8,128)(2,1)S(1)}, bf16[132,8,128]{2,1,0:T(8,128)(2,1)S(1)}, u32[]{:S(2)}, u32[]{:S(2)}) collective-permute-start(bf16[132,8,128]{2,1,0:T(8,128)(2,1)S(1)} %slice.227), channel_id=1, source_target_pairs={{0,2},{2,0},{1,3},{3,1},{4,6},{6,4},{5,7},{7,5},{8,10},{10,8},{9,1... | collective-permute-start | bytes 811016 | tf_op jit(solution)/shard_map/ppermute | solution.py:210
  88.0 1.9 %copy-start.1 = (bf16[4,33,33]{2,0,1:T(4,128)(2,1)S(1)}, bf16[4,33,33]{2,0,1:T(4,128)(2,1)}, u32[]{:S(2)}) copy-start(bf16[4,33,33]{2,0,1:T(4,128)(2,1)} %param.23) | copy-start | bytes 26140

commit v18 on v17

--- a/solution.py
+++ b/solution.py
@@ -191,7 +191,7 @@
     return coupling_table(order, kernel_index, collision_kernels)
 
 
-def paired_collision(grown, table):
+def paired_collision(grown, table, open_cells):
     local_bins, width_x, width_z, width_y = grown.shape
     swap = [(0, 1), (1, 0)]
     me = lax.axis_index("bins")
@@ -209,9 +209,18 @@
         change = change.reshape(2 * local_bins, width_z, width_y)
         returned.append(lax.ppermute(change[local_bins:], "bins", swap))
         kept.append(change[:local_bins])
+    hx = width_x // 2
+    waiting = returned[-1]
+    returned[-1] = jnp.zeros_like(waiting)
     pair = jnp.stack([jnp.stack(kept, axis=1), jnp.stack(returned, axis=1)], axis=1)
     pair = jnp.where(me == 0, pair, pair[:, ::-1])
-    return pair.reshape(local_bins, width_x, width_z, width_y).astype(jnp.float32)
+    change = pair.reshape(local_bins, width_x, width_z, width_y).astype(jnp.float32)
+    early = (grown + change) * open_cells
+    last = (1 - me) * hx + hx - 1
+    late = (
+        lax.dynamic_index_in_dim(grown, last, axis=1) + waiting[:, None].astype(jnp.float32)
+    ) * lax.dynamic_index_in_dim(open_cells, last, axis=0)
+    return lax.dynamic_update_slice_in_dim(early, late, last, axis=1)
 
 
 def body(
@@ -269,10 +278,10 @@
     temp_next = potential_temp + heating_gain * midway * heating
     vapor_next = supersaturation * jnp.exp(-condense_rate * uptake)
     if paired:
-        change = paired_collision(grown, table)
+        mass_next = paired_collision(grown, table, open_cells)
     else:
         change = spread_collision(grown, bin_order, kernel_index, collision_kernels)
-    mass_next = (grown + change) * open_cells
+        mass_next = (grown + change) * open_cells
     return (mass_next, temp_next, vapor_next)
 
 

time: 90.1 us -> 91.6 us (1.017)
  local copies, waits for them, and re-layouts: 5.61 us -> 7 us
  other arithmetic: 10.9 us -> 12 us
    convert_element_type x1, other arithmetic: 0.38 us -> 2 us  [paired_collision(): grown.astype(jnp.bfloat16)]
    mul x1, other arithmetic: 1.84 us -> 0.4 us  [paired_collision(): early = (grown + change) * open_cells]
    unnamed x45 -> x47, local copies, waits for them, and re-layouts: 2.32 us -> 3.65 us
  transfers between devices with their start and end apart: 8 -> 8, of which waited for: 7 -> 7; matrix products, arithmetic and copies ran while one was open for 23% -> 24% of each run, Pallas kernels for 0% -> 0%
where the time goes in v18:
time: 91.6 us; the launch traced here: 91.3 us
  waiting for transfers between devices  29.8 us (33%)
  matrix products  16.4 us (18%)
  starting transfers between devices  14.2 us (16%)
  other arithmetic  12 us (13%)
  Pallas kernels  10.8 us (12%)
  local copies, waits for them, and re-layouts  7 us (8%)
  between operations  1.21 us (1%)
    ppermute x2, waiting for transfers between devices, advect_kernel_call(): lax.ppermute(message, 'tiles', pairs)  16 us
    dot_general x16, matrix products, collide(): jnp.dot(table, iterate.astype(jnp.bfloat16), preferred_element_type=jnp.f...  12.6 us
    pallas_call x1, Pallas kernels, advect_kernel_call(): pl.pallas_call(functools.partial(advect_kernel, section_weights), out_sha...  7.84 us
    ppermute x2, waiting for transfers between devices, paired_collision(): arrived = lax.ppermute(away[:, chunk], 'bins', swap)  6.48 us
    ppermute x2, starting transfers between devices, advect_kernel_call(): lax.ppermute(message, 'tiles', pairs)  6.26 us
    ppermute x2, waiting for transfers between devices, paired_collision(): returned.append(lax.ppermute(change[local_bins:], 'bins', swap))  4.56 us
    add x6, other arithmetic, collide(): iterate + collision_rate * products[all_bins:] * products[:all_bins]  3.9 us
    unnamed x47, local copies, waits for them, and re-layouts  3.65 us
  transfers between devices with their start and end apart: 8, of which 7 were waited for; matrix products, arithmetic and copies ran while one was open for 24% of the time, Pallas kernels for 0%

profile of v18, /device:TPU:0, one launch (start us, length us, event | category | flops | bytes accessed | tf_op | source)
XLA Modules:
  0.0 91.3 jit_solution(2269269395482211685)
XLA Ops:
  0.7 2.9 %shard_map.139 = (bf16[136,3,8,128]{3,2,1,0:T(8,128)(2,1)}, bf16[136,3,8,128]{3,2,1,0:T(8,128)(2,1)}) custom-call(f32[132,4,8,128]{3,2,1,0:T(8,128)} %q_ref.3, f32[4,8,128]{2,1,0:T(8,128)} %east_ref.1, f32[4,8,128]{2,1,0:T(8,128)} %north_ref.1, s32[4,128]{1,0:T(4,128)} %terrain_ref.1), custom_call_target="tpu_custom_call" | custom-call | tf_op jit(solution)/shard_map/pallas_call | solution.py:51
  3.6 5.0 %collective-permute-start = (bf16[136,3,8,128]{3,2,1,0:T(8,128)(2,1)}, bf16[136,3,8,128]{3,2,1,0:T(8,128)(2,1)S(1)}, u32[]{:S(2)}, u32[]{:S(2)}) collective-permute-start(bf16[136,3,8,128]{3,2,1,0:T(8,128)(2,1)} %get-tuple-element.11), channel_id=1, source_target_pairs={{0,4},{4,8},{8,12},{1,5},{5,9},{9,13},{2,6},{6,10},{10,14},{3,7},{... | collective-permute-start | bytes 2506760 | tf_op jit(solution)/shard_map/ppermute | solution.py:98
  8.6 1.3 %collective-permute-start.1 = (bf16[136,3,8,128]{3,2,1,0:T(8,128)(2,1)}, bf16[136,3,8,128]{3,2,1,0:T(8,128)(2,1)S(1)}, u32[]{:S(2)}, u32[]{:S(2)}) collective-permute-start(bf16[136,3,8,128]{3,2,1,0:T(8,128)(2,1)} %get-tuple-element.13), channel_id=1, source_target_pairs={{4,0},{8,4},{12,8},{5,1},{9,5},{13,9},{6,2},{10,6},{14,10},{7,3},{... | collective-permute-start | bytes 2506760 | tf_op jit(solution)/shard_map/ppermute | solution.py:98
  10.5 2.0 %multiply_reduce_fusion = f32[264,8,33]{0,2,1:T(8,128)S(1)} fusion(f32[264,8]{0,1:T(8,128)S(1)} %fusion.67, f32[8,8,33,33]{3,1,2,0:T(8,128)S(1)} %fusion.58, s32[264]{0:T(512)S(1)} %get-tuple-element.37), kind=kOutput, calls=%fused_computation | convolution fusion | flops 221851072 | bytes 567072 | tf_op jit(solution)/shard_map/bm,acmn->bacn/dot_general | solution.py:153
  12.8 1.1 %fusion.3 = bf16[264,264]{0,1:T(8,128)(2,1)S(1)} fusion(f32[264,8,33]{0,2,1:T(8,128)S(1)} %multiply_reduce_fusion, f32[264,8]{0,1:T(8,128)S(1)} %fusion.67, f32[264,33]{0,1:T(8,128)S(1)} %fusion.55), kind=kOutput, calls=%fused_computation.16 | convolution fusion | flops 220936320 | bytes 461472 | tf_op jit(solution)/shard_map/bcn,dc,dn->bd/dot_general | solution.py:155
  14.1 0.7 compare_select_fusion
  14.8 11.9 %collective-permute-done.left_ref.refs_0_.refs_1_.refs_2_.refs_3_ = bf16[136,3,8,128]{3,2,1,0:T(8,128)(2,1)S(1)} collective-permute-done((bf16[136,3,8,128]{3,2,1,0:T(8,128)(2,1)}, bf16[136,3,8,128]{3,2,1,0:T(8,128)(2,1)S(1)}, u32[]{:S(2)}, u32[]{:S(2)}) %collective-permute-start) | collective-permute-done | bytes 835616 | tf_op jit(solution)/shard_map/ppermute | solution.py:98
  26.7 4.1 %collective-permute-done.1.right_ref.refs_4_.refs_5_.refs_6_.refs_7_ = bf16[136,3,8,128]{3,2,1,0:T(8,128)(2,1)S(1)} collective-permute-done((bf16[136,3,8,128]{3,2,1,0:T(8,128)(2,1)}, bf16[136,3,8,128]{3,2,1,0:T(8,128)(2,1)S(1)}, u32[]{:S(2)}, u32[]{:S(2)}) %collective-permute-start.1) | collective-permute-done | bytes 835616 | tf_op jit(solution)/shard_map/ppermute | solution.py:98
  30.7 0.9 %copy-done.3 = bf16[136,3,8,128]{3,2,1,0:T(8,128)(2,1)} copy-done((bf16[136,3,8,128]{3,2,1,0:T(8,128)(2,1)}, bf16[136,3,8,128]{3,2,1,0:T(8,128)(2,1)S(1)}, u32[]{:S(2)}) %copy-start.3) | copy-done | bytes 835608
  31.7 7.8 %shard_map.140 = (f32[132,4,8,128]{3,2,1,0:T(8,128)}, f32[132,4,1,128]{3,2,1,0:T(1,128)}) custom-call(f32[132,4,8,128]{3,2,1,0:T(8,128)} %q_ref.3, bf16[136,3,8,128]{3,2,1,0:T(8,128)(2,1)} %copy-done.2, bf16[136,3,8,128]{3,2,1,0:T(8,128)(2,1)} %copy-done.3, bf16[136,3,8,128]{3,2,1,0:T(8,128)(2,1)} %copy-done.2, bf16[136,3,8,128]{3,2,1,0:T(8,128)(2,1)} %copy-done.2, ...), custom_call_target="tpu_custom_call" | custom-call | flops 43253760 | bytes 10813440 | tf_op jit(solution)/shard_map/pallas_call | solution.py:111
  39.5 1.3 %collective-permute-start.2 = (f32[132,4,1,128]{3,2,1,0:T(1,128)}, f32[132,4,1,128]{3,2,1,0:T(1,128)S(1)}, u32[]{:S(2)}, u32[]{:S(2)}) collective-permute-start(f32[132,4,1,128]{3,2,1,0:T(1,128)} %get-tuple-element.15), channel_id=1, source_target_pairs={{1,0},{3,2},{5,4},{7,6},{9,8},{11,10},{13,12},{15,14},{17,16},{19,... | collective-permute-start | bytes 811016 | tf_op jit(solution)/shard_map/ppermute | solution.py:126
  40.9 2.0 %slice.137 = f32[132,4,7,128]{3,2,1,0:T(8,128)S(1)} slice(f32[132,4,8,128]{3,2,1,0:T(8,128)} %get-tuple-element.14), slice={[0:132], [0:4], [1:8], [0:128]} | slice | bytes 3784704 | tf_op jit(solution)/shard_map/slice | solution.py:261
  43.2 2.0 %multiply_reduce_fusion.1 = (f32[4,8,128]{2,1,0:T(8,128)S(1)}, f32[4,8,128]{2,1,0:T(8,128)S(1)}, f32[132,4,8,128]{3,2,1,0:T(8,128)}) fusion(f32[132]{0:T(256)S(1)} %get-tuple-element.42, f32[132]{0:T(256)S(1)} %copy-done.14, f32[132,4,1,128]{3,2,1,0:T(1,128)S(1)} %collective-permute-done.2, f32[132,4,7,128]{3,2,1,0:T(8,128)S(1)} %slice.137, ...), kind=kLoop, calls=%fused_computation.6 | loop fusion | flops 4317184 | bytes 6522944 | tf_op jit(solution)/shard_map/reduce_sum | solution.py:267
  45.2 1.5 %collective-permute-start.3 = (f32[2,4,8,128]{3,2,1,0:T(8,128)S(1)}, f32[2,4,8,128]{3,2,1,0:T(8,128)S(1)}, u32[]{:S(2)}, u32[]{:S(2)}) collective-permute-start(f32[2,4,8,128]{3,2,1,0:T(8,128)S(1)} %pad_maximum_fusion.6), channel_id=1, source_target_pairs={{0,2},{2,0},{1,3},{3,1},{4,6},{6,4},{5,7},{7,5},{8,10},{10,8},{9,1... | collective-permute-start | bytes 98312 | tf_op jit(solution)/shard_map/ppermute | solution.py:272
  46.8 2.6 %collective-permute-done.3 = f32[2,4,8,128]{3,2,1,0:T(8,128)S(1)} collective-permute-done((f32[2,4,8,128]{3,2,1,0:T(8,128)S(1)}, f32[2,4,8,128]{3,2,1,0:T(8,128)S(1)}, u32[]{:S(2)}, u32[]{:S(2)}) %collective-permute-start.3) | collective-permute-done | bytes 32800 | tf_op jit(solution)/shard_map/ppermute | solution.py:272
  49.4 0.6 fusion.63
  50.0 2.0 %fusion.79 = (bf16[132,4,8,128]{3,2,1,0:T(8,128)(2,1)S(1)}, f32[132,4,8,128]{3,2,1,0:T(8,128)S(1)}) fusion(f32[132,4,8,128]{3,2,1,0:T(8,128)} %get-tuple-element.25, f32[4,8,128]{2,1,0:T(8,128)S(1)} %get-tuple-element.22, f32[132]{0:T(256)S(1)} %get-tuple-element.41), kind=kLoop, calls=%fused_computation.151 | loop fusion | flops 2162688 | bytes 5423632 | tf_op jit(solution)/shard_map/convert_element_type | solution.py:198
  52.2 0.8 slice_bitcast_fusion.2
  53.0 1.5 %collective-permute-start.4 = (bf16[132,8,128]{2,1,0:T(8,128)(2,1)}, bf16[132,8,128]{2,1,0:T(8,128)(2,1)S(1)}, u32[]{:S(2)}, u32[]{:S(2)}) collective-permute-start(bf16[132,8,128]{2,1,0:T(8,128)(2,1)} %get-tuple-element.34), channel_id=1, source_target_pairs={{0,2},{2,0},{1,3},{3,1},{4,6},{6,4},{5,7},{7,5},{8,10},{10,8},{9,1... | collective-permute-start | bytes 811016 | tf_op jit(solution)/shard_map/ppermute | solution.py:203
  54.6 0.8 copy-done.6
  56.1 6.5 %collective-permute-done.4 = bf16[132,8,128]{2,1,0:T(8,128)(2,1)S(1)} collective-permute-done((bf16[132,8,128]{2,1,0:T(8,128)(2,1)}, bf16[132,8,128]{2,1,0:T(8,128)(2,1)S(1)}, u32[]{:S(2)}, u32[]{:S(2)}) %collective-permute-start.4) | collective-permute-done | bytes 270368 | tf_op jit(solution)/shard_map/ppermute | solution.py:203
  62.6 0.8 fusion.54
  63.4 0.8 fusion.48
  64.8 0.8 fusion.46
  65.6 0.8 fusion.44
  66.4 0.7 fusion.17
  67.1 0.8 fusion.42
  67.8 0.8 fusion.40
  68.7 0.6 fusion.15
  69.3 0.8 fusion.38
  70.0 0.8 fusion.36
  70.8 0.7 fusion.4
  71.7 1.6 %collective-permute-start.6 = (bf16[132,8,128]{2,1,0:T(8,128)(2,1)S(1)}, bf16[132,8,128]{2,1,0:T(8,128)(2,1)S(1)}, u32[]{:S(2)}, u32[]{:S(2)}) collective-permute-start(bf16[132,8,128]{2,1,0:T(8,128)(2,1)S(1)} %slice.225), channel_id=1, source_target_pairs={{0,2},{2,0},{1,3},{3,1},{4,6},{6,4},{5,7},{7,5},{8,10},{10,8},{9,1... | collective-permute-start | bytes 811016 | tf_op jit(solution)/shard_map/ppermute | solution.py:210
  73.3 0.8 fusion.53
  74.1 0.8 fusion.34
  74.9 0.6 fusion.12
  75.5 0.8 fusion.32
  76.3 0.8 fusion.30
  77.2 0.9 fusion.10
  78.6 0.8 fusion.28
  79.4 0.8 fusion.26
  80.2 0.6 fusion.8
  80.8 0.8 fusion.24
  81.6 0.8 fusion.22
  82.4 0.7 fusion.5
  83.4 1.5 %collective-permute-start.7 = (bf16[132,8,128]{2,1,0:T(8,128)(2,1)S(1)}, bf16[132,8,128]{2,1,0:T(8,128)(2,1)S(1)}, u32[]{:S(2)}, u32[]{:S(2)}) collective-permute-start(bf16[132,8,128]{2,1,0:T(8,128)(2,1)S(1)} %slice.227), channel_id=1, source_target_pairs={{0,2},{2,0},{1,3},{3,1},{4,6},{6,4},{5,7},{7,5},{8,10},{10,8},{9,1... | collective-permute-start | bytes 811016 | tf_op jit(solution)/shard_map/ppermute | solution.py:210
  85.9 4.0 %collective-permute-done.7 = bf16[132,8,128]{2,1,0:T(8,128)(2,1)S(1)} collective-permute-done((bf16[132,8,128]{2,1,0:T(8,128)(2,1)S(1)}, bf16[132,8,128]{2,1,0:T(8,128)(2,1)S(1)}, u32[]{:S(2)}, u32[]{:S(2)}) %collective-permute-start.7) | collective-permute-done | bytes 270368 | tf_op jit(solution)/shard_map/ppermute | solution.py:210
  90.0 1.3 %copy-done.5 = f32[132,4,8,128]{3,2,1,0:T(8,128)} copy-done((f32[132,4,8,128]{3,2,1,0:T(8,128)}, f32[132,4,8,128]{3,2,1,0:T(8,128)S(1)}, u32[]{:S(2)}) %copy-start.5) | copy-done | bytes 2162712
  (74 shorter events, 4.9 us)
Async XLA Ops:
  0.6 9.5 %copy-start = (bf16[4,33,33]{2,0,1:T(4,128)(2,1)S(1)}, bf16[4,33,33]{2,0,1:T(4,128)(2,1)}, u32[]{:S(2)}) copy-start(bf16[4,33,33]{2,0,1:T(4,128)(2,1)} %param.23) | copy-start | bytes 26140
  0.6 9.2 %copy-start.15 = (s32[264]{0:T(512)S(1)}, s32[264]{0:T(512)}, u32[]{:S(2)}) copy-start(s32[264]{0:T(512)} %param.21) | copy-start | bytes 3172
  0.7 9.4 %copy-start.12 = (s32[8,8]{1,0:T(8,128)S(1)}, s32[8,8]{1,0:T(8,128)}, u32[]{:S(2)}) copy-start(s32[8,8]{1,0:T(8,128)} %param.22) | copy-start | bytes 772
  3.6 23.1 %collective-permute-start = (bf16[136,3,8,128]{3,2,1,0:T(8,128)(2,1)}, bf16[136,3,8,128]{3,2,1,0:T(8,128)(2,1)S(1)}, u32[]{:S(2)}, u32[]{:S(2)}) collective-permute-start(bf16[136,3,8,128]{3,2,1,0:T(8,128)(2,1)} %get-tuple-element.11), channel_id=1, source_target_pairs={{0,4},{4,8},{8,12},{1,5},{5,9},{9,13},{2,6},{6,10},{10,14},{3,7},{... | collective-permute-start | bytes 2506760 | tf_op jit(solution)/shard_map/ppermute | solution.py:98
  8.6 22.2 %collective-permute-start.1 = (bf16[136,3,8,128]{3,2,1,0:T(8,128)(2,1)}, bf16[136,3,8,128]{3,2,1,0:T(8,128)(2,1)S(1)}, u32[]{:S(2)}, u32[]{:S(2)}) collective-permute-start(bf16[136,3,8,128]{3,2,1,0:T(8,128)(2,1)} %get-tuple-element.13), channel_id=1, source_target_pairs={{4,0},{8,4},{12,8},{5,1},{9,5},{13,9},{6,2},{10,6},{14,10},{7,3},{... | collective-permute-start | bytes 2506760 | tf_op jit(solution)/shard_map/ppermute | solution.py:98
  12.5 1.6 %copy-start.7 = (f32[4,8,128]{2,1,0:T(8,128)S(1)}, f32[4,8,128]{2,1,0:T(8,128)}, u32[]{:S(2)}) copy-start(f32[4,8,128]{2,1,0:T(8,128)} %east_ref.1) | copy-start | bytes 49156
  12.5 1.6 %copy-start.8 = (f32[4,8,128]{2,1,0:T(8,128)S(1)}, f32[4,8,128]{2,1,0:T(8,128)}, u32[]{:S(2)}) copy-start(f32[4,8,128]{2,1,0:T(8,128)} %north_ref.1) | copy-start | bytes 49156
  12.5 1.6 %copy-start.9 = (s32[4,128]{1,0:T(4,128)S(1)}, s32[4,128]{1,0:T(4,128)}, u32[]{:S(2)}) copy-start(s32[4,128]{1,0:T(4,128)} %terrain_ref.1) | copy-start | bytes 6148
  26.7 4.1 %copy-start.2 = (bf16[136,3,8,128]{3,2,1,0:T(8,128)(2,1)}, bf16[136,3,8,128]{3,2,1,0:T(8,128)(2,1)S(1)}, u32[]{:S(2)}) copy-start(bf16[136,3,8,128]{3,2,1,0:T(8,128)(2,1)S(1)} %collective-permute-done.left_ref.refs_0_.refs_1_.refs_2_.refs_3_) | copy-start | bytes 2506756
  30.7 0.9 %copy-start.3 = (bf16[136,3,8,128]{3,2,1,0:T(8,128)(2,1)}, bf16[136,3,8,128]{3,2,1,0:T(8,128)(2,1)S(1)}, u32[]{:S(2)}) copy-start(bf16[136,3,8,128]{3,2,1,0:T(8,128)(2,1)S(1)} %collective-permute-done.1.right_ref.refs_4_.refs_5_.refs_6_.refs_7_) | copy-start | bytes 2506756
  31.7 9.1 %copy-start.13 = (f32[132]{0:T(256)S(1)}, f32[132]{0:T(256)}, u32[]{:S(2)}) copy-start(f32[132]{0:T(256)} %param.18) | copy-start | bytes 1588
  31.7 9.2 %copy-start.14 = (f32[132]{0:T(256)S(1)}, f32[132]{0:T(256)}, u32[]{:S(2)}) copy-start(f32[132]{0:T(256)} %param.19) | copy-start | bytes 1588
  31.7 9.2 %copy-start.16 = (f32[132]{0:T(256)S(1)}, f32[132]{0:T(256)}, u32[]{:S(2)}) copy-start(f32[132]{0:T(256)} %param.20) | copy-start | bytes 1588
  39.5 3.6 %collective-permute-start.2 = (f32[132,4,1,128]{3,2,1,0:T(1,128)}, f32[132,4,1,128]{3,2,1,0:T(1,128)S(1)}, u32[]{:S(2)}, u32[]{:S(2)}) collective-permute-start(f32[132,4,1,128]{3,2,1,0:T(1,128)} %get-tuple-element.15), channel_id=1, source_target_pairs={{1,0},{3,2},{5,4},{7,6},{9,8},{11,10},{13,12},{15,14},{17,16},{19,... | collective-permute-start | bytes 811016 | tf_op jit(solution)/shard_map/ppermute | solution.py:126
  40.9 2.3 %copy-start.4 = (f32[132,4,8,128]{3,2,1,0:T(8,128)S(1)}, f32[132,4,8,128]{3,2,1,0:T(8,128)}, u32[]{:S(2)}) copy-start(f32[132,4,8,128]{3,2,1,0:T(8,128)} %get-tuple-element.14) | copy-start | bytes 6488068
  43.2 6.2 %copy-start.10 = (f32[4,8,128]{2,1,0:T(8,128)S(1)}, f32[4,8,128]{2,1,0:T(8,128)}, u32[]{:S(2)}) copy-start(f32[4,8,128]{2,1,0:T(8,128)} %param.16) | copy-start | bytes 49156
  43.2 6.2 %copy-start.11 = (f32[4,8,128]{2,1,0:T(8,128)S(1)}, f32[4,8,128]{2,1,0:T(8,128)}, u32[]{:S(2)}) copy-start(f32[4,8,128]{2,1,0:T(8,128)} %param.15) | copy-start | bytes 49156
  45.2 4.1 %collective-permute-start.3 = (f32[2,4,8,128]{3,2,1,0:T(8,128)S(1)}, f32[2,4,8,128]{3,2,1,0:T(8,128)S(1)}, u32[]{:S(2)}, u32[]{:S(2)}) collective-permute-start(f32[2,4,8,128]{3,2,1,0:T(8,128)S(1)} %pad_maximum_fusion.6), channel_id=1, source_target_pairs={{0,2},{2,0},{1,3},{3,1},{4,6},{6,4},{5,7},{7,5},{8,10},{10,8},{9,1... | collective-permute-start | bytes 98312 | tf_op jit(solution)/shard_map/ppermute | solution.py:272
  53.0 9.5 %collective-permute-start.4 = (bf16[132,8,128]{2,1,0:T(8,128)(2,1)}, bf16[132,8,128]{2,1,0:T(8,128)(2,1)S(1)}, u32[]{:S(2)}, u32[]{:S(2)}) collective-permute-start(bf16[132,8,128]{2,1,0:T(8,128)(2,1)} %get-tuple-element.34), channel_id=1, source_target_pairs={{0,2},{2,0},{1,3},{3,1},{4,6},{6,4},{5,7},{7,5},{8,10},{10,8},{9,1... | collective-permute-start | bytes 811016 | tf_op jit(solution)/shard_map/ppermute | solution.py:203
  54.5 1.0 %copy-start.6 = (bf16[132,8,128]{2,1,0:T(8,128)(2,1)S(1)}, bf16[132,8,128]{2,1,0:T(8,128)(2,1)}, u32[]{:S(2)}) copy-start(bf16[132,8,128]{2,1,0:T(8,128)(2,1)} %get-tuple-element.35) | copy-start | bytes 811012
  55.5 17.8 %collective-permute-start.5 = (bf16[132,8,128]{2,1,0:T(8,128)(2,1)S(1)}, bf16[132,8,128]{2,1,0:T(8,128)(2,1)S(1)}, u32[]{:S(2)}, u32[]{:S(2)}) collective-permute-start(bf16[132,8,128]{2,1,0:T(8,128)(2,1)S(1)} %copy-done.6), channel_id=1, source_target_pairs={{0,2},{2,0},{1,3},{3,1},{4,6},{6,4},{5,7},{7,5},{8,10},{10,8},{9,1... | collective-permute-start | bytes 811016 | tf_op jit(solution)/shard_map/ppermute | solution.py:203
  71.7 6.9 %collective-permute-start.6 = (bf16[132,8,128]{2,1,0:T(8,128)(2,1)S(1)}, bf16[132,8,128]{2,1,0:T(8,128)(2,1)S(1)}, u32[]{:S(2)}, u32[]{:S(2)}) collective-permute-start(bf16[132,8,128]{2,1,0:T(8,128)(2,1)S(1)} %slice.225), channel_id=1, source_target_pairs={{0,2},{2,0},{1,3},{3,1},{4,6},{6,4},{5,7},{7,5},{8,10},{10,8},{9,1... | collective-permute-start | bytes 811016 | tf_op jit(solution)/shard_map/ppermute | solution.py:210
  83.4 6.5 %collective-permute-start.7 = (bf16[132,8,128]{2,1,0:T(8,128)(2,1)S(1)}, bf16[132,8,128]{2,1,0:T(8,128)(2,1)S(1)}, u32[]{:S(2)}, u32[]{:S(2)}) collective-permute-start(bf16[132,8,128]{2,1,0:T(8,128)(2,1)S(1)} %slice.227), channel_id=1, source_target_pairs={{0,2},{2,0},{1,3},{3,1},{4,6},{6,4},{5,7},{7,5},{8,10},{10,8},{9,1... | collective-permute-start | bytes 811016 | tf_op jit(solution)/shard_map/ppermute | solution.py:210
  85.4 5.9 %copy-start.1 = (bf16[4,33,33]{2,0,1:T(4,128)(2,1)S(1)}, bf16[4,33,33]{2,0,1:T(4,128)(2,1)}, u32[]{:S(2)}) copy-start(bf16[4,33,33]{2,0,1:T(4,128)(2,1)} %param.23) | copy-start | bytes 26140
  90.0 1.3 %copy-start.5 = (f32[132,4,8,128]{3,2,1,0:T(8,128)}, f32[132,4,8,128]{3,2,1,0:T(8,128)S(1)}, u32[]{:S(2)}) copy-start(f32[132,4,8,128]{3,2,1,0:T(8,128)S(1)} %fusion.21) | copy-start | bytes 6488068
